TPU v7x, 32 devices: a whole 2x2x4 slice. The times are simulated.
32 devices in a mesh: ctx: 4 (over x, core), ep: 8 (over z, y).
Axes of the slice: x: 2, y: 2, z: 4, core: 2. Of those that a mesh axis runs over, the one named last changes fastest.
Arguments:
- query_latent: bfloat16 [1, 512, 128, 512], P(None, 'ctx', 'ep'), may hold values from -6 to 6
- query_rope: bfloat16 [1, 128, 64, 512], P(None, 'ep', None, 'ctx'), may hold values from -12 to 12
- key_latent: bfloat16 [1, 512, 512], P(None, 'ctx'), may hold values from -6 to 6
- key_rope: bfloat16 [1, 64, 512], P(None, None, 'ctx'), may hold values from -14 to 14
- output_grad: bfloat16 [1, 512, 128, 512], P(None, 'ctx', 'ep'), may hold values from -6 to 6
Outputs:
- attended: bfloat16 [1, 512, 128, 512], P(None, 'ctx', 'ep')
- query_latent_grad: bfloat16 [1, 512, 128, 512], P(None, 'ctx', 'ep')
- query_rope_grad: bfloat16 [1, 128, 64, 512], P(None, 'ep', None, 'ctx')
- key_latent_grad: bfloat16 [1, 512, 512], P(None, 'ctx')
- key_rope_grad: bfloat16 [1, 64, 512], P(None, None, 'ctx')
All inputs are finite; a program needn't handle non-finite values.
Results may differ from a plain program's by a relative error of at most 0.018.
Values may be sent and summed in bfloat16 or wider, within the bound.
No kernel may reach another device: no remote copies, remote signals or barrier semaphores. Data moves between devices by JAX's collectives and lax.ppermute only.
A program may use at most 64 MiB of HBM per device.

v0:
```python
import jax
import jax.numpy as jnp
from jax import lax
from jax.sharding import PartitionSpec as P

scale_factor = 192.0 ** (-0.5)


def body(query_latent, query_rope, key_latent, key_rope, output_grad):
    block_len = query_latent.shape[1]
    whole_latent, whole_rope = (
        lax.all_gather(key_latent, "ctx", axis=1, tiled=True),
        lax.all_gather(key_rope, "ctx", axis=2, tiled=True),
    )
    length = whole_latent.shape[1]
    offset = lax.axis_index("ctx") * block_len
    query_place = offset + jnp.arange(block_len, dtype=jnp.int32)
    allowed = jnp.arange(length, dtype=jnp.int32)[None, :] <= query_place[:, None]
    scores = jnp.einsum(
        "sthd,sjd->shtj", query_latent, whole_latent, preferred_element_type=jnp.float32
    )
    scores = scores + jnp.einsum(
        "shdt,sdj->shtj", query_rope, whole_rope, preferred_element_type=jnp.float32
    )
    scores = jnp.where(allowed, scores * scale_factor, jnp.float32(-1e30))
    row_max = jnp.max(scores, axis=-1, keepdims=True)
    powers = jnp.exp(scores - row_max)
    weights = powers / jnp.sum(powers, axis=-1, keepdims=True)
    rounded_weights = weights.astype(jnp.bfloat16)
    attended = jnp.einsum(
        "shtj,sjd->sthd", rounded_weights, whole_latent, preferred_element_type=jnp.float32
    ).astype(jnp.bfloat16)
    row_dots = jnp.einsum(
        "sthd,sthd->sht", output_grad, attended, preferred_element_type=jnp.float32
    )
    weight_grad = jnp.einsum(
        "sthd,sjd->shtj", output_grad, whole_latent, preferred_element_type=jnp.float32
    )
    score_grad = (weights * (weight_grad - row_dots[..., None])).astype(jnp.bfloat16)
    latent_qgrad = (
        scale_factor
        * jnp.einsum("shtj,sjd->sthd", score_grad, whole_latent, preferred_element_type=jnp.float32)
    ).astype(jnp.bfloat16)
    rope_qgrad = (
        scale_factor
        * jnp.einsum("shtj,sdj->shdt", score_grad, whole_rope, preferred_element_type=jnp.float32)
    ).astype(jnp.bfloat16)
    latent_term = scale_factor * jnp.einsum(
        "shtj,sthd->sjd", score_grad, query_latent, preferred_element_type=jnp.float32
    )
    latent_term = latent_term + jnp.einsum(
        "shtj,sthd->sjd", rounded_weights, output_grad, preferred_element_type=jnp.float32
    )
    rope_term = scale_factor * jnp.einsum(
        "shtj,shdt->sdj", score_grad, query_rope, preferred_element_type=jnp.float32
    )
    latent_part, rope_part = (
        lax.psum_scatter(
            latent_term.astype(jnp.bfloat16), "ctx", scatter_dimension=1, tiled=True
        ).astype(jnp.float32),
        lax.psum_scatter(
            rope_term.astype(jnp.bfloat16), "ctx", scatter_dimension=2, tiled=True
        ).astype(jnp.float32),
    )
    latent_total, rope_total = (
        lax.psum(latent_part.astype(jnp.bfloat16), "ep").astype(jnp.float32),
        lax.psum(rope_part.astype(jnp.bfloat16), "ep").astype(jnp.float32),
    )
    latent_kgrad = latent_total.astype(jnp.bfloat16)
    rope_kgrad = rope_total.astype(jnp.bfloat16)
    return (attended, latent_qgrad, rope_qgrad, latent_kgrad, rope_kgrad)


def solution(mesh):
    placed = (
        P(None, "ctx", "ep", None),
        P(None, "ep", None, "ctx"),
        P(None, "ctx", None),
        P(None, None, "ctx"),
        P(None, "ctx", "ep", None),
    )
    return jax.shard_map(
        body,
        mesh=mesh,
        in_specs=placed,
        out_specs=(
            P(None, "ctx", "ep", None),
            P(None, "ctx", "ep", None),
            P(None, "ep", None, "ctx"),
            P(None, "ctx", None),
            P(None, None, "ctx"),
        ),
        check_vma=False,
    )
```

profile of v0, /device:TPU:0, one launch (start us, length us, event | category | flops | bytes accessed | tf_op | source)
XLA Modules:
  0.0 172.1 jit_solution(7928292447915737085)
XLA Ops:
  7.2 0.0 copy-start
  7.2 0.0 reduce-scatter.5.cloned.1.call-start
  7.2 9.0 %all_gather.6 = bf16[1,512,512]{2,1,0:T(8,128)(2,1)S(1)} all-gather(bf16[1,128,512]{2,1,0:T(8,128)(2,1)} %param.7), channel_id=1, replica_groups=mesh['ctx'=4,'ep'=8] {'ctx'}, dimensions={1}, use_global_device_ids=true | all-gather | bytes 655360 | tf_op jit(solution)/shard_map/all_gather | solution.py:12
  16.2 5.5 %all_gather.7 = bf16[1,64,512]{2,1,0:T(8,128)(2,1)S(1)} all-gather(bf16[1,64,128]{2,1,0:T(8,128)(2,1)} %param.8), channel_id=1, replica_groups=mesh['ctx'=4,'ep'=8] {'ctx'}, dimensions={2}, use_global_device_ids=true | all-gather | bytes 81920 | tf_op jit(solution)/shard_map/all_gather | solution.py:13
  21.7 0.1 iota_compare_fusion
  21.7 0.0 copy-done
  21.7 0.0 copy-start.7
  21.7 2.8 %fusion.23 = f32[512,128,16]{1,0,2:T(8,128)S(1)} fusion(bf16[128,16,512]{2,1,0:T(8,128)(2,1)S(1)} %bitcast.149, bf16[1,512,512]{2,1,0:T(8,128)(2,1)S(1)} %all_gather.6), kind=kOutput, calls=%fused_computation.26 | convolution fusion | flops 1073741824 | bytes 6815744 | tf_op jit(solution)/shard_map/sthd,sjd->shtj/dot_general | solution.py:19
  24.5 0.0 copy-done.7
  24.6 0.9 fusion.90
  25.5 0.0 copy-start.2
  25.5 0.6 fusion.5
  26.1 0.0 copy-start.4
  26.1 2.6 %fusion.91 = (f32[16,128,512]{2,1,0:T(8,128)S(1)}, bf16[16,128,512]{2,1,0:T(8,128)(2,1)}) fusion(bf16[1,512,512]{2,1,0:T(8,128)(2,1)S(1)} %all_gather.6, f32[16,128]{1,0:T(8,128)S(1)} %fusion.5, f32[1,16,128,512]{2,3,1,0:T(8,128)S(1)} %get-tuple-element.16, f32[16,128]{1,0:T(8,128)S(1)} %get-tuple-element.15), kind=kOutput, calls=%fused_computation.56 | convolution fusion | flops 1078984704 | bytes 11026432 | tf_op jit(solution)/shard_map/shtj,sjd->sthd/dot_general | solution.py:30
  28.7 0.0 copy-done.2
  28.7 0.2 copy-done.4
  28.9 2.4 %multiply_reduce_fusion = f32[16,128]{0,1:T(8,128)S(1)} fusion(f32[16,128,512]{2,1,0:T(8,128)S(1)} %get-tuple-element.17, bf16[1,128,16,512]{3,2,1,0:T(8,128)(2,1)S(1)} %copy-done.4), kind=kLoop, calls=%fused_computation.6 | loop fusion | flops 3143680 | bytes 6299648
  31.3 0.1 copy.40
  31.4 0.0 copy-start.3
  31.4 0.0 copy-start.5
  31.4 5.8 %fusion.28 = f32[512,512]{1,0:T(8,128)S(1)} fusion(bf16[128,16,512]{2,1,0:T(8,128)(2,1)} %bitcast.151, f32[16,128]{1,0:T(8,128)S(1)} %fusion.5, f32[1,16,128,512]{2,3,1,0:T(8,128)} %copy-done.2, f32[16,128]{1,0:T(8,128)S(1)} %get-tuple-element.15), kind=kOutput, calls=%fused_computation.29 | convolution fusion | flops 1076887552 | bytes 7356416 | tf_op jit(solution)/shard_map/shtj,sthd->sjd/dot_general | solution.py:51
  37.2 0.0 copy-done.3
  37.2 0.0 copy-done.5
  37.2 3.6 %fusion.1 = bf16[1,16,128,512]{2,3,1,0:T(8,128)(2,1)S(1)} fusion(f32[16,128]{1,0:T(8,128)S(1)} %copy.40, bf16[128,16,512]{2,1,0:T(8,128)(2,1)S(1)} %bitcast.152, f32[16,128]{1,0:T(8,128)S(1)} %fusion.5, f32[1,16,128,512]{2,3,1,0:T(8,128)S(1)} %copy-done.3, f32[16,128]{1,0:T(8,128)S(1)} %get-tuple-element.15, bf16[1,512,512]{2,1,0:T(8,128)(2,1)S(1)} %all_gather.6), kind=kOutput, calls=%fused_computation.2 | convolution fusion | flops 1078984704 | bytes 8937472 | tf_op jit(solution)/shard_map/sthd,sjd->shtj/dot_general | solution.py:36
  40.8 0.0 copy-start.1
  40.8 1.3 copy-done.1
  42.1 3.4 %fusion.53 = bf16[1,512,512]{2,1,0:T(8,128)(2,1)} fusion(f32[512,512]{1,0:T(8,128)S(1)} %fusion.28, bf16[128,16,512]{2,1,0:T(8,128)(2,1)S(1)} %bitcast.150, bf16[1,16,128,512]{2,3,1,0:T(8,128)(2,1)S(1)} %fusion.1), kind=kOutput, calls=%fused_computation.34 | convolution fusion | flops 1074528256 | bytes 5767168 | tf_op jit(solution)/shard_map/shtj,sthd->sjd/dot_general | solution.py:48
  45.5 0.0 reduce-scatter.5.cloned.1.call-update
  45.5 0.0 reduce-scatter.7.cloned.1.call-start
  45.6 2.3 %fusion.77 = bf16[1,64,512]{2,1,0:T(8,128)(2,1)S(1)} fusion(bf16[1,16,128,512]{2,3,1,0:T(8,128)(2,1)} %copy-done.1, bf16[1,16,64,128]{3,2,1,0:T(8,128)(2,1)S(1)} %copy-done.7), kind=kOutput, calls=%fused_computation.42 | convolution fusion | flops 134283264 | bytes 2424832 | tf_op jit(solution)/shard_map/shtj,shdt->sdj/dot_general | solution.py:54
  47.9 0.2 copy.44
  48.1 0.7 copy.69
  48.8 0.0 reduce-scatter.7.cloned.1.call-update
  48.8 0.0 all-reduce.2.cloned.1.call-start
  48.9 4.2 %fusion.25 = bf16[1,128,16,512]{3,1,2,0:T(8,128)(2,1)} fusion(bf16[1,16,128,512]{2,3,1,0:T(8,128)(2,1)} %copy-done.1, bf16[1,512,512]{2,1,0:T(8,128)(2,1)S(1)} %all_gather.6), kind=kOutput, calls=%fused_computation.28 | convolution fusion | flops 1075838976 | bytes 4718592 | tf_op jit(solution)/shard_map/shtj,sjd->sthd/dot_general | solution.py:42
  53.1 15.1 %reduce-scatter.5.cloned.1.call-done = bf16[1,128,512]{2,1,0:T(8,128)(2,1)} async-done(((bf16[1,512,512]{2,1,0:T(8,128)(2,1)}), bf16[1,128,512]{2,1,0:T(8,128)(2,1)}) %reduce-scatter.5.cloned.1.call-update) | async-done | bytes 131088 | tf_op jit(solution)/shard_map/reduce_scatter | solution.py:58
  68.2 0.0 all-reduce.2.cloned.1.call-update
  68.3 0.0 copy-start.6
  68.3 2.9 %fusion.65 = bf16[1,16,64,128]{3,2,1,0:T(8,128)(2,1)} fusion(bf16[1,16,128,512]{2,3,1,0:T(8,128)(2,1)} %copy-done.1, bf16[1,64,512]{2,1,0:T(8,128)(2,1)S(1)} %all_gather.7), kind=kOutput, calls=%fused_computation.38 | convolution fusion | flops 134479872 | bytes 2424832 | tf_op jit(solution)/shard_map/shtj,sdj->shdt/dot_general | solution.py:46
  71.2 4.1 %copy.31 = bf16[1,128,16,512]{3,2,1,0:T(8,128)(2,1)} copy(bf16[1,128,16,512]{3,1,2,0:T(8,128)(2,1)} %fusion.25) | data formatting | bytes 4194304
  75.3 0.0 copy-done.6
  75.3 2.5 %copy.30 = bf16[1,128,16,512]{3,2,1,0:T(8,128)(2,1)} copy(bf16[1,128,16,512]{3,1,2,0:T(8,128)(2,1)S(1)} %bitcast.153) | data formatting | bytes 4194304
  77.8 13.2 %reduce-scatter.7.cloned.1.call-done = bf16[128,64]{1,0:T(8,128)(2,1)} async-done(((bf16[512,64]{1,0:T(8,128)(2,1)}), bf16[128,64]{1,0:T(8,128)(2,1)}) %reduce-scatter.7.cloned.1.call-update) | async-done | bytes 16400
  91.0 0.8 reshape_bitcast_fusion
  91.8 0.1 copy.45
  91.9 37.7 %psum.15 = bf16[1,64,128]{2,1,0:T(8,128)(2,1)} all-reduce(bf16[1,64,128]{2,1,0:T(8,128)(2,1)S(1)} %copy.45), channel_id=1, replica_groups=mesh['ctx'=4,'ep'=8] {'ep'}, use_global_device_ids=true, to_apply=%region_5.6 | all-reduce | flops 8192 | bytes 32768 | tf_op jit(solution)/shard_map/psum | solution.py:67
  129.6 34.5 %all-reduce.2.cloned.1.call-done = bf16[1,128,512]{2,1,0:T(8,128)(2,1)} async-done(((bf16[1,128,512]{2,1,0:T(8,128)(2,1)}), bf16[1,128,512]{2,1,0:T(8,128)(2,1)}) %all-reduce.2.cloned.1.call-update) | async-done | bytes 131088 | tf_op jit(solution)/shard_map/psum | solution.py:66
  164.0 1.6 copy.71
  (1 shorter events, 0.0 us)
Async XLA Ops:
  7.2 14.6 %copy-start = (bf16[1,128,16,512]{3,2,1,0:T(8,128)(2,1)S(1)}, bf16[1,128,16,512]{3,2,1,0:T(8,128)(2,1)}, u32[]{:S(2)}) copy-start(bf16[1,128,16,512]{3,2,1,0:T(8,128)(2,1)} %param.5) | copy-start | bytes 6291460
  7.2 61.1 %reduce-scatter.5.cloned.1.call-start = ((), (), s32[]{:S(2)}) async-start(), calls=%async_computation.2 | async-start | bytes 655360 | tf_op jit(solution)/shard_map/reduce_scatter | solution.py:58
  21.7 2.8 %copy-start.7 = (bf16[1,16,64,128]{3,2,1,0:T(8,128)(2,1)S(1)}, bf16[1,16,64,128]{3,2,1,0:T(8,128)(2,1)}, u32[]{:S(2)}) copy-start(bf16[1,16,64,128]{3,2,1,0:T(8,128)(2,1)} %param.6) | copy-start | bytes 786436
  25.5 3.3 %copy-start.2 = (f32[1,16,128,512]{2,3,1,0:T(8,128)}, f32[1,16,128,512]{2,3,1,0:T(8,128)S(1)}, u32[]{:S(2)}) copy-start(f32[1,16,128,512]{2,3,1,0:T(8,128)S(1)} %get-tuple-element.16) | copy-start | bytes 12582916
  26.1 2.9 %copy-start.4 = (bf16[1,128,16,512]{3,2,1,0:T(8,128)(2,1)S(1)}, bf16[1,128,16,512]{3,2,1,0:T(8,128)(2,1)}, u32[]{:S(2)}) copy-start(bf16[1,128,16,512]{3,2,1,0:T(8,128)(2,1)} %param.9) | copy-start | bytes 6291460
  31.4 5.8 %copy-start.3 = (f32[1,16,128,512]{2,3,1,0:T(8,128)S(1)}, f32[1,16,128,512]{2,3,1,0:T(8,128)}, u32[]{:S(2)}) copy-start(f32[1,16,128,512]{2,3,1,0:T(8,128)} %copy-done.2) | copy-start | bytes 12582916
  31.4 5.8 %copy-start.5 = (bf16[1,128,16,512]{3,2,1,0:T(8,128)(2,1)S(1)}, bf16[1,128,16,512]{3,2,1,0:T(8,128)(2,1)}, u32[]{:S(2)}) copy-start(bf16[1,128,16,512]{3,2,1,0:T(8,128)(2,1)} %param.9) | copy-start | bytes 6291460
  40.8 1.3 copy-start.1
  45.5 45.5 %reduce-scatter.7.cloned.1.call-start = ((), (), s32[]{:S(2)}) async-start(), calls=%async_computation.4 | async-start | bytes 163840
  48.8 115.2 %all-reduce.2.cloned.1.call-start = ((), (), s32[]{:S(2)}) async-start(), calls=%async_computation.3 | async-start | bytes 262144 | tf_op jit(solution)/shard_map/psum | solution.py:66
  68.3 7.0 %copy-start.6 = (bf16[16,128,512]{2,1,0:T(8,128)(2,1)S(1)}, bf16[16,128,512]{2,1,0:T(8,128)(2,1)}, u32[]{:S(2)}) copy-start(bf16[16,128,512]{2,1,0:T(8,128)(2,1)} %get-tuple-element.18) | copy-start | bytes 6291460
Sparse Core Ops, SparseCore 0:
  45.7 22.5 reduce-scatter.4
  71.4 19.5 reduce-scatter.6
  94.3 69.6 all-reduce.1
where the time goes:
time: 173 us; the launch traced here: 172 us
  waiting for transfers between devices  62.9 us (36%)
  blocking collectives  52.1 us (30%)
  matrix products  28.6 us (17%)
  between operations  13.9 us (8%)
  local copies, waits for them, and re-layouts  11.5 us (7%)
  other arithmetic  3.03 us (2%)
    psum x1, blocking collectives, body(): lax.psum(rope_part.astype(jnp.bfloat16), 'ep').astype(jnp.float32)  37.7 us
    psum x1, waiting for transfers between devices, body(): lax.psum(latent_part.astype(jnp.bfloat16), 'ep').astype(jnp.float32)  34.5 us
    reduce_scatter x1, waiting for transfers between devices, body(): lax.psum_scatter(latent_term.astype(jnp.bfloat16), 'ctx', scatter_dimensi...  15.1 us
    unnamed x4, waiting for transfers between devices  13.3 us
    unnamed x23, local copies, waits for them, and re-layouts  11.4 us
    all_gather x1, blocking collectives, body(): lax.all_gather(key_latent, 'ctx', axis=1, tiled=True)  8.96 us
    dot_general x1, matrix products, body(): jnp.einsum('shtj,sthd->sjd', rounded_weights, output_grad, preferred_elem...  5.81 us
    all_gather x1, blocking collectives, body(): lax.all_gather(key_rope, 'ctx', axis=2, tiled=True)  5.46 us
  transfers between devices with their start and end apart: 3, of which 3 were waited for; matrix products, arithmetic and copies ran while one was open for 10% of the time, Pallas kernels for 0%

commit v1 on v0

--- a/solution.py
+++ b/solution.py
@@ -6,12 +6,37 @@
 scale_factor = 192.0 ** (-0.5)
 
 
+def causal_reduce_ctx(blocks, n_ctx):
+    here = lax.axis_index("ctx")
+    total = jnp.take(blocks, here, axis=0).astype(jnp.float32)
+    for shift in range(1, n_ctx):
+        sent = jnp.take(blocks, jnp.maximum(here - shift, 0), axis=0)
+        got = lax.ppermute(sent, "ctx", [(i, i - shift) for i in range(shift, n_ctx)])
+        total = total + got.astype(jnp.float32)
+    return total
+
+
+def butterfly_sum_ep(total, n_ep):
+    if n_ep & (n_ep - 1):
+        return lax.psum(total.astype(jnp.bfloat16), "ep").astype(jnp.float32)
+    bit = 1
+    while bit < n_ep:
+        mine = total.astype(jnp.bfloat16)
+        theirs = lax.ppermute(mine, "ep", [(i, i ^ bit) for i in range(n_ep)])
+        total = mine.astype(jnp.float32) + theirs.astype(jnp.float32)
+        bit *= 2
+    return total
+
+
 def body(query_latent, query_rope, key_latent, key_rope, output_grad):
+    n_ctx = lax.axis_size("ctx")
+    n_ep = lax.axis_size("ep")
     block_len = query_latent.shape[1]
-    whole_latent, whole_rope = (
-        lax.all_gather(key_latent, "ctx", axis=1, tiled=True),
-        lax.all_gather(key_rope, "ctx", axis=2, tiled=True),
-    )
+    kvr = key_latent.shape[2]
+    local_keys = jnp.concatenate([key_latent[0], key_rope[0].T], axis=1)
+    whole_keys = lax.all_gather(local_keys, "ctx", axis=0, tiled=True)
+    whole_latent = whole_keys[None, :, :kvr]
+    whole_rope = whole_keys[:, kvr:].T[None]
     length = whole_latent.shape[1]
     offset = lax.axis_index("ctx") * block_len
     query_place = offset + jnp.arange(block_len, dtype=jnp.int32)
@@ -46,28 +71,19 @@
         * jnp.einsum("shtj,sdj->shdt", score_grad, whole_rope, preferred_element_type=jnp.float32)
     ).astype(jnp.bfloat16)
     latent_term = scale_factor * jnp.einsum(
-        "shtj,sthd->sjd", score_grad, query_latent, preferred_element_type=jnp.float32
+        "shtj,sthd->jd", score_grad, query_latent, preferred_element_type=jnp.float32
     )
     latent_term = latent_term + jnp.einsum(
-        "shtj,sthd->sjd", rounded_weights, output_grad, preferred_element_type=jnp.float32
+        "shtj,sthd->jd", rounded_weights, output_grad, preferred_element_type=jnp.float32
     )
     rope_term = scale_factor * jnp.einsum(
-        "shtj,shdt->sdj", score_grad, query_rope, preferred_element_type=jnp.float32
+        "shtj,shdt->jd", score_grad, query_rope, preferred_element_type=jnp.float32
     )
-    latent_part, rope_part = (
-        lax.psum_scatter(
-            latent_term.astype(jnp.bfloat16), "ctx", scatter_dimension=1, tiled=True
-        ).astype(jnp.float32),
-        lax.psum_scatter(
-            rope_term.astype(jnp.bfloat16), "ctx", scatter_dimension=2, tiled=True
-        ).astype(jnp.float32),
-    )
-    latent_total, rope_total = (
-        lax.psum(latent_part.astype(jnp.bfloat16), "ep").astype(jnp.float32),
-        lax.psum(rope_part.astype(jnp.bfloat16), "ep").astype(jnp.float32),
-    )
-    latent_kgrad = latent_total.astype(jnp.bfloat16)
-    rope_kgrad = rope_total.astype(jnp.bfloat16)
+    terms = jnp.concatenate([latent_term, rope_term], axis=1).astype(jnp.bfloat16)
+    total = causal_reduce_ctx(terms.reshape(n_ctx, block_len, -1), n_ctx)
+    total = butterfly_sum_ep(total, n_ep).astype(jnp.bfloat16)
+    latent_kgrad = total[None, :, :kvr]
+    rope_kgrad = total[:, kvr:].T[None]
     return (attended, latent_qgrad, rope_qgrad, latent_kgrad, rope_kgrad)
 
 

time: 173 us -> 94.3 us (0.55)
  waiting for transfers between devices: 62.9 us -> 16.8 us
  blocking collectives: 52.1 us -> 9.33 us
  between operations: 13.9 us -> 0.78 us
  starting transfers between devices: 0.12 us -> 9.74 us
  local copies, waits for them, and re-layouts: 11.5 us -> 17 us
  matrix products: 28.6 us -> 33.1 us
  other arithmetic: 3.03 us -> 7.04 us
    psum x1 -> x0, blocking collectives: 37.7 us -> none  [body(): lax.psum(rope_part.astype(jnp.bfloat16), 'ep').astype(jnp.float32)]
    psum x1 -> x0, waiting for transfers between devices: 34.5 us -> none  [body(): lax.psum(latent_part.astype(jnp.bfloat16), 'ep').astype(jnp.float32)]
    ppermute x0 -> x6, waiting for transfers between devices: none -> 16.8 us  [the longest x3 10.1 us: butterfly_sum_ep(): theirs = lax.ppermute(mine, 'ep', [(i, i ^ bit) for i in range(n_ep)])]
    reduce_scatter x1 -> x0, waiting for transfers between devices: 15.1 us -> none  [body(): lax.psum_scatter(latent_term.astype(jnp.bfloat16), 'ctx', scatter_dimensi...]
    unnamed x4 -> x0, waiting for transfers between devices: 13.3 us -> none
    ppermute x0 -> x6, starting transfers between devices: none -> 9.74 us  [the longest x3 5.87 us: butterfly_sum_ep(): theirs = lax.ppermute(mine, 'ep', [(i, i ^ bit) for i in range(n_ep)])]
    all_gather x2 -> x1, blocking collectives: 14.4 us -> 9.33 us  [body(): whole_keys = lax.all_gather(local_keys, 'ctx', axis=0, tiled=True)]
    unnamed x23 -> x15, local copies, waits for them, and re-layouts: 11.4 us -> 16.2 us
  transfers between devices with their start and end apart: 3 -> 6, of which waited for: 3 -> 4; matrix products, arithmetic and copies ran while one was open for 10% -> 17% of each run, Pallas kernels for 0% -> 0%
where the time goes in v1:
time: 94.3 us; the launch traced here: 93.7 us
  matrix products  33.1 us (35%)
  local copies, waits for them, and re-layouts  17 us (18%)
  waiting for transfers between devices  16.8 us (18%)
  starting transfers between devices  9.74 us (10%)
  blocking collectives  9.33 us (10%)
  other arithmetic  7.04 us (7%)
    unnamed x15, local copies, waits for them, and re-layouts  16.2 us
    ppermute x3, waiting for transfers between devices, butterfly_sum_ep(): theirs = lax.ppermute(mine, 'ep', [(i, i ^ bit) for i in range(n_ep)])  10.1 us
    all_gather x1, blocking collectives, body(): whole_keys = lax.all_gather(local_keys, 'ctx', axis=0, tiled=True)  9.33 us
    dot_general x1, matrix products, body(): jnp.einsum('shtj,sthd->jd', rounded_weights, output_grad, preferred_eleme...  6.77 us
    ppermute x3, waiting for transfers between devices, causal_reduce_ctx(): lax.ppermute(sent, 'ctx', [(i, i - shift) for i in range(shift, n_ctx)])  6.64 us
    ppermute x3, starting transfers between devices, butterfly_sum_ep(): theirs = lax.ppermute(mine, 'ep', [(i, i ^ bit) for i in range(n_ep)])  5.87 us
    dot_general x1, matrix products, body(): jnp.einsum('sthd,sjd->shtj', output_grad, whole_latent, preferred_element...  4.71 us
    dot_general x1, matrix products, body(): jnp.einsum('shtj,sthd->jd', score_grad, query_latent, preferred_element_t...  4.44 us
  transfers between devices with their start and end apart: 6, of which 4 were waited for; matrix products, arithmetic and copies ran while one was open for 17% of the time, Pallas kernels for 0%

profile of v1, /device:TPU:0, one launch (start us, length us, event | category | flops | bytes accessed | tf_op | source)
XLA Modules:
  0.0 93.7 jit_solution(13140443794704222318)
XLA Ops:
  0.6 0.0 copy-start
  0.6 1.0 %copy.27 = bf16[1,64,128]{1,2,0:T(8,128)(2,1)S(1)} copy(bf16[1,64,128]{2,1,0:T(8,128)(2,1)} %param.10) | data formatting | bytes 32768 | tf_op args[3]
  1.6 0.9 pad_maximum_fusion
  2.6 9.3 %all_gather.3 = bf16[512,576]{1,0:T(8,128)(2,1)S(1)} all-gather(bf16[128,576]{1,0:T(8,128)(2,1)S(1)} %pad_maximum_fusion), channel_id=1, replica_groups=mesh['ctx'=4,'ep'=8] {'ctx'}, dimensions={0}, use_global_device_ids=true | all-gather | bytes 737280 | tf_op jit(solution)/shard_map/all_gather | solution.py:37
  11.9 0.1 iota_compare_fusion
  11.9 0.0 copy-done
  12.0 0.0 copy-start.4
  12.0 2.8 %fusion.23 = f32[512,128,16]{1,0,2:T(8,128)S(1)} fusion(bf16[128,16,512]{2,1,0:T(8,128)(2,1)S(1)} %bitcast.145, bf16[512,576]{1,0:T(8,128)(2,1)S(1)} %all_gather.3), kind=kOutput, calls=%fused_computation.27 | convolution fusion | flops 1073741824 | bytes 6815744 | tf_op jit(solution)/shard_map/sthd,sjd->shtj/dot_general | solution.py:44
  14.8 0.0 copy-done.4
  14.8 0.9 fusion.88
  15.7 0.0 copy-start.1
  15.7 0.6 fusion.5
  16.3 4.1 %bitcast_convert_fusion = (f32[16,128,512]{1,2,0:T(8,128)}, bf16[512,16,128]{2,0,1:T(8,128)(2,1)}) fusion(f32[16,128]{1,0:T(8,128)S(1)} %fusion.5, f32[1,16,128,512]{2,3,1,0:T(8,128)S(1)} %get-tuple-element.31, f32[16,128]{1,0:T(8,128)S(1)} %get-tuple-element.30, bf16[512,576]{1,0:T(8,128)(2,1)S(1)} %all_gather.3), kind=kOutput, calls=%fused_computation.18 | convolution fusion | flops 1078984704 | bytes 11026432 | tf_op jit(solution)/shard_map/shtj,sjd->sthd/dot_general | solution.py:55
  20.4 0.0 copy-done.1
  20.4 5.5 %copy.52 = f32[16,128,512]{2,0,1:T(8,128)} copy(f32[16,128,512]{1,2,0:T(8,128)} %get-tuple-element.32) | data formatting | bytes 8388608
  25.9 3.3 %multiply_reduce_fusion = f32[16,128]{0,1:T(8,128)S(1)} fusion(f32[16,128,512]{2,0,1:T(8,128)} %copy.52, bf16[1,128,16,512]{3,2,1,0:T(8,128)(2,1)} %param.11), kind=kLoop, calls=%fused_computation.6 | loop fusion | flops 3143680 | bytes 6299648
  29.3 0.1 copy.53
  29.3 0.0 copy-start.2
  29.3 0.0 copy-start.3
  29.3 6.8 %fusion.28 = f32[512,512]{1,0:T(8,128)} fusion(bf16[128,16,512]{2,1,0:T(8,128)(2,1)} %bitcast.147, f32[16,128]{1,0:T(8,128)S(1)} %fusion.5, f32[1,16,128,512]{2,3,1,0:T(8,128)} %copy-done.1, f32[16,128]{1,0:T(8,128)S(1)} %get-tuple-element.30), kind=kOutput, calls=%fused_computation.30 | convolution fusion | flops 1076887552 | bytes 7356416 | tf_op jit(solution)/shard_map/shtj,sthd->jd/dot_general | solution.py:76
  36.1 0.0 copy-done.2
  36.1 0.0 copy-done.3
  36.1 4.7 %fusion.1 = bf16[1,16,128,512]{2,3,1,0:T(8,128)(2,1)} fusion(f32[16,128]{1,0:T(8,128)S(1)} %copy.53, bf16[128,16,512]{2,1,0:T(8,128)(2,1)S(1)} %bitcast.148, f32[16,128]{1,0:T(8,128)S(1)} %fusion.5, f32[1,16,128,512]{2,3,1,0:T(8,128)S(1)} %copy-done.2, f32[16,128]{1,0:T(8,128)S(1)} %get-tuple-element.30, bf16[512,576]{1,0:T(8,128)(2,1)S(1)} %all_gather.3), kind=kOutput, calls=%fused_computation.2 | convolution fusion | flops 1078984704 | bytes 8937472 | tf_op jit(solution)/shard_map/sthd,sjd->shtj/dot_general | solution.py:61
  40.8 2.3 %fusion.69 = bf16[512,64]{0,1:T(8,128)(2,1)S(1)} fusion(bf16[1,16,128,512]{2,3,1,0:T(8,128)(2,1)} %fusion.1, bf16[1,16,64,128]{3,2,1,0:T(8,128)(2,1)S(1)} %copy-done.4), kind=kOutput, calls=%fused_computation.45 | convolution fusion | flops 134283264 | bytes 2424832 | tf_op jit(solution)/shard_map/shtj,shdt->jd/dot_general | solution.py:79
  43.2 4.4 %fusion.48 = bf16[512,512]{1,0:T(8,128)(2,1)S(1)} fusion(f32[512,512]{1,0:T(8,128)} %fusion.28, bf16[128,16,512]{2,1,0:T(8,128)(2,1)S(1)} %bitcast.146, bf16[1,16,128,512]{2,3,1,0:T(8,128)(2,1)} %fusion.1), kind=kOutput, calls=%fused_computation.34 | convolution fusion | flops 1074528256 | bytes 5767168 | tf_op jit(solution)/shard_map/shtj,sthd->jd/dot_general | solution.py:73
  47.6 0.1 copy.63
  47.7 0.8 fusion.82
  48.6 1.3 %collective-permute-start.2 = (bf16[128,576]{1,0:T(8,128)(2,1)}, bf16[128,576]{1,0:T(8,128)(2,1)}, u32[]{:S(2)}, u32[]{:S(2)}) collective-permute-start(bf16[128,576]{1,0:T(8,128)(2,1)} %get-tuple-element.29), channel_id=1, source_target_pairs={{24,0},{25,1},{26,2},{27,3},{28,4},{29,5},{30,6},{31,7}} | collective-permute-start | bytes 442376 | tf_op jit(solution)/shard_map/ppermute | solution.py:14
  49.9 1.3 %collective-permute-start.1 = (bf16[128,576]{1,0:T(8,128)(2,1)}, bf16[128,576]{1,0:T(8,128)(2,1)}, u32[]{:S(2)}, u32[]{:S(2)}) collective-permute-start(bf16[128,576]{1,0:T(8,128)(2,1)} %get-tuple-element.28), channel_id=1, source_target_pairs={{16,0},{24,8},{17,1},{25,9},{18,2},{26,10},{19,3},{27,11},{20,4},{... | collective-permute-start | bytes 442376 | tf_op jit(solution)/shard_map/ppermute | solution.py:14
  51.2 1.3 %collective-permute-start = (bf16[128,576]{1,0:T(8,128)(2,1)}, bf16[128,576]{1,0:T(8,128)(2,1)}, u32[]{:S(2)}, u32[]{:S(2)}) collective-permute-start(bf16[128,576]{1,0:T(8,128)(2,1)} %get-tuple-element.27), channel_id=1, source_target_pairs={{8,0},{16,8},{24,16},{9,1},{17,9},{25,17},{10,2},{18,10},{26,18},{... | collective-permute-start | bytes 442376 | tf_op jit(solution)/shard_map/ppermute | solution.py:14
  52.5 3.0 %collective-permute-done.2 = bf16[128,576]{1,0:T(8,128)(2,1)} collective-permute-done((bf16[128,576]{1,0:T(8,128)(2,1)}, bf16[128,576]{1,0:T(8,128)(2,1)}, u32[]{:S(2)}, u32[]{:S(2)}) %collective-permute-start.2) | collective-permute-done | bytes 147488 | tf_op jit(solution)/shard_map/ppermute | solution.py:14
  55.5 3.6 %collective-permute-done.1 = bf16[128,576]{1,0:T(8,128)(2,1)} collective-permute-done((bf16[128,576]{1,0:T(8,128)(2,1)}, bf16[128,576]{1,0:T(8,128)(2,1)}, u32[]{:S(2)}, u32[]{:S(2)}) %collective-permute-start.1) | collective-permute-done | bytes 147488 | tf_op jit(solution)/shard_map/ppermute | solution.py:14
  59.1 0.0 collective-permute-done
  59.1 1.2 %add_convert_fusion.3 = bf16[128,576]{1,0:T(8,128)(2,1)S(1)} fusion(bf16[128,576]{1,0:T(8,128)(2,1)} %collective-permute-done.2, bf16[128,576]{1,0:T(8,128)(2,1)} %collective-permute-done.1, bf16[128,576]{1,0:T(8,128)(2,1)} %collective-permute-done, s32[]{:T(128)S(6)} %select_n.22, bf16[4,128,512]{2,1,0:T(8,128)(2,1)S(1)} %bitcast.151, ...), kind=kLoop, calls=%fused_computation.54 | loop fusion | flops 958464 | bytes 1179653 | tf_op jit(solution)/shard_map/convert_element_type | solution.py:24
  60.3 1.6 %collective-permute-start.3 = (bf16[128,576]{1,0:T(8,128)(2,1)S(1)}, bf16[128,576]{1,0:T(8,128)(2,1)S(1)}, u32[]{:S(2)}, u32[]{:S(2)}) collective-permute-start(bf16[128,576]{1,0:T(8,128)(2,1)S(1)} %add_convert_fusion.3), channel_id=1, source_target_pairs={{0,1},{1,0},{2,3},{3,2},{4,5},{5,4},{6,7},{7,6},{8,9},{9,8},{10,11... | collective-permute-start | bytes 442376 | tf_op jit(solution)/shard_map/ppermute | solution.py:25
  61.9 4.9 %collective-permute-done.3 = bf16[128,576]{1,0:T(8,128)(2,1)S(1)} collective-permute-done((bf16[128,576]{1,0:T(8,128)(2,1)S(1)}, bf16[128,576]{1,0:T(8,128)(2,1)S(1)}, u32[]{:S(2)}, u32[]{:S(2)}) %collective-permute-start.3) | collective-permute-done | bytes 147488 | tf_op jit(solution)/shard_map/ppermute | solution.py:25
  66.8 1.6 %collective-permute-start.4 = (bf16[128,576]{1,0:T(8,128)(2,1)S(1)}, bf16[128,576]{1,0:T(8,128)(2,1)S(1)}, u32[]{:S(2)}, u32[]{:S(2)}) collective-permute-start(bf16[128,576]{1,0:T(8,128)(2,1)S(1)} %add_convert_fusion.2), channel_id=1, source_target_pairs={{0,2},{1,3},{2,0},{3,1},{4,6},{5,7},{6,4},{7,5},{8,10},{9,11},{10,... | collective-permute-start | bytes 442376 | tf_op jit(solution)/shard_map/ppermute | solution.py:25
  68.5 4.2 %fusion.25 = bf16[1,128,16,512]{1,3,2,0:T(8,128)(2,1)} fusion(bf16[1,16,128,512]{2,3,1,0:T(8,128)(2,1)} %fusion.1, bf16[512,576]{1,0:T(8,128)(2,1)S(1)} %all_gather.3), kind=kOutput, calls=%fused_computation.29 | convolution fusion | flops 1075838976 | bytes 4718592 | tf_op jit(solution)/shard_map/shtj,sjd->sthd/dot_general | solution.py:67
  72.7 4.5 %copy.41 = bf16[1,128,16,512]{3,2,1,0:T(8,128)(2,1)} copy(bf16[1,128,16,512]{1,3,2,0:T(8,128)(2,1)} %bitcast.149) | data formatting | bytes 4194304
  77.2 4.5 %copy.42 = bf16[1,128,16,512]{3,2,1,0:T(8,128)(2,1)} copy(bf16[1,128,16,512]{1,3,2,0:T(8,128)(2,1)} %fusion.25) | data formatting | bytes 4194304
  81.6 0.0 collective-permute-done.4
  81.7 2.6 %collective-permute-start.5 = (bf16[128,576]{1,0:T(8,128)(2,1)S(1)}, bf16[128,576]{1,0:T(8,128)(2,1)S(1)}, u32[]{:S(2)}, u32[]{:S(2)}) collective-permute-start(bf16[128,576]{1,0:T(8,128)(2,1)S(1)} %add_convert_fusion.1), channel_id=1, source_target_pairs={{0,4},{1,5},{2,6},{3,7},{4,0},{5,1},{6,2},{7,3},{8,12},{9,13},{10,... | collective-permute-start | bytes 442376 | tf_op jit(solution)/shard_map/ppermute | solution.py:25
  84.3 2.8 %fusion.60 = bf16[1,16,64,128]{3,2,1,0:T(8,128)(2,1)} fusion(bf16[1,16,128,512]{2,3,1,0:T(8,128)(2,1)} %fusion.1, bf16[512,576]{1,0:T(8,128)(2,1)S(1)} %all_gather.3), kind=kOutput, calls=%fused_computation.42 | convolution fusion | flops 134479872 | bytes 2490368 | tf_op jit(solution)/shard_map/shtj,sdj->shdt/dot_general | solution.py:71
  87.1 5.2 %collective-permute-done.5 = bf16[128,576]{1,0:T(8,128)(2,1)S(1)} collective-permute-done((bf16[128,576]{1,0:T(8,128)(2,1)S(1)}, bf16[128,576]{1,0:T(8,128)(2,1)S(1)}, u32[]{:S(2)}, u32[]{:S(2)}) %collective-permute-start.5) | collective-permute-done | bytes 147488 | tf_op jit(solution)/shard_map/ppermute | solution.py:25
  92.4 0.7 slice_bitcast_fusion.5
  93.0 0.7 copy.43
  (5 shorter events, 0.1 us)
Async XLA Ops:
  0.6 11.3 %copy-start = (bf16[1,128,16,512]{3,2,1,0:T(8,128)(2,1)S(1)}, bf16[1,128,16,512]{3,2,1,0:T(8,128)(2,1)}, u32[]{:S(2)}) copy-start(bf16[1,128,16,512]{3,2,1,0:T(8,128)(2,1)} %param.7) | copy-start | bytes 6291460
  12.0 2.8 %copy-start.4 = (bf16[1,16,64,128]{3,2,1,0:T(8,128)(2,1)S(1)}, bf16[1,16,64,128]{3,2,1,0:T(8,128)(2,1)}, u32[]{:S(2)}) copy-start(bf16[1,16,64,128]{3,2,1,0:T(8,128)(2,1)} %param.8) | copy-start | bytes 786436
  15.7 4.7 %copy-start.1 = (f32[1,16,128,512]{2,3,1,0:T(8,128)}, f32[1,16,128,512]{2,3,1,0:T(8,128)S(1)}, u32[]{:S(2)}) copy-start(f32[1,16,128,512]{2,3,1,0:T(8,128)S(1)} %get-tuple-element.31) | copy-start | bytes 12582916
  29.3 6.8 %copy-start.2 = (f32[1,16,128,512]{2,3,1,0:T(8,128)S(1)}, f32[1,16,128,512]{2,3,1,0:T(8,128)}, u32[]{:S(2)}) copy-start(f32[1,16,128,512]{2,3,1,0:T(8,128)} %copy-done.1) | copy-start | bytes 12582916
  29.3 6.8 %copy-start.3 = (bf16[1,128,16,512]{3,2,1,0:T(8,128)(2,1)S(1)}, bf16[1,128,16,512]{3,2,1,0:T(8,128)(2,1)}, u32[]{:S(2)}) copy-start(bf16[1,128,16,512]{3,2,1,0:T(8,128)(2,1)} %param.11) | copy-start | bytes 6291460
  48.6 6.9 %collective-permute-start.2 = (bf16[128,576]{1,0:T(8,128)(2,1)}, bf16[128,576]{1,0:T(8,128)(2,1)}, u32[]{:S(2)}, u32[]{:S(2)}) collective-permute-start(bf16[128,576]{1,0:T(8,128)(2,1)} %get-tuple-element.29), channel_id=1, source_target_pairs={{24,0},{25,1},{26,2},{27,3},{28,4},{29,5},{30,6},{31,7}} | collective-permute-start | bytes 442376 | tf_op jit(solution)/shard_map/ppermute | solution.py:14
  49.9 9.2 %collective-permute-start.1 = (bf16[128,576]{1,0:T(8,128)(2,1)}, bf16[128,576]{1,0:T(8,128)(2,1)}, u32[]{:S(2)}, u32[]{:S(2)}) collective-permute-start(bf16[128,576]{1,0:T(8,128)(2,1)} %get-tuple-element.28), channel_id=1, source_target_pairs={{16,0},{24,8},{17,1},{25,9},{18,2},{26,10},{19,3},{27,11},{20,4},{... | collective-permute-start | bytes 442376 | tf_op jit(solution)/shard_map/ppermute | solution.py:14
  51.2 7.9 %collective-permute-start = (bf16[128,576]{1,0:T(8,128)(2,1)}, bf16[128,576]{1,0:T(8,128)(2,1)}, u32[]{:S(2)}, u32[]{:S(2)}) collective-permute-start(bf16[128,576]{1,0:T(8,128)(2,1)} %get-tuple-element.27), channel_id=1, source_target_pairs={{8,0},{16,8},{24,16},{9,1},{17,9},{25,17},{10,2},{18,10},{26,18},{... | collective-permute-start | bytes 442376 | tf_op jit(solution)/shard_map/ppermute | solution.py:14
  60.3 6.5 %collective-permute-start.3 = (bf16[128,576]{1,0:T(8,128)(2,1)S(1)}, bf16[128,576]{1,0:T(8,128)(2,1)S(1)}, u32[]{:S(2)}, u32[]{:S(2)}) collective-permute-start(bf16[128,576]{1,0:T(8,128)(2,1)S(1)} %add_convert_fusion.3), channel_id=1, source_target_pairs={{0,1},{1,0},{2,3},{3,2},{4,5},{5,4},{6,7},{7,6},{8,9},{9,8},{10,11... | collective-permute-start | bytes 442376 | tf_op jit(solution)/shard_map/ppermute | solution.py:25
  66.8 14.8 %collective-permute-start.4 = (bf16[128,576]{1,0:T(8,128)(2,1)S(1)}, bf16[128,576]{1,0:T(8,128)(2,1)S(1)}, u32[]{:S(2)}, u32[]{:S(2)}) collective-permute-start(bf16[128,576]{1,0:T(8,128)(2,1)S(1)} %add_convert_fusion.2), channel_id=1, source_target_pairs={{0,2},{1,3},{2,0},{3,1},{4,6},{5,7},{6,4},{7,5},{8,10},{9,11},{10,... | collective-permute-start | bytes 442376 | tf_op jit(solution)/shard_map/ppermute | solution.py:25
  81.7 10.6 %collective-permute-start.5 = (bf16[128,576]{1,0:T(8,128)(2,1)S(1)}, bf16[128,576]{1,0:T(8,128)(2,1)S(1)}, u32[]{:S(2)}, u32[]{:S(2)}) collective-permute-start(bf16[128,576]{1,0:T(8,128)(2,1)S(1)} %add_convert_fusion.1), channel_id=1, source_target_pairs={{0,4},{1,5},{2,6},{3,7},{4,0},{5,1},{6,2},{7,3},{8,12},{9,13},{10,... | collective-permute-start | bytes 442376 | tf_op jit(solution)/shard_map/ppermute | solution.py:25

commit v2 on v1

--- a/solution.py
+++ b/solution.py
@@ -16,16 +16,30 @@
     return total
 
 
-def butterfly_sum_ep(total, n_ep):
+def halving_sum_ep(total, n_ep):
     if n_ep & (n_ep - 1):
-        return lax.psum(total.astype(jnp.bfloat16), "ep").astype(jnp.float32)
-    bit = 1
-    while bit < n_ep:
-        mine = total.astype(jnp.bfloat16)
-        theirs = lax.ppermute(mine, "ep", [(i, i ^ bit) for i in range(n_ep)])
-        total = mine.astype(jnp.float32) + theirs.astype(jnp.float32)
-        bit *= 2
-    return total
+        return lax.psum(total.astype(jnp.bfloat16), "ep").astype(jnp.bfloat16)
+    n_bits = n_ep.bit_length() - 1
+    here = lax.axis_index("ep")
+    rows, cols = total.shape
+    parts = total.reshape((2,) * n_bits + (rows // n_ep, cols))
+    for k in range(n_bits):
+        axis = n_bits - 1 - k
+        mine = (here >> k) & 1
+        keep = jnp.take(parts, mine, axis=axis)
+        sent = jnp.take(parts, 1 - mine, axis=axis).astype(jnp.bfloat16)
+        got = lax.ppermute(sent, "ep", [(i, i ^ (1 << k)) for i in range(n_ep)])
+        parts = keep + got.astype(jnp.float32)
+        n_left = n_bits - 1 - k
+        parts = parts.reshape((2,) * n_left + (rows // n_ep, cols)) if n_left else parts
+    whole = parts.astype(jnp.bfloat16)
+    for k in reversed(range(n_bits)):
+        mine = (here >> k) & 1
+        got = lax.ppermute(whole, "ep", [(i, i ^ (1 << k)) for i in range(n_ep)])
+        low = jnp.where(mine == 0, whole, got)
+        high = jnp.where(mine == 0, got, whole)
+        whole = jnp.stack([low, high], axis=n_bits - 1 - k)
+    return whole.reshape(rows, cols)
 
 
 def body(query_latent, query_rope, key_latent, key_rope, output_grad):
@@ -81,7 +95,7 @@
     )
     terms = jnp.concatenate([latent_term, rope_term], axis=1).astype(jnp.bfloat16)
     total = causal_reduce_ctx(terms.reshape(n_ctx, block_len, -1), n_ctx)
-    total = butterfly_sum_ep(total, n_ep).astype(jnp.bfloat16)
+    total = halving_sum_ep(total, n_ep)
     latent_kgrad = total[None, :, :kvr]
     rope_kgrad = total[:, kvr:].T[None]
     return (attended, latent_qgrad, rope_qgrad, latent_kgrad, rope_kgrad)

time: 94.3 us -> 102 us (1.082)
  starting transfers between devices: 9.74 us -> 15.8 us
    ppermute x3 -> x6, starting transfers between devices: 5.87 us -> 11.7 us  [the longest x3 5.88 us: halving_sum_ep(): got = lax.ppermute(sent, 'ep', [(i, i ^ 1 << k) for i in range(n_ep)])]
    add x0 -> x3, other arithmetic: none -> 2.11 us  [the longest x1 1.17 us: causal_reduce_ctx(): total = total + got.astype(jnp.float32)]
    convert_element_type x4, other arithmetic: 1.3 us -> 0.05 us  [the longest x3 0.05 us: halving_sum_ep(): sent = jnp.take(parts, 1 - mine, axis=axis).astype(jnp.bfloat16)]
    unnamed x15 -> x17, local copies, waits for them, and re-layouts: 16.2 us -> 16.9 us
    ppermute x3 -> x6, waiting for transfers between devices: 10.1 us -> 9.88 us  [the longest x3 7.69 us: halving_sum_ep(): got = lax.ppermute(sent, 'ep', [(i, i ^ 1 << k) for i in range(n_ep)])]
  transfers between devices with their start and end apart: 6 -> 9, of which waited for: 4 -> 6; matrix products, arithmetic and copies ran while one was open for 17% -> 16% of each run, Pallas kernels for 0% -> 0%
where the time goes in v2:
time: 102 us; the launch traced here: 101 us
  matrix products  33.1 us (32%)
  local copies, waits for them, and re-layouts  17.7 us (17%)
  waiting for transfers between devices  16.3 us (16%)
  starting transfers between devices  15.8 us (15%)
  blocking collectives  9.33 us (9%)
  other arithmetic  8.02 us (8%)
    unnamed x17, local copies, waits for them, and re-layouts  16.9 us
    all_gather x1, blocking collectives, body(): whole_keys = lax.all_gather(local_keys, 'ctx', axis=0, tiled=True)  9.33 us
    ppermute x3, waiting for transfers between devices, halving_sum_ep(): got = lax.ppermute(sent, 'ep', [(i, i ^ 1 << k) for i in range(n_ep)])  7.69 us
    dot_general x1, matrix products, body(): jnp.einsum('shtj,sthd->jd', rounded_weights, output_grad, preferred_eleme...  6.77 us
    ppermute x3, waiting for transfers between devices, causal_reduce_ctx(): lax.ppermute(sent, 'ctx', [(i, i - shift) for i in range(shift, n_ctx)])  6.4 us
    ppermute x3, starting transfers between devices, halving_sum_ep(): got = lax.ppermute(sent, 'ep', [(i, i ^ 1 << k) for i in range(n_ep)])  5.88 us
    ppermute x3, starting transfers between devices, halving_sum_ep(): got = lax.ppermute(whole, 'ep', [(i, i ^ 1 << k) for i in range(n_ep)])  5.79 us
    dot_general x1, matrix products, body(): jnp.einsum('sthd,sjd->shtj', output_grad, whole_latent, preferred_element...  4.7 us
  transfers between devices with their start and end apart: 9, of which 6 were waited for; matrix products, arithmetic and copies ran while one was open for 16% of the time, Pallas kernels for 0%

profile of v2, /device:TPU:0, one launch (start us, length us, event | category | flops | bytes accessed | tf_op | source)
XLA Modules:
  0.0 101.1 jit_solution(4417357890290526066)
XLA Ops:
  0.6 0.0 copy-start
  0.6 1.0 copy.51
  1.6 0.9 pad_maximum_fusion
  2.6 9.3 %all_gather.3 = bf16[512,576]{1,0:T(8,128)(2,1)S(1)} all-gather(bf16[128,576]{1,0:T(8,128)(2,1)S(1)} %pad_maximum_fusion), channel_id=1, replica_groups=mesh['ctx'=4,'ep'=8] {'ctx'}, dimensions={0}, use_global_device_ids=true | all-gather | bytes 737280 | tf_op jit(solution)/shard_map/all_gather | solution.py:51
  11.9 0.1 iota_compare_fusion
  12.0 0.0 copy-start.4
  12.0 2.8 %fusion.23 = f32[512,128,16]{1,0,2:T(8,128)S(1)} fusion(bf16[128,16,512]{2,1,0:T(8,128)(2,1)S(1)} %bitcast.189, bf16[512,576]{1,0:T(8,128)(2,1)S(1)} %all_gather.3), kind=kOutput, calls=%fused_computation.27 | convolution fusion | flops 1073741824 | bytes 6815744 | tf_op jit(solution)/shard_map/sthd,sjd->shtj/dot_general | solution.py:58
  14.8 0.0 copy-done.4
  14.8 0.9 fusion.93
  15.7 0.6 fusion.5
  16.3 4.1 %bitcast_convert_fusion = (f32[16,128,512]{1,2,0:T(8,128)}, bf16[512,16,128]{2,0,1:T(8,128)(2,1)}) fusion(f32[16,128]{1,0:T(8,128)S(1)} %fusion.5, f32[1,16,128,512]{2,3,1,0:T(8,128)S(1)} %get-tuple-element.78, f32[16,128]{1,0:T(8,128)S(1)} %get-tuple-element.77, bf16[512,576]{1,0:T(8,128)(2,1)S(1)} %all_gather.3), kind=kOutput, calls=%fused_computation.18 | convolution fusion | flops 1078984704 | bytes 11026432 | tf_op jit(solution)/shard_map/shtj,sjd->sthd/dot_general | solution.py:69
  20.4 0.0 copy-done.1
  20.4 5.5 %copy.81 = f32[16,128,512]{2,0,1:T(8,128)} copy(f32[16,128,512]{1,2,0:T(8,128)} %get-tuple-element.79) | data formatting | bytes 8388608
  25.9 3.3 %multiply_reduce_fusion = f32[16,128]{0,1:T(8,128)S(1)} fusion(f32[16,128,512]{2,0,1:T(8,128)} %copy.81, bf16[1,128,16,512]{3,2,1,0:T(8,128)(2,1)} %param.17), kind=kLoop, calls=%fused_computation.6 | loop fusion | flops 3143680 | bytes 6299648
  29.3 0.1 copy.82
  29.3 6.8 %fusion.28 = f32[512,512]{1,0:T(8,128)} fusion(bf16[128,16,512]{2,1,0:T(8,128)(2,1)} %bitcast.191, f32[16,128]{1,0:T(8,128)S(1)} %fusion.5, f32[1,16,128,512]{2,3,1,0:T(8,128)} %copy-done.1, f32[16,128]{1,0:T(8,128)S(1)} %get-tuple-element.77), kind=kOutput, calls=%fused_computation.30 | convolution fusion | flops 1076887552 | bytes 7356416 | tf_op jit(solution)/shard_map/shtj,sthd->jd/dot_general | solution.py:90
  36.1 4.7 %fusion.1 = bf16[1,16,128,512]{2,3,1,0:T(8,128)(2,1)} fusion(f32[16,128]{1,0:T(8,128)S(1)} %copy.82, bf16[128,16,512]{2,1,0:T(8,128)(2,1)S(1)} %bitcast.192, f32[16,128]{1,0:T(8,128)S(1)} %fusion.5, f32[1,16,128,512]{2,3,1,0:T(8,128)S(1)} %copy-done.2, f32[16,128]{1,0:T(8,128)S(1)} %get-tuple-element.77, bf16[512,576]{1,0:T(8,128)(2,1)S(1)} %all_gather.3), kind=kOutput, calls=%fused_computation.2 | convolution fusion | flops 1078984704 | bytes 8937472 | tf_op jit(solution)/shard_map/sthd,sjd->shtj/dot_general | solution.py:75
  40.8 2.3 %fusion.69 = bf16[512,64]{0,1:T(8,128)(2,1)S(1)} fusion(bf16[1,16,128,512]{2,3,1,0:T(8,128)(2,1)} %fusion.1, bf16[1,16,64,128]{3,2,1,0:T(8,128)(2,1)S(1)} %copy-done.4), kind=kOutput, calls=%fused_computation.45 | convolution fusion | flops 134283264 | bytes 2424832 | tf_op jit(solution)/shard_map/shtj,shdt->jd/dot_general | solution.py:93
  43.1 4.4 %fusion.48 = bf16[512,512]{1,0:T(8,128)(2,1)S(1)} fusion(f32[512,512]{1,0:T(8,128)} %fusion.28, bf16[128,16,512]{2,1,0:T(8,128)(2,1)S(1)} %bitcast.190, bf16[1,16,128,512]{2,3,1,0:T(8,128)(2,1)} %fusion.1), kind=kOutput, calls=%fused_computation.34 | convolution fusion | flops 1074528256 | bytes 5767168 | tf_op jit(solution)/shard_map/shtj,sthd->jd/dot_general | solution.py:87
  47.6 0.1 copy.92
  47.7 0.8 fusion.82
  48.5 1.3 %collective-permute-start.2 = (bf16[128,576]{1,0:T(8,128)(2,1)}, bf16[128,576]{1,0:T(8,128)(2,1)}, u32[]{:S(2)}, u32[]{:S(2)}) collective-permute-start(bf16[128,576]{1,0:T(8,128)(2,1)} %get-tuple-element.70), channel_id=1, source_target_pairs={{24,0},{25,1},{26,2},{27,3},{28,4},{29,5},{30,6},{31,7}} | collective-permute-start | bytes 442376 | tf_op jit(solution)/shard_map/ppermute | solution.py:14
  49.8 1.3 %collective-permute-start.1 = (bf16[128,576]{1,0:T(8,128)(2,1)}, bf16[128,576]{1,0:T(8,128)(2,1)}, u32[]{:S(2)}, u32[]{:S(2)}) collective-permute-start(bf16[128,576]{1,0:T(8,128)(2,1)} %get-tuple-element.69), channel_id=1, source_target_pairs={{16,0},{24,8},{17,1},{25,9},{18,2},{26,10},{19,3},{27,11},{20,4},{... | collective-permute-start | bytes 442376 | tf_op jit(solution)/shard_map/ppermute | solution.py:14
  51.1 1.5 %collective-permute-start = (bf16[128,576]{1,0:T(8,128)(2,1)}, bf16[128,576]{1,0:T(8,128)(2,1)}, u32[]{:S(2)}, u32[]{:S(2)}) collective-permute-start(bf16[128,576]{1,0:T(8,128)(2,1)} %get-tuple-element.68), channel_id=1, source_target_pairs={{8,0},{16,8},{24,16},{9,1},{17,9},{25,17},{10,2},{18,10},{26,18},{... | collective-permute-start | bytes 442376 | tf_op jit(solution)/shard_map/ppermute | solution.py:14
  52.7 2.8 %collective-permute-done.2 = bf16[128,576]{1,0:T(8,128)(2,1)} collective-permute-done((bf16[128,576]{1,0:T(8,128)(2,1)}, bf16[128,576]{1,0:T(8,128)(2,1)}, u32[]{:S(2)}, u32[]{:S(2)}) %collective-permute-start.2) | collective-permute-done | bytes 147488 | tf_op jit(solution)/shard_map/ppermute | solution.py:14
  55.5 3.6 %collective-permute-done.1 = bf16[128,576]{1,0:T(8,128)(2,1)} collective-permute-done((bf16[128,576]{1,0:T(8,128)(2,1)}, bf16[128,576]{1,0:T(8,128)(2,1)}, u32[]{:S(2)}, u32[]{:S(2)}) %collective-permute-start.1) | collective-permute-done | bytes 147488 | tf_op jit(solution)/shard_map/ppermute | solution.py:14
  59.1 0.0 collective-permute-done
  59.1 1.2 %convert_add_fusion = f32[128,576]{1,0:T(8,128)S(1)} fusion(bf16[128,576]{1,0:T(8,128)(2,1)} %collective-permute-done.2, bf16[128,576]{1,0:T(8,128)(2,1)} %collective-permute-done.1, bf16[128,576]{1,0:T(8,128)(2,1)} %collective-permute-done, s32[]{:T(128)S(6)} %select_n.101, bf16[4,128,512]{2,1,0:T(8,128)(2,1)S(1)} %bitcast.195, ...), kind=kLoop, calls=%fused_computation.51 | loop fusion | flops 884736 | bytes 1327109 | tf_op jit(solution)/shard_map/add | solution.py:15
  60.2 0.7 copy-done.5
  61.0 1.6 %collective-permute-start.3 = (bf16[2,2,16,576]{3,2,1,0:T(8,128)(2,1)S(1)}, bf16[2,2,16,576]{3,2,1,0:T(8,128)(2,1)S(1)}, u32[]{:S(2)}, u32[]{:S(2)}) collective-permute-start(bf16[2,2,16,576]{3,2,1,0:T(8,128)(2,1)S(1)} %bitcast_convert_fusion.1), channel_id=1, source_target_pairs={{0,1},{1,0},{2,3},{3,2},{4,5},{5,4},{6,7},{7,6},{8,9},{9,8},{10,11... | collective-permute-start | bytes 221192 | tf_op jit(solution)/shard_map/ppermute | solution.py:31
  62.6 3.2 %collective-permute-done.3 = bf16[2,2,16,576]{3,2,1,0:T(8,128)(2,1)S(1)} collective-permute-done((bf16[2,2,16,576]{3,2,1,0:T(8,128)(2,1)S(1)}, bf16[2,2,16,576]{3,2,1,0:T(8,128)(2,1)S(1)}, u32[]{:S(2)}, u32[]{:S(2)}) %collective-permute-start.3) | collective-permute-done | bytes 73760 | tf_op jit(solution)/shard_map/ppermute | solution.py:31
  65.7 0.9 fusion.87
  66.7 1.6 %collective-permute-start.4 = (bf16[2,16,576]{2,1,0:T(8,128)(2,1)S(1)}, bf16[2,16,576]{2,1,0:T(8,128)(2,1)S(1)}, u32[]{:S(2)}, u32[]{:S(2)}) collective-permute-start(bf16[2,16,576]{2,1,0:T(8,128)(2,1)S(1)} %bitcast_convert_fusion.2), channel_id=1, source_target_pairs={{0,2},{1,3},{2,0},{3,1},{4,6},{5,7},{6,4},{7,5},{8,10},{9,11},{10,... | collective-permute-start | bytes 110600 | tf_op jit(solution)/shard_map/ppermute | solution.py:31
  68.3 2.4 %collective-permute-done.4 = bf16[2,16,576]{2,1,0:T(8,128)(2,1)S(1)} collective-permute-done((bf16[2,16,576]{2,1,0:T(8,128)(2,1)S(1)}, bf16[2,16,576]{2,1,0:T(8,128)(2,1)S(1)}, u32[]{:S(2)}, u32[]{:S(2)}) %collective-permute-start.4) | collective-permute-done | bytes 36896 | tf_op jit(solution)/shard_map/ppermute | solution.py:31
  70.8 2.7 %collective-permute-start.5 = (bf16[16,576]{1,0:T(8,128)(2,1)S(1)}, bf16[16,576]{1,0:T(8,128)(2,1)S(1)}, u32[]{:S(2)}, u32[]{:S(2)}) collective-permute-start(bf16[16,576]{1,0:T(8,128)(2,1)S(1)} %bitcast_convert_fusion.3), channel_id=1, source_target_pairs={{0,4},{1,5},{2,6},{3,7},{4,0},{5,1},{6,2},{7,3},{8,12},{9,13},{10,... | collective-permute-start | bytes 55304 | tf_op jit(solution)/shard_map/ppermute | solution.py:31
  73.5 2.1 %collective-permute-done.5 = bf16[16,576]{1,0:T(8,128)(2,1)S(1)} collective-permute-done((bf16[16,576]{1,0:T(8,128)(2,1)S(1)}, bf16[16,576]{1,0:T(8,128)(2,1)S(1)}, u32[]{:S(2)}, u32[]{:S(2)}) %collective-permute-start.5) | collective-permute-done | bytes 18464 | tf_op jit(solution)/shard_map/ppermute | solution.py:31
  75.6 2.7 %collective-permute-start.6 = (bf16[16,576]{1,0:T(8,128)(2,1)S(1)}, bf16[16,576]{1,0:T(8,128)(2,1)S(1)}, u32[]{:S(2)}, u32[]{:S(2)}) collective-permute-start(bf16[16,576]{1,0:T(8,128)(2,1)S(1)} %fusion.90), channel_id=1, source_target_pairs={{0,4},{1,5},{2,6},{3,7},{4,0},{5,1},{6,2},{7,3},{8,12},{9,13},{10,... | collective-permute-start | bytes 55304 | tf_op jit(solution)/shard_map/ppermute | solution.py:38
  78.2 2.2 %collective-permute-done.6 = bf16[16,576]{1,0:T(8,128)(2,1)S(1)} collective-permute-done((bf16[16,576]{1,0:T(8,128)(2,1)S(1)}, bf16[16,576]{1,0:T(8,128)(2,1)S(1)}, u32[]{:S(2)}, u32[]{:S(2)}) %collective-permute-start.6) | collective-permute-done | bytes 18464 | tf_op jit(solution)/shard_map/ppermute | solution.py:38
  80.4 1.5 %collective-permute-start.7 = (bf16[2,16,576]{2,1,0:T(8,128)(2,1)S(1)}, bf16[2,16,576]{2,1,0:T(8,128)(2,1)S(1)}, u32[]{:S(2)}, u32[]{:S(2)}) collective-permute-start(bf16[2,16,576]{2,1,0:T(8,128)(2,1)S(1)} %pad_maximum_fusion.3), channel_id=1, source_target_pairs={{0,2},{1,3},{2,0},{3,1},{4,6},{5,7},{6,4},{7,5},{8,10},{9,11},{10,... | collective-permute-start | bytes 110600 | tf_op jit(solution)/shard_map/ppermute | solution.py:38
  82.0 4.2 %fusion.25 = bf16[1,128,16,512]{1,3,2,0:T(8,128)(2,1)} fusion(bf16[1,16,128,512]{2,3,1,0:T(8,128)(2,1)} %fusion.1, bf16[512,576]{1,0:T(8,128)(2,1)S(1)} %all_gather.3), kind=kOutput, calls=%fused_computation.29 | convolution fusion | flops 1075838976 | bytes 4718592 | tf_op jit(solution)/shard_map/shtj,sjd->sthd/dot_general | solution.py:81
  86.2 0.0 collective-permute-done.7
  86.2 1.6 %collective-permute-start.8 = (bf16[2,2,16,576]{3,2,0,1:T(8,128)(2,1)S(1)}, bf16[2,2,16,576]{3,2,0,1:T(8,128)(2,1)S(1)}, u32[]{:S(2)}, u32[]{:S(2)}) collective-permute-start(bf16[2,2,16,576]{3,2,0,1:T(8,128)(2,1)S(1)} %pad_maximum_fusion.2), channel_id=1, source_target_pairs={{0,1},{1,0},{2,3},{3,2},{4,5},{5,4},{6,7},{7,6},{8,9},{9,8},{10,11... | collective-permute-start | bytes 221192 | tf_op jit(solution)/shard_map/ppermute | solution.py:38
  87.8 2.8 %fusion.60 = bf16[1,16,64,128]{3,2,1,0:T(8,128)(2,1)} fusion(bf16[1,16,128,512]{2,3,1,0:T(8,128)(2,1)} %fusion.1, bf16[512,576]{1,0:T(8,128)(2,1)S(1)} %all_gather.3), kind=kOutput, calls=%fused_computation.42 | convolution fusion | flops 134479872 | bytes 2490368 | tf_op jit(solution)/shard_map/shtj,sdj->shdt/dot_general | solution.py:85
  90.6 4.5 %copy.70 = bf16[1,128,16,512]{3,2,1,0:T(8,128)(2,1)} copy(bf16[1,128,16,512]{1,3,2,0:T(8,128)(2,1)} %bitcast.193) | data formatting | bytes 4194304
  95.1 4.5 %copy.71 = bf16[1,128,16,512]{3,2,1,0:T(8,128)(2,1)} copy(bf16[1,128,16,512]{1,3,2,0:T(8,128)(2,1)} %fusion.25) | data formatting | bytes 4194304
  99.6 0.0 collective-permute-done.8
  99.7 0.7 slice_bitcast_fusion.5
  100.4 0.7 copy.72
  (21 shorter events, 0.2 us)
Async XLA Ops:
  0.6 11.3 %copy-start = (bf16[1,128,16,512]{3,2,1,0:T(8,128)(2,1)S(1)}, bf16[1,128,16,512]{3,2,1,0:T(8,128)(2,1)}, u32[]{:S(2)}) copy-start(bf16[1,128,16,512]{3,2,1,0:T(8,128)(2,1)} %param.13) | copy-start | bytes 6291460
  12.0 2.8 %copy-start.4 = (bf16[1,16,64,128]{3,2,1,0:T(8,128)(2,1)S(1)}, bf16[1,16,64,128]{3,2,1,0:T(8,128)(2,1)}, u32[]{:S(2)}) copy-start(bf16[1,16,64,128]{3,2,1,0:T(8,128)(2,1)} %param.14) | copy-start | bytes 786436
  15.7 4.7 %copy-start.1 = (f32[1,16,128,512]{2,3,1,0:T(8,128)}, f32[1,16,128,512]{2,3,1,0:T(8,128)S(1)}, u32[]{:S(2)}) copy-start(f32[1,16,128,512]{2,3,1,0:T(8,128)S(1)} %get-tuple-element.78) | copy-start | bytes 12582916
  29.3 6.8 %copy-start.2 = (f32[1,16,128,512]{2,3,1,0:T(8,128)S(1)}, f32[1,16,128,512]{2,3,1,0:T(8,128)}, u32[]{:S(2)}) copy-start(f32[1,16,128,512]{2,3,1,0:T(8,128)} %copy-done.1) | copy-start | bytes 12582916
  29.3 6.8 %copy-start.3 = (bf16[1,128,16,512]{3,2,1,0:T(8,128)(2,1)S(1)}, bf16[1,128,16,512]{3,2,1,0:T(8,128)(2,1)}, u32[]{:S(2)}) copy-start(bf16[1,128,16,512]{3,2,1,0:T(8,128)(2,1)} %param.17) | copy-start | bytes 6291460
  48.5 6.9 %collective-permute-start.2 = (bf16[128,576]{1,0:T(8,128)(2,1)}, bf16[128,576]{1,0:T(8,128)(2,1)}, u32[]{:S(2)}, u32[]{:S(2)}) collective-permute-start(bf16[128,576]{1,0:T(8,128)(2,1)} %get-tuple-element.70), channel_id=1, source_target_pairs={{24,0},{25,1},{26,2},{27,3},{28,4},{29,5},{30,6},{31,7}} | collective-permute-start | bytes 442376 | tf_op jit(solution)/shard_map/ppermute | solution.py:14
  49.8 9.2 %collective-permute-start.1 = (bf16[128,576]{1,0:T(8,128)(2,1)}, bf16[128,576]{1,0:T(8,128)(2,1)}, u32[]{:S(2)}, u32[]{:S(2)}) collective-permute-start(bf16[128,576]{1,0:T(8,128)(2,1)} %get-tuple-element.69), channel_id=1, source_target_pairs={{16,0},{24,8},{17,1},{25,9},{18,2},{26,10},{19,3},{27,11},{20,4},{... | collective-permute-start | bytes 442376 | tf_op jit(solution)/shard_map/ppermute | solution.py:14
  51.1 7.9 %collective-permute-start = (bf16[128,576]{1,0:T(8,128)(2,1)}, bf16[128,576]{1,0:T(8,128)(2,1)}, u32[]{:S(2)}, u32[]{:S(2)}) collective-permute-start(bf16[128,576]{1,0:T(8,128)(2,1)} %get-tuple-element.68), channel_id=1, source_target_pairs={{8,0},{16,8},{24,16},{9,1},{17,9},{25,17},{10,2},{18,10},{26,18},{... | collective-permute-start | bytes 442376 | tf_op jit(solution)/shard_map/ppermute | solution.py:14
  60.2 0.7 copy-start.5
  61.0 4.8 %collective-permute-start.3 = (bf16[2,2,16,576]{3,2,1,0:T(8,128)(2,1)S(1)}, bf16[2,2,16,576]{3,2,1,0:T(8,128)(2,1)S(1)}, u32[]{:S(2)}, u32[]{:S(2)}) collective-permute-start(bf16[2,2,16,576]{3,2,1,0:T(8,128)(2,1)S(1)} %bitcast_convert_fusion.1), channel_id=1, source_target_pairs={{0,1},{1,0},{2,3},{3,2},{4,5},{5,4},{6,7},{7,6},{8,9},{9,8},{10,11... | collective-permute-start | bytes 221192 | tf_op jit(solution)/shard_map/ppermute | solution.py:31
  66.7 4.1 %collective-permute-start.4 = (bf16[2,16,576]{2,1,0:T(8,128)(2,1)S(1)}, bf16[2,16,576]{2,1,0:T(8,128)(2,1)S(1)}, u32[]{:S(2)}, u32[]{:S(2)}) collective-permute-start(bf16[2,16,576]{2,1,0:T(8,128)(2,1)S(1)} %bitcast_convert_fusion.2), channel_id=1, source_target_pairs={{0,2},{1,3},{2,0},{3,1},{4,6},{5,7},{6,4},{7,5},{8,10},{9,11},{10,... | collective-permute-start | bytes 110600 | tf_op jit(solution)/shard_map/ppermute | solution.py:31
  70.8 4.7 %collective-permute-start.5 = (bf16[16,576]{1,0:T(8,128)(2,1)S(1)}, bf16[16,576]{1,0:T(8,128)(2,1)S(1)}, u32[]{:S(2)}, u32[]{:S(2)}) collective-permute-start(bf16[16,576]{1,0:T(8,128)(2,1)S(1)} %bitcast_convert_fusion.3), channel_id=1, source_target_pairs={{0,4},{1,5},{2,6},{3,7},{4,0},{5,1},{6,2},{7,3},{8,12},{9,13},{10,... | collective-permute-start | bytes 55304 | tf_op jit(solution)/shard_map/ppermute | solution.py:31
  75.6 4.9 %collective-permute-start.6 = (bf16[16,576]{1,0:T(8,128)(2,1)S(1)}, bf16[16,576]{1,0:T(8,128)(2,1)S(1)}, u32[]{:S(2)}, u32[]{:S(2)}) collective-permute-start(bf16[16,576]{1,0:T(8,128)(2,1)S(1)} %fusion.90), channel_id=1, source_target_pairs={{0,4},{1,5},{2,6},{3,7},{4,0},{5,1},{6,2},{7,3},{8,12},{9,13},{10,... | collective-permute-start | bytes 55304 | tf_op jit(solution)/shard_map/ppermute | solution.py:38
  80.4 5.7 %collective-permute-start.7 = (bf16[2,16,576]{2,1,0:T(8,128)(2,1)S(1)}, bf16[2,16,576]{2,1,0:T(8,128)(2,1)S(1)}, u32[]{:S(2)}, u32[]{:S(2)}) collective-permute-start(bf16[2,16,576]{2,1,0:T(8,128)(2,1)S(1)} %pad_maximum_fusion.3), channel_id=1, source_target_pairs={{0,2},{1,3},{2,0},{3,1},{4,6},{5,7},{6,4},{7,5},{8,10},{9,11},{10,... | collective-permute-start | bytes 110600 | tf_op jit(solution)/shard_map/ppermute | solution.py:38
  86.2 13.4 %collective-permute-start.8 = (bf16[2,2,16,576]{3,2,0,1:T(8,128)(2,1)S(1)}, bf16[2,2,16,576]{3,2,0,1:T(8,128)(2,1)S(1)}, u32[]{:S(2)}, u32[]{:S(2)}) collective-permute-start(bf16[2,2,16,576]{3,2,0,1:T(8,128)(2,1)S(1)} %pad_maximum_fusion.2), channel_id=1, source_target_pairs={{0,1},{1,0},{2,3},{3,2},{4,5},{5,4},{6,7},{7,6},{8,9},{9,8},{10,11... | collective-permute-start | bytes 221192 | tf_op jit(solution)/shard_map/ppermute | solution.py:38

commit v3 on v1

v3 whole, which is shorter than its diff:
```python
import jax
import jax.numpy as jnp
from jax import lax
from jax.experimental import pallas as pl
from jax.experimental.pallas import tpu as pltpu
from jax.sharding import PartitionSpec as P

scale_factor = 192.0 ** (-0.5)


def causal_reduce_ctx(blocks, n_ctx):
    here = lax.axis_index("ctx")
    total = jnp.take(blocks, here, axis=0).astype(jnp.float32)
    for shift in range(1, n_ctx):
        sent = jnp.take(blocks, jnp.maximum(here - shift, 0), axis=0)
        got = lax.ppermute(sent, "ctx", [(i, i - shift) for i in range(shift, n_ctx)])
        total = total + got.astype(jnp.float32)
    return total


def butterfly_sum_ep(total, n_ep):
    if n_ep & (n_ep - 1):
        return lax.psum(total.astype(jnp.bfloat16), "ep").astype(jnp.float32)
    bit = 1
    while bit < n_ep:
        mine = total.astype(jnp.bfloat16)
        theirs = lax.ppermute(mine, "ep", [(i, i ^ bit) for i in range(n_ep)])
        total = mine.astype(jnp.float32) + theirs.astype(jnp.float32)
        bit *= 2
    return total


def attention_kernel(ql_ref, qr_ref, qrt_ref, k_ref, kr_ref, do_ref, mask_ref,
                     att_ref, lqg_ref, rqg_ref, lt_ref, rt_ref):
    head = pl.program_id(0)
    f32 = jnp.float32
    nt = (((1,), (1,)), ((), ()))
    tn = (((0,), (0,)), ((), ()))
    q = ql_ref[...]
    k = k_ref[...]
    kr = kr_ref[...]
    dout = do_ref[...]
    scores = lax.dot_general(q, k, nt, preferred_element_type=f32)
    scores = scores + jnp.dot(qrt_ref[0], kr, preferred_element_type=f32)
    scores = jnp.where(mask_ref[...] != 0, scores * scale_factor, f32(-1e30))
    row_max = jnp.max(scores, axis=-1, keepdims=True)
    powers = jnp.exp(scores - row_max)
    weights = powers / jnp.sum(powers, axis=-1, keepdims=True)
    rounded = weights.astype(jnp.bfloat16)
    att = jnp.dot(rounded, k, preferred_element_type=f32).astype(jnp.bfloat16)
    att_ref[...] = att
    row_dots = jnp.sum(dout.astype(f32) * att.astype(f32), axis=-1, keepdims=True)
    weight_grad = lax.dot_general(dout, k, nt, preferred_element_type=f32)
    score_grad = (weights * (weight_grad - row_dots)).astype(jnp.bfloat16)
    lqg_ref[...] = (scale_factor * jnp.dot(score_grad, k, preferred_element_type=f32)).astype(jnp.bfloat16)
    rqg_ref[0] = (
        scale_factor * lax.dot_general(kr, score_grad, nt, preferred_element_type=f32)
    ).astype(jnp.bfloat16)
    lt = scale_factor * lax.dot_general(score_grad, q, tn, preferred_element_type=f32)
    lt = lt + lax.dot_general(rounded, dout, tn, preferred_element_type=f32)
    rt = scale_factor * jnp.dot(qr_ref[0], score_grad, preferred_element_type=f32)

    @pl.when(head == 0)
    def _():
        lt_ref[...] = lt
        rt_ref[...] = rt

    @pl.when(head > 0)
    def _():
        lt_ref[...] += lt
        rt_ref[...] += rt


def body(query_latent, query_rope, key_latent, key_rope, output_grad):
    n_ctx = lax.axis_size("ctx")
    n_ep = lax.axis_size("ep")
    _, block_len, heads, kvr = query_latent.shape
    rope = query_rope.shape[2]
    local_keys = jnp.concatenate([key_latent[0], key_rope[0].T], axis=1)
    whole_keys = lax.all_gather(local_keys, "ctx", axis=0, tiled=True)
    whole_latent = whole_keys[:, :kvr]
    whole_rope = whole_keys[:, kvr:].T
    length = whole_latent.shape[0]
    offset = lax.axis_index("ctx") * block_len
    query_place = offset + jnp.arange(block_len, dtype=jnp.int32)
    allowed = (jnp.arange(length, dtype=jnp.int32)[None, :] <= query_place[:, None]).astype(jnp.int32)
    ql = query_latent.reshape(block_len, heads * kvr)
    dout = output_grad.reshape(block_len, heads * kvr)
    qr = query_rope[0]
    qrt = jnp.swapaxes(qr, 1, 2)
    by_head = pl.BlockSpec((block_len, kvr), lambda h: (0, h))
    rope_head = pl.BlockSpec((1, rope, block_len), lambda h: (h, 0, 0))
    fixed = lambda shape: pl.BlockSpec(shape, lambda h: (0,) * len(shape))
    att, lqg, rqg, lt, rt = pl.pallas_call(
        attention_kernel,
        grid=(heads,),
        in_specs=[
            by_head,
            rope_head,
            pl.BlockSpec((1, block_len, rope), lambda h: (h, 0, 0)),
            fixed((length, kvr)),
            fixed((rope, length)),
            by_head,
            fixed((block_len, length)),
        ],
        out_specs=[
            by_head,
            by_head,
            rope_head,
            fixed((length, kvr)),
            fixed((rope, length)),
        ],
        out_shape=[
            jax.ShapeDtypeStruct((block_len, heads * kvr), jnp.bfloat16),
            jax.ShapeDtypeStruct((block_len, heads * kvr), jnp.bfloat16),
            jax.ShapeDtypeStruct((heads, rope, block_len), jnp.bfloat16),
            jax.ShapeDtypeStruct((length, kvr), jnp.float32),
            jax.ShapeDtypeStruct((rope, length), jnp.float32),
        ],
        compiler_params=pltpu.CompilerParams(dimension_semantics=("arbitrary",)),
    )(ql, qr, qrt, whole_latent, whole_rope, dout, allowed)
    attended = att.reshape(query_latent.shape)
    latent_qgrad = lqg.reshape(query_latent.shape)
    rope_qgrad = rqg[None]
    terms = jnp.concatenate([lt, rt.T], axis=1).astype(jnp.bfloat16)
    total = causal_reduce_ctx(terms.reshape(n_ctx, block_len, -1), n_ctx)
    total = butterfly_sum_ep(total, n_ep).astype(jnp.bfloat16)
    latent_kgrad = total[None, :, :kvr]
    rope_kgrad = total[:, kvr:].T[None]
    return (attended, latent_qgrad, rope_qgrad, latent_kgrad, rope_kgrad)


def solution(mesh):
    placed = (
        P(None, "ctx", "ep", None),
        P(None, "ep", None, "ctx"),
        P(None, "ctx", None),
        P(None, None, "ctx"),
        P(None, "ctx", "ep", None),
    )
    return jax.shard_map(
        body,
        mesh=mesh,
        in_specs=placed,
        out_specs=(
            P(None, "ctx", "ep", None),
            P(None, "ctx", "ep", None),
            P(None, "ep", None, "ctx"),
            P(None, "ctx", None),
            P(None, None, "ctx"),
        ),
        check_vma=False,
    )
```

time: 94.3 us -> 85.6 us (0.908)
  matrix products: 33.1 us -> 0 us
  Pallas kernels: 0 us -> 27 us
  other arithmetic: 7.04 us -> 4.94 us
  local copies, waits for them, and re-layouts: 17 us -> 15.1 us
  waiting for transfers between devices: 16.8 us -> 18.6 us
    dot_general x9 -> x0, matrix products: 33.1 us -> none  [the longest x1 6.77 us: body(): jnp.einsum('shtj,sthd->jd', rounded_weights, output_grad, preferred_eleme...]
    pallas_call x0 -> x1, Pallas kernels: none -> 27 us  [body(): pl.pallas_call(attention_kernel, grid=(heads,), in_specs=[by_head, rope_h...]
    unnamed x15 -> x17, local copies, waits for them, and re-layouts: 16.2 us -> 12.7 us
    unnamed x1 -> x0, other arithmetic: 3.35 us -> none
    ppermute x3, waiting for transfers between devices: 6.64 us -> 8.73 us  [causal_reduce_ctx(): lax.ppermute(sent, 'ctx', [(i, i - shift) for i in range(shift, n_ctx)])]
    another operation x0 -> x1, other arithmetic: none -> 1.29 us
    convert_element_type x3, other arithmetic: 1.26 us -> 0.19 us  [butterfly_sum_ep(): mine = total.astype(jnp.bfloat16)]
    transpose x0 -> x1, other arithmetic: none -> 1.06 us  [body(): terms = jnp.concatenate([lt, rt.T], axis=1).astype(jnp.bfloat16)]
  transfers between devices with their start and end apart: 6 -> 6, of which waited for: 4 -> 5; matrix products, arithmetic and copies ran while one was open for 17% -> 5% of each run, Pallas kernels for 0% -> 0%
where the time goes in v3:
time: 85.6 us; the launch traced here: 85.3 us
  Pallas kernels  27 us (32%)
  waiting for transfers between devices  18.6 us (22%)
  local copies, waits for them, and re-layouts  15.1 us (18%)
  starting transfers between devices  9.86 us (12%)
  blocking collectives  8.98 us (10%)
  other arithmetic  4.94 us (6%)
    pallas_call x1, Pallas kernels, body(): pl.pallas_call(attention_kernel, grid=(heads,), in_specs=[by_head, rope_h...  27 us
    unnamed x17, local copies, waits for them, and re-layouts  12.7 us
    ppermute x3, waiting for transfers between devices, butterfly_sum_ep(): theirs = lax.ppermute(mine, 'ep', [(i, i ^ bit) for i in range(n_ep)])  9.89 us
    all_gather x1, blocking collectives, body(): whole_keys = lax.all_gather(local_keys, 'ctx', axis=0, tiled=True)  8.98 us
    ppermute x3, waiting for transfers between devices, causal_reduce_ctx(): lax.ppermute(sent, 'ctx', [(i, i - shift) for i in range(shift, n_ctx)])  8.73 us
    ppermute x3, starting transfers between devices, butterfly_sum_ep(): theirs = lax.ppermute(mine, 'ep', [(i, i ^ bit) for i in range(n_ep)])  6 us
    ppermute x3, starting transfers between devices, causal_reduce_ctx(): lax.ppermute(sent, 'ctx', [(i, i - shift) for i in range(shift, n_ctx)])  3.86 us
  transfers between devices with their start and end apart: 6, of which 5 were waited for; matrix products, arithmetic and copies ran while one was open for 5% of the time, Pallas kernels for 0%

profile of v3, /device:TPU:0, one launch (start us, length us, event | category | flops | bytes accessed | tf_op | source)
XLA Modules:
  0.0 85.3 jit_solution(1374864877886679028)
XLA Ops:
  0.6 0.0 copy-start
  0.6 1.2 %copy.17 = bf16[1,128,512]{1,2,0:T(8,128)(2,1)S(1)} copy(bf16[1,128,512]{2,1,0:T(8,128)(2,1)} %param.9) | data formatting | bytes 262144 | tf_op args[2]
  1.8 0.7 pad_maximum_fusion
  2.6 9.0 %all_gather.3 = bf16[512,576]{0,1:T(8,128)(2,1)S(1)} all-gather(bf16[128,576]{0,1:T(8,128)(2,1)S(1)} %pad_maximum_fusion), channel_id=1, replica_groups=mesh['ctx'=4,'ep'=8] {'ctx'}, dimensions={0}, use_global_device_ids=true | all-gather | bytes 737280 | tf_op jit(solution)/shard_map/all_gather | solution.py:80
  11.6 0.6 slice_bitcast_fusion.1.kr_ref
  12.2 0.8 fusion.mask_ref
  13.0 1.0 %copy.19.k_ref = bf16[512,512]{1,0:T(8,128)(2,1)} copy(bf16[512,512]{0,1:T(8,128)(2,1)S(1)} %slice.25) | data formatting | bytes 1048576 | tf_op jit(solution)/shard_map/slice | solution.py:81
  14.0 0.0 copy-done
  14.0 0.0 copy-start.1
  14.0 2.7 %copy.24 = bf16[16,8,16,512]{3,1,2,0:T(8,128)(2,1)} copy(bf16[16,8,16,512]{3,2,1,0:T(8,128)(2,1)S(1)} %bitcast.48) | data formatting | bytes 4194304
  16.7 0.0 copy-done.1
  16.7 0.0 copy-start.4
  16.7 2.7 %copy.25 = bf16[16,8,16,512]{3,1,2,0:T(8,128)(2,1)} copy(bf16[16,8,16,512]{3,2,1,0:T(8,128)(2,1)S(1)} %bitcast.49) | data formatting | bytes 4194304
  19.4 0.0 copy-done.4
  19.5 1.1 %copy.16 = bf16[1,16,64,128]{2,3,1,0:T(8,128)(2,1)} copy(bf16[1,16,64,128]{3,2,1,0:T(8,128)(2,1)S(1)} %copy-done.4) | data formatting | bytes 524288 | tf_op args[1]
  20.5 27.0 %shard_map.92 = (bf16[128,8192]{1,0:T(8,128)(2,1)}, bf16[128,8192]{1,0:T(8,128)(2,1)}, bf16[16,64,128]{2,1,0:T(8,128)(2,1)}, f32[512,512]{1,0:T(8,128)}, f32[64,512]{1,0:T(8,128)}) custom-call(bf16[128,8192]{1,0:T(8,128)(2,1)} %bitcast.43, bf16[16,64,128]{2,1,0:T(8,128)(2,1)} %bitcast.56, bf16[16,128,64]{2,1,0:T(8,128)(2,1)} %bitcast.47, ...), custom_call_target="tpu_custom_call" | custom-call | tf_op jit(solution)/shard_map/pallas_call | solution.py:94
  47.5 1.3 %convert.9 = bf16[512,512]{1,0:T(8,128)(2,1)S(1)} convert(f32[512,512]{1,0:T(8,128)} %get-tuple-element.14) | non-fusion elementwise | flops 262144 | bytes 1572864 | tf_op jit(solution)/shard_map/convert.4
  48.8 0.0 copy-start.3
  48.8 1.1 %convert_bitcast_fusion = bf16[512,64]{0,1:T(8,128)(2,1)S(1)} fusion(f32[64,512]{1,0:T(8,128)} %get-tuple-element.15), kind=kLoop, calls=%fused_computation.29 | loop fusion | flops 32768 | bytes 196608 | tf_op jit(solution)/shard_map/transpose | solution.py:125
  49.9 0.1 copy.23
  50.0 0.8 fusion.9
  50.8 1.3 %collective-permute-start = (bf16[128,576]{1,0:T(8,128)(2,1)}, bf16[128,576]{1,0:T(8,128)(2,1)S(1)}, u32[]{:S(2)}, u32[]{:S(2)}) collective-permute-start(bf16[128,576]{1,0:T(8,128)(2,1)} %get-tuple-element.32), channel_id=1, source_target_pairs={{8,0},{16,8},{24,16},{9,1},{17,9},{25,17},{10,2},{18,10},{26,18},{... | collective-permute-start | bytes 442376 | tf_op jit(solution)/shard_map/ppermute | solution.py:16
  52.1 1.3 %collective-permute-start.1 = (bf16[128,576]{1,0:T(8,128)(2,1)}, bf16[128,576]{1,0:T(8,128)(2,1)S(1)}, u32[]{:S(2)}, u32[]{:S(2)}) collective-permute-start(bf16[128,576]{1,0:T(8,128)(2,1)} %get-tuple-element.33), channel_id=1, source_target_pairs={{16,0},{24,8},{17,1},{25,9},{18,2},{26,10},{19,3},{27,11},{20,4},{... | collective-permute-start | bytes 442376 | tf_op jit(solution)/shard_map/ppermute | solution.py:16
  53.4 1.3 %collective-permute-start.2 = (bf16[128,576]{1,0:T(8,128)(2,1)S(1)}, bf16[128,576]{1,0:T(8,128)(2,1)S(1)}, u32[]{:S(2)}, u32[]{:S(2)}) collective-permute-start(bf16[128,576]{1,0:T(8,128)(2,1)S(1)} %get-tuple-element.34), channel_id=1, source_target_pairs={{24,0},{25,1},{26,2},{27,3},{28,4},{29,5},{30,6},{31,7}} | collective-permute-start | bytes 442376 | tf_op jit(solution)/shard_map/ppermute | solution.py:16
  54.7 0.0 collective-permute-done
  54.7 7.2 %collective-permute-done.1 = bf16[128,576]{1,0:T(8,128)(2,1)S(1)} collective-permute-done((bf16[128,576]{1,0:T(8,128)(2,1)}, bf16[128,576]{1,0:T(8,128)(2,1)S(1)}, u32[]{:S(2)}, u32[]{:S(2)}) %collective-permute-start.1) | collective-permute-done | bytes 147488 | tf_op jit(solution)/shard_map/ppermute | solution.py:16
  61.9 1.6 %collective-permute-done.2 = bf16[128,576]{1,0:T(8,128)(2,1)S(1)} collective-permute-done((bf16[128,576]{1,0:T(8,128)(2,1)S(1)}, bf16[128,576]{1,0:T(8,128)(2,1)S(1)}, u32[]{:S(2)}, u32[]{:S(2)}) %collective-permute-start.2) | collective-permute-done | bytes 147488 | tf_op jit(solution)/shard_map/ppermute | solution.py:16
  63.5 0.1 add_convert_fusion.3
  63.6 1.6 %collective-permute-start.3 = (bf16[128,576]{1,0:T(8,128)(2,1)S(1)}, bf16[128,576]{1,0:T(8,128)(2,1)S(1)}, u32[]{:S(2)}, u32[]{:S(2)}) collective-permute-start(bf16[128,576]{1,0:T(8,128)(2,1)S(1)} %add_convert_fusion.3), channel_id=1, source_target_pairs={{0,1},{1,0},{2,3},{3,2},{4,5},{5,4},{6,7},{7,6},{8,9},{9,8},{10,11... | collective-permute-start | bytes 442376 | tf_op jit(solution)/shard_map/ppermute | solution.py:27
  65.2 3.8 %collective-permute-done.3 = bf16[128,576]{1,0:T(8,128)(2,1)S(1)} collective-permute-done((bf16[128,576]{1,0:T(8,128)(2,1)S(1)}, bf16[128,576]{1,0:T(8,128)(2,1)S(1)}, u32[]{:S(2)}, u32[]{:S(2)}) %collective-permute-start.3) | collective-permute-done | bytes 147488 | tf_op jit(solution)/shard_map/ppermute | solution.py:27
  69.0 1.7 %collective-permute-start.4 = (bf16[128,576]{1,0:T(8,128)(2,1)S(1)}, bf16[128,576]{1,0:T(8,128)(2,1)S(1)}, u32[]{:S(2)}, u32[]{:S(2)}) collective-permute-start(bf16[128,576]{1,0:T(8,128)(2,1)S(1)} %add_convert_fusion.2), channel_id=1, source_target_pairs={{0,2},{1,3},{2,0},{3,1},{4,6},{5,7},{6,4},{7,5},{8,10},{9,11},{10,... | collective-permute-start | bytes 442376 | tf_op jit(solution)/shard_map/ppermute | solution.py:27
  70.7 5.2 %collective-permute-done.4 = bf16[128,576]{1,0:T(8,128)(2,1)S(1)} collective-permute-done((bf16[128,576]{1,0:T(8,128)(2,1)S(1)}, bf16[128,576]{1,0:T(8,128)(2,1)S(1)}, u32[]{:S(2)}, u32[]{:S(2)}) %collective-permute-start.4) | collective-permute-done | bytes 147488 | tf_op jit(solution)/shard_map/ppermute | solution.py:27
  75.9 2.7 %collective-permute-start.5 = (bf16[128,576]{1,0:T(8,128)(2,1)S(1)}, bf16[128,576]{1,0:T(8,128)(2,1)S(1)}, u32[]{:S(2)}, u32[]{:S(2)}) collective-permute-start(bf16[128,576]{1,0:T(8,128)(2,1)S(1)} %add_convert_fusion.1), channel_id=1, source_target_pairs={{0,4},{1,5},{2,6},{3,7},{4,0},{5,1},{6,2},{7,3},{8,12},{9,13},{10,... | collective-permute-start | bytes 442376 | tf_op jit(solution)/shard_map/ppermute | solution.py:27
  78.6 0.0 copy-done.3
  78.6 0.0 copy-start.2
  78.6 2.1 %copy.26 = bf16[16,8,16,512]{3,2,1,0:T(8,128)(2,1)} copy(bf16[16,8,16,512]{3,1,2,0:T(8,128)(2,1)S(1)} %bitcast.51) | data formatting | bytes 4194304
  80.8 0.0 copy-done.2
  80.8 2.1 %copy.27 = bf16[16,8,16,512]{3,2,1,0:T(8,128)(2,1)} copy(bf16[16,8,16,512]{3,1,2,0:T(8,128)(2,1)S(1)} %bitcast.50) | data formatting | bytes 4194304
  82.9 0.9 %collective-permute-done.5 = bf16[128,576]{1,0:T(8,128)(2,1)S(1)} collective-permute-done((bf16[128,576]{1,0:T(8,128)(2,1)S(1)}, bf16[128,576]{1,0:T(8,128)(2,1)S(1)}, u32[]{:S(2)}, u32[]{:S(2)}) %collective-permute-start.5) | collective-permute-done | bytes 147488 | tf_op jit(solution)/shard_map/ppermute | solution.py:27
  83.9 0.7 slice_bitcast_fusion
  84.6 0.7 copy.21
  (6 shorter events, 0.2 us)
Async XLA Ops:
  0.6 13.4 %copy-start = (bf16[1,128,16,512]{3,2,1,0:T(8,128)(2,1)S(1)}, bf16[1,128,16,512]{3,2,1,0:T(8,128)(2,1)}, u32[]{:S(2)}) copy-start(bf16[1,128,16,512]{3,2,1,0:T(8,128)(2,1)} %param.7) | copy-start | bytes 6291460
  14.0 2.7 %copy-start.1 = (bf16[1,128,16,512]{3,2,1,0:T(8,128)(2,1)S(1)}, bf16[1,128,16,512]{3,2,1,0:T(8,128)(2,1)}, u32[]{:S(2)}) copy-start(bf16[1,128,16,512]{3,2,1,0:T(8,128)(2,1)} %param.11) | copy-start | bytes 6291460
  16.7 2.7 %copy-start.4 = (bf16[1,16,64,128]{3,2,1,0:T(8,128)(2,1)S(1)}, bf16[1,16,64,128]{3,2,1,0:T(8,128)(2,1)}, u32[]{:S(2)}) copy-start(bf16[1,16,64,128]{3,2,1,0:T(8,128)(2,1)} %param.8) | copy-start | bytes 786436
  48.8 29.8 %copy-start.3 = (bf16[128,8192]{1,0:T(8,128)(2,1)S(1)}, bf16[128,8192]{1,0:T(8,128)(2,1)}, u32[]{:S(2)}) copy-start(bf16[128,8192]{1,0:T(8,128)(2,1)} %get-tuple-element.11) | copy-start | bytes 6291460
  50.8 3.9 %collective-permute-start = (bf16[128,576]{1,0:T(8,128)(2,1)}, bf16[128,576]{1,0:T(8,128)(2,1)S(1)}, u32[]{:S(2)}, u32[]{:S(2)}) collective-permute-start(bf16[128,576]{1,0:T(8,128)(2,1)} %get-tuple-element.32), channel_id=1, source_target_pairs={{8,0},{16,8},{24,16},{9,1},{17,9},{25,17},{10,2},{18,10},{26,18},{... | collective-permute-start | bytes 442376 | tf_op jit(solution)/shard_map/ppermute | solution.py:16
  52.1 9.8 %collective-permute-start.1 = (bf16[128,576]{1,0:T(8,128)(2,1)}, bf16[128,576]{1,0:T(8,128)(2,1)S(1)}, u32[]{:S(2)}, u32[]{:S(2)}) collective-permute-start(bf16[128,576]{1,0:T(8,128)(2,1)} %get-tuple-element.33), channel_id=1, source_target_pairs={{16,0},{24,8},{17,1},{25,9},{18,2},{26,10},{19,3},{27,11},{20,4},{... | collective-permute-start | bytes 442376 | tf_op jit(solution)/shard_map/ppermute | solution.py:16
  53.4 10.0 %collective-permute-start.2 = (bf16[128,576]{1,0:T(8,128)(2,1)S(1)}, bf16[128,576]{1,0:T(8,128)(2,1)S(1)}, u32[]{:S(2)}, u32[]{:S(2)}) collective-permute-start(bf16[128,576]{1,0:T(8,128)(2,1)S(1)} %get-tuple-element.34), channel_id=1, source_target_pairs={{24,0},{25,1},{26,2},{27,3},{28,4},{29,5},{30,6},{31,7}} | collective-permute-start | bytes 442376 | tf_op jit(solution)/shard_map/ppermute | solution.py:16
  63.6 5.4 %collective-permute-start.3 = (bf16[128,576]{1,0:T(8,128)(2,1)S(1)}, bf16[128,576]{1,0:T(8,128)(2,1)S(1)}, u32[]{:S(2)}, u32[]{:S(2)}) collective-permute-start(bf16[128,576]{1,0:T(8,128)(2,1)S(1)} %add_convert_fusion.3), channel_id=1, source_target_pairs={{0,1},{1,0},{2,3},{3,2},{4,5},{5,4},{6,7},{7,6},{8,9},{9,8},{10,11... | collective-permute-start | bytes 442376 | tf_op jit(solution)/shard_map/ppermute | solution.py:27
  69.0 6.8 %collective-permute-start.4 = (bf16[128,576]{1,0:T(8,128)(2,1)S(1)}, bf16[128,576]{1,0:T(8,128)(2,1)S(1)}, u32[]{:S(2)}, u32[]{:S(2)}) collective-permute-start(bf16[128,576]{1,0:T(8,128)(2,1)S(1)} %add_convert_fusion.2), channel_id=1, source_target_pairs={{0,2},{1,3},{2,0},{3,1},{4,6},{5,7},{6,4},{7,5},{8,10},{9,11},{10,... | collective-permute-start | bytes 442376 | tf_op jit(solution)/shard_map/ppermute | solution.py:27
  75.9 8.0 %collective-permute-start.5 = (bf16[128,576]{1,0:T(8,128)(2,1)S(1)}, bf16[128,576]{1,0:T(8,128)(2,1)S(1)}, u32[]{:S(2)}, u32[]{:S(2)}) collective-permute-start(bf16[128,576]{1,0:T(8,128)(2,1)S(1)} %add_convert_fusion.1), channel_id=1, source_target_pairs={{0,4},{1,5},{2,6},{3,7},{4,0},{5,1},{6,2},{7,3},{8,12},{9,13},{10,... | collective-permute-start | bytes 442376 | tf_op jit(solution)/shard_map/ppermute | solution.py:27
  78.6 2.2 %copy-start.2 = (bf16[128,8192]{1,0:T(8,128)(2,1)S(1)}, bf16[128,8192]{1,0:T(8,128)(2,1)}, u32[]{:S(2)}) copy-start(bf16[128,8192]{1,0:T(8,128)(2,1)} %get-tuple-element.12) | copy-start | bytes 6291460

commit v4 on v3

v4 whole, which is shorter than its diff:
```python
import jax
import jax.numpy as jnp
from jax import lax
from jax.experimental import pallas as pl
from jax.experimental.pallas import tpu as pltpu
from jax.sharding import PartitionSpec as P

scale_factor = 192.0 ** (-0.5)


def causal_reduce_ctx(blocks, n_ctx):
    here = lax.axis_index("ctx")
    total = jnp.take(blocks, here, axis=0).astype(jnp.float32)
    for shift in range(1, n_ctx):
        sent = jnp.take(blocks, jnp.maximum(here - shift, 0), axis=0)
        got = lax.ppermute(sent, "ctx", [(i, i - shift) for i in range(shift, n_ctx)])
        total = total + got.astype(jnp.float32)
    return total


def butterfly_sum_ep(total, n_ep):
    if n_ep & (n_ep - 1):
        return lax.psum(total.astype(jnp.bfloat16), "ep").astype(jnp.float32)
    bit = 1
    while bit < n_ep:
        mine = total.astype(jnp.bfloat16)
        theirs = lax.ppermute(mine, "ep", [(i, i ^ bit) for i in range(n_ep)])
        total = mine.astype(jnp.float32) + theirs.astype(jnp.float32)
        bit *= 2
    return total


def attention_kernel(offset_ref, ql_ref, qr_ref, k_ref, kr_ref, do_ref,
                     att_ref, lqg_ref, rqg_ref, lt_ref, rt_ref):
    step = pl.program_id(0)
    t_blk, heads, kvr = ql_ref.shape
    rope = qr_ref.shape[2]
    rows = t_blk * heads
    f32 = jnp.float32
    nt = (((1,), (1,)), ((), ()))
    tn = (((0,), (0,)), ((), ()))
    q = ql_ref[...].reshape(rows, kvr)
    qr = qr_ref[...].reshape(rows, rope)
    k = k_ref[...]
    kr = kr_ref[...]
    dout = do_ref[...].reshape(rows, kvr)
    length = k.shape[0]
    scores = lax.dot_general(q, k, nt, preferred_element_type=f32)
    scores = scores + jnp.dot(qr, kr, preferred_element_type=f32)
    row = lax.broadcasted_iota(jnp.int32, (rows, length), 0)
    col = lax.broadcasted_iota(jnp.int32, (rows, length), 1)
    allowed = row >= heads * (col - offset_ref[0] - step * t_blk)
    scores = jnp.where(allowed, scores * scale_factor, f32(-1e30))
    row_max = jnp.max(scores, axis=-1, keepdims=True)
    powers = jnp.exp(scores - row_max)
    weights = powers / jnp.sum(powers, axis=-1, keepdims=True)
    rounded = weights.astype(jnp.bfloat16)
    att = jnp.dot(rounded, k, preferred_element_type=f32).astype(jnp.bfloat16)
    att_ref[...] = att.reshape(t_blk, heads, kvr)
    row_dots = jnp.sum(dout.astype(f32) * att.astype(f32), axis=-1, keepdims=True)
    weight_grad = lax.dot_general(dout, k, nt, preferred_element_type=f32)
    score_grad = (weights * (weight_grad - row_dots)).astype(jnp.bfloat16)
    lqg = scale_factor * jnp.dot(score_grad, k, preferred_element_type=f32)
    lqg_ref[...] = lqg.astype(jnp.bfloat16).reshape(t_blk, heads, kvr)
    rqg = scale_factor * lax.dot_general(score_grad, kr, nt, preferred_element_type=f32)
    rqg_ref[...] = rqg.astype(jnp.bfloat16).reshape(t_blk, heads, rope)
    lt = scale_factor * lax.dot_general(score_grad, q, tn, preferred_element_type=f32)
    lt = lt + lax.dot_general(rounded, dout, tn, preferred_element_type=f32)
    rt = scale_factor * lax.dot_general(score_grad, qr, tn, preferred_element_type=f32)

    @pl.when(step == 0)
    def _():
        lt_ref[...] = lt
        rt_ref[...] = rt

    @pl.when(step > 0)
    def _():
        lt_ref[...] += lt
        rt_ref[...] += rt


def body(query_latent, query_rope, key_latent, key_rope, output_grad):
    n_ctx = lax.axis_size("ctx")
    n_ep = lax.axis_size("ep")
    _, block_len, heads, kvr = query_latent.shape
    rope = query_rope.shape[2]
    local_keys = jnp.concatenate([key_latent[0], key_rope[0].T], axis=1)
    whole_keys = lax.all_gather(local_keys, "ctx", axis=0, tiled=True)
    whole_latent = whole_keys[:, :kvr]
    whole_rope = whole_keys[:, kvr:].T
    length = whole_latent.shape[0]
    offset = (lax.axis_index("ctx") * block_len).astype(jnp.int32).reshape(1)
    qr = jnp.transpose(query_rope[0], (2, 0, 1))
    t_blk = max(1, min(block_len, 256 // heads))
    while block_len % t_blk:
        t_blk -= 1
    by_rows = pl.BlockSpec((t_blk, heads, kvr), lambda i, off: (i, 0, 0))
    rope_rows = pl.BlockSpec((t_blk, heads, rope), lambda i, off: (i, 0, 0))
    fixed = lambda shape: pl.BlockSpec(shape, lambda i, off: (0,) * len(shape))
    att, lqg, rqg, lt, rt = pl.pallas_call(
        attention_kernel,
        grid_spec=pltpu.PrefetchScalarGridSpec(
            num_scalar_prefetch=1,
            grid=(block_len // t_blk,),
            in_specs=[
                by_rows,
                rope_rows,
                fixed((length, kvr)),
                fixed((rope, length)),
                by_rows,
            ],
            out_specs=[
                by_rows,
                by_rows,
                rope_rows,
                fixed((length, kvr)),
                fixed((length, rope)),
            ],
        ),
        out_shape=[
            jax.ShapeDtypeStruct((block_len, heads, kvr), jnp.bfloat16),
            jax.ShapeDtypeStruct((block_len, heads, kvr), jnp.bfloat16),
            jax.ShapeDtypeStruct((block_len, heads, rope), jnp.bfloat16),
            jax.ShapeDtypeStruct((length, kvr), jnp.float32),
            jax.ShapeDtypeStruct((length, rope), jnp.float32),
        ],
        compiler_params=pltpu.CompilerParams(dimension_semantics=("arbitrary",)),
    )(offset, query_latent[0], qr, whole_latent, whole_rope, output_grad[0])
    attended = att[None]
    latent_qgrad = lqg[None]
    rope_qgrad = jnp.transpose(rqg, (1, 2, 0))[None]
    terms = jnp.concatenate([lt, rt], axis=1).astype(jnp.bfloat16)
    total = causal_reduce_ctx(terms.reshape(n_ctx, block_len, -1), n_ctx)
    total = butterfly_sum_ep(total, n_ep).astype(jnp.bfloat16)
    latent_kgrad = total[None, :, :kvr]
    rope_kgrad = total[:, kvr:].T[None]
    return (attended, latent_qgrad, rope_qgrad, latent_kgrad, rope_kgrad)


def solution(mesh):
    placed = (
        P(None, "ctx", "ep", None),
        P(None, "ep", None, "ctx"),
        P(None, "ctx", None),
        P(None, None, "ctx"),
        P(None, "ctx", "ep", None),
    )
    return jax.shard_map(
        body,
        mesh=mesh,
        in_specs=placed,
        out_specs=(
            P(None, "ctx", "ep", None),
            P(None, "ctx", "ep", None),
            P(None, "ep", None, "ctx"),
            P(None, "ctx", None),
            P(None, None, "ctx"),
        ),
        check_vma=False,
    )
```

time: 85.6 us -> 67.7 us (0.79)
  Pallas kernels: 27 us -> 16.3 us
  local copies, waits for them, and re-layouts: 15.1 us -> 6.46 us
  waiting for transfers between devices: 18.6 us -> 21.6 us
  other arithmetic: 4.94 us -> 3.38 us
    pallas_call x1, Pallas kernels: 27 us -> 16.3 us  [body(): pl.pallas_call(attention_kernel, grid_spec=pltpu.PrefetchScalarGridSpec(n...]
    unnamed x17 -> x8, local copies, waits for them, and re-layouts: 12.7 us -> 4.13 us
    ppermute x3, waiting for transfers between devices: 9.89 us -> 13 us  [butterfly_sum_ep(): theirs = lax.ppermute(mine, 'ep', [(i, i ^ bit) for i in range(n_ep)])]
    transpose x1 -> x0, other arithmetic: 1.06 us -> none  [body(): terms = jnp.concatenate([lt, rt.T], axis=1).astype(jnp.bfloat16)]
    another operation x1 -> x2, other arithmetic: 1.29 us -> 2.32 us
  transfers between devices with their start and end apart: 6 -> 6, of which waited for: 5 -> 5; matrix products, arithmetic and copies ran while one was open for 5% -> 2% of each run, Pallas kernels for 0% -> 0%
where the time goes in v4:
time: 67.7 us; the launch traced here: 67.3 us
  waiting for transfers between devices  21.6 us (32%)
  Pallas kernels  16.3 us (24%)
  starting transfers between devices  9.87 us (15%)
  blocking collectives  8.98 us (13%)
  local copies, waits for them, and re-layouts  6.46 us (10%)
  other arithmetic  3.38 us (5%)
  between operations  0.75 us (1%)
    pallas_call x1, Pallas kernels, body(): pl.pallas_call(attention_kernel, grid_spec=pltpu.PrefetchScalarGridSpec(n...  16.3 us
    ppermute x3, waiting for transfers between devices, butterfly_sum_ep(): theirs = lax.ppermute(mine, 'ep', [(i, i ^ bit) for i in range(n_ep)])  13 us
    all_gather x1, blocking collectives, body(): whole_keys = lax.all_gather(local_keys, 'ctx', axis=0, tiled=True)  8.98 us
    ppermute x3, waiting for transfers between devices, causal_reduce_ctx(): lax.ppermute(sent, 'ctx', [(i, i - shift) for i in range(shift, n_ctx)])  8.52 us
    ppermute x3, starting transfers between devices, butterfly_sum_ep(): theirs = lax.ppermute(mine, 'ep', [(i, i ^ bit) for i in range(n_ep)])  5.99 us
    unnamed x8, local copies, waits for them, and re-layouts  4.13 us
    ppermute x3, starting transfers between devices, causal_reduce_ctx(): lax.ppermute(sent, 'ctx', [(i, i - shift) for i in range(shift, n_ctx)])  3.88 us
    another operation x2, other arithmetic  2.32 us
  transfers between devices with their start and end apart: 6, of which 5 were waited for; matrix products, arithmetic and copies ran while one was open for 2% of the time, Pallas kernels for 0%

profile of v4, /device:TPU:0, one launch (start us, length us, event | category | flops | bytes accessed | tf_op | source)
XLA Modules:
  0.0 67.3 jit_solution(5151339382045147433)
XLA Ops:
  0.6 0.0 copy-start.1
  0.6 1.1 %copy.17 = bf16[1,128,512]{1,2,0:T(8,128)(2,1)S(1)} copy(bf16[1,128,512]{2,1,0:T(8,128)(2,1)} %param.9) | data formatting | bytes 262144 | tf_op args[2]
  1.7 0.7 %pad_maximum_fusion = bf16[128,576]{0,1:T(8,128)(2,1)S(1)} fusion(bf16[128,64]{0,1:T(8,128)(2,1)} %bitcast.44, bf16[128,512]{0,1:T(8,128)(2,1)S(1)} %bitcast.43), kind=kLoop, calls=%fused_computation.24 | loop fusion | flops 294912 | bytes 294912 | tf_op jit(solution)/shard_map/concatenate | solution.py:87
  2.4 9.0 %all_gather.3 = bf16[512,576]{0,1:T(8,128)(2,1)S(1)} all-gather(bf16[128,576]{0,1:T(8,128)(2,1)S(1)} %pad_maximum_fusion), channel_id=1, replica_groups=mesh['ctx'=4,'ep'=8] {'ctx'}, dimensions={0}, use_global_device_ids=true | all-gather | bytes 737280 | tf_op jit(solution)/shard_map/all_gather | solution.py:88
  11.5 0.6 slice_bitcast_fusion.1.kr_ref
  12.1 1.0 %copy.18.k_ref = bf16[512,512]{1,0:T(8,128)(2,1)} copy(bf16[512,512]{0,1:T(8,128)(2,1)S(1)} %slice.25) | data formatting | bytes 1048576 | tf_op jit(solution)/shard_map/slice | solution.py:89
  13.1 0.0 copy-done.1
  13.1 1.2 %copy.16 = bf16[1,16,64,128]{2,1,3,0:T(8,128)(2,1)} copy(bf16[1,16,64,128]{3,2,1,0:T(8,128)(2,1)S(1)} %copy-done.1) | data formatting | bytes 524288 | tf_op args[1]
  14.3 16.3 %shard_map.92 = (bf16[128,16,512]{2,1,0:T(8,128)(2,1)}, bf16[128,16,512]{2,1,0:T(8,128)(2,1)}, bf16[128,16,64]{2,1,0:T(8,128)(2,1)}, f32[512,512]{1,0:T(8,128)}, f32[512,64]{1,0:T(8,128)}) custom-call(s32[1]{0:T(128)} %bitcast.offset_ref, bf16[128,16,512]{2,1,0:T(8,128)(2,1)} %bitcast.37, bf16[128,16,64]{2,1,0:T(8,128)(2,1)} %bitcast.39, ...), custom_call_target="tpu_custom_call" | custom-call | tf_op jit(solution)/shard_map/pallas_call | solution.py:100
  30.7 1.3 %convert.8 = bf16[512,512]{1,0:T(8,128)(2,1)S(1)} convert(f32[512,512]{1,0:T(8,128)} %get-tuple-element.14) | non-fusion elementwise | flops 262144 | bytes 1572864 | tf_op jit(solution)/shard_map/convert.3
  32.0 0.0 copy-start
  32.0 1.0 %convert.9 = bf16[512,64]{1,0:T(8,128)(2,1)S(1)} convert(f32[512,64]{1,0:T(8,128)} %get-tuple-element.15) | non-fusion elementwise | flops 32768 | bytes 196608 | tf_op jit(solution)/shard_map/convert.2
  33.0 0.1 fusion.8
  33.1 1.3 %collective-permute-start = (bf16[128,576]{1,0:T(8,128)(2,1)S(1)}, bf16[128,576]{1,0:T(8,128)(2,1)S(1)}, u32[]{:S(2)}, u32[]{:S(2)}) collective-permute-start(bf16[128,576]{1,0:T(8,128)(2,1)S(1)} %get-tuple-element.37), channel_id=1, source_target_pairs={{8,0},{16,8},{24,16},{9,1},{17,9},{25,17},{10,2},{18,10},{26,18},{... | collective-permute-start | bytes 442376 | tf_op jit(solution)/shard_map/ppermute | solution.py:16
  34.4 1.3 %collective-permute-start.1 = (bf16[128,576]{1,0:T(8,128)(2,1)S(1)}, bf16[128,576]{1,0:T(8,128)(2,1)S(1)}, u32[]{:S(2)}, u32[]{:S(2)}) collective-permute-start(bf16[128,576]{1,0:T(8,128)(2,1)S(1)} %get-tuple-element.38), channel_id=1, source_target_pairs={{16,0},{24,8},{17,1},{25,9},{18,2},{26,10},{19,3},{27,11},{20,4},{... | collective-permute-start | bytes 442376 | tf_op jit(solution)/shard_map/ppermute | solution.py:16
  35.7 1.3 %collective-permute-start.2 = (bf16[128,576]{1,0:T(8,128)(2,1)S(1)}, bf16[128,576]{1,0:T(8,128)(2,1)S(1)}, u32[]{:S(2)}, u32[]{:S(2)}) collective-permute-start(bf16[128,576]{1,0:T(8,128)(2,1)S(1)} %get-tuple-element.39), channel_id=1, source_target_pairs={{24,0},{25,1},{26,2},{27,3},{28,4},{29,5},{30,6},{31,7}} | collective-permute-start | bytes 442376 | tf_op jit(solution)/shard_map/ppermute | solution.py:16
  37.0 0.0 collective-permute-done
  37.0 6.9 %collective-permute-done.1 = bf16[128,576]{1,0:T(8,128)(2,1)S(1)} collective-permute-done((bf16[128,576]{1,0:T(8,128)(2,1)S(1)}, bf16[128,576]{1,0:T(8,128)(2,1)S(1)}, u32[]{:S(2)}, u32[]{:S(2)}) %collective-permute-start.1) | collective-permute-done | bytes 147488 | tf_op jit(solution)/shard_map/ppermute | solution.py:16
  44.0 1.6 %collective-permute-done.2 = bf16[128,576]{1,0:T(8,128)(2,1)S(1)} collective-permute-done((bf16[128,576]{1,0:T(8,128)(2,1)S(1)}, bf16[128,576]{1,0:T(8,128)(2,1)S(1)}, u32[]{:S(2)}, u32[]{:S(2)}) %collective-permute-start.2) | collective-permute-done | bytes 147488 | tf_op jit(solution)/shard_map/ppermute | solution.py:16
  45.5 0.1 add_convert_fusion.3
  45.6 1.6 %collective-permute-start.3 = (bf16[128,576]{1,0:T(8,128)(2,1)S(1)}, bf16[128,576]{1,0:T(8,128)(2,1)S(1)}, u32[]{:S(2)}, u32[]{:S(2)}) collective-permute-start(bf16[128,576]{1,0:T(8,128)(2,1)S(1)} %add_convert_fusion.3), channel_id=1, source_target_pairs={{0,1},{1,0},{2,3},{3,2},{4,5},{5,4},{6,7},{7,6},{8,9},{9,8},{10,11... | collective-permute-start | bytes 442376 | tf_op jit(solution)/shard_map/ppermute | solution.py:27
  47.2 3.8 %collective-permute-done.3 = bf16[128,576]{1,0:T(8,128)(2,1)S(1)} collective-permute-done((bf16[128,576]{1,0:T(8,128)(2,1)S(1)}, bf16[128,576]{1,0:T(8,128)(2,1)S(1)}, u32[]{:S(2)}, u32[]{:S(2)}) %collective-permute-start.3) | collective-permute-done | bytes 147488 | tf_op jit(solution)/shard_map/ppermute | solution.py:27
  51.1 1.7 %collective-permute-start.4 = (bf16[128,576]{1,0:T(8,128)(2,1)S(1)}, bf16[128,576]{1,0:T(8,128)(2,1)S(1)}, u32[]{:S(2)}, u32[]{:S(2)}) collective-permute-start(bf16[128,576]{1,0:T(8,128)(2,1)S(1)} %add_convert_fusion.2), channel_id=1, source_target_pairs={{0,2},{1,3},{2,0},{3,1},{4,6},{5,7},{6,4},{7,5},{8,10},{9,11},{10,... | collective-permute-start | bytes 442376 | tf_op jit(solution)/shard_map/ppermute | solution.py:27
  52.7 5.2 %collective-permute-done.4 = bf16[128,576]{1,0:T(8,128)(2,1)S(1)} collective-permute-done((bf16[128,576]{1,0:T(8,128)(2,1)S(1)}, bf16[128,576]{1,0:T(8,128)(2,1)S(1)}, u32[]{:S(2)}, u32[]{:S(2)}) %collective-permute-start.4) | collective-permute-done | bytes 147488 | tf_op jit(solution)/shard_map/ppermute | solution.py:27
  58.0 2.7 %collective-permute-start.5 = (bf16[128,576]{1,0:T(8,128)(2,1)S(1)}, bf16[128,576]{1,0:T(8,128)(2,1)S(1)}, u32[]{:S(2)}, u32[]{:S(2)}) collective-permute-start(bf16[128,576]{1,0:T(8,128)(2,1)S(1)} %add_convert_fusion.1), channel_id=1, source_target_pairs={{0,4},{1,5},{2,6},{3,7},{4,0},{5,1},{6,2},{7,3},{8,12},{9,13},{10,... | collective-permute-start | bytes 442376 | tf_op jit(solution)/shard_map/ppermute | solution.py:27
  60.7 0.0 copy-done
  60.7 1.1 %copy.19 = bf16[1,16,64,128]{3,2,1,0:T(8,128)(2,1)} copy(bf16[1,16,64,128]{2,1,3,0:T(8,128)(2,1)S(1)} %bitcast.42) | data formatting | bytes 524288
  61.9 4.1 %collective-permute-done.5 = bf16[128,576]{1,0:T(8,128)(2,1)S(1)} collective-permute-done((bf16[128,576]{1,0:T(8,128)(2,1)S(1)}, bf16[128,576]{1,0:T(8,128)(2,1)S(1)}, u32[]{:S(2)}, u32[]{:S(2)}) %collective-permute-start.5) | collective-permute-done | bytes 147488 | tf_op jit(solution)/shard_map/ppermute | solution.py:27
  66.0 0.7 slice_bitcast_fusion
  66.6 0.7 %copy.20 = bf16[1,64,128]{2,1,0:T(8,128)(2,1)} copy(bf16[1,64,128]{1,2,0:T(8,128)(2,1)S(1)} %slice_bitcast_fusion.2) | data formatting | bytes 32768
  (5 shorter events, 0.2 us)
Async XLA Ops:
  0.6 12.5 %copy-start.1 = (bf16[1,16,64,128]{3,2,1,0:T(8,128)(2,1)S(1)}, bf16[1,16,64,128]{3,2,1,0:T(8,128)(2,1)}, u32[]{:S(2)}) copy-start(bf16[1,16,64,128]{3,2,1,0:T(8,128)(2,1)} %param.8) | copy-start | bytes 786436
  32.0 28.8 %copy-start = (bf16[128,16,64]{2,1,0:T(8,128)(2,1)S(1)}, bf16[128,16,64]{2,1,0:T(8,128)(2,1)}, u32[]{:S(2)}) copy-start(bf16[128,16,64]{2,1,0:T(8,128)(2,1)} %get-tuple-element.13) | copy-start | bytes 786436
  33.1 3.9 %collective-permute-start = (bf16[128,576]{1,0:T(8,128)(2,1)S(1)}, bf16[128,576]{1,0:T(8,128)(2,1)S(1)}, u32[]{:S(2)}, u32[]{:S(2)}) collective-permute-start(bf16[128,576]{1,0:T(8,128)(2,1)S(1)} %get-tuple-element.37), channel_id=1, source_target_pairs={{8,0},{16,8},{24,16},{9,1},{17,9},{25,17},{10,2},{18,10},{26,18},{... | collective-permute-start | bytes 442376 | tf_op jit(solution)/shard_map/ppermute | solution.py:16
  34.4 9.6 %collective-permute-start.1 = (bf16[128,576]{1,0:T(8,128)(2,1)S(1)}, bf16[128,576]{1,0:T(8,128)(2,1)S(1)}, u32[]{:S(2)}, u32[]{:S(2)}) collective-permute-start(bf16[128,576]{1,0:T(8,128)(2,1)S(1)} %get-tuple-element.38), channel_id=1, source_target_pairs={{16,0},{24,8},{17,1},{25,9},{18,2},{26,10},{19,3},{27,11},{20,4},{... | collective-permute-start | bytes 442376 | tf_op jit(solution)/shard_map/ppermute | solution.py:16
  35.7 9.8 %collective-permute-start.2 = (bf16[128,576]{1,0:T(8,128)(2,1)S(1)}, bf16[128,576]{1,0:T(8,128)(2,1)S(1)}, u32[]{:S(2)}, u32[]{:S(2)}) collective-permute-start(bf16[128,576]{1,0:T(8,128)(2,1)S(1)} %get-tuple-element.39), channel_id=1, source_target_pairs={{24,0},{25,1},{26,2},{27,3},{28,4},{29,5},{30,6},{31,7}} | collective-permute-start | bytes 442376 | tf_op jit(solution)/shard_map/ppermute | solution.py:16
  45.6 5.4 %collective-permute-start.3 = (bf16[128,576]{1,0:T(8,128)(2,1)S(1)}, bf16[128,576]{1,0:T(8,128)(2,1)S(1)}, u32[]{:S(2)}, u32[]{:S(2)}) collective-permute-start(bf16[128,576]{1,0:T(8,128)(2,1)S(1)} %add_convert_fusion.3), channel_id=1, source_target_pairs={{0,1},{1,0},{2,3},{3,2},{4,5},{5,4},{6,7},{7,6},{8,9},{9,8},{10,11... | collective-permute-start | bytes 442376 | tf_op jit(solution)/shard_map/ppermute | solution.py:27
  51.1 6.8 %collective-permute-start.4 = (bf16[128,576]{1,0:T(8,128)(2,1)S(1)}, bf16[128,576]{1,0:T(8,128)(2,1)S(1)}, u32[]{:S(2)}, u32[]{:S(2)}) collective-permute-start(bf16[128,576]{1,0:T(8,128)(2,1)S(1)} %add_convert_fusion.2), channel_id=1, source_target_pairs={{0,2},{1,3},{2,0},{3,1},{4,6},{5,7},{6,4},{7,5},{8,10},{9,11},{10,... | collective-permute-start | bytes 442376 | tf_op jit(solution)/shard_map/ppermute | solution.py:27
  58.0 8.0 %collective-permute-start.5 = (bf16[128,576]{1,0:T(8,128)(2,1)S(1)}, bf16[128,576]{1,0:T(8,128)(2,1)S(1)}, u32[]{:S(2)}, u32[]{:S(2)}) collective-permute-start(bf16[128,576]{1,0:T(8,128)(2,1)S(1)} %add_convert_fusion.1), channel_id=1, source_target_pairs={{0,4},{1,5},{2,6},{3,7},{4,0},{5,1},{6,2},{7,3},{8,12},{9,13},{10,... | collective-permute-start | bytes 442376 | tf_op jit(solution)/shard_map/ppermute | solution.py:27

commit v5 on v4

--- a/solution.py
+++ b/solution.py
@@ -30,8 +30,8 @@
     return total
 
 
-def attention_kernel(offset_ref, ql_ref, qr_ref, k_ref, kr_ref, do_ref,
-                     att_ref, lqg_ref, rqg_ref, lt_ref, rt_ref):
+def attention_kernel(offset_ref, ql_ref, qr_ref, keys_ref, do_ref,
+                     att_ref, lqg_ref, rqg_ref, terms_ref, lt_acc, rt_acc):
     step = pl.program_id(0)
     t_blk, heads, kvr = ql_ref.shape
     rope = qr_ref.shape[2]
@@ -41,12 +41,12 @@
     tn = (((0,), (0,)), ((), ()))
     q = ql_ref[...].reshape(rows, kvr)
     qr = qr_ref[...].reshape(rows, rope)
-    k = k_ref[...]
-    kr = kr_ref[...]
+    k = keys_ref[:, :kvr]
+    kr = keys_ref[:, kvr:]
     dout = do_ref[...].reshape(rows, kvr)
     length = k.shape[0]
     scores = lax.dot_general(q, k, nt, preferred_element_type=f32)
-    scores = scores + jnp.dot(qr, kr, preferred_element_type=f32)
+    scores = scores + lax.dot_general(qr, kr, nt, preferred_element_type=f32)
     row = lax.broadcasted_iota(jnp.int32, (rows, length), 0)
     col = lax.broadcasted_iota(jnp.int32, (rows, length), 1)
     allowed = row >= heads * (col - offset_ref[0] - step * t_blk)
@@ -62,7 +62,7 @@
     score_grad = (weights * (weight_grad - row_dots)).astype(jnp.bfloat16)
     lqg = scale_factor * jnp.dot(score_grad, k, preferred_element_type=f32)
     lqg_ref[...] = lqg.astype(jnp.bfloat16).reshape(t_blk, heads, kvr)
-    rqg = scale_factor * lax.dot_general(score_grad, kr, nt, preferred_element_type=f32)
+    rqg = scale_factor * jnp.dot(score_grad, kr, preferred_element_type=f32)
     rqg_ref[...] = rqg.astype(jnp.bfloat16).reshape(t_blk, heads, rope)
     lt = scale_factor * lax.dot_general(score_grad, q, tn, preferred_element_type=f32)
     lt = lt + lax.dot_general(rounded, dout, tn, preferred_element_type=f32)
@@ -70,13 +70,18 @@
 
     @pl.when(step == 0)
     def _():
-        lt_ref[...] = lt
-        rt_ref[...] = rt
+        lt_acc[...] = lt
+        rt_acc[...] = rt
 
     @pl.when(step > 0)
     def _():
-        lt_ref[...] += lt
-        rt_ref[...] += rt
+        lt_acc[...] += lt
+        rt_acc[...] += rt
+
+    @pl.when(step == pl.num_programs(0) - 1)
+    def _():
+        terms_ref[:, :kvr] = lt_acc[...].astype(jnp.bfloat16)
+        terms_ref[:, kvr:] = rt_acc[...].astype(jnp.bfloat16)
 
 
 def body(query_latent, query_rope, key_latent, key_rope, output_grad):
@@ -86,9 +91,7 @@
     rope = query_rope.shape[2]
     local_keys = jnp.concatenate([key_latent[0], key_rope[0].T], axis=1)
     whole_keys = lax.all_gather(local_keys, "ctx", axis=0, tiled=True)
-    whole_latent = whole_keys[:, :kvr]
-    whole_rope = whole_keys[:, kvr:].T
-    length = whole_latent.shape[0]
+    length = whole_keys.shape[0]
     offset = (lax.axis_index("ctx") * block_len).astype(jnp.int32).reshape(1)
     qr = jnp.transpose(query_rope[0], (2, 0, 1))
     t_blk = max(1, min(block_len, 256 // heads))
@@ -96,40 +99,30 @@
         t_blk -= 1
     by_rows = pl.BlockSpec((t_blk, heads, kvr), lambda i, off: (i, 0, 0))
     rope_rows = pl.BlockSpec((t_blk, heads, rope), lambda i, off: (i, 0, 0))
-    fixed = lambda shape: pl.BlockSpec(shape, lambda i, off: (0,) * len(shape))
-    att, lqg, rqg, lt, rt = pl.pallas_call(
+    fixed = pl.BlockSpec((length, kvr + rope), lambda i, off: (0, 0))
+    att, lqg, rqg, terms = pl.pallas_call(
         attention_kernel,
         grid_spec=pltpu.PrefetchScalarGridSpec(
             num_scalar_prefetch=1,
             grid=(block_len // t_blk,),
-            in_specs=[
-                by_rows,
-                rope_rows,
-                fixed((length, kvr)),
-                fixed((rope, length)),
-                by_rows,
-            ],
-            out_specs=[
-                by_rows,
-                by_rows,
-                rope_rows,
-                fixed((length, kvr)),
-                fixed((length, rope)),
+            in_specs=[by_rows, rope_rows, fixed, by_rows],
+            out_specs=[by_rows, by_rows, rope_rows, fixed],
+            scratch_shapes=[
+                pltpu.VMEM((length, kvr), jnp.float32),
+                pltpu.VMEM((length, rope), jnp.float32),
             ],
         ),
         out_shape=[
             jax.ShapeDtypeStruct((block_len, heads, kvr), jnp.bfloat16),
             jax.ShapeDtypeStruct((block_len, heads, kvr), jnp.bfloat16),
             jax.ShapeDtypeStruct((block_len, heads, rope), jnp.bfloat16),
-            jax.ShapeDtypeStruct((length, kvr), jnp.float32),
-            jax.ShapeDtypeStruct((length, rope), jnp.float32),
+            jax.ShapeDtypeStruct((length, kvr + rope), jnp.bfloat16),
         ],
         compiler_params=pltpu.CompilerParams(dimension_semantics=("arbitrary",)),
-    )(offset, query_latent[0], qr, whole_latent, whole_rope, output_grad[0])
+    )(offset, query_latent[0], qr, whole_keys, output_grad[0])
     attended = att[None]
     latent_qgrad = lqg[None]
     rope_qgrad = jnp.transpose(rqg, (1, 2, 0))[None]
-    terms = jnp.concatenate([lt, rt], axis=1).astype(jnp.bfloat16)
     total = causal_reduce_ctx(terms.reshape(n_ctx, block_len, -1), n_ctx)
     total = butterfly_sum_ep(total, n_ep).astype(jnp.bfloat16)
     latent_kgrad = total[None, :, :kvr]

time: 67.7 us -> 68.5 us (1.012)
  Pallas kernels: 16.3 us -> 17.5 us
  local copies, waits for them, and re-layouts: 6.46 us -> 5.47 us
  blocking collectives: 8.98 us -> 9.78 us
    another operation x2 -> x0, other arithmetic: 2.32 us -> none
    pallas_call x1, Pallas kernels: 16.3 us -> 17.5 us  [body(): pl.pallas_call(attention_kernel, grid_spec=pltpu.PrefetchScalarGridSpec(n...]
    select_n x1, other arithmetic: 0.1 us -> 1.2 us  [causal_reduce_ctx(): sent = jnp.take(blocks, jnp.maximum(here - shift, 0), axis=0)]
    slice x2 -> x0, local copies, waits for them, and re-layouts: 1.03 us -> none  [body(): whole_latent = whole_keys[:, :kvr]]
    convert_element_type x3, other arithmetic: 0.19 us -> 1.09 us  [butterfly_sum_ep(): mine = total.astype(jnp.bfloat16)]
    all_gather x1, blocking collectives: 8.98 us -> 9.78 us  [body(): whole_keys = lax.all_gather(local_keys, 'ctx', axis=0, tiled=True)]
    unnamed x8 -> x6, local copies, waits for them, and re-layouts: 4.13 us -> 4.8 us
where the time goes in v5:
time: 68.5 us; the launch traced here: 68.1 us
  waiting for transfers between devices  21.5 us (31%)
  Pallas kernels  17.5 us (26%)
  starting transfers between devices  9.91 us (14%)
  blocking collectives  9.78 us (14%)
  local copies, waits for them, and re-layouts  5.47 us (8%)
  other arithmetic  3.26 us (5%)
  between operations  0.71 us (1%)
    pallas_call x1, Pallas kernels, body(): pl.pallas_call(attention_kernel, grid_spec=pltpu.PrefetchScalarGridSpec(n...  17.5 us
    ppermute x3, waiting for transfers between devices, butterfly_sum_ep(): theirs = lax.ppermute(mine, 'ep', [(i, i ^ bit) for i in range(n_ep)])  13 us
    all_gather x1, blocking collectives, body(): whole_keys = lax.all_gather(local_keys, 'ctx', axis=0, tiled=True)  9.78 us
    ppermute x3, waiting for transfers between devices, causal_reduce_ctx(): lax.ppermute(sent, 'ctx', [(i, i - shift) for i in range(shift, n_ctx)])  8.5 us
    ppermute x3, starting transfers between devices, butterfly_sum_ep(): theirs = lax.ppermute(mine, 'ep', [(i, i ^ bit) for i in range(n_ep)])  6.03 us
    unnamed x6, local copies, waits for them, and re-layouts  4.8 us
    ppermute x3, starting transfers between devices, causal_reduce_ctx(): lax.ppermute(sent, 'ctx', [(i, i - shift) for i in range(shift, n_ctx)])  3.88 us
  transfers between devices with their start and end apart: 6, of which 5 were waited for; matrix products, arithmetic and copies ran while one was open for 2% of the time, Pallas kernels for 0%

profile of v5, /device:TPU:0, one launch (start us, length us, event | category | flops | bytes accessed | tf_op | source)
XLA Modules:
  0.0 68.1 jit_solution(13003788849869612117)
XLA Ops:
  0.6 0.8 %copy.18 = bf16[1,64,128]{1,2,0:T(8,128)(2,1)S(1)} copy(bf16[1,64,128]{2,1,0:T(8,128)(2,1)} %param.10) | data formatting | bytes 32768 | tf_op args[3]
  1.5 0.9 %pad_maximum_fusion = bf16[128,576]{1,0:T(8,128)(2,1)S(1)} fusion(bf16[128,64]{1,0:T(8,128)(2,1)S(1)} %bitcast.36, bf16[128,512]{1,0:T(8,128)(2,1)} %bitcast.37), kind=kLoop, calls=%fused_computation.4 | loop fusion | flops 294912 | bytes 294912 | tf_op jit(solution)/shard_map/concatenate | solution.py:92
  2.4 9.8 %all_gather.3.keys_ref = bf16[512,576]{1,0:T(8,128)(2,1)} all-gather(bf16[128,576]{1,0:T(8,128)(2,1)S(1)} %pad_maximum_fusion), channel_id=1, replica_groups=mesh['ctx'=4,'ep'=8] {'ctx'}, dimensions={0}, use_global_device_ids=true | all-gather | bytes 737280 | tf_op jit(solution)/shard_map/all_gather | solution.py:93
  12.2 2.1 %copy.17 = bf16[1,16,64,128]{2,1,3,0:T(8,128)(2,1)} copy(bf16[1,16,64,128]{3,2,1,0:T(8,128)(2,1)} %param.8) | data formatting | bytes 524288 | tf_op args[1]
  14.3 17.5 %shard_map.92 = (bf16[128,16,512]{2,1,0:T(8,128)(2,1)}, bf16[128,16,512]{2,1,0:T(8,128)(2,1)}, bf16[128,16,64]{2,1,0:T(8,128)(2,1)}, bf16[512,576]{1,0:T(8,128)(2,1)}) custom-call(s32[1]{0:T(128)} %bitcast.offset_ref, bf16[128,16,512]{2,1,0:T(8,128)(2,1)} %bitcast.30, bf16[128,16,64]{2,1,0:T(8,128)(2,1)} %bitcast.32, bf16[512,576]{1,0:T(8,128)(2,1)} %all_gather.3.keys_ref, ...), custom_call_target="tpu_custom_call" | custom-call | tf_op jit(solution)/shard_map/pallas_call | solution.py:103
  31.8 0.0 copy-start
  31.8 1.2 %select_bitcast_fusion.2 = (bf16[128,576]{1,0:T(8,128)(2,1)S(1)}, bf16[128,576]{1,0:T(8,128)(2,1)S(1)}, bf16[128,576]{1,0:T(8,128)(2,1)S(1)}) fusion(bf16[4,128,576]{2,1,0:T(8,128)(2,1)} %bitcast.33, s32[]{:T(128)S(6)} %max.9, pred[]{:T(512)S(6)} %le.11, s32[]{:T(128)S(6)} %max.11, pred[]{:T(512)S(6)} %le.13, s32[]{:T(128)S(6)} %max.10, pred[]{:T(512)S(6)} %le.12), kind=kLoop, calls=%fused_computation.7 | loop fusion | flops 221184 | bytes 884751 | tf_op jit(solution)/shard_map/jit(_take)/select_n | solution.py:15
  33.0 1.3 %collective-permute-start = (bf16[128,576]{1,0:T(8,128)(2,1)S(1)}, bf16[128,576]{1,0:T(8,128)(2,1)S(1)}, u32[]{:S(2)}, u32[]{:S(2)}) collective-permute-start(bf16[128,576]{1,0:T(8,128)(2,1)S(1)} %get-tuple-element.35), channel_id=1, source_target_pairs={{8,0},{16,8},{24,16},{9,1},{17,9},{25,17},{10,2},{18,10},{26,18},{... | collective-permute-start | bytes 442376 | tf_op jit(solution)/shard_map/ppermute | solution.py:16
  34.3 1.3 %collective-permute-start.1 = (bf16[128,576]{1,0:T(8,128)(2,1)S(1)}, bf16[128,576]{1,0:T(8,128)(2,1)S(1)}, u32[]{:S(2)}, u32[]{:S(2)}) collective-permute-start(bf16[128,576]{1,0:T(8,128)(2,1)S(1)} %get-tuple-element.37), channel_id=1, source_target_pairs={{16,0},{24,8},{17,1},{25,9},{18,2},{26,10},{19,3},{27,11},{20,4},{... | collective-permute-start | bytes 442376 | tf_op jit(solution)/shard_map/ppermute | solution.py:16
  35.6 1.3 %collective-permute-start.2 = (bf16[128,576]{1,0:T(8,128)(2,1)S(1)}, bf16[128,576]{1,0:T(8,128)(2,1)S(1)}, u32[]{:S(2)}, u32[]{:S(2)}) collective-permute-start(bf16[128,576]{1,0:T(8,128)(2,1)S(1)} %get-tuple-element.36), channel_id=1, source_target_pairs={{24,0},{25,1},{26,2},{27,3},{28,4},{29,5},{30,6},{31,7}} | collective-permute-start | bytes 442376 | tf_op jit(solution)/shard_map/ppermute | solution.py:16
  36.9 0.0 collective-permute-done
  36.9 6.9 %collective-permute-done.1 = bf16[128,576]{1,0:T(8,128)(2,1)S(1)} collective-permute-done((bf16[128,576]{1,0:T(8,128)(2,1)S(1)}, bf16[128,576]{1,0:T(8,128)(2,1)S(1)}, u32[]{:S(2)}, u32[]{:S(2)}) %collective-permute-start.1) | collective-permute-done | bytes 147488 | tf_op jit(solution)/shard_map/ppermute | solution.py:16
  43.8 1.6 %collective-permute-done.2 = bf16[128,576]{1,0:T(8,128)(2,1)S(1)} collective-permute-done((bf16[128,576]{1,0:T(8,128)(2,1)S(1)}, bf16[128,576]{1,0:T(8,128)(2,1)S(1)}, u32[]{:S(2)}, u32[]{:S(2)}) %collective-permute-start.2) | collective-permute-done | bytes 147488 | tf_op jit(solution)/shard_map/ppermute | solution.py:16
  45.4 1.0 %add_convert_fusion.3 = bf16[128,576]{1,0:T(8,128)(2,1)S(1)} fusion(bf16[128,576]{1,0:T(8,128)(2,1)S(1)} %collective-permute-done.2, bf16[128,576]{1,0:T(8,128)(2,1)S(1)} %collective-permute-done.1, bf16[128,576]{1,0:T(8,128)(2,1)S(1)} %collective-permute-done, bf16[4,128,576]{2,1,0:T(8,128)(2,1)} %bitcast.34, s32[]{:T(128)S(6)} %select_n.17, pred[]{:T(512)S(6)} %and.11), kind=kLoop, calls=%fused_computation.3 | loop fusion | flops 663552 | bytes 737285 | tf_op jit(solution)/shard_map/convert_element_type | solution.py:26
  46.4 1.6 %collective-permute-start.3 = (bf16[128,576]{1,0:T(8,128)(2,1)S(1)}, bf16[128,576]{1,0:T(8,128)(2,1)S(1)}, u32[]{:S(2)}, u32[]{:S(2)}) collective-permute-start(bf16[128,576]{1,0:T(8,128)(2,1)S(1)} %add_convert_fusion.3), channel_id=1, source_target_pairs={{0,1},{1,0},{2,3},{3,2},{4,5},{5,4},{6,7},{7,6},{8,9},{9,8},{10,11... | collective-permute-start | bytes 442376 | tf_op jit(solution)/shard_map/ppermute | solution.py:27
  48.0 3.8 %collective-permute-done.3 = bf16[128,576]{1,0:T(8,128)(2,1)S(1)} collective-permute-done((bf16[128,576]{1,0:T(8,128)(2,1)S(1)}, bf16[128,576]{1,0:T(8,128)(2,1)S(1)}, u32[]{:S(2)}, u32[]{:S(2)}) %collective-permute-start.3) | collective-permute-done | bytes 147488 | tf_op jit(solution)/shard_map/ppermute | solution.py:27
  51.8 1.7 %collective-permute-start.4 = (bf16[128,576]{1,0:T(8,128)(2,1)S(1)}, bf16[128,576]{1,0:T(8,128)(2,1)S(1)}, u32[]{:S(2)}, u32[]{:S(2)}) collective-permute-start(bf16[128,576]{1,0:T(8,128)(2,1)S(1)} %add_convert_fusion.2), channel_id=1, source_target_pairs={{0,2},{1,3},{2,0},{3,1},{4,6},{5,7},{6,4},{7,5},{8,10},{9,11},{10,... | collective-permute-start | bytes 442376 | tf_op jit(solution)/shard_map/ppermute | solution.py:27
  53.5 5.2 %collective-permute-done.4 = bf16[128,576]{1,0:T(8,128)(2,1)S(1)} collective-permute-done((bf16[128,576]{1,0:T(8,128)(2,1)S(1)}, bf16[128,576]{1,0:T(8,128)(2,1)S(1)}, u32[]{:S(2)}, u32[]{:S(2)}) %collective-permute-start.4) | collective-permute-done | bytes 147488 | tf_op jit(solution)/shard_map/ppermute | solution.py:27
  58.7 2.8 %collective-permute-start.5 = (bf16[128,576]{1,0:T(8,128)(2,1)S(1)}, bf16[128,576]{1,0:T(8,128)(2,1)S(1)}, u32[]{:S(2)}, u32[]{:S(2)}) collective-permute-start(bf16[128,576]{1,0:T(8,128)(2,1)S(1)} %add_convert_fusion.1), channel_id=1, source_target_pairs={{0,4},{1,5},{2,6},{3,7},{4,0},{5,1},{6,2},{7,3},{8,12},{9,13},{10,... | collective-permute-start | bytes 442376 | tf_op jit(solution)/shard_map/ppermute | solution.py:27
  61.5 0.0 copy-done
  61.5 1.1 %copy.19 = bf16[1,16,64,128]{3,2,1,0:T(8,128)(2,1)} copy(bf16[1,16,64,128]{2,1,3,0:T(8,128)(2,1)S(1)} %bitcast.35) | data formatting | bytes 524288
  62.6 4.1 %collective-permute-done.5 = bf16[128,576]{1,0:T(8,128)(2,1)S(1)} collective-permute-done((bf16[128,576]{1,0:T(8,128)(2,1)S(1)}, bf16[128,576]{1,0:T(8,128)(2,1)S(1)}, u32[]{:S(2)}, u32[]{:S(2)}) %collective-permute-start.5) | collective-permute-done | bytes 147488 | tf_op jit(solution)/shard_map/ppermute | solution.py:27
  66.7 0.7 slice_bitcast_fusion
  67.4 0.7 %copy.20 = bf16[1,64,128]{2,1,0:T(8,128)(2,1)} copy(bf16[1,64,128]{1,2,0:T(8,128)(2,1)S(1)} %slice_bitcast_fusion.1) | data formatting | bytes 32768
  (4 shorter events, 0.1 us)
Async XLA Ops:
  31.8 29.7 %copy-start = (bf16[128,16,64]{2,1,0:T(8,128)(2,1)S(1)}, bf16[128,16,64]{2,1,0:T(8,128)(2,1)}, u32[]{:S(2)}) copy-start(bf16[128,16,64]{2,1,0:T(8,128)(2,1)} %get-tuple-element.12) | copy-start | bytes 786436
  33.0 3.9 %collective-permute-start = (bf16[128,576]{1,0:T(8,128)(2,1)S(1)}, bf16[128,576]{1,0:T(8,128)(2,1)S(1)}, u32[]{:S(2)}, u32[]{:S(2)}) collective-permute-start(bf16[128,576]{1,0:T(8,128)(2,1)S(1)} %get-tuple-element.35), channel_id=1, source_target_pairs={{8,0},{16,8},{24,16},{9,1},{17,9},{25,17},{10,2},{18,10},{26,18},{... | collective-permute-start | bytes 442376 | tf_op jit(solution)/shard_map/ppermute | solution.py:16
  34.3 9.5 %collective-permute-start.1 = (bf16[128,576]{1,0:T(8,128)(2,1)S(1)}, bf16[128,576]{1,0:T(8,128)(2,1)S(1)}, u32[]{:S(2)}, u32[]{:S(2)}) collective-permute-start(bf16[128,576]{1,0:T(8,128)(2,1)S(1)} %get-tuple-element.37), channel_id=1, source_target_pairs={{16,0},{24,8},{17,1},{25,9},{18,2},{26,10},{19,3},{27,11},{20,4},{... | collective-permute-start | bytes 442376 | tf_op jit(solution)/shard_map/ppermute | solution.py:16
  35.6 9.8 %collective-permute-start.2 = (bf16[128,576]{1,0:T(8,128)(2,1)S(1)}, bf16[128,576]{1,0:T(8,128)(2,1)S(1)}, u32[]{:S(2)}, u32[]{:S(2)}) collective-permute-start(bf16[128,576]{1,0:T(8,128)(2,1)S(1)} %get-tuple-element.36), channel_id=1, source_target_pairs={{24,0},{25,1},{26,2},{27,3},{28,4},{29,5},{30,6},{31,7}} | collective-permute-start | bytes 442376 | tf_op jit(solution)/shard_map/ppermute | solution.py:16
  46.4 5.4 %collective-permute-start.3 = (bf16[128,576]{1,0:T(8,128)(2,1)S(1)}, bf16[128,576]{1,0:T(8,128)(2,1)S(1)}, u32[]{:S(2)}, u32[]{:S(2)}) collective-permute-start(bf16[128,576]{1,0:T(8,128)(2,1)S(1)} %add_convert_fusion.3), channel_id=1, source_target_pairs={{0,1},{1,0},{2,3},{3,2},{4,5},{5,4},{6,7},{7,6},{8,9},{9,8},{10,11... | collective-permute-start | bytes 442376 | tf_op jit(solution)/shard_map/ppermute | solution.py:27
  51.8 6.8 %collective-permute-start.4 = (bf16[128,576]{1,0:T(8,128)(2,1)S(1)}, bf16[128,576]{1,0:T(8,128)(2,1)S(1)}, u32[]{:S(2)}, u32[]{:S(2)}) collective-permute-start(bf16[128,576]{1,0:T(8,128)(2,1)S(1)} %add_convert_fusion.2), channel_id=1, source_target_pairs={{0,2},{1,3},{2,0},{3,1},{4,6},{5,7},{6,4},{7,5},{8,10},{9,11},{10,... | collective-permute-start | bytes 442376 | tf_op jit(solution)/shard_map/ppermute | solution.py:27
  58.7 8.0 %collective-permute-start.5 = (bf16[128,576]{1,0:T(8,128)(2,1)S(1)}, bf16[128,576]{1,0:T(8,128)(2,1)S(1)}, u32[]{:S(2)}, u32[]{:S(2)}) collective-permute-start(bf16[128,576]{1,0:T(8,128)(2,1)S(1)} %add_convert_fusion.1), channel_id=1, source_target_pairs={{0,4},{1,5},{2,6},{3,7},{4,0},{5,1},{6,2},{7,3},{8,12},{9,13},{10,... | collective-permute-start | bytes 442376 | tf_op jit(solution)/shard_map/ppermute | solution.py:27

commit v6 on v5

--- a/solution.py
+++ b/solution.py
@@ -10,10 +10,24 @@
 
 def causal_reduce_ctx(blocks, n_ctx):
     here = lax.axis_index("ctx")
-    total = jnp.take(blocks, here, axis=0).astype(jnp.float32)
-    for shift in range(1, n_ctx):
-        sent = jnp.take(blocks, jnp.maximum(here - shift, 0), axis=0)
-        got = lax.ppermute(sent, "ctx", [(i, i - shift) for i in range(shift, n_ctx)])
+    if n_ctx % 2:
+        total = jnp.take(blocks, here, axis=0).astype(jnp.float32)
+        for shift in range(1, n_ctx):
+            sent = jnp.take(blocks, jnp.maximum(here - shift, 0), axis=0)
+            got = lax.ppermute(sent, "ctx", [(i, i - shift) for i in range(shift, n_ctx)])
+            total = total + got.astype(jnp.float32)
+        return total
+    pairs = n_ctx // 2
+    side = here % 2
+    by_parity = blocks.reshape(pairs, 2, *blocks.shape[1:])
+    mine = jnp.take(by_parity, side, axis=1)
+    theirs = jnp.take(by_parity, 1 - side, axis=1)
+    got = lax.ppermute(theirs, "ctx", [(i, i ^ 1) for i in range(n_ctx)])
+    summed = (mine.astype(jnp.float32) + got.astype(jnp.float32)).astype(jnp.bfloat16)
+    total = jnp.take(summed, here // 2, axis=0).astype(jnp.float32)
+    for shift in range(1, pairs):
+        sent = jnp.take(summed, jnp.maximum(here // 2 - shift, 0), axis=0)
+        got = lax.ppermute(sent, "ctx", [(i, i - 2 * shift) for i in range(2 * shift, n_ctx)])
         total = total + got.astype(jnp.float32)
     return total
 

time: 68.5 us -> 65.1 us (0.950)
  starting transfers between devices: 9.91 us -> 7.6 us
  waiting for transfers between devices: 21.5 us -> 20.4 us
    ppermute x3 -> x2, starting transfers between devices: 3.88 us -> 1.72 us  [the longest x1 1.29 us: causal_reduce_ctx(): lax.ppermute(sent, 'ctx', [(i, i - 2 * shift) for i in range(2 * shift, n...]
    convert_element_type x0 -> x1, other arithmetic: none -> 1.07 us  [causal_reduce_ctx(): (mine.astype(jnp.float32) + got.astype(jnp.float32)).astype(jnp.bfloat16)]
    convert_element_type x3, other arithmetic: 1.09 us -> 0.14 us  [butterfly_sum_ep(): mine = total.astype(jnp.bfloat16)]
    ppermute x3, waiting for transfers between devices: 13 us -> 12.1 us  [butterfly_sum_ep(): theirs = lax.ppermute(mine, 'ep', [(i, i ^ bit) for i in range(n_ep)])]
    ppermute x3 -> x2, waiting for transfers between devices: 8.5 us -> 8.31 us  [the longest x1 7.04 us: causal_reduce_ctx(): lax.ppermute(sent, 'ctx', [(i, i - 2 * shift) for i in range(2 * shift, n...]
  transfers between devices with their start and end apart: 6 -> 5, of which waited for: 5 -> 5; matrix products, arithmetic and copies ran while one was open for 2% -> 2% of each run, Pallas kernels for 0% -> 0%
where the time goes in v6:
time: 65.1 us; the launch traced here: 64.8 us
  waiting for transfers between devices  20.4 us (31%)
  Pallas kernels  17.5 us (27%)
  blocking collectives  9.78 us (15%)
  starting transfers between devices  7.6 us (12%)
  local copies, waits for them, and re-layouts  5.47 us (8%)
  other arithmetic  3.29 us (5%)
  between operations  0.73 us (1%)
    pallas_call x1, Pallas kernels, body(): pl.pallas_call(attention_kernel, grid_spec=pltpu.PrefetchScalarGridSpec(n...  17.5 us
    ppermute x3, waiting for transfers between devices, butterfly_sum_ep(): theirs = lax.ppermute(mine, 'ep', [(i, i ^ bit) for i in range(n_ep)])  12.1 us
    all_gather x1, blocking collectives, body(): whole_keys = lax.all_gather(local_keys, 'ctx', axis=0, tiled=True)  9.78 us
    ppermute x1, waiting for transfers between devices, causal_reduce_ctx(): lax.ppermute(sent, 'ctx', [(i, i - 2 * shift) for i in range(2 * shift, n...  7.04 us
    ppermute x3, starting transfers between devices, butterfly_sum_ep(): theirs = lax.ppermute(mine, 'ep', [(i, i ^ bit) for i in range(n_ep)])  5.88 us
    unnamed x6, local copies, waits for them, and re-layouts  4.8 us
  transfers between devices with their start and end apart: 5, of which 5 were waited for; matrix products, arithmetic and copies ran while one was open for 2% of the time, Pallas kernels for 0%

profile of v6, /device:TPU:0, one launch (start us, length us, event | category | flops | bytes accessed | tf_op | source)
XLA Modules:
  0.0 64.8 jit_solution(14617945086919230203)
XLA Ops:
  0.7 2.1 %copy.15 = bf16[1,16,64,128]{2,1,3,0:T(8,128)(2,1)} copy(bf16[1,16,64,128]{3,2,1,0:T(8,128)(2,1)} %param.10) | data formatting | bytes 524288 | tf_op args[1]
  2.8 0.8 %copy.16 = bf16[1,64,128]{1,2,0:T(8,128)(2,1)S(1)} copy(bf16[1,64,128]{2,1,0:T(8,128)(2,1)} %param.12) | data formatting | bytes 32768 | tf_op args[3]
  3.6 0.9 %pad_maximum_fusion = bf16[128,576]{1,0:T(8,128)(2,1)S(1)} fusion(bf16[128,64]{1,0:T(8,128)(2,1)S(1)} %bitcast.48, bf16[128,512]{1,0:T(8,128)(2,1)} %bitcast.49), kind=kLoop, calls=%fused_computation.9 | loop fusion | flops 294912 | bytes 294912 | tf_op jit(solution)/shard_map/concatenate | solution.py:106
  4.6 9.8 %all_gather.3.keys_ref = bf16[512,576]{1,0:T(8,128)(2,1)} all-gather(bf16[128,576]{1,0:T(8,128)(2,1)S(1)} %pad_maximum_fusion), channel_id=1, replica_groups=mesh['ctx'=4,'ep'=8] {'ctx'}, dimensions={0}, use_global_device_ids=true | all-gather | bytes 737280 | tf_op jit(solution)/shard_map/all_gather | solution.py:107
  14.3 17.5 %shard_map.92 = (bf16[128,16,512]{2,1,0:T(8,128)(2,1)}, bf16[128,16,512]{2,1,0:T(8,128)(2,1)}, bf16[128,16,64]{2,1,0:T(8,128)(2,1)}, bf16[512,576]{1,0:T(8,128)(2,1)}) custom-call(s32[1]{0:T(128)} %bitcast.offset_ref, bf16[128,16,512]{2,1,0:T(8,128)(2,1)} %bitcast.42, bf16[128,16,64]{2,1,0:T(8,128)(2,1)} %bitcast.44, bf16[512,576]{1,0:T(8,128)(2,1)} %all_gather.3.keys_ref, ...), custom_call_target="tpu_custom_call" | custom-call | tf_op jit(solution)/shard_map/pallas_call | solution.py:117
  31.8 0.0 copy-start
  31.8 1.1 %fusion = bf16[2,128,576]{2,1,0:T(8,128)(2,1)S(1)} fusion(bf16[2,2,128,576]{3,2,1,0:T(8,128)(2,1)} %bitcast.45, s32[]{:T(128)S(6)} %select_n.38, pred[]{:T(512)S(6)} %and.27), kind=kLoop, calls=%fused_computation.2 | loop fusion | flops 147456 | bytes 589829 | tf_op jit(solution)/shard_map/jit(_take)/select_n | solution.py:24
  32.9 0.4 collective-permute-start
  33.3 1.3 %collective-permute-done = bf16[2,128,576]{2,1,0:T(8,128)(2,1)S(1)} collective-permute-done((bf16[2,128,576]{2,1,0:T(8,128)(2,1)S(1)}, bf16[2,128,576]{2,1,0:T(8,128)(2,1)S(1)}, u32[]{:S(2)}, u32[]{:S(2)}) %collective-permute-start) | collective-permute-done | bytes 294944 | tf_op jit(solution)/shard_map/ppermute | solution.py:25
  34.6 1.1 %add_convert_fusion = bf16[2,128,576]{2,1,0:T(8,128)(2,1)S(1)} fusion(bf16[2,128,576]{2,1,0:T(8,128)(2,1)S(1)} %collective-permute-done, bf16[2,2,128,576]{3,2,1,0:T(8,128)(2,1)} %bitcast.46, s32[]{:T(128)S(6)} %select_n.36, pred[]{:T(512)S(6)} %and.26), kind=kLoop, calls=%fused_computation | loop fusion | flops 737280 | bytes 884741 | tf_op jit(solution)/shard_map/convert_element_type | solution.py:26
  35.7 1.3 %collective-permute-start.1 = (bf16[128,576]{1,0:T(8,128)(2,1)S(1)}, bf16[128,576]{1,0:T(8,128)(2,1)S(1)}, u32[]{:S(2)}, u32[]{:S(2)}) collective-permute-start(bf16[128,576]{1,0:T(8,128)(2,1)S(1)} %select_bitcast_fusion), channel_id=1, source_target_pairs={{16,0},{24,8},{17,1},{25,9},{18,2},{26,10},{19,3},{27,11},{20,4},{... | collective-permute-start | bytes 442376 | tf_op jit(solution)/shard_map/ppermute | solution.py:30
  37.0 7.0 %collective-permute-done.1 = bf16[128,576]{1,0:T(8,128)(2,1)S(1)} collective-permute-done((bf16[128,576]{1,0:T(8,128)(2,1)S(1)}, bf16[128,576]{1,0:T(8,128)(2,1)S(1)}, u32[]{:S(2)}, u32[]{:S(2)}) %collective-permute-start.1) | collective-permute-done | bytes 147488 | tf_op jit(solution)/shard_map/ppermute | solution.py:30
  44.0 0.1 add_convert_fusion.4
  44.1 1.6 %collective-permute-start.2 = (bf16[128,576]{1,0:T(8,128)(2,1)S(1)}, bf16[128,576]{1,0:T(8,128)(2,1)S(1)}, u32[]{:S(2)}, u32[]{:S(2)}) collective-permute-start(bf16[128,576]{1,0:T(8,128)(2,1)S(1)} %add_convert_fusion.4), channel_id=1, source_target_pairs={{0,1},{1,0},{2,3},{3,2},{4,5},{5,4},{6,7},{7,6},{8,9},{9,8},{10,11... | collective-permute-start | bytes 442376 | tf_op jit(solution)/shard_map/ppermute | solution.py:41
  45.7 4.1 %collective-permute-done.2 = bf16[128,576]{1,0:T(8,128)(2,1)S(1)} collective-permute-done((bf16[128,576]{1,0:T(8,128)(2,1)S(1)}, bf16[128,576]{1,0:T(8,128)(2,1)S(1)}, u32[]{:S(2)}, u32[]{:S(2)}) %collective-permute-start.2) | collective-permute-done | bytes 147488 | tf_op jit(solution)/shard_map/ppermute | solution.py:41
  49.9 1.6 %collective-permute-start.3 = (bf16[128,576]{1,0:T(8,128)(2,1)S(1)}, bf16[128,576]{1,0:T(8,128)(2,1)S(1)}, u32[]{:S(2)}, u32[]{:S(2)}) collective-permute-start(bf16[128,576]{1,0:T(8,128)(2,1)S(1)} %add_convert_fusion.3), channel_id=1, source_target_pairs={{0,2},{1,3},{2,0},{3,1},{4,6},{5,7},{6,4},{7,5},{8,10},{9,11},{10,... | collective-permute-start | bytes 442376 | tf_op jit(solution)/shard_map/ppermute | solution.py:41
  51.5 3.7 %collective-permute-done.3 = bf16[128,576]{1,0:T(8,128)(2,1)S(1)} collective-permute-done((bf16[128,576]{1,0:T(8,128)(2,1)S(1)}, bf16[128,576]{1,0:T(8,128)(2,1)S(1)}, u32[]{:S(2)}, u32[]{:S(2)}) %collective-permute-start.3) | collective-permute-done | bytes 147488 | tf_op jit(solution)/shard_map/ppermute | solution.py:41
  55.3 2.7 %collective-permute-start.4 = (bf16[128,576]{1,0:T(8,128)(2,1)S(1)}, bf16[128,576]{1,0:T(8,128)(2,1)S(1)}, u32[]{:S(2)}, u32[]{:S(2)}) collective-permute-start(bf16[128,576]{1,0:T(8,128)(2,1)S(1)} %add_convert_fusion.2), channel_id=1, source_target_pairs={{0,4},{1,5},{2,6},{3,7},{4,0},{5,1},{6,2},{7,3},{8,12},{9,13},{10,... | collective-permute-start | bytes 442376 | tf_op jit(solution)/shard_map/ppermute | solution.py:41
  57.9 0.0 copy-done
  57.9 1.1 %copy.19 = bf16[1,16,64,128]{3,2,1,0:T(8,128)(2,1)} copy(bf16[1,16,64,128]{2,1,3,0:T(8,128)(2,1)S(1)} %bitcast.47) | data formatting | bytes 524288
  59.1 4.3 %collective-permute-done.4 = bf16[128,576]{1,0:T(8,128)(2,1)S(1)} collective-permute-done((bf16[128,576]{1,0:T(8,128)(2,1)S(1)}, bf16[128,576]{1,0:T(8,128)(2,1)S(1)}, u32[]{:S(2)}, u32[]{:S(2)}) %collective-permute-start.4) | collective-permute-done | bytes 147488 | tf_op jit(solution)/shard_map/ppermute | solution.py:41
  63.4 0.7 %slice_bitcast_fusion = bf16[1,128,512]{2,1,0:T(8,128)(2,1)} fusion(bf16[128,576]{1,0:T(8,128)(2,1)S(1)} %add_convert_fusion.1), kind=kLoop, calls=%fused_computation.11 | loop fusion | bytes 262144 | tf_op jit(solution)/shard_map/broadcast_in_dim | solution.py:142
  64.1 0.7 %copy.20 = bf16[1,64,128]{2,1,0:T(8,128)(2,1)} copy(bf16[1,64,128]{1,2,0:T(8,128)(2,1)S(1)} %slice_bitcast_fusion.1) | data formatting | bytes 32768
  (5 shorter events, 0.2 us)
Async XLA Ops:
  31.8 26.2 %copy-start = (bf16[128,16,64]{2,1,0:T(8,128)(2,1)S(1)}, bf16[128,16,64]{2,1,0:T(8,128)(2,1)}, u32[]{:S(2)}) copy-start(bf16[128,16,64]{2,1,0:T(8,128)(2,1)} %get-tuple-element.13) | copy-start | bytes 786436
  32.9 1.7 %collective-permute-start = (bf16[2,128,576]{2,1,0:T(8,128)(2,1)S(1)}, bf16[2,128,576]{2,1,0:T(8,128)(2,1)S(1)}, u32[]{:S(2)}, u32[]{:S(2)}) collective-permute-start(bf16[2,128,576]{2,1,0:T(8,128)(2,1)S(1)} %fusion), channel_id=1, source_target_pairs={{0,8},{8,0},{16,24},{24,16},{1,9},{9,1},{17,25},{25,17},{2,10},{10... | collective-permute-start | bytes 884744 | tf_op jit(solution)/shard_map/ppermute | solution.py:25
  35.7 8.4 %collective-permute-start.1 = (bf16[128,576]{1,0:T(8,128)(2,1)S(1)}, bf16[128,576]{1,0:T(8,128)(2,1)S(1)}, u32[]{:S(2)}, u32[]{:S(2)}) collective-permute-start(bf16[128,576]{1,0:T(8,128)(2,1)S(1)} %select_bitcast_fusion), channel_id=1, source_target_pairs={{16,0},{24,8},{17,1},{25,9},{18,2},{26,10},{19,3},{27,11},{20,4},{... | collective-permute-start | bytes 442376 | tf_op jit(solution)/shard_map/ppermute | solution.py:30
  44.1 5.7 %collective-permute-start.2 = (bf16[128,576]{1,0:T(8,128)(2,1)S(1)}, bf16[128,576]{1,0:T(8,128)(2,1)S(1)}, u32[]{:S(2)}, u32[]{:S(2)}) collective-permute-start(bf16[128,576]{1,0:T(8,128)(2,1)S(1)} %add_convert_fusion.4), channel_id=1, source_target_pairs={{0,1},{1,0},{2,3},{3,2},{4,5},{5,4},{6,7},{7,6},{8,9},{9,8},{10,11... | collective-permute-start | bytes 442376 | tf_op jit(solution)/shard_map/ppermute | solution.py:41
  49.9 5.4 %collective-permute-start.3 = (bf16[128,576]{1,0:T(8,128)(2,1)S(1)}, bf16[128,576]{1,0:T(8,128)(2,1)S(1)}, u32[]{:S(2)}, u32[]{:S(2)}) collective-permute-start(bf16[128,576]{1,0:T(8,128)(2,1)S(1)} %add_convert_fusion.3), channel_id=1, source_target_pairs={{0,2},{1,3},{2,0},{3,1},{4,6},{5,7},{6,4},{7,5},{8,10},{9,11},{10,... | collective-permute-start | bytes 442376 | tf_op jit(solution)/shard_map/ppermute | solution.py:41
  55.3 8.1 %collective-permute-start.4 = (bf16[128,576]{1,0:T(8,128)(2,1)S(1)}, bf16[128,576]{1,0:T(8,128)(2,1)S(1)}, u32[]{:S(2)}, u32[]{:S(2)}) collective-permute-start(bf16[128,576]{1,0:T(8,128)(2,1)S(1)} %add_convert_fusion.2), channel_id=1, source_target_pairs={{0,4},{1,5},{2,6},{3,7},{4,0},{5,1},{6,2},{7,3},{8,12},{9,13},{10,... | collective-permute-start | bytes 442376 | tf_op jit(solution)/shard_map/ppermute | solution.py:41

commit v7 on v6

--- a/solution.py
+++ b/solution.py
@@ -108,7 +108,7 @@
     length = whole_keys.shape[0]
     offset = (lax.axis_index("ctx") * block_len).astype(jnp.int32).reshape(1)
     qr = jnp.transpose(query_rope[0], (2, 0, 1))
-    t_blk = max(1, min(block_len, 256 // heads))
+    t_blk = max(1, min(block_len, 512 // heads))
     while block_len % t_blk:
         t_blk -= 1
     by_rows = pl.BlockSpec((t_blk, heads, kvr), lambda i, off: (i, 0, 0))

time: 65.1 us -> 61.4 us (0.943)
  Pallas kernels: 17.5 us -> 13.7 us
    pallas_call x1, Pallas kernels: 17.5 us -> 13.7 us  [body(): pl.pallas_call(attention_kernel, grid_spec=pltpu.PrefetchScalarGridSpec(n...]
where the time goes in v7:
time: 61.4 us; the launch traced here: 61 us
  waiting for transfers between devices  20.3 us (33%)
  Pallas kernels  13.7 us (22%)
  blocking collectives  9.78 us (16%)
  starting transfers between devices  7.72 us (13%)
  local copies, waits for them, and re-layouts  5.47 us (9%)
  other arithmetic  3.29 us (5%)
  between operations  0.73 us (1%)
    pallas_call x1, Pallas kernels, body(): pl.pallas_call(attention_kernel, grid_spec=pltpu.PrefetchScalarGridSpec(n...  13.7 us
    ppermute x3, waiting for transfers between devices, butterfly_sum_ep(): theirs = lax.ppermute(mine, 'ep', [(i, i ^ bit) for i in range(n_ep)])  12 us
    all_gather x1, blocking collectives, body(): whole_keys = lax.all_gather(local_keys, 'ctx', axis=0, tiled=True)  9.78 us
    ppermute x1, waiting for transfers between devices, causal_reduce_ctx(): lax.ppermute(sent, 'ctx', [(i, i - 2 * shift) for i in range(2 * shift, n...  7.01 us
    ppermute x3, starting transfers between devices, butterfly_sum_ep(): theirs = lax.ppermute(mine, 'ep', [(i, i ^ bit) for i in range(n_ep)])  6.03 us
    unnamed x6, local copies, waits for them, and re-layouts  4.8 us
    ppermute x1, waiting for transfers between devices, causal_reduce_ctx(): got = lax.ppermute(theirs, 'ctx', [(i, i ^ 1) for i in range(n_ctx)])  1.31 us
    ppermute x1, starting transfers between devices, causal_reduce_ctx(): lax.ppermute(sent, 'ctx', [(i, i - 2 * shift) for i in range(2 * shift, n...  1.29 us
  transfers between devices with their start and end apart: 5, of which 5 were waited for; matrix products, arithmetic and copies ran while one was open for 2% of the time, Pallas kernels for 0%

profile of v7, /device:TPU:0, one launch (start us, length us, event | category | flops | bytes accessed | tf_op | source)
XLA Modules:
  0.0 61.0 jit_solution(3750316628843001718)
XLA Ops:
  0.7 2.1 %copy.15 = bf16[1,16,64,128]{2,1,3,0:T(8,128)(2,1)} copy(bf16[1,16,64,128]{3,2,1,0:T(8,128)(2,1)} %param.10) | data formatting | bytes 524288 | tf_op args[1]
  2.8 0.8 %copy.16 = bf16[1,64,128]{1,2,0:T(8,128)(2,1)S(1)} copy(bf16[1,64,128]{2,1,0:T(8,128)(2,1)} %param.12) | data formatting | bytes 32768 | tf_op args[3]
  3.6 0.9 %pad_maximum_fusion = bf16[128,576]{1,0:T(8,128)(2,1)S(1)} fusion(bf16[128,64]{1,0:T(8,128)(2,1)S(1)} %bitcast.48, bf16[128,512]{1,0:T(8,128)(2,1)} %bitcast.49), kind=kLoop, calls=%fused_computation.9 | loop fusion | flops 294912 | bytes 294912 | tf_op jit(solution)/shard_map/concatenate | solution.py:106
  4.6 9.8 %all_gather.3.keys_ref = bf16[512,576]{1,0:T(8,128)(2,1)} all-gather(bf16[128,576]{1,0:T(8,128)(2,1)S(1)} %pad_maximum_fusion), channel_id=1, replica_groups=mesh['ctx'=4,'ep'=8] {'ctx'}, dimensions={0}, use_global_device_ids=true | all-gather | bytes 737280 | tf_op jit(solution)/shard_map/all_gather | solution.py:107
  14.3 13.7 %shard_map.92 = (bf16[128,16,512]{2,1,0:T(8,128)(2,1)}, bf16[128,16,512]{2,1,0:T(8,128)(2,1)}, bf16[128,16,64]{2,1,0:T(8,128)(2,1)}, bf16[512,576]{1,0:T(8,128)(2,1)}) custom-call(s32[1]{0:T(128)} %bitcast.offset_ref, bf16[128,16,512]{2,1,0:T(8,128)(2,1)} %bitcast.42, bf16[128,16,64]{2,1,0:T(8,128)(2,1)} %bitcast.44, bf16[512,576]{1,0:T(8,128)(2,1)} %all_gather.3.keys_ref, ...), custom_call_target="tpu_custom_call" | custom-call | tf_op jit(solution)/shard_map/pallas_call | solution.py:117
  28.1 0.0 copy-start
  28.1 1.1 %fusion = bf16[2,128,576]{2,1,0:T(8,128)(2,1)S(1)} fusion(bf16[2,2,128,576]{3,2,1,0:T(8,128)(2,1)} %bitcast.45, s32[]{:T(128)S(6)} %select_n.38, pred[]{:T(512)S(6)} %and.27), kind=kLoop, calls=%fused_computation.2 | loop fusion | flops 147456 | bytes 589829 | tf_op jit(solution)/shard_map/jit(_take)/select_n | solution.py:24
  29.2 0.4 collective-permute-start
  29.6 1.3 %collective-permute-done = bf16[2,128,576]{2,1,0:T(8,128)(2,1)S(1)} collective-permute-done((bf16[2,128,576]{2,1,0:T(8,128)(2,1)S(1)}, bf16[2,128,576]{2,1,0:T(8,128)(2,1)S(1)}, u32[]{:S(2)}, u32[]{:S(2)}) %collective-permute-start) | collective-permute-done | bytes 294944 | tf_op jit(solution)/shard_map/ppermute | solution.py:25
  30.9 1.1 %add_convert_fusion = bf16[2,128,576]{2,1,0:T(8,128)(2,1)S(1)} fusion(bf16[2,128,576]{2,1,0:T(8,128)(2,1)S(1)} %collective-permute-done, bf16[2,2,128,576]{3,2,1,0:T(8,128)(2,1)} %bitcast.46, s32[]{:T(128)S(6)} %select_n.36, pred[]{:T(512)S(6)} %and.26), kind=kLoop, calls=%fused_computation | loop fusion | flops 737280 | bytes 884741 | tf_op jit(solution)/shard_map/convert_element_type | solution.py:26
  32.0 1.3 %collective-permute-start.1 = (bf16[128,576]{1,0:T(8,128)(2,1)S(1)}, bf16[128,576]{1,0:T(8,128)(2,1)S(1)}, u32[]{:S(2)}, u32[]{:S(2)}) collective-permute-start(bf16[128,576]{1,0:T(8,128)(2,1)S(1)} %select_bitcast_fusion), channel_id=1, source_target_pairs={{16,0},{24,8},{17,1},{25,9},{18,2},{26,10},{19,3},{27,11},{20,4},{... | collective-permute-start | bytes 442376 | tf_op jit(solution)/shard_map/ppermute | solution.py:30
  33.3 7.0 %collective-permute-done.1 = bf16[128,576]{1,0:T(8,128)(2,1)S(1)} collective-permute-done((bf16[128,576]{1,0:T(8,128)(2,1)S(1)}, bf16[128,576]{1,0:T(8,128)(2,1)S(1)}, u32[]{:S(2)}, u32[]{:S(2)}) %collective-permute-start.1) | collective-permute-done | bytes 147488 | tf_op jit(solution)/shard_map/ppermute | solution.py:30
  40.3 0.1 add_convert_fusion.4
  40.4 1.6 %collective-permute-start.2 = (bf16[128,576]{1,0:T(8,128)(2,1)S(1)}, bf16[128,576]{1,0:T(8,128)(2,1)S(1)}, u32[]{:S(2)}, u32[]{:S(2)}) collective-permute-start(bf16[128,576]{1,0:T(8,128)(2,1)S(1)} %add_convert_fusion.4), channel_id=1, source_target_pairs={{0,1},{1,0},{2,3},{3,2},{4,5},{5,4},{6,7},{7,6},{8,9},{9,8},{10,11... | collective-permute-start | bytes 442376 | tf_op jit(solution)/shard_map/ppermute | solution.py:41
  42.0 4.1 %collective-permute-done.2 = bf16[128,576]{1,0:T(8,128)(2,1)S(1)} collective-permute-done((bf16[128,576]{1,0:T(8,128)(2,1)S(1)}, bf16[128,576]{1,0:T(8,128)(2,1)S(1)}, u32[]{:S(2)}, u32[]{:S(2)}) %collective-permute-start.2) | collective-permute-done | bytes 147488 | tf_op jit(solution)/shard_map/ppermute | solution.py:41
  46.1 1.7 %collective-permute-start.3 = (bf16[128,576]{1,0:T(8,128)(2,1)S(1)}, bf16[128,576]{1,0:T(8,128)(2,1)S(1)}, u32[]{:S(2)}, u32[]{:S(2)}) collective-permute-start(bf16[128,576]{1,0:T(8,128)(2,1)S(1)} %add_convert_fusion.3), channel_id=1, source_target_pairs={{0,2},{1,3},{2,0},{3,1},{4,6},{5,7},{6,4},{7,5},{8,10},{9,11},{10,... | collective-permute-start | bytes 442376 | tf_op jit(solution)/shard_map/ppermute | solution.py:41
  47.8 3.7 %collective-permute-done.3 = bf16[128,576]{1,0:T(8,128)(2,1)S(1)} collective-permute-done((bf16[128,576]{1,0:T(8,128)(2,1)S(1)}, bf16[128,576]{1,0:T(8,128)(2,1)S(1)}, u32[]{:S(2)}, u32[]{:S(2)}) %collective-permute-start.3) | collective-permute-done | bytes 147488 | tf_op jit(solution)/shard_map/ppermute | solution.py:41
  51.5 2.7 %collective-permute-start.4 = (bf16[128,576]{1,0:T(8,128)(2,1)S(1)}, bf16[128,576]{1,0:T(8,128)(2,1)S(1)}, u32[]{:S(2)}, u32[]{:S(2)}) collective-permute-start(bf16[128,576]{1,0:T(8,128)(2,1)S(1)} %add_convert_fusion.2), channel_id=1, source_target_pairs={{0,4},{1,5},{2,6},{3,7},{4,0},{5,1},{6,2},{7,3},{8,12},{9,13},{10,... | collective-permute-start | bytes 442376 | tf_op jit(solution)/shard_map/ppermute | solution.py:41
  54.2 0.0 copy-done
  54.2 1.1 %copy.19 = bf16[1,16,64,128]{3,2,1,0:T(8,128)(2,1)} copy(bf16[1,16,64,128]{2,1,3,0:T(8,128)(2,1)S(1)} %bitcast.47) | data formatting | bytes 524288
  55.4 4.2 %collective-permute-done.4 = bf16[128,576]{1,0:T(8,128)(2,1)S(1)} collective-permute-done((bf16[128,576]{1,0:T(8,128)(2,1)S(1)}, bf16[128,576]{1,0:T(8,128)(2,1)S(1)}, u32[]{:S(2)}, u32[]{:S(2)}) %collective-permute-start.4) | collective-permute-done | bytes 147488 | tf_op jit(solution)/shard_map/ppermute | solution.py:41
  59.7 0.7 %slice_bitcast_fusion = bf16[1,128,512]{2,1,0:T(8,128)(2,1)} fusion(bf16[128,576]{1,0:T(8,128)(2,1)S(1)} %add_convert_fusion.1), kind=kLoop, calls=%fused_computation.11 | loop fusion | bytes 262144 | tf_op jit(solution)/shard_map/broadcast_in_dim | solution.py:142
  60.3 0.7 %copy.20 = bf16[1,64,128]{2,1,0:T(8,128)(2,1)} copy(bf16[1,64,128]{1,2,0:T(8,128)(2,1)S(1)} %slice_bitcast_fusion.1) | data formatting | bytes 32768
  (5 shorter events, 0.2 us)
Async XLA Ops:
  28.1 26.2 %copy-start = (bf16[128,16,64]{2,1,0:T(8,128)(2,1)S(1)}, bf16[128,16,64]{2,1,0:T(8,128)(2,1)}, u32[]{:S(2)}) copy-start(bf16[128,16,64]{2,1,0:T(8,128)(2,1)} %get-tuple-element.13) | copy-start | bytes 786436
  29.2 1.7 %collective-permute-start = (bf16[2,128,576]{2,1,0:T(8,128)(2,1)S(1)}, bf16[2,128,576]{2,1,0:T(8,128)(2,1)S(1)}, u32[]{:S(2)}, u32[]{:S(2)}) collective-permute-start(bf16[2,128,576]{2,1,0:T(8,128)(2,1)S(1)} %fusion), channel_id=1, source_target_pairs={{0,8},{8,0},{16,24},{24,16},{1,9},{9,1},{17,25},{25,17},{2,10},{10... | collective-permute-start | bytes 884744 | tf_op jit(solution)/shard_map/ppermute | solution.py:25
  32.0 8.3 %collective-permute-start.1 = (bf16[128,576]{1,0:T(8,128)(2,1)S(1)}, bf16[128,576]{1,0:T(8,128)(2,1)S(1)}, u32[]{:S(2)}, u32[]{:S(2)}) collective-permute-start(bf16[128,576]{1,0:T(8,128)(2,1)S(1)} %select_bitcast_fusion), channel_id=1, source_target_pairs={{16,0},{24,8},{17,1},{25,9},{18,2},{26,10},{19,3},{27,11},{20,4},{... | collective-permute-start | bytes 442376 | tf_op jit(solution)/shard_map/ppermute | solution.py:30
  40.4 5.7 %collective-permute-start.2 = (bf16[128,576]{1,0:T(8,128)(2,1)S(1)}, bf16[128,576]{1,0:T(8,128)(2,1)S(1)}, u32[]{:S(2)}, u32[]{:S(2)}) collective-permute-start(bf16[128,576]{1,0:T(8,128)(2,1)S(1)} %add_convert_fusion.4), channel_id=1, source_target_pairs={{0,1},{1,0},{2,3},{3,2},{4,5},{5,4},{6,7},{7,6},{8,9},{9,8},{10,11... | collective-permute-start | bytes 442376 | tf_op jit(solution)/shard_map/ppermute | solution.py:41
  46.1 5.4 %collective-permute-start.3 = (bf16[128,576]{1,0:T(8,128)(2,1)S(1)}, bf16[128,576]{1,0:T(8,128)(2,1)S(1)}, u32[]{:S(2)}, u32[]{:S(2)}) collective-permute-start(bf16[128,576]{1,0:T(8,128)(2,1)S(1)} %add_convert_fusion.3), channel_id=1, source_target_pairs={{0,2},{1,3},{2,0},{3,1},{4,6},{5,7},{6,4},{7,5},{8,10},{9,11},{10,... | collective-permute-start | bytes 442376 | tf_op jit(solution)/shard_map/ppermute | solution.py:41
  51.5 8.1 %collective-permute-start.4 = (bf16[128,576]{1,0:T(8,128)(2,1)S(1)}, bf16[128,576]{1,0:T(8,128)(2,1)S(1)}, u32[]{:S(2)}, u32[]{:S(2)}) collective-permute-start(bf16[128,576]{1,0:T(8,128)(2,1)S(1)} %add_convert_fusion.2), channel_id=1, source_target_pairs={{0,4},{1,5},{2,6},{3,7},{4,0},{5,1},{6,2},{7,3},{8,12},{9,13},{10,... | collective-permute-start | bytes 442376 | tf_op jit(solution)/shard_map/ppermute | solution.py:41

commit v8 on v7

--- a/solution.py
+++ b/solution.py
@@ -108,7 +108,7 @@
     length = whole_keys.shape[0]
     offset = (lax.axis_index("ctx") * block_len).astype(jnp.int32).reshape(1)
     qr = jnp.transpose(query_rope[0], (2, 0, 1))
-    t_blk = max(1, min(block_len, 512 // heads))
+    t_blk = max(1, min(block_len, 1024 // heads))
     while block_len % t_blk:
         t_blk -= 1
     by_rows = pl.BlockSpec((t_blk, heads, kvr), lambda i, off: (i, 0, 0))

time: 61.4 us -> 61 us (level)
  no operation moved by 1% of the time
where the time goes in v8:
time: 61 us; the launch traced here: 60.7 us
  waiting for transfers between devices  20.4 us (33%)
  Pallas kernels  13.4 us (22%)
  blocking collectives  9.78 us (16%)
  starting transfers between devices  7.59 us (12%)
  local copies, waits for them, and re-layouts  5.47 us (9%)
  other arithmetic  3.29 us (5%)
  between operations  0.73 us (1%)
    pallas_call x1, Pallas kernels, body(): pl.pallas_call(attention_kernel, grid_spec=pltpu.PrefetchScalarGridSpec(n...  13.4 us
    ppermute x3, waiting for transfers between devices, butterfly_sum_ep(): theirs = lax.ppermute(mine, 'ep', [(i, i ^ bit) for i in range(n_ep)])  12.1 us
    all_gather x1, blocking collectives, body(): whole_keys = lax.all_gather(local_keys, 'ctx', axis=0, tiled=True)  9.78 us
    ppermute x1, waiting for transfers between devices, causal_reduce_ctx(): lax.ppermute(sent, 'ctx', [(i, i - 2 * shift) for i in range(2 * shift, n...  7.04 us
    ppermute x3, starting transfers between devices, butterfly_sum_ep(): theirs = lax.ppermute(mine, 'ep', [(i, i ^ bit) for i in range(n_ep)])  5.88 us
    unnamed x6, local copies, waits for them, and re-layouts  4.8 us
    ppermute x1, starting transfers between devices, causal_reduce_ctx(): lax.ppermute(sent, 'ctx', [(i, i - 2 * shift) for i in range(2 * shift, n...  1.29 us
    ppermute x1, waiting for transfers between devices, causal_reduce_ctx(): got = lax.ppermute(theirs, 'ctx', [(i, i ^ 1) for i in range(n_ctx)])  1.27 us
  transfers between devices with their start and end apart: 5, of which 5 were waited for; matrix products, arithmetic and copies ran while one was open for 2% of the time, Pallas kernels for 0%

profile of v8, /device:TPU:0, one launch (start us, length us, event | category | flops | bytes accessed | tf_op | source)
XLA Modules:
  0.0 60.7 jit_solution(9007358346505114955)
XLA Ops:
  0.7 2.1 %copy.15 = bf16[1,16,64,128]{2,1,3,0:T(8,128)(2,1)} copy(bf16[1,16,64,128]{3,2,1,0:T(8,128)(2,1)} %param.10) | data formatting | bytes 524288 | tf_op args[1]
  2.8 0.8 %copy.16 = bf16[1,64,128]{1,2,0:T(8,128)(2,1)S(1)} copy(bf16[1,64,128]{2,1,0:T(8,128)(2,1)} %param.12) | data formatting | bytes 32768 | tf_op args[3]
  3.6 0.9 %pad_maximum_fusion = bf16[128,576]{1,0:T(8,128)(2,1)S(1)} fusion(bf16[128,64]{1,0:T(8,128)(2,1)S(1)} %bitcast.48, bf16[128,512]{1,0:T(8,128)(2,1)} %bitcast.49), kind=kLoop, calls=%fused_computation.9 | loop fusion | flops 294912 | bytes 294912 | tf_op jit(solution)/shard_map/concatenate | solution.py:106
  4.6 9.8 %all_gather.3.keys_ref = bf16[512,576]{1,0:T(8,128)(2,1)} all-gather(bf16[128,576]{1,0:T(8,128)(2,1)S(1)} %pad_maximum_fusion), channel_id=1, replica_groups=mesh['ctx'=4,'ep'=8] {'ctx'}, dimensions={0}, use_global_device_ids=true | all-gather | bytes 737280 | tf_op jit(solution)/shard_map/all_gather | solution.py:107
  14.3 13.4 %shard_map.92 = (bf16[128,16,512]{2,1,0:T(8,128)(2,1)}, bf16[128,16,512]{2,1,0:T(8,128)(2,1)}, bf16[128,16,64]{2,1,0:T(8,128)(2,1)}, bf16[512,576]{1,0:T(8,128)(2,1)}) custom-call(s32[1]{0:T(128)} %bitcast.offset_ref, bf16[128,16,512]{2,1,0:T(8,128)(2,1)} %bitcast.42, bf16[128,16,64]{2,1,0:T(8,128)(2,1)} %bitcast.44, bf16[512,576]{1,0:T(8,128)(2,1)} %all_gather.3.keys_ref, ...), custom_call_target="tpu_custom_call" | custom-call | tf_op jit(solution)/shard_map/pallas_call | solution.py:117
  27.8 0.0 copy-start
  27.8 1.1 %fusion = bf16[2,128,576]{2,1,0:T(8,128)(2,1)S(1)} fusion(bf16[2,2,128,576]{3,2,1,0:T(8,128)(2,1)} %bitcast.45, s32[]{:T(128)S(6)} %select_n.38, pred[]{:T(512)S(6)} %and.27), kind=kLoop, calls=%fused_computation.2 | loop fusion | flops 147456 | bytes 589829 | tf_op jit(solution)/shard_map/jit(_take)/select_n | solution.py:24
  28.8 0.4 collective-permute-start
  29.3 1.3 %collective-permute-done = bf16[2,128,576]{2,1,0:T(8,128)(2,1)S(1)} collective-permute-done((bf16[2,128,576]{2,1,0:T(8,128)(2,1)S(1)}, bf16[2,128,576]{2,1,0:T(8,128)(2,1)S(1)}, u32[]{:S(2)}, u32[]{:S(2)}) %collective-permute-start) | collective-permute-done | bytes 294944 | tf_op jit(solution)/shard_map/ppermute | solution.py:25
  30.5 1.1 %add_convert_fusion = bf16[2,128,576]{2,1,0:T(8,128)(2,1)S(1)} fusion(bf16[2,128,576]{2,1,0:T(8,128)(2,1)S(1)} %collective-permute-done, bf16[2,2,128,576]{3,2,1,0:T(8,128)(2,1)} %bitcast.46, s32[]{:T(128)S(6)} %select_n.36, pred[]{:T(512)S(6)} %and.26), kind=kLoop, calls=%fused_computation | loop fusion | flops 737280 | bytes 884741 | tf_op jit(solution)/shard_map/convert_element_type | solution.py:26
  31.7 1.3 %collective-permute-start.1 = (bf16[128,576]{1,0:T(8,128)(2,1)S(1)}, bf16[128,576]{1,0:T(8,128)(2,1)S(1)}, u32[]{:S(2)}, u32[]{:S(2)}) collective-permute-start(bf16[128,576]{1,0:T(8,128)(2,1)S(1)} %select_bitcast_fusion), channel_id=1, source_target_pairs={{16,0},{24,8},{17,1},{25,9},{18,2},{26,10},{19,3},{27,11},{20,4},{... | collective-permute-start | bytes 442376 | tf_op jit(solution)/shard_map/ppermute | solution.py:30
  33.0 7.0 %collective-permute-done.1 = bf16[128,576]{1,0:T(8,128)(2,1)S(1)} collective-permute-done((bf16[128,576]{1,0:T(8,128)(2,1)S(1)}, bf16[128,576]{1,0:T(8,128)(2,1)S(1)}, u32[]{:S(2)}, u32[]{:S(2)}) %collective-permute-start.1) | collective-permute-done | bytes 147488 | tf_op jit(solution)/shard_map/ppermute | solution.py:30
  40.0 0.1 add_convert_fusion.4
  40.1 1.6 %collective-permute-start.2 = (bf16[128,576]{1,0:T(8,128)(2,1)S(1)}, bf16[128,576]{1,0:T(8,128)(2,1)S(1)}, u32[]{:S(2)}, u32[]{:S(2)}) collective-permute-start(bf16[128,576]{1,0:T(8,128)(2,1)S(1)} %add_convert_fusion.4), channel_id=1, source_target_pairs={{0,1},{1,0},{2,3},{3,2},{4,5},{5,4},{6,7},{7,6},{8,9},{9,8},{10,11... | collective-permute-start | bytes 442376 | tf_op jit(solution)/shard_map/ppermute | solution.py:41
  41.7 4.1 %collective-permute-done.2 = bf16[128,576]{1,0:T(8,128)(2,1)S(1)} collective-permute-done((bf16[128,576]{1,0:T(8,128)(2,1)S(1)}, bf16[128,576]{1,0:T(8,128)(2,1)S(1)}, u32[]{:S(2)}, u32[]{:S(2)}) %collective-permute-start.2) | collective-permute-done | bytes 147488 | tf_op jit(solution)/shard_map/ppermute | solution.py:41
  45.8 1.6 %collective-permute-start.3 = (bf16[128,576]{1,0:T(8,128)(2,1)S(1)}, bf16[128,576]{1,0:T(8,128)(2,1)S(1)}, u32[]{:S(2)}, u32[]{:S(2)}) collective-permute-start(bf16[128,576]{1,0:T(8,128)(2,1)S(1)} %add_convert_fusion.3), channel_id=1, source_target_pairs={{0,2},{1,3},{2,0},{3,1},{4,6},{5,7},{6,4},{7,5},{8,10},{9,11},{10,... | collective-permute-start | bytes 442376 | tf_op jit(solution)/shard_map/ppermute | solution.py:41
  47.5 3.7 %collective-permute-done.3 = bf16[128,576]{1,0:T(8,128)(2,1)S(1)} collective-permute-done((bf16[128,576]{1,0:T(8,128)(2,1)S(1)}, bf16[128,576]{1,0:T(8,128)(2,1)S(1)}, u32[]{:S(2)}, u32[]{:S(2)}) %collective-permute-start.3) | collective-permute-done | bytes 147488 | tf_op jit(solution)/shard_map/ppermute | solution.py:41
  51.3 2.7 %collective-permute-start.4 = (bf16[128,576]{1,0:T(8,128)(2,1)S(1)}, bf16[128,576]{1,0:T(8,128)(2,1)S(1)}, u32[]{:S(2)}, u32[]{:S(2)}) collective-permute-start(bf16[128,576]{1,0:T(8,128)(2,1)S(1)} %add_convert_fusion.2), channel_id=1, source_target_pairs={{0,4},{1,5},{2,6},{3,7},{4,0},{5,1},{6,2},{7,3},{8,12},{9,13},{10,... | collective-permute-start | bytes 442376 | tf_op jit(solution)/shard_map/ppermute | solution.py:41
  53.9 0.0 copy-done
  53.9 1.1 %copy.19 = bf16[1,16,64,128]{3,2,1,0:T(8,128)(2,1)} copy(bf16[1,16,64,128]{2,1,3,0:T(8,128)(2,1)S(1)} %bitcast.47) | data formatting | bytes 524288
  55.1 4.3 %collective-permute-done.4 = bf16[128,576]{1,0:T(8,128)(2,1)S(1)} collective-permute-done((bf16[128,576]{1,0:T(8,128)(2,1)S(1)}, bf16[128,576]{1,0:T(8,128)(2,1)S(1)}, u32[]{:S(2)}, u32[]{:S(2)}) %collective-permute-start.4) | collective-permute-done | bytes 147488 | tf_op jit(solution)/shard_map/ppermute | solution.py:41
  59.4 0.7 %slice_bitcast_fusion = bf16[1,128,512]{2,1,0:T(8,128)(2,1)} fusion(bf16[128,576]{1,0:T(8,128)(2,1)S(1)} %add_convert_fusion.1), kind=kLoop, calls=%fused_computation.11 | loop fusion | bytes 262144 | tf_op jit(solution)/shard_map/broadcast_in_dim | solution.py:142
  60.0 0.7 %copy.20 = bf16[1,64,128]{2,1,0:T(8,128)(2,1)} copy(bf16[1,64,128]{1,2,0:T(8,128)(2,1)S(1)} %slice_bitcast_fusion.1) | data formatting | bytes 32768
  (5 shorter events, 0.2 us)
Async XLA Ops:
  27.8 26.2 %copy-start = (bf16[128,16,64]{2,1,0:T(8,128)(2,1)S(1)}, bf16[128,16,64]{2,1,0:T(8,128)(2,1)}, u32[]{:S(2)}) copy-start(bf16[128,16,64]{2,1,0:T(8,128)(2,1)} %get-tuple-element.13) | copy-start | bytes 786436
  28.8 1.7 %collective-permute-start = (bf16[2,128,576]{2,1,0:T(8,128)(2,1)S(1)}, bf16[2,128,576]{2,1,0:T(8,128)(2,1)S(1)}, u32[]{:S(2)}, u32[]{:S(2)}) collective-permute-start(bf16[2,128,576]{2,1,0:T(8,128)(2,1)S(1)} %fusion), channel_id=1, source_target_pairs={{0,8},{8,0},{16,24},{24,16},{1,9},{9,1},{17,25},{25,17},{2,10},{10... | collective-permute-start | bytes 884744 | tf_op jit(solution)/shard_map/ppermute | solution.py:25
  31.7 8.4 %collective-permute-start.1 = (bf16[128,576]{1,0:T(8,128)(2,1)S(1)}, bf16[128,576]{1,0:T(8,128)(2,1)S(1)}, u32[]{:S(2)}, u32[]{:S(2)}) collective-permute-start(bf16[128,576]{1,0:T(8,128)(2,1)S(1)} %select_bitcast_fusion), channel_id=1, source_target_pairs={{16,0},{24,8},{17,1},{25,9},{18,2},{26,10},{19,3},{27,11},{20,4},{... | collective-permute-start | bytes 442376 | tf_op jit(solution)/shard_map/ppermute | solution.py:30
  40.1 5.7 %collective-permute-start.2 = (bf16[128,576]{1,0:T(8,128)(2,1)S(1)}, bf16[128,576]{1,0:T(8,128)(2,1)S(1)}, u32[]{:S(2)}, u32[]{:S(2)}) collective-permute-start(bf16[128,576]{1,0:T(8,128)(2,1)S(1)} %add_convert_fusion.4), channel_id=1, source_target_pairs={{0,1},{1,0},{2,3},{3,2},{4,5},{5,4},{6,7},{7,6},{8,9},{9,8},{10,11... | collective-permute-start | bytes 442376 | tf_op jit(solution)/shard_map/ppermute | solution.py:41
  45.8 5.4 %collective-permute-start.3 = (bf16[128,576]{1,0:T(8,128)(2,1)S(1)}, bf16[128,576]{1,0:T(8,128)(2,1)S(1)}, u32[]{:S(2)}, u32[]{:S(2)}) collective-permute-start(bf16[128,576]{1,0:T(8,128)(2,1)S(1)} %add_convert_fusion.3), channel_id=1, source_target_pairs={{0,2},{1,3},{2,0},{3,1},{4,6},{5,7},{6,4},{7,5},{8,10},{9,11},{10,... | collective-permute-start | bytes 442376 | tf_op jit(solution)/shard_map/ppermute | solution.py:41
  51.3 8.1 %collective-permute-start.4 = (bf16[128,576]{1,0:T(8,128)(2,1)S(1)}, bf16[128,576]{1,0:T(8,128)(2,1)S(1)}, u32[]{:S(2)}, u32[]{:S(2)}) collective-permute-start(bf16[128,576]{1,0:T(8,128)(2,1)S(1)} %add_convert_fusion.2), channel_id=1, source_target_pairs={{0,4},{1,5},{2,6},{3,7},{4,0},{5,1},{6,2},{7,3},{8,12},{9,13},{10,... | collective-permute-start | bytes 442376 | tf_op jit(solution)/shard_map/ppermute | solution.py:41

commit v9 on v8

--- a/solution.py
+++ b/solution.py
@@ -45,7 +45,7 @@
 
 
 def attention_kernel(offset_ref, ql_ref, qr_ref, keys_ref, do_ref,
-                     att_ref, lqg_ref, rqg_ref, terms_ref, lt_acc, rt_acc):
+                     att_ref, sg_ref, terms_ref, lt_acc, rt_acc):
     step = pl.program_id(0)
     t_blk, heads, kvr = ql_ref.shape
     rope = qr_ref.shape[2]
@@ -74,10 +74,7 @@
     row_dots = jnp.sum(dout.astype(f32) * att.astype(f32), axis=-1, keepdims=True)
     weight_grad = lax.dot_general(dout, k, nt, preferred_element_type=f32)
     score_grad = (weights * (weight_grad - row_dots)).astype(jnp.bfloat16)
-    lqg = scale_factor * jnp.dot(score_grad, k, preferred_element_type=f32)
-    lqg_ref[...] = lqg.astype(jnp.bfloat16).reshape(t_blk, heads, kvr)
-    rqg = scale_factor * jnp.dot(score_grad, kr, preferred_element_type=f32)
-    rqg_ref[...] = rqg.astype(jnp.bfloat16).reshape(t_blk, heads, rope)
+    sg_ref[...] = score_grad.reshape(t_blk, heads, length)
     lt = scale_factor * lax.dot_general(score_grad, q, tn, preferred_element_type=f32)
     lt = lt + lax.dot_general(rounded, dout, tn, preferred_element_type=f32)
     rt = scale_factor * lax.dot_general(score_grad, qr, tn, preferred_element_type=f32)
@@ -98,6 +95,17 @@
         terms_ref[:, kvr:] = rt_acc[...].astype(jnp.bfloat16)
 
 
+def query_grad_kernel(sg_ref, keys_ref, lqg_ref, rqg_ref):
+    t_blk, heads, length = sg_ref.shape
+    kvr = lqg_ref.shape[2]
+    rope = rqg_ref.shape[2]
+    score_grad = sg_ref[...].reshape(t_blk * heads, length)
+    lqg = scale_factor * jnp.dot(score_grad, keys_ref[:, :kvr], preferred_element_type=jnp.float32)
+    lqg_ref[...] = lqg.astype(jnp.bfloat16).reshape(t_blk, heads, kvr)
+    rqg = scale_factor * jnp.dot(score_grad, keys_ref[:, kvr:], preferred_element_type=jnp.float32)
+    rqg_ref[...] = rqg.astype(jnp.bfloat16).reshape(t_blk, heads, rope)
+
+
 def body(query_latent, query_rope, key_latent, key_rope, output_grad):
     n_ctx = lax.axis_size("ctx")
     n_ep = lax.axis_size("ep")
@@ -114,13 +122,14 @@
     by_rows = pl.BlockSpec((t_blk, heads, kvr), lambda i, off: (i, 0, 0))
     rope_rows = pl.BlockSpec((t_blk, heads, rope), lambda i, off: (i, 0, 0))
     fixed = pl.BlockSpec((length, kvr + rope), lambda i, off: (0, 0))
-    att, lqg, rqg, terms = pl.pallas_call(
+    sg_rows = pl.BlockSpec((t_blk, heads, length), lambda i, off: (i, 0, 0))
+    att, score_grad, terms = pl.pallas_call(
         attention_kernel,
         grid_spec=pltpu.PrefetchScalarGridSpec(
             num_scalar_prefetch=1,
             grid=(block_len // t_blk,),
             in_specs=[by_rows, rope_rows, fixed, by_rows],
-            out_specs=[by_rows, by_rows, rope_rows, fixed],
+            out_specs=[by_rows, sg_rows, fixed],
             scratch_shapes=[
                 pltpu.VMEM((length, kvr), jnp.float32),
                 pltpu.VMEM((length, rope), jnp.float32),
@@ -128,12 +137,28 @@
         ),
         out_shape=[
             jax.ShapeDtypeStruct((block_len, heads, kvr), jnp.bfloat16),
-            jax.ShapeDtypeStruct((block_len, heads, kvr), jnp.bfloat16),
-            jax.ShapeDtypeStruct((block_len, heads, rope), jnp.bfloat16),
+            jax.ShapeDtypeStruct((block_len, heads, length), jnp.bfloat16),
             jax.ShapeDtypeStruct((length, kvr + rope), jnp.bfloat16),
         ],
         compiler_params=pltpu.CompilerParams(dimension_semantics=("arbitrary",)),
     )(offset, query_latent[0], qr, whole_keys, output_grad[0])
+    lqg, rqg = pl.pallas_call(
+        query_grad_kernel,
+        grid=(block_len // t_blk,),
+        in_specs=[
+            pl.BlockSpec((t_blk, heads, length), lambda i: (i, 0, 0)),
+            pl.BlockSpec((length, kvr + rope), lambda i: (0, 0)),
+        ],
+        out_specs=[
+            pl.BlockSpec((t_blk, heads, kvr), lambda i: (i, 0, 0)),
+            pl.BlockSpec((t_blk, heads, rope), lambda i: (i, 0, 0)),
+        ],
+        out_shape=[
+            jax.ShapeDtypeStruct((block_len, heads, kvr), jnp.bfloat16),
+            jax.ShapeDtypeStruct((block_len, heads, rope), jnp.bfloat16),
+        ],
+        compiler_params=pltpu.CompilerParams(dimension_semantics=("arbitrary",)),
+    )(score_grad, whole_keys)
     attended = att[None]
     latent_qgrad = lqg[None]
     rope_qgrad = jnp.transpose(rqg, (1, 2, 0))[None]

time: 61 us -> 61.6 us (level)
  waiting for transfers between devices: 20.4 us -> 16.1 us
  Pallas kernels: 13.4 us -> 17.2 us
  local copies, waits for them, and re-layouts: 5.47 us -> 6.47 us
    pallas_call x0 -> x1, Pallas kernels: none -> 4.44 us  [body(): pl.pallas_call(query_grad_kernel, grid=(block_len // t_blk,), in_specs=[p...]
    ppermute x3, waiting for transfers between devices: 12.1 us -> 7.76 us  [butterfly_sum_ep(): theirs = lax.ppermute(mine, 'ep', [(i, i ^ bit) for i in range(n_ep)])]
    unnamed x6 -> x4, local copies, waits for them, and re-layouts: 4.8 us -> 5.81 us
    pallas_call x1, Pallas kernels: 13.4 us -> 12.8 us  [body(): pl.pallas_call(attention_kernel, grid_spec=pltpu.PrefetchScalarGridSpec(n...]
  transfers between devices with their start and end apart: 5 -> 5, of which waited for: 5 -> 4; matrix products, arithmetic and copies ran while one was open for 2% -> 3% of each run, Pallas kernels for 0% -> 7%
where the time goes in v9:
time: 61.6 us; the launch traced here: 61.2 us
  Pallas kernels  17.2 us (28%)
  waiting for transfers between devices  16.1 us (26%)
  blocking collectives  9.78 us (16%)
  starting transfers between devices  7.7 us (12%)
  local copies, waits for them, and re-layouts  6.47 us (11%)
  other arithmetic  3.24 us (5%)
  between operations  0.73 us (1%)
    pallas_call x1, Pallas kernels, body(): pl.pallas_call(attention_kernel, grid_spec=pltpu.PrefetchScalarGridSpec(n...  12.8 us
    all_gather x1, blocking collectives, body(): whole_keys = lax.all_gather(local_keys, 'ctx', axis=0, tiled=True)  9.78 us
    ppermute x3, waiting for transfers between devices, butterfly_sum_ep(): theirs = lax.ppermute(mine, 'ep', [(i, i ^ bit) for i in range(n_ep)])  7.76 us
    ppermute x1, waiting for transfers between devices, causal_reduce_ctx(): lax.ppermute(sent, 'ctx', [(i, i - 2 * shift) for i in range(2 * shift, n...  7.01 us
    ppermute x3, starting transfers between devices, butterfly_sum_ep(): theirs = lax.ppermute(mine, 'ep', [(i, i ^ bit) for i in range(n_ep)])  6.02 us
    unnamed x4, local copies, waits for them, and re-layouts  5.81 us
    pallas_call x1, Pallas kernels, body(): pl.pallas_call(query_grad_kernel, grid=(block_len // t_blk,), in_specs=[p...  4.44 us
    ppermute x1, waiting for transfers between devices, causal_reduce_ctx(): got = lax.ppermute(theirs, 'ctx', [(i, i ^ 1) for i in range(n_ctx)])  1.3 us
  transfers between devices with their start and end apart: 5, of which 4 were waited for; matrix products, arithmetic and copies ran while one was open for 3% of the time, Pallas kernels for 7%

profile of v9, /device:TPU:0, one launch (start us, length us, event | category | flops | bytes accessed | tf_op | source)
XLA Modules:
  0.0 61.2 jit_solution(7012693302415781528)
XLA Ops:
  0.7 0.8 %copy.16 = bf16[1,64,128]{1,2,0:T(8,128)(2,1)S(1)} copy(bf16[1,64,128]{2,1,0:T(8,128)(2,1)} %param.12) | data formatting | bytes 32768 | tf_op args[3]
  1.5 0.9 %pad_maximum_fusion = bf16[128,576]{1,0:T(8,128)(2,1)S(1)} fusion(bf16[128,64]{1,0:T(8,128)(2,1)S(1)} %bitcast.48, bf16[128,512]{1,0:T(8,128)(2,1)} %bitcast.49), kind=kLoop, calls=%fused_computation.9 | loop fusion | flops 294912 | bytes 294912 | tf_op jit(solution)/shard_map/concatenate | solution.py:114
  2.4 9.8 %all_gather.3.keys_ref = bf16[512,576]{1,0:T(8,128)(2,1)} all-gather(bf16[128,576]{1,0:T(8,128)(2,1)S(1)} %pad_maximum_fusion), channel_id=1, replica_groups=mesh['ctx'=4,'ep'=8] {'ctx'}, dimensions={0}, use_global_device_ids=true | all-gather | bytes 737280 | tf_op jit(solution)/shard_map/all_gather | solution.py:115
  12.2 2.1 %copy.15 = bf16[1,16,64,128]{2,1,3,0:T(8,128)(2,1)} copy(bf16[1,16,64,128]{3,2,1,0:T(8,128)(2,1)} %param.10) | data formatting | bytes 524288 | tf_op args[1]
  14.3 12.8 %shard_map.92 = (bf16[128,16,512]{2,1,0:T(8,128)(2,1)}, bf16[128,16,512]{2,1,0:T(8,128)(2,1)}, bf16[512,576]{1,0:T(8,128)(2,1)}) custom-call(s32[1]{0:T(128)} %bitcast.offset_ref, bf16[128,16,512]{2,1,0:T(8,128)(2,1)} %bitcast.42, bf16[128,16,64]{2,1,0:T(8,128)(2,1)} %bitcast.44, bf16[512,576]{1,0:T(8,128)(2,1)} %all_gather.3.keys_ref, ...), custom_call_target="tpu_custom_call" | custom-call | tf_op jit(solution)/shard_map/pallas_call | solution.py:126
  27.1 1.0 %fusion = bf16[2,128,576]{2,1,0:T(8,128)(2,1)S(1)} fusion(bf16[2,2,128,576]{3,2,1,0:T(8,128)(2,1)} %bitcast.45, s32[]{:T(128)S(6)} %select_n.38, pred[]{:T(512)S(6)} %and.27), kind=kLoop, calls=%fused_computation.2 | loop fusion | flops 147456 | bytes 589829 | tf_op jit(solution)/shard_map/jit(_take)/select_n | solution.py:24
  28.1 0.4 collective-permute-start
  28.5 1.3 %collective-permute-done = bf16[2,128,576]{2,1,0:T(8,128)(2,1)S(1)} collective-permute-done((bf16[2,128,576]{2,1,0:T(8,128)(2,1)S(1)}, bf16[2,128,576]{2,1,0:T(8,128)(2,1)S(1)}, u32[]{:S(2)}, u32[]{:S(2)}) %collective-permute-start) | collective-permute-done | bytes 294944 | tf_op jit(solution)/shard_map/ppermute | solution.py:25
  29.8 1.1 %add_convert_fusion = bf16[2,128,576]{2,1,0:T(8,128)(2,1)S(1)} fusion(bf16[2,128,576]{2,1,0:T(8,128)(2,1)S(1)} %collective-permute-done, bf16[2,2,128,576]{3,2,1,0:T(8,128)(2,1)} %bitcast.46, s32[]{:T(128)S(6)} %select_n.36, pred[]{:T(512)S(6)} %and.26), kind=kLoop, calls=%fused_computation | loop fusion | flops 737280 | bytes 884741 | tf_op jit(solution)/shard_map/convert_element_type | solution.py:26
  30.9 1.3 %collective-permute-start.1 = (bf16[128,576]{1,0:T(8,128)(2,1)S(1)}, bf16[128,576]{1,0:T(8,128)(2,1)S(1)}, u32[]{:S(2)}, u32[]{:S(2)}) collective-permute-start(bf16[128,576]{1,0:T(8,128)(2,1)S(1)} %select_bitcast_fusion), channel_id=1, source_target_pairs={{16,0},{24,8},{17,1},{25,9},{18,2},{26,10},{19,3},{27,11},{20,4},{... | collective-permute-start | bytes 442376 | tf_op jit(solution)/shard_map/ppermute | solution.py:30
  32.3 7.0 %collective-permute-done.1 = bf16[128,576]{1,0:T(8,128)(2,1)S(1)} collective-permute-done((bf16[128,576]{1,0:T(8,128)(2,1)S(1)}, bf16[128,576]{1,0:T(8,128)(2,1)S(1)}, u32[]{:S(2)}, u32[]{:S(2)}) %collective-permute-start.1) | collective-permute-done | bytes 147488 | tf_op jit(solution)/shard_map/ppermute | solution.py:30
  39.3 0.1 add_convert_fusion.4
  39.3 1.6 %collective-permute-start.2 = (bf16[128,576]{1,0:T(8,128)(2,1)S(1)}, bf16[128,576]{1,0:T(8,128)(2,1)S(1)}, u32[]{:S(2)}, u32[]{:S(2)}) collective-permute-start(bf16[128,576]{1,0:T(8,128)(2,1)S(1)} %add_convert_fusion.4), channel_id=1, source_target_pairs={{0,1},{1,0},{2,3},{3,2},{4,5},{5,4},{6,7},{7,6},{8,9},{9,8},{10,11... | collective-permute-start | bytes 442376 | tf_op jit(solution)/shard_map/ppermute | solution.py:41
  40.9 4.1 %collective-permute-done.2 = bf16[128,576]{1,0:T(8,128)(2,1)S(1)} collective-permute-done((bf16[128,576]{1,0:T(8,128)(2,1)S(1)}, bf16[128,576]{1,0:T(8,128)(2,1)S(1)}, u32[]{:S(2)}, u32[]{:S(2)}) %collective-permute-start.2) | collective-permute-done | bytes 147488 | tf_op jit(solution)/shard_map/ppermute | solution.py:41
  45.1 1.7 %collective-permute-start.3 = (bf16[128,576]{1,0:T(8,128)(2,1)S(1)}, bf16[128,576]{1,0:T(8,128)(2,1)S(1)}, u32[]{:S(2)}, u32[]{:S(2)}) collective-permute-start(bf16[128,576]{1,0:T(8,128)(2,1)S(1)} %add_convert_fusion.3), channel_id=1, source_target_pairs={{0,2},{1,3},{2,0},{3,1},{4,6},{5,7},{6,4},{7,5},{8,10},{9,11},{10,... | collective-permute-start | bytes 442376 | tf_op jit(solution)/shard_map/ppermute | solution.py:41
  46.8 3.7 %collective-permute-done.3 = bf16[128,576]{1,0:T(8,128)(2,1)S(1)} collective-permute-done((bf16[128,576]{1,0:T(8,128)(2,1)S(1)}, bf16[128,576]{1,0:T(8,128)(2,1)S(1)}, u32[]{:S(2)}, u32[]{:S(2)}) %collective-permute-start.3) | collective-permute-done | bytes 147488 | tf_op jit(solution)/shard_map/ppermute | solution.py:41
  50.5 2.7 %collective-permute-start.4 = (bf16[128,576]{1,0:T(8,128)(2,1)S(1)}, bf16[128,576]{1,0:T(8,128)(2,1)S(1)}, u32[]{:S(2)}, u32[]{:S(2)}) collective-permute-start(bf16[128,576]{1,0:T(8,128)(2,1)S(1)} %add_convert_fusion.2), channel_id=1, source_target_pairs={{0,4},{1,5},{2,6},{3,7},{4,0},{5,1},{6,2},{7,3},{8,12},{9,13},{10,... | collective-permute-start | bytes 442376 | tf_op jit(solution)/shard_map/ppermute | solution.py:41
  53.2 4.4 %shard_map.93 = (bf16[128,16,512]{2,1,0:T(8,128)(2,1)}, bf16[128,16,64]{2,1,0:T(8,128)(2,1)}) custom-call(bf16[128,16,512]{2,1,0:T(8,128)(2,1)} %get-tuple-element.13.sg_ref, bf16[512,576]{1,0:T(8,128)(2,1)} %all_gather.3.keys_ref), custom_call_target="tpu_custom_call" | custom-call | tf_op jit(solution)/shard_map/pallas_call | solution.py:145
  57.6 2.1 %copy.19 = bf16[1,16,64,128]{3,2,1,0:T(8,128)(2,1)} copy(bf16[1,16,64,128]{2,1,3,0:T(8,128)(2,1)} %bitcast.47) | data formatting | bytes 524288
  59.8 0.0 collective-permute-done.4
  59.8 0.7 %slice_bitcast_fusion = bf16[1,128,512]{2,1,0:T(8,128)(2,1)} fusion(bf16[128,576]{1,0:T(8,128)(2,1)S(1)} %add_convert_fusion.1), kind=kLoop, calls=%fused_computation.11 | loop fusion | bytes 262144 | tf_op jit(solution)/shard_map/broadcast_in_dim | solution.py:167
  60.5 0.7 %copy.20 = bf16[1,64,128]{2,1,0:T(8,128)(2,1)} copy(bf16[1,64,128]{1,2,0:T(8,128)(2,1)S(1)} %slice_bitcast_fusion.1) | data formatting | bytes 32768
  (5 shorter events, 0.2 us)
Async XLA Ops:
  28.1 1.7 %collective-permute-start = (bf16[2,128,576]{2,1,0:T(8,128)(2,1)S(1)}, bf16[2,128,576]{2,1,0:T(8,128)(2,1)S(1)}, u32[]{:S(2)}, u32[]{:S(2)}) collective-permute-start(bf16[2,128,576]{2,1,0:T(8,128)(2,1)S(1)} %fusion), channel_id=1, source_target_pairs={{0,8},{8,0},{16,24},{24,16},{1,9},{9,1},{17,25},{25,17},{2,10},{10... | collective-permute-start | bytes 884744 | tf_op jit(solution)/shard_map/ppermute | solution.py:25
  30.9 8.3 %collective-permute-start.1 = (bf16[128,576]{1,0:T(8,128)(2,1)S(1)}, bf16[128,576]{1,0:T(8,128)(2,1)S(1)}, u32[]{:S(2)}, u32[]{:S(2)}) collective-permute-start(bf16[128,576]{1,0:T(8,128)(2,1)S(1)} %select_bitcast_fusion), channel_id=1, source_target_pairs={{16,0},{24,8},{17,1},{25,9},{18,2},{26,10},{19,3},{27,11},{20,4},{... | collective-permute-start | bytes 442376 | tf_op jit(solution)/shard_map/ppermute | solution.py:30
  39.3 5.7 %collective-permute-start.2 = (bf16[128,576]{1,0:T(8,128)(2,1)S(1)}, bf16[128,576]{1,0:T(8,128)(2,1)S(1)}, u32[]{:S(2)}, u32[]{:S(2)}) collective-permute-start(bf16[128,576]{1,0:T(8,128)(2,1)S(1)} %add_convert_fusion.4), channel_id=1, source_target_pairs={{0,1},{1,0},{2,3},{3,2},{4,5},{5,4},{6,7},{7,6},{8,9},{9,8},{10,11... | collective-permute-start | bytes 442376 | tf_op jit(solution)/shard_map/ppermute | solution.py:41
  45.1 5.4 %collective-permute-start.3 = (bf16[128,576]{1,0:T(8,128)(2,1)S(1)}, bf16[128,576]{1,0:T(8,128)(2,1)S(1)}, u32[]{:S(2)}, u32[]{:S(2)}) collective-permute-start(bf16[128,576]{1,0:T(8,128)(2,1)S(1)} %add_convert_fusion.3), channel_id=1, source_target_pairs={{0,2},{1,3},{2,0},{3,1},{4,6},{5,7},{6,4},{7,5},{8,10},{9,11},{10,... | collective-permute-start | bytes 442376 | tf_op jit(solution)/shard_map/ppermute | solution.py:41
  50.5 9.3 %collective-permute-start.4 = (bf16[128,576]{1,0:T(8,128)(2,1)S(1)}, bf16[128,576]{1,0:T(8,128)(2,1)S(1)}, u32[]{:S(2)}, u32[]{:S(2)}) collective-permute-start(bf16[128,576]{1,0:T(8,128)(2,1)S(1)} %add_convert_fusion.2), channel_id=1, source_target_pairs={{0,4},{1,5},{2,6},{3,7},{4,0},{5,1},{6,2},{7,3},{8,12},{9,13},{10,... | collective-permute-start | bytes 442376 | tf_op jit(solution)/shard_map/ppermute | solution.py:41

commit v10 on v8

--- a/solution.py
+++ b/solution.py
@@ -61,13 +61,13 @@
     length = k.shape[0]
     scores = lax.dot_general(q, k, nt, preferred_element_type=f32)
     scores = scores + lax.dot_general(qr, kr, nt, preferred_element_type=f32)
-    row = lax.broadcasted_iota(jnp.int32, (rows, length), 0)
-    col = lax.broadcasted_iota(jnp.int32, (rows, length), 1)
-    allowed = row >= heads * (col - offset_ref[0] - step * t_blk)
-    scores = jnp.where(allowed, scores * scale_factor, f32(-1e30))
+    row = lax.broadcasted_iota(jnp.int32, (rows, 1), 0)
+    last_key = offset_ref[0] + step * t_blk + row // heads
+    col = lax.broadcasted_iota(jnp.int32, (1, length), 1)
+    scores = jnp.where(col <= last_key, scores * scale_factor, f32(-1e30))
     row_max = jnp.max(scores, axis=-1, keepdims=True)
     powers = jnp.exp(scores - row_max)
-    weights = powers / jnp.sum(powers, axis=-1, keepdims=True)
+    weights = powers * (1.0 / jnp.sum(powers, axis=-1, keepdims=True))
     rounded = weights.astype(jnp.bfloat16)
     att = jnp.dot(rounded, k, preferred_element_type=f32).astype(jnp.bfloat16)
     att_ref[...] = att.reshape(t_blk, heads, kvr)

time: 61 us -> 61.2 us (level)
  no operation moved by 1% of the time
where the time goes in v10:
time: 61.2 us; the launch traced here: 60.9 us
  waiting for transfers between devices  20.5 us (33%)
  Pallas kernels  13.5 us (22%)
  blocking collectives  9.78 us (16%)
  starting transfers between devices  7.6 us (12%)
  local copies, waits for them, and re-layouts  5.47 us (9%)
  other arithmetic  3.29 us (5%)
  between operations  0.73 us (1%)
    pallas_call x1, Pallas kernels, body(): pl.pallas_call(attention_kernel, grid_spec=pltpu.PrefetchScalarGridSpec(n...  13.5 us
    ppermute x3, waiting for transfers between devices, butterfly_sum_ep(): theirs = lax.ppermute(mine, 'ep', [(i, i ^ bit) for i in range(n_ep)])  12.1 us
    all_gather x1, blocking collectives, body(): whole_keys = lax.all_gather(local_keys, 'ctx', axis=0, tiled=True)  9.78 us
    ppermute x1, waiting for transfers between devices, causal_reduce_ctx(): lax.ppermute(sent, 'ctx', [(i, i - 2 * shift) for i in range(2 * shift, n...  7.04 us
    ppermute x3, starting transfers between devices, butterfly_sum_ep(): theirs = lax.ppermute(mine, 'ep', [(i, i ^ bit) for i in range(n_ep)])  5.89 us
    unnamed x6, local copies, waits for them, and re-layouts  4.8 us
    ppermute x1, starting transfers between devices, causal_reduce_ctx(): lax.ppermute(sent, 'ctx', [(i, i - 2 * shift) for i in range(2 * shift, n...  1.29 us
    ppermute x1, waiting for transfers between devices, causal_reduce_ctx(): got = lax.ppermute(theirs, 'ctx', [(i, i ^ 1) for i in range(n_ctx)])  1.28 us
  transfers between devices with their start and end apart: 5, of which 5 were waited for; matrix products, arithmetic and copies ran while one was open for 2% of the time, Pallas kernels for 0%

profile of v10, /device:TPU:0, one launch (start us, length us, event | category | flops | bytes accessed | tf_op | source)
XLA Modules:
  0.0 60.9 jit_solution(12682560155252175318)
XLA Ops:
  0.7 2.1 %copy.15 = bf16[1,16,64,128]{2,1,3,0:T(8,128)(2,1)} copy(bf16[1,16,64,128]{3,2,1,0:T(8,128)(2,1)} %param.10) | data formatting | bytes 524288 | tf_op args[1]
  2.8 0.8 %copy.16 = bf16[1,64,128]{1,2,0:T(8,128)(2,1)S(1)} copy(bf16[1,64,128]{2,1,0:T(8,128)(2,1)} %param.12) | data formatting | bytes 32768 | tf_op args[3]
  3.6 0.9 %pad_maximum_fusion = bf16[128,576]{1,0:T(8,128)(2,1)S(1)} fusion(bf16[128,64]{1,0:T(8,128)(2,1)S(1)} %bitcast.48, bf16[128,512]{1,0:T(8,128)(2,1)} %bitcast.49), kind=kLoop, calls=%fused_computation.9 | loop fusion | flops 294912 | bytes 294912 | tf_op jit(solution)/shard_map/concatenate | solution.py:106
  4.6 9.8 %all_gather.3.keys_ref = bf16[512,576]{1,0:T(8,128)(2,1)} all-gather(bf16[128,576]{1,0:T(8,128)(2,1)S(1)} %pad_maximum_fusion), channel_id=1, replica_groups=mesh['ctx'=4,'ep'=8] {'ctx'}, dimensions={0}, use_global_device_ids=true | all-gather | bytes 737280 | tf_op jit(solution)/shard_map/all_gather | solution.py:107
  14.3 13.5 %shard_map.92 = (bf16[128,16,512]{2,1,0:T(8,128)(2,1)}, bf16[128,16,512]{2,1,0:T(8,128)(2,1)}, bf16[128,16,64]{2,1,0:T(8,128)(2,1)}, bf16[512,576]{1,0:T(8,128)(2,1)}) custom-call(s32[1]{0:T(128)} %bitcast.offset_ref, bf16[128,16,512]{2,1,0:T(8,128)(2,1)} %bitcast.42, bf16[128,16,64]{2,1,0:T(8,128)(2,1)} %bitcast.44, bf16[512,576]{1,0:T(8,128)(2,1)} %all_gather.3.keys_ref, ...), custom_call_target="tpu_custom_call" | custom-call | tf_op jit(solution)/shard_map/pallas_call | solution.py:117
  27.9 0.0 copy-start
  27.9 1.1 %fusion = bf16[2,128,576]{2,1,0:T(8,128)(2,1)S(1)} fusion(bf16[2,2,128,576]{3,2,1,0:T(8,128)(2,1)} %bitcast.45, s32[]{:T(128)S(6)} %select_n.38, pred[]{:T(512)S(6)} %and.27), kind=kLoop, calls=%fused_computation.2 | loop fusion | flops 147456 | bytes 589829 | tf_op jit(solution)/shard_map/jit(_take)/select_n | solution.py:24
  29.0 0.4 collective-permute-start
  29.4 1.3 %collective-permute-done = bf16[2,128,576]{2,1,0:T(8,128)(2,1)S(1)} collective-permute-done((bf16[2,128,576]{2,1,0:T(8,128)(2,1)S(1)}, bf16[2,128,576]{2,1,0:T(8,128)(2,1)S(1)}, u32[]{:S(2)}, u32[]{:S(2)}) %collective-permute-start) | collective-permute-done | bytes 294944 | tf_op jit(solution)/shard_map/ppermute | solution.py:25
  30.7 1.1 %add_convert_fusion = bf16[2,128,576]{2,1,0:T(8,128)(2,1)S(1)} fusion(bf16[2,128,576]{2,1,0:T(8,128)(2,1)S(1)} %collective-permute-done, bf16[2,2,128,576]{3,2,1,0:T(8,128)(2,1)} %bitcast.46, s32[]{:T(128)S(6)} %select_n.36, pred[]{:T(512)S(6)} %and.26), kind=kLoop, calls=%fused_computation | loop fusion | flops 737280 | bytes 884741 | tf_op jit(solution)/shard_map/convert_element_type | solution.py:26
  31.8 1.3 %collective-permute-start.1 = (bf16[128,576]{1,0:T(8,128)(2,1)S(1)}, bf16[128,576]{1,0:T(8,128)(2,1)S(1)}, u32[]{:S(2)}, u32[]{:S(2)}) collective-permute-start(bf16[128,576]{1,0:T(8,128)(2,1)S(1)} %select_bitcast_fusion), channel_id=1, source_target_pairs={{16,0},{24,8},{17,1},{25,9},{18,2},{26,10},{19,3},{27,11},{20,4},{... | collective-permute-start | bytes 442376 | tf_op jit(solution)/shard_map/ppermute | solution.py:30
  33.1 7.0 %collective-permute-done.1 = bf16[128,576]{1,0:T(8,128)(2,1)S(1)} collective-permute-done((bf16[128,576]{1,0:T(8,128)(2,1)S(1)}, bf16[128,576]{1,0:T(8,128)(2,1)S(1)}, u32[]{:S(2)}, u32[]{:S(2)}) %collective-permute-start.1) | collective-permute-done | bytes 147488 | tf_op jit(solution)/shard_map/ppermute | solution.py:30
  40.1 0.1 add_convert_fusion.4
  40.2 1.6 %collective-permute-start.2 = (bf16[128,576]{1,0:T(8,128)(2,1)S(1)}, bf16[128,576]{1,0:T(8,128)(2,1)S(1)}, u32[]{:S(2)}, u32[]{:S(2)}) collective-permute-start(bf16[128,576]{1,0:T(8,128)(2,1)S(1)} %add_convert_fusion.4), channel_id=1, source_target_pairs={{0,1},{1,0},{2,3},{3,2},{4,5},{5,4},{6,7},{7,6},{8,9},{9,8},{10,11... | collective-permute-start | bytes 442376 | tf_op jit(solution)/shard_map/ppermute | solution.py:41
  41.8 4.1 %collective-permute-done.2 = bf16[128,576]{1,0:T(8,128)(2,1)S(1)} collective-permute-done((bf16[128,576]{1,0:T(8,128)(2,1)S(1)}, bf16[128,576]{1,0:T(8,128)(2,1)S(1)}, u32[]{:S(2)}, u32[]{:S(2)}) %collective-permute-start.2) | collective-permute-done | bytes 147488 | tf_op jit(solution)/shard_map/ppermute | solution.py:41
  45.9 1.6 %collective-permute-start.3 = (bf16[128,576]{1,0:T(8,128)(2,1)S(1)}, bf16[128,576]{1,0:T(8,128)(2,1)S(1)}, u32[]{:S(2)}, u32[]{:S(2)}) collective-permute-start(bf16[128,576]{1,0:T(8,128)(2,1)S(1)} %add_convert_fusion.3), channel_id=1, source_target_pairs={{0,2},{1,3},{2,0},{3,1},{4,6},{5,7},{6,4},{7,5},{8,10},{9,11},{10,... | collective-permute-start | bytes 442376 | tf_op jit(solution)/shard_map/ppermute | solution.py:41
  47.6 3.7 %collective-permute-done.3 = bf16[128,576]{1,0:T(8,128)(2,1)S(1)} collective-permute-done((bf16[128,576]{1,0:T(8,128)(2,1)S(1)}, bf16[128,576]{1,0:T(8,128)(2,1)S(1)}, u32[]{:S(2)}, u32[]{:S(2)}) %collective-permute-start.3) | collective-permute-done | bytes 147488 | tf_op jit(solution)/shard_map/ppermute | solution.py:41
  51.4 2.7 %collective-permute-start.4 = (bf16[128,576]{1,0:T(8,128)(2,1)S(1)}, bf16[128,576]{1,0:T(8,128)(2,1)S(1)}, u32[]{:S(2)}, u32[]{:S(2)}) collective-permute-start(bf16[128,576]{1,0:T(8,128)(2,1)S(1)} %add_convert_fusion.2), channel_id=1, source_target_pairs={{0,4},{1,5},{2,6},{3,7},{4,0},{5,1},{6,2},{7,3},{8,12},{9,13},{10,... | collective-permute-start | bytes 442376 | tf_op jit(solution)/shard_map/ppermute | solution.py:41
  54.0 0.0 copy-done
  54.0 1.1 %copy.19 = bf16[1,16,64,128]{3,2,1,0:T(8,128)(2,1)} copy(bf16[1,16,64,128]{2,1,3,0:T(8,128)(2,1)S(1)} %bitcast.47) | data formatting | bytes 524288
  55.2 4.3 %collective-permute-done.4 = bf16[128,576]{1,0:T(8,128)(2,1)S(1)} collective-permute-done((bf16[128,576]{1,0:T(8,128)(2,1)S(1)}, bf16[128,576]{1,0:T(8,128)(2,1)S(1)}, u32[]{:S(2)}, u32[]{:S(2)}) %collective-permute-start.4) | collective-permute-done | bytes 147488 | tf_op jit(solution)/shard_map/ppermute | solution.py:41
  59.5 0.7 %slice_bitcast_fusion = bf16[1,128,512]{2,1,0:T(8,128)(2,1)} fusion(bf16[128,576]{1,0:T(8,128)(2,1)S(1)} %add_convert_fusion.1), kind=kLoop, calls=%fused_computation.11 | loop fusion | bytes 262144 | tf_op jit(solution)/shard_map/broadcast_in_dim | solution.py:142
  60.2 0.7 %copy.20 = bf16[1,64,128]{2,1,0:T(8,128)(2,1)} copy(bf16[1,64,128]{1,2,0:T(8,128)(2,1)S(1)} %slice_bitcast_fusion.1) | data formatting | bytes 32768
  (5 shorter events, 0.2 us)
Async XLA Ops:
  27.9 26.2 %copy-start = (bf16[128,16,64]{2,1,0:T(8,128)(2,1)S(1)}, bf16[128,16,64]{2,1,0:T(8,128)(2,1)}, u32[]{:S(2)}) copy-start(bf16[128,16,64]{2,1,0:T(8,128)(2,1)} %get-tuple-element.13) | copy-start | bytes 786436
  29.0 1.7 %collective-permute-start = (bf16[2,128,576]{2,1,0:T(8,128)(2,1)S(1)}, bf16[2,128,576]{2,1,0:T(8,128)(2,1)S(1)}, u32[]{:S(2)}, u32[]{:S(2)}) collective-permute-start(bf16[2,128,576]{2,1,0:T(8,128)(2,1)S(1)} %fusion), channel_id=1, source_target_pairs={{0,8},{8,0},{16,24},{24,16},{1,9},{9,1},{17,25},{25,17},{2,10},{10... | collective-permute-start | bytes 884744 | tf_op jit(solution)/shard_map/ppermute | solution.py:25
  31.8 8.4 %collective-permute-start.1 = (bf16[128,576]{1,0:T(8,128)(2,1)S(1)}, bf16[128,576]{1,0:T(8,128)(2,1)S(1)}, u32[]{:S(2)}, u32[]{:S(2)}) collective-permute-start(bf16[128,576]{1,0:T(8,128)(2,1)S(1)} %select_bitcast_fusion), channel_id=1, source_target_pairs={{16,0},{24,8},{17,1},{25,9},{18,2},{26,10},{19,3},{27,11},{20,4},{... | collective-permute-start | bytes 442376 | tf_op jit(solution)/shard_map/ppermute | solution.py:30
  40.2 5.7 %collective-permute-start.2 = (bf16[128,576]{1,0:T(8,128)(2,1)S(1)}, bf16[128,576]{1,0:T(8,128)(2,1)S(1)}, u32[]{:S(2)}, u32[]{:S(2)}) collective-permute-start(bf16[128,576]{1,0:T(8,128)(2,1)S(1)} %add_convert_fusion.4), channel_id=1, source_target_pairs={{0,1},{1,0},{2,3},{3,2},{4,5},{5,4},{6,7},{7,6},{8,9},{9,8},{10,11... | collective-permute-start | bytes 442376 | tf_op jit(solution)/shard_map/ppermute | solution.py:41
  45.9 5.4 %collective-permute-start.3 = (bf16[128,576]{1,0:T(8,128)(2,1)S(1)}, bf16[128,576]{1,0:T(8,128)(2,1)S(1)}, u32[]{:S(2)}, u32[]{:S(2)}) collective-permute-start(bf16[128,576]{1,0:T(8,128)(2,1)S(1)} %add_convert_fusion.3), channel_id=1, source_target_pairs={{0,2},{1,3},{2,0},{3,1},{4,6},{5,7},{6,4},{7,5},{8,10},{9,11},{10,... | collective-permute-start | bytes 442376 | tf_op jit(solution)/shard_map/ppermute | solution.py:41
  51.4 8.1 %collective-permute-start.4 = (bf16[128,576]{1,0:T(8,128)(2,1)S(1)}, bf16[128,576]{1,0:T(8,128)(2,1)S(1)}, u32[]{:S(2)}, u32[]{:S(2)}) collective-permute-start(bf16[128,576]{1,0:T(8,128)(2,1)S(1)} %add_convert_fusion.2), channel_id=1, source_target_pairs={{0,4},{1,5},{2,6},{3,7},{4,0},{5,1},{6,2},{7,3},{8,12},{9,13},{10,... | collective-permute-start | bytes 442376 | tf_op jit(solution)/shard_map/ppermute | solution.py:41

commit v11 on v10

--- a/solution.py
+++ b/solution.py
@@ -18,10 +18,7 @@
             total = total + got.astype(jnp.float32)
         return total
     pairs = n_ctx // 2
-    side = here % 2
-    by_parity = blocks.reshape(pairs, 2, *blocks.shape[1:])
-    mine = jnp.take(by_parity, side, axis=1)
-    theirs = jnp.take(by_parity, 1 - side, axis=1)
+    mine, theirs = blocks[:pairs], blocks[pairs:]
     got = lax.ppermute(theirs, "ctx", [(i, i ^ 1) for i in range(n_ctx)])
     summed = (mine.astype(jnp.float32) + got.astype(jnp.float32)).astype(jnp.bfloat16)
     total = jnp.take(summed, here // 2, axis=0).astype(jnp.float32)
@@ -94,8 +91,19 @@
 
     @pl.when(step == pl.num_programs(0) - 1)
     def _():
-        terms_ref[:, :kvr] = lt_acc[...].astype(jnp.bfloat16)
-        terms_ref[:, kvr:] = rt_acc[...].astype(jnp.bfloat16)
+        n_blocks, block_len = terms_ref.shape[0], terms_ref.shape[1]
+        pairs = n_blocks // 2
+        side = (offset_ref[0] // block_len) % 2 if n_blocks % 2 == 0 else 0
+        for slot in range(n_blocks):
+            if n_blocks % 2:
+                start = slot * block_len
+            elif slot < pairs:
+                start = (2 * slot + side) * block_len
+            else:
+                start = (2 * (slot - pairs) + 1 - side) * block_len
+            start = pl.multiple_of(start, block_len)
+            terms_ref[slot, :, :kvr] = lt_acc[pl.ds(start, block_len), :].astype(jnp.bfloat16)
+            terms_ref[slot, :, kvr:] = rt_acc[pl.ds(start, block_len), :].astype(jnp.bfloat16)
 
 
 def body(query_latent, query_rope, key_latent, key_rope, output_grad):
@@ -114,13 +122,14 @@
     by_rows = pl.BlockSpec((t_blk, heads, kvr), lambda i, off: (i, 0, 0))
     rope_rows = pl.BlockSpec((t_blk, heads, rope), lambda i, off: (i, 0, 0))
     fixed = pl.BlockSpec((length, kvr + rope), lambda i, off: (0, 0))
+    term_blocks = pl.BlockSpec((n_ctx, block_len, kvr + rope), lambda i, off: (0, 0, 0))
     att, lqg, rqg, terms = pl.pallas_call(
         attention_kernel,
         grid_spec=pltpu.PrefetchScalarGridSpec(
             num_scalar_prefetch=1,
             grid=(block_len // t_blk,),
             in_specs=[by_rows, rope_rows, fixed, by_rows],
-            out_specs=[by_rows, by_rows, rope_rows, fixed],
+            out_specs=[by_rows, by_rows, rope_rows, term_blocks],
             scratch_shapes=[
                 pltpu.VMEM((length, kvr), jnp.float32),
                 pltpu.VMEM((length, rope), jnp.float32),
@@ -130,14 +139,14 @@
             jax.ShapeDtypeStruct((block_len, heads, kvr), jnp.bfloat16),
             jax.ShapeDtypeStruct((block_len, heads, kvr), jnp.bfloat16),
             jax.ShapeDtypeStruct((block_len, heads, rope), jnp.bfloat16),
-            jax.ShapeDtypeStruct((length, kvr + rope), jnp.bfloat16),
+            jax.ShapeDtypeStruct((n_ctx, block_len, kvr + rope), jnp.bfloat16),
         ],
         compiler_params=pltpu.CompilerParams(dimension_semantics=("arbitrary",)),
     )(offset, query_latent[0], qr, whole_keys, output_grad[0])
     attended = att[None]
     latent_qgrad = lqg[None]
     rope_qgrad = jnp.transpose(rqg, (1, 2, 0))[None]
-    total = causal_reduce_ctx(terms.reshape(n_ctx, block_len, -1), n_ctx)
+    total = causal_reduce_ctx(terms, n_ctx)
     total = butterfly_sum_ep(total, n_ep).astype(jnp.bfloat16)
     latent_kgrad = total[None, :, :kvr]
     rope_kgrad = total[:, kvr:].T[None]

time: 61.2 us -> 61.1 us (level)
  other arithmetic: 3.29 us -> 2.19 us
  local copies, waits for them, and re-layouts: 5.47 us -> 6.53 us
    select_n x1 -> x0, other arithmetic: 1.08 us -> none  [causal_reduce_ctx(): theirs = jnp.take(by_parity, 1 - side, axis=1)]
    slice x0 -> x1, local copies, waits for them, and re-layouts: none -> 1.06 us  [causal_reduce_ctx(): mine, theirs = (blocks[:pairs], blocks[pairs:])]
where the time goes in v11:
time: 61.1 us; the launch traced here: 60.8 us
  waiting for transfers between devices  20.5 us (34%)
  Pallas kernels  13.5 us (22%)
  blocking collectives  9.78 us (16%)
  starting transfers between devices  7.59 us (12%)
  local copies, waits for them, and re-layouts  6.53 us (11%)
  other arithmetic  2.19 us (4%)
  between operations  0.71 us (1%)
    pallas_call x1, Pallas kernels, body(): pl.pallas_call(attention_kernel, grid_spec=pltpu.PrefetchScalarGridSpec(n...  13.5 us
    ppermute x3, waiting for transfers between devices, butterfly_sum_ep(): theirs = lax.ppermute(mine, 'ep', [(i, i ^ bit) for i in range(n_ep)])  12.1 us
    all_gather x1, blocking collectives, body(): whole_keys = lax.all_gather(local_keys, 'ctx', axis=0, tiled=True)  9.78 us
    ppermute x1, waiting for transfers between devices, causal_reduce_ctx(): lax.ppermute(sent, 'ctx', [(i, i - 2 * shift) for i in range(2 * shift, n...  7.05 us
    ppermute x3, starting transfers between devices, butterfly_sum_ep(): theirs = lax.ppermute(mine, 'ep', [(i, i ^ bit) for i in range(n_ep)])  5.87 us
    unnamed x6, local copies, waits for them, and re-layouts  4.8 us
    ppermute x1, starting transfers between devices, causal_reduce_ctx(): lax.ppermute(sent, 'ctx', [(i, i - 2 * shift) for i in range(2 * shift, n...  1.29 us
    ppermute x1, waiting for transfers between devices, causal_reduce_ctx(): got = lax.ppermute(theirs, 'ctx', [(i, i ^ 1) for i in range(n_ctx)])  1.27 us
  transfers between devices with their start and end apart: 5, of which 5 were waited for; matrix products, arithmetic and copies ran while one was open for 2% of the time, Pallas kernels for 0%

profile of v11, /device:TPU:0, one launch (start us, length us, event | category | flops | bytes accessed | tf_op | source)
XLA Modules:
  0.0 60.8 jit_solution(1675905782076542054)
XLA Ops:
  0.6 2.1 %copy.10 = bf16[1,16,64,128]{2,1,3,0:T(8,128)(2,1)} copy(bf16[1,16,64,128]{3,2,1,0:T(8,128)(2,1)} %param.8) | data formatting | bytes 524288 | tf_op args[1]
  2.8 0.8 %copy.11 = bf16[1,64,128]{1,2,0:T(8,128)(2,1)S(1)} copy(bf16[1,64,128]{2,1,0:T(8,128)(2,1)} %param.10) | data formatting | bytes 32768 | tf_op args[3]
  3.6 0.9 %pad_maximum_fusion = bf16[128,576]{1,0:T(8,128)(2,1)S(1)} fusion(bf16[128,64]{1,0:T(8,128)(2,1)S(1)} %bitcast.29, bf16[128,512]{1,0:T(8,128)(2,1)} %bitcast.30), kind=kLoop, calls=%fused_computation.5 | loop fusion | flops 294912 | bytes 294912 | tf_op jit(solution)/shard_map/concatenate | solution.py:114
  4.5 9.8 %all_gather.3.keys_ref = bf16[512,576]{1,0:T(8,128)(2,1)} all-gather(bf16[128,576]{1,0:T(8,128)(2,1)S(1)} %pad_maximum_fusion), channel_id=1, replica_groups=mesh['ctx'=4,'ep'=8] {'ctx'}, dimensions={0}, use_global_device_ids=true | all-gather | bytes 737280 | tf_op jit(solution)/shard_map/all_gather | solution.py:115
  14.3 13.5 %shard_map.92 = (bf16[128,16,512]{2,1,0:T(8,128)(2,1)}, bf16[128,16,512]{2,1,0:T(8,128)(2,1)}, bf16[128,16,64]{2,1,0:T(8,128)(2,1)}, bf16[4,128,576]{2,1,0:T(8,128)(2,1)}) custom-call(s32[1]{0:T(128)} %bitcast.offset_ref, bf16[128,16,512]{2,1,0:T(8,128)(2,1)} %bitcast.25, bf16[128,16,64]{2,1,0:T(8,128)(2,1)} %bitcast.27, ...), custom_call_target="tpu_custom_call" | custom-call | tf_op jit(solution)/shard_map/pallas_call | solution.py:126
  27.9 0.0 copy-start
  27.9 1.1 %slice.13 = bf16[2,128,576]{2,1,0:T(8,128)(2,1)S(1)} slice(bf16[4,128,576]{2,1,0:T(8,128)(2,1)} %get-tuple-element.13), slice={[2:4], [0:128], [0:576]} | slice | bytes 589824 | tf_op jit(solution)/shard_map/slice | solution.py:21
  28.9 0.4 collective-permute-start
  29.4 1.3 %collective-permute-done = bf16[2,128,576]{2,1,0:T(8,128)(2,1)S(1)} collective-permute-done((bf16[2,128,576]{2,1,0:T(8,128)(2,1)S(1)}, bf16[2,128,576]{2,1,0:T(8,128)(2,1)S(1)}, u32[]{:S(2)}, u32[]{:S(2)}) %collective-permute-start) | collective-permute-done | bytes 294944 | tf_op jit(solution)/shard_map/ppermute | solution.py:22
  30.6 1.1 %add_convert_fusion = bf16[2,128,576]{2,1,0:T(8,128)(2,1)S(1)} fusion(bf16[2,128,576]{2,1,0:T(8,128)(2,1)S(1)} %collective-permute-done, bf16[4,128,576]{2,1,0:T(8,128)(2,1)} %get-tuple-element.13), kind=kLoop, calls=%fused_computation | loop fusion | flops 589824 | bytes 884736 | tf_op jit(solution)/shard_map/convert_element_type | solution.py:23
  31.7 1.3 %collective-permute-start.1 = (bf16[128,576]{1,0:T(8,128)(2,1)S(1)}, bf16[128,576]{1,0:T(8,128)(2,1)S(1)}, u32[]{:S(2)}, u32[]{:S(2)}) collective-permute-start(bf16[128,576]{1,0:T(8,128)(2,1)S(1)} %select_bitcast_fusion), channel_id=1, source_target_pairs={{16,0},{24,8},{17,1},{25,9},{18,2},{26,10},{19,3},{27,11},{20,4},{... | collective-permute-start | bytes 442376 | tf_op jit(solution)/shard_map/ppermute | solution.py:27
  33.0 7.0 %collective-permute-done.1 = bf16[128,576]{1,0:T(8,128)(2,1)S(1)} collective-permute-done((bf16[128,576]{1,0:T(8,128)(2,1)S(1)}, bf16[128,576]{1,0:T(8,128)(2,1)S(1)}, u32[]{:S(2)}, u32[]{:S(2)}) %collective-permute-start.1) | collective-permute-done | bytes 147488 | tf_op jit(solution)/shard_map/ppermute | solution.py:27
  40.1 0.1 add_convert_fusion.4
  40.1 1.6 %collective-permute-start.2 = (bf16[128,576]{1,0:T(8,128)(2,1)S(1)}, bf16[128,576]{1,0:T(8,128)(2,1)S(1)}, u32[]{:S(2)}, u32[]{:S(2)}) collective-permute-start(bf16[128,576]{1,0:T(8,128)(2,1)S(1)} %add_convert_fusion.4), channel_id=1, source_target_pairs={{0,1},{1,0},{2,3},{3,2},{4,5},{5,4},{6,7},{7,6},{8,9},{9,8},{10,11... | collective-permute-start | bytes 442376 | tf_op jit(solution)/shard_map/ppermute | solution.py:38
  41.7 4.1 %collective-permute-done.2 = bf16[128,576]{1,0:T(8,128)(2,1)S(1)} collective-permute-done((bf16[128,576]{1,0:T(8,128)(2,1)S(1)}, bf16[128,576]{1,0:T(8,128)(2,1)S(1)}, u32[]{:S(2)}, u32[]{:S(2)}) %collective-permute-start.2) | collective-permute-done | bytes 147488 | tf_op jit(solution)/shard_map/ppermute | solution.py:38
  45.9 1.6 %collective-permute-start.3 = (bf16[128,576]{1,0:T(8,128)(2,1)S(1)}, bf16[128,576]{1,0:T(8,128)(2,1)S(1)}, u32[]{:S(2)}, u32[]{:S(2)}) collective-permute-start(bf16[128,576]{1,0:T(8,128)(2,1)S(1)} %add_convert_fusion.3), channel_id=1, source_target_pairs={{0,2},{1,3},{2,0},{3,1},{4,6},{5,7},{6,4},{7,5},{8,10},{9,11},{10,... | collective-permute-start | bytes 442376 | tf_op jit(solution)/shard_map/ppermute | solution.py:38
  47.5 3.7 %collective-permute-done.3 = bf16[128,576]{1,0:T(8,128)(2,1)S(1)} collective-permute-done((bf16[128,576]{1,0:T(8,128)(2,1)S(1)}, bf16[128,576]{1,0:T(8,128)(2,1)S(1)}, u32[]{:S(2)}, u32[]{:S(2)}) %collective-permute-start.3) | collective-permute-done | bytes 147488 | tf_op jit(solution)/shard_map/ppermute | solution.py:38
  51.3 2.7 %collective-permute-start.4 = (bf16[128,576]{1,0:T(8,128)(2,1)S(1)}, bf16[128,576]{1,0:T(8,128)(2,1)S(1)}, u32[]{:S(2)}, u32[]{:S(2)}) collective-permute-start(bf16[128,576]{1,0:T(8,128)(2,1)S(1)} %add_convert_fusion.2), channel_id=1, source_target_pairs={{0,4},{1,5},{2,6},{3,7},{4,0},{5,1},{6,2},{7,3},{8,12},{9,13},{10,... | collective-permute-start | bytes 442376 | tf_op jit(solution)/shard_map/ppermute | solution.py:38
  54.0 0.0 copy-done
  54.0 1.1 %copy.12 = bf16[1,16,64,128]{3,2,1,0:T(8,128)(2,1)} copy(bf16[1,16,64,128]{2,1,3,0:T(8,128)(2,1)S(1)} %bitcast.28) | data formatting | bytes 524288
  55.1 4.3 %collective-permute-done.4 = bf16[128,576]{1,0:T(8,128)(2,1)S(1)} collective-permute-done((bf16[128,576]{1,0:T(8,128)(2,1)S(1)}, bf16[128,576]{1,0:T(8,128)(2,1)S(1)}, u32[]{:S(2)}, u32[]{:S(2)}) %collective-permute-start.4) | collective-permute-done | bytes 147488 | tf_op jit(solution)/shard_map/ppermute | solution.py:38
  59.4 0.7 %slice_bitcast_fusion = bf16[1,128,512]{2,1,0:T(8,128)(2,1)} fusion(bf16[128,576]{1,0:T(8,128)(2,1)S(1)} %add_convert_fusion.1), kind=kLoop, calls=%fused_computation.7 | loop fusion | bytes 262144 | tf_op jit(solution)/shard_map/broadcast_in_dim | solution.py:151
  60.1 0.7 %copy.13 = bf16[1,64,128]{2,1,0:T(8,128)(2,1)} copy(bf16[1,64,128]{1,2,0:T(8,128)(2,1)S(1)} %slice_bitcast_fusion.1) | data formatting | bytes 32768
  (5 shorter events, 0.2 us)
Async XLA Ops:
  27.9 26.1 %copy-start = (bf16[128,16,64]{2,1,0:T(8,128)(2,1)S(1)}, bf16[128,16,64]{2,1,0:T(8,128)(2,1)}, u32[]{:S(2)}) copy-start(bf16[128,16,64]{2,1,0:T(8,128)(2,1)} %get-tuple-element.12) | copy-start | bytes 786436
  28.9 1.7 %collective-permute-start = (bf16[2,128,576]{2,1,0:T(8,128)(2,1)S(1)}, bf16[2,128,576]{2,1,0:T(8,128)(2,1)S(1)}, u32[]{:S(2)}, u32[]{:S(2)}) collective-permute-start(bf16[2,128,576]{2,1,0:T(8,128)(2,1)S(1)} %slice.13), channel_id=1, source_target_pairs={{0,8},{8,0},{16,24},{24,16},{1,9},{9,1},{17,25},{25,17},{2,10},{10... | collective-permute-start | bytes 884744 | tf_op jit(solution)/shard_map/ppermute | solution.py:22
  31.7 8.4 %collective-permute-start.1 = (bf16[128,576]{1,0:T(8,128)(2,1)S(1)}, bf16[128,576]{1,0:T(8,128)(2,1)S(1)}, u32[]{:S(2)}, u32[]{:S(2)}) collective-permute-start(bf16[128,576]{1,0:T(8,128)(2,1)S(1)} %select_bitcast_fusion), channel_id=1, source_target_pairs={{16,0},{24,8},{17,1},{25,9},{18,2},{26,10},{19,3},{27,11},{20,4},{... | collective-permute-start | bytes 442376 | tf_op jit(solution)/shard_map/ppermute | solution.py:27
  40.1 5.7 %collective-permute-start.2 = (bf16[128,576]{1,0:T(8,128)(2,1)S(1)}, bf16[128,576]{1,0:T(8,128)(2,1)S(1)}, u32[]{:S(2)}, u32[]{:S(2)}) collective-permute-start(bf16[128,576]{1,0:T(8,128)(2,1)S(1)} %add_convert_fusion.4), channel_id=1, source_target_pairs={{0,1},{1,0},{2,3},{3,2},{4,5},{5,4},{6,7},{7,6},{8,9},{9,8},{10,11... | collective-permute-start | bytes 442376 | tf_op jit(solution)/shard_map/ppermute | solution.py:38
  45.9 5.4 %collective-permute-start.3 = (bf16[128,576]{1,0:T(8,128)(2,1)S(1)}, bf16[128,576]{1,0:T(8,128)(2,1)S(1)}, u32[]{:S(2)}, u32[]{:S(2)}) collective-permute-start(bf16[128,576]{1,0:T(8,128)(2,1)S(1)} %add_convert_fusion.3), channel_id=1, source_target_pairs={{0,2},{1,3},{2,0},{3,1},{4,6},{5,7},{6,4},{7,5},{8,10},{9,11},{10,... | collective-permute-start | bytes 442376 | tf_op jit(solution)/shard_map/ppermute | solution.py:38
  51.3 8.1 %collective-permute-start.4 = (bf16[128,576]{1,0:T(8,128)(2,1)S(1)}, bf16[128,576]{1,0:T(8,128)(2,1)S(1)}, u32[]{:S(2)}, u32[]{:S(2)}) collective-permute-start(bf16[128,576]{1,0:T(8,128)(2,1)S(1)} %add_convert_fusion.2), channel_id=1, source_target_pairs={{0,4},{1,5},{2,6},{3,7},{4,0},{5,1},{6,2},{7,3},{8,12},{9,13},{10,... | collective-permute-start | bytes 442376 | tf_op jit(solution)/shard_map/ppermute | solution.py:38

commit v12 on v10

--- a/solution.py
+++ b/solution.py
@@ -8,7 +8,7 @@
 scale_factor = 192.0 ** (-0.5)
 
 
-def causal_reduce_ctx(blocks, n_ctx):
+def causal_reduce_ctx(blocks, theirs, n_ctx):
     here = lax.axis_index("ctx")
     if n_ctx % 2:
         total = jnp.take(blocks, here, axis=0).astype(jnp.float32)
@@ -18,10 +18,7 @@
             total = total + got.astype(jnp.float32)
         return total
     pairs = n_ctx // 2
-    side = here % 2
-    by_parity = blocks.reshape(pairs, 2, *blocks.shape[1:])
-    mine = jnp.take(by_parity, side, axis=1)
-    theirs = jnp.take(by_parity, 1 - side, axis=1)
+    mine = blocks
     got = lax.ppermute(theirs, "ctx", [(i, i ^ 1) for i in range(n_ctx)])
     summed = (mine.astype(jnp.float32) + got.astype(jnp.float32)).astype(jnp.bfloat16)
     total = jnp.take(summed, here // 2, axis=0).astype(jnp.float32)
@@ -45,7 +42,7 @@
 
 
 def attention_kernel(offset_ref, ql_ref, qr_ref, keys_ref, do_ref,
-                     att_ref, lqg_ref, rqg_ref, terms_ref, lt_acc, rt_acc):
+                     att_ref, lqg_ref, rqg_ref, mine_ref, theirs_ref, lt_acc, rt_acc):
     step = pl.program_id(0)
     t_blk, heads, kvr = ql_ref.shape
     rope = qr_ref.shape[2]
@@ -94,8 +91,22 @@
 
     @pl.when(step == pl.num_programs(0) - 1)
     def _():
-        terms_ref[:, :kvr] = lt_acc[...].astype(jnp.bfloat16)
-        terms_ref[:, kvr:] = rt_acc[...].astype(jnp.bfloat16)
+        block_len = mine_ref.shape[1]
+        n_blocks = lt_acc.shape[0] // block_len
+        even = n_blocks % 2 == 0
+        side = (offset_ref[0] // block_len) % 2 if even else 0
+        for slot in range(mine_ref.shape[0]):
+            start = (2 * slot + side) * block_len if even else slot * block_len
+            start = pl.multiple_of(start, block_len)
+            mine_ref[slot, :, :kvr] = lt_acc[pl.ds(start, block_len), :].astype(jnp.bfloat16)
+            mine_ref[slot, :, kvr:] = rt_acc[pl.ds(start, block_len), :].astype(jnp.bfloat16)
+        for slot in range(theirs_ref.shape[0]):
+            if even:
+                start = pl.multiple_of((2 * slot + 1 - side) * block_len, block_len)
+                theirs_ref[slot, :, :kvr] = lt_acc[pl.ds(start, block_len), :].astype(jnp.bfloat16)
+                theirs_ref[slot, :, kvr:] = rt_acc[pl.ds(start, block_len), :].astype(jnp.bfloat16)
+            else:
+                theirs_ref[slot] = jnp.zeros(theirs_ref.shape[1:], jnp.bfloat16)
 
 
 def body(query_latent, query_rope, key_latent, key_rope, output_grad):
@@ -114,13 +125,17 @@
     by_rows = pl.BlockSpec((t_blk, heads, kvr), lambda i, off: (i, 0, 0))
     rope_rows = pl.BlockSpec((t_blk, heads, rope), lambda i, off: (i, 0, 0))
     fixed = pl.BlockSpec((length, kvr + rope), lambda i, off: (0, 0))
-    att, lqg, rqg, terms = pl.pallas_call(
+    n_mine = n_ctx // 2 if n_ctx % 2 == 0 else n_ctx
+    n_theirs = n_ctx // 2 if n_ctx % 2 == 0 else 1
+    mine_blocks = pl.BlockSpec((n_mine, block_len, kvr + rope), lambda i, off: (0, 0, 0))
+    their_blocks = pl.BlockSpec((n_theirs, block_len, kvr + rope), lambda i, off: (0, 0, 0))
+    att, lqg, rqg, mine, theirs = pl.pallas_call(
         attention_kernel,
         grid_spec=pltpu.PrefetchScalarGridSpec(
             num_scalar_prefetch=1,
             grid=(block_len // t_blk,),
             in_specs=[by_rows, rope_rows, fixed, by_rows],
-            out_specs=[by_rows, by_rows, rope_rows, fixed],
+            out_specs=[by_rows, by_rows, rope_rows, mine_blocks, their_blocks],
             scratch_shapes=[
                 pltpu.VMEM((length, kvr), jnp.float32),
                 pltpu.VMEM((length, rope), jnp.float32),
@@ -130,14 +145,15 @@
             jax.ShapeDtypeStruct((block_len, heads, kvr), jnp.bfloat16),
             jax.ShapeDtypeStruct((block_len, heads, kvr), jnp.bfloat16),
             jax.ShapeDtypeStruct((block_len, heads, rope), jnp.bfloat16),
-            jax.ShapeDtypeStruct((length, kvr + rope), jnp.bfloat16),
+            jax.ShapeDtypeStruct((n_mine, block_len, kvr + rope), jnp.bfloat16),
+            jax.ShapeDtypeStruct((n_theirs, block_len, kvr + rope), jnp.bfloat16),
         ],
         compiler_params=pltpu.CompilerParams(dimension_semantics=("arbitrary",)),
     )(offset, query_latent[0], qr, whole_keys, output_grad[0])
     attended = att[None]
     latent_qgrad = lqg[None]
     rope_qgrad = jnp.transpose(rqg, (1, 2, 0))[None]
-    total = causal_reduce_ctx(terms.reshape(n_ctx, block_len, -1), n_ctx)
+    total = causal_reduce_ctx(mine, theirs, n_ctx)
     total = butterfly_sum_ep(total, n_ep).astype(jnp.bfloat16)
     latent_kgrad = total[None, :, :kvr]
     rope_kgrad = total[:, kvr:].T[None]

time: 61.2 us -> 60.3 us (0.985)
  other arithmetic: 3.29 us -> 2.19 us
    select_n x1 -> x0, other arithmetic: 1.08 us -> none  [causal_reduce_ctx(): theirs = jnp.take(by_parity, 1 - side, axis=1)]
where the time goes in v12:
time: 60.3 us; the launch traced here: 60 us
  waiting for transfers between devices  20.7 us (34%)
  Pallas kernels  13.6 us (23%)
  blocking collectives  9.78 us (16%)
  starting transfers between devices  7.58 us (13%)
  local copies, waits for them, and re-layouts  5.48 us (9%)
  other arithmetic  2.19 us (4%)
  between operations  0.71 us (1%)
    pallas_call x1, Pallas kernels, body(): pl.pallas_call(attention_kernel, grid_spec=pltpu.PrefetchScalarGridSpec(n...  13.6 us
    ppermute x3, waiting for transfers between devices, butterfly_sum_ep(): theirs = lax.ppermute(mine, 'ep', [(i, i ^ bit) for i in range(n_ep)])  12.1 us
    all_gather x1, blocking collectives, body(): whole_keys = lax.all_gather(local_keys, 'ctx', axis=0, tiled=True)  9.78 us
    ppermute x1, waiting for transfers between devices, causal_reduce_ctx(): lax.ppermute(sent, 'ctx', [(i, i - 2 * shift) for i in range(2 * shift, n...  7.04 us
    ppermute x3, starting transfers between devices, butterfly_sum_ep(): theirs = lax.ppermute(mine, 'ep', [(i, i ^ bit) for i in range(n_ep)])  5.87 us
    unnamed x6, local copies, waits for them, and re-layouts  4.81 us
    ppermute x1, waiting for transfers between devices, causal_reduce_ctx(): got = lax.ppermute(theirs, 'ctx', [(i, i ^ 1) for i in range(n_ctx)])  1.49 us
    ppermute x1, starting transfers between devices, causal_reduce_ctx(): lax.ppermute(sent, 'ctx', [(i, i - 2 * shift) for i in range(2 * shift, n...  1.29 us
  transfers between devices with their start and end apart: 5, of which 5 were waited for; matrix products, arithmetic and copies ran while one was open for 2% of the time, Pallas kernels for 0%

profile of v12, /device:TPU:0, one launch (start us, length us, event | category | flops | bytes accessed | tf_op | source)
XLA Modules:
  0.0 60.0 jit_solution(8931365980258125219)
XLA Ops:
  0.6 2.1 %copy.10 = bf16[1,16,64,128]{2,1,3,0:T(8,128)(2,1)} copy(bf16[1,16,64,128]{3,2,1,0:T(8,128)(2,1)} %param.8) | data formatting | bytes 524288 | tf_op args[1]
  2.8 0.8 %copy.11 = bf16[1,64,128]{1,2,0:T(8,128)(2,1)S(1)} copy(bf16[1,64,128]{2,1,0:T(8,128)(2,1)} %param.10) | data formatting | bytes 32768 | tf_op args[3]
  3.6 0.9 %pad_maximum_fusion = bf16[128,576]{1,0:T(8,128)(2,1)S(1)} fusion(bf16[128,64]{1,0:T(8,128)(2,1)S(1)} %bitcast.29, bf16[128,512]{1,0:T(8,128)(2,1)} %bitcast.30), kind=kLoop, calls=%fused_computation.5 | loop fusion | flops 294912 | bytes 294912 | tf_op jit(solution)/shard_map/concatenate | solution.py:117
  4.5 9.8 %all_gather.3.keys_ref = bf16[512,576]{1,0:T(8,128)(2,1)} all-gather(bf16[128,576]{1,0:T(8,128)(2,1)S(1)} %pad_maximum_fusion), channel_id=1, replica_groups=mesh['ctx'=4,'ep'=8] {'ctx'}, dimensions={0}, use_global_device_ids=true | all-gather | bytes 737280 | tf_op jit(solution)/shard_map/all_gather | solution.py:118
  14.3 13.6 %shard_map.92 = (bf16[128,16,512]{2,1,0:T(8,128)(2,1)}, bf16[128,16,512]{2,1,0:T(8,128)(2,1)}, bf16[128,16,64]{2,1,0:T(8,128)(2,1)}, bf16[2,128,576]{2,1,0:T(8,128)(2,1)}, bf16[2,128,576]{2,1,0:T(8,128)(2,1)}) custom-call(s32[1]{0:T(128)} %bitcast.offset_ref, bf16[128,16,512]{2,1,0:T(8,128)(2,1)} %bitcast.25, bf16[128,16,64]{2,1,0:T(8,128)(2,1)} %bitcast.27, ...), custom_call_target="tpu_custom_call" | custom-call | tf_op jit(solution)/shard_map/pallas_call | solution.py:132
  27.9 0.0 copy-start
  27.9 0.4 collective-permute-start
  28.3 1.5 %collective-permute-done = bf16[2,128,576]{2,1,0:T(8,128)(2,1)S(1)} collective-permute-done((bf16[2,128,576]{2,1,0:T(8,128)(2,1)}, bf16[2,128,576]{2,1,0:T(8,128)(2,1)S(1)}, u32[]{:S(2)}, u32[]{:S(2)}) %collective-permute-start) | collective-permute-done | bytes 294944 | tf_op jit(solution)/shard_map/ppermute | solution.py:22
  29.8 1.1 %add_convert_fusion = bf16[2,128,576]{2,1,0:T(8,128)(2,1)S(1)} fusion(bf16[2,128,576]{2,1,0:T(8,128)(2,1)S(1)} %collective-permute-done, bf16[2,128,576]{2,1,0:T(8,128)(2,1)} %get-tuple-element.14), kind=kLoop, calls=%fused_computation | loop fusion | flops 589824 | bytes 884736 | tf_op jit(solution)/shard_map/convert_element_type | solution.py:23
  30.9 1.3 %collective-permute-start.1 = (bf16[128,576]{1,0:T(8,128)(2,1)S(1)}, bf16[128,576]{1,0:T(8,128)(2,1)S(1)}, u32[]{:S(2)}, u32[]{:S(2)}) collective-permute-start(bf16[128,576]{1,0:T(8,128)(2,1)S(1)} %select_bitcast_fusion), channel_id=1, source_target_pairs={{16,0},{24,8},{17,1},{25,9},{18,2},{26,10},{19,3},{27,11},{20,4},{... | collective-permute-start | bytes 442376 | tf_op jit(solution)/shard_map/ppermute | solution.py:27
  32.2 7.0 %collective-permute-done.1 = bf16[128,576]{1,0:T(8,128)(2,1)S(1)} collective-permute-done((bf16[128,576]{1,0:T(8,128)(2,1)S(1)}, bf16[128,576]{1,0:T(8,128)(2,1)S(1)}, u32[]{:S(2)}, u32[]{:S(2)}) %collective-permute-start.1) | collective-permute-done | bytes 147488 | tf_op jit(solution)/shard_map/ppermute | solution.py:27
  39.2 0.1 add_convert_fusion.4
  39.3 1.6 %collective-permute-start.2 = (bf16[128,576]{1,0:T(8,128)(2,1)S(1)}, bf16[128,576]{1,0:T(8,128)(2,1)S(1)}, u32[]{:S(2)}, u32[]{:S(2)}) collective-permute-start(bf16[128,576]{1,0:T(8,128)(2,1)S(1)} %add_convert_fusion.4), channel_id=1, source_target_pairs={{0,1},{1,0},{2,3},{3,2},{4,5},{5,4},{6,7},{7,6},{8,9},{9,8},{10,11... | collective-permute-start | bytes 442376 | tf_op jit(solution)/shard_map/ppermute | solution.py:38
  40.9 4.1 %collective-permute-done.2 = bf16[128,576]{1,0:T(8,128)(2,1)S(1)} collective-permute-done((bf16[128,576]{1,0:T(8,128)(2,1)S(1)}, bf16[128,576]{1,0:T(8,128)(2,1)S(1)}, u32[]{:S(2)}, u32[]{:S(2)}) %collective-permute-start.2) | collective-permute-done | bytes 147488 | tf_op jit(solution)/shard_map/ppermute | solution.py:38
  45.1 1.6 %collective-permute-start.3 = (bf16[128,576]{1,0:T(8,128)(2,1)S(1)}, bf16[128,576]{1,0:T(8,128)(2,1)S(1)}, u32[]{:S(2)}, u32[]{:S(2)}) collective-permute-start(bf16[128,576]{1,0:T(8,128)(2,1)S(1)} %add_convert_fusion.3), channel_id=1, source_target_pairs={{0,2},{1,3},{2,0},{3,1},{4,6},{5,7},{6,4},{7,5},{8,10},{9,11},{10,... | collective-permute-start | bytes 442376 | tf_op jit(solution)/shard_map/ppermute | solution.py:38
  46.7 3.7 %collective-permute-done.3 = bf16[128,576]{1,0:T(8,128)(2,1)S(1)} collective-permute-done((bf16[128,576]{1,0:T(8,128)(2,1)S(1)}, bf16[128,576]{1,0:T(8,128)(2,1)S(1)}, u32[]{:S(2)}, u32[]{:S(2)}) %collective-permute-start.3) | collective-permute-done | bytes 147488 | tf_op jit(solution)/shard_map/ppermute | solution.py:38
  50.5 2.6 %collective-permute-start.4 = (bf16[128,576]{1,0:T(8,128)(2,1)S(1)}, bf16[128,576]{1,0:T(8,128)(2,1)S(1)}, u32[]{:S(2)}, u32[]{:S(2)}) collective-permute-start(bf16[128,576]{1,0:T(8,128)(2,1)S(1)} %add_convert_fusion.2), channel_id=1, source_target_pairs={{0,4},{1,5},{2,6},{3,7},{4,0},{5,1},{6,2},{7,3},{8,12},{9,13},{10,... | collective-permute-start | bytes 442376 | tf_op jit(solution)/shard_map/ppermute | solution.py:38
  53.1 0.0 copy-done
  53.1 1.1 %copy.12 = bf16[1,16,64,128]{3,2,1,0:T(8,128)(2,1)} copy(bf16[1,16,64,128]{2,1,3,0:T(8,128)(2,1)S(1)} %bitcast.28) | data formatting | bytes 524288
  54.3 4.3 %collective-permute-done.4 = bf16[128,576]{1,0:T(8,128)(2,1)S(1)} collective-permute-done((bf16[128,576]{1,0:T(8,128)(2,1)S(1)}, bf16[128,576]{1,0:T(8,128)(2,1)S(1)}, u32[]{:S(2)}, u32[]{:S(2)}) %collective-permute-start.4) | collective-permute-done | bytes 147488 | tf_op jit(solution)/shard_map/ppermute | solution.py:38
  58.6 0.7 %slice_bitcast_fusion = bf16[1,128,512]{2,1,0:T(8,128)(2,1)} fusion(bf16[128,576]{1,0:T(8,128)(2,1)S(1)} %add_convert_fusion.1), kind=kLoop, calls=%fused_computation.7 | loop fusion | bytes 262144 | tf_op jit(solution)/shard_map/broadcast_in_dim | solution.py:158
  59.3 0.7 %copy.13 = bf16[1,64,128]{2,1,0:T(8,128)(2,1)} copy(bf16[1,64,128]{1,2,0:T(8,128)(2,1)S(1)} %slice_bitcast_fusion.1) | data formatting | bytes 32768
  (5 shorter events, 0.2 us)
Async XLA Ops:
  27.9 25.3 %copy-start = (bf16[128,16,64]{2,1,0:T(8,128)(2,1)S(1)}, bf16[128,16,64]{2,1,0:T(8,128)(2,1)}, u32[]{:S(2)}) copy-start(bf16[128,16,64]{2,1,0:T(8,128)(2,1)} %get-tuple-element.13) | copy-start | bytes 786436
  27.9 1.9 %collective-permute-start = (bf16[2,128,576]{2,1,0:T(8,128)(2,1)}, bf16[2,128,576]{2,1,0:T(8,128)(2,1)S(1)}, u32[]{:S(2)}, u32[]{:S(2)}) collective-permute-start(bf16[2,128,576]{2,1,0:T(8,128)(2,1)} %get-tuple-element.15), channel_id=1, source_target_pairs={{0,8},{8,0},{16,24},{24,16},{1,9},{9,1},{17,25},{25,17},{2,10},{10... | collective-permute-start | bytes 884744 | tf_op jit(solution)/shard_map/ppermute | solution.py:22
  30.9 8.3 %collective-permute-start.1 = (bf16[128,576]{1,0:T(8,128)(2,1)S(1)}, bf16[128,576]{1,0:T(8,128)(2,1)S(1)}, u32[]{:S(2)}, u32[]{:S(2)}) collective-permute-start(bf16[128,576]{1,0:T(8,128)(2,1)S(1)} %select_bitcast_fusion), channel_id=1, source_target_pairs={{16,0},{24,8},{17,1},{25,9},{18,2},{26,10},{19,3},{27,11},{20,4},{... | collective-permute-start | bytes 442376 | tf_op jit(solution)/shard_map/ppermute | solution.py:27
  39.3 5.7 %collective-permute-start.2 = (bf16[128,576]{1,0:T(8,128)(2,1)S(1)}, bf16[128,576]{1,0:T(8,128)(2,1)S(1)}, u32[]{:S(2)}, u32[]{:S(2)}) collective-permute-start(bf16[128,576]{1,0:T(8,128)(2,1)S(1)} %add_convert_fusion.4), channel_id=1, source_target_pairs={{0,1},{1,0},{2,3},{3,2},{4,5},{5,4},{6,7},{7,6},{8,9},{9,8},{10,11... | collective-permute-start | bytes 442376 | tf_op jit(solution)/shard_map/ppermute | solution.py:38
  45.1 5.4 %collective-permute-start.3 = (bf16[128,576]{1,0:T(8,128)(2,1)S(1)}, bf16[128,576]{1,0:T(8,128)(2,1)S(1)}, u32[]{:S(2)}, u32[]{:S(2)}) collective-permute-start(bf16[128,576]{1,0:T(8,128)(2,1)S(1)} %add_convert_fusion.3), channel_id=1, source_target_pairs={{0,2},{1,3},{2,0},{3,1},{4,6},{5,7},{6,4},{7,5},{8,10},{9,11},{10,... | collective-permute-start | bytes 442376 | tf_op jit(solution)/shard_map/ppermute | solution.py:38
  50.5 8.1 %collective-permute-start.4 = (bf16[128,576]{1,0:T(8,128)(2,1)S(1)}, bf16[128,576]{1,0:T(8,128)(2,1)S(1)}, u32[]{:S(2)}, u32[]{:S(2)}) collective-permute-start(bf16[128,576]{1,0:T(8,128)(2,1)S(1)} %add_convert_fusion.2), channel_id=1, source_target_pairs={{0,4},{1,5},{2,6},{3,7},{4,0},{5,1},{6,2},{7,3},{8,12},{9,13},{10,... | collective-permute-start | bytes 442376 | tf_op jit(solution)/shard_map/ppermute | solution.py:38

commit v13 on v12

--- a/solution.py
+++ b/solution.py
@@ -29,15 +29,20 @@
     return total
 
 
-def butterfly_sum_ep(total, n_ep):
+def butterfly_sum_ep(total, n_ctx, n_ep):
     if n_ep & (n_ep - 1):
         return lax.psum(total.astype(jnp.bfloat16), "ep").astype(jnp.float32)
-    bit = 1
-    while bit < n_ep:
+    bits = [1 << k for k in range(n_ep.bit_length() - 1)]
+    orders = [bits, bits[1:] + bits[:1]]
+    for step in range(len(bits)):
+        pairs = [
+            (c * n_ep + e, c * n_ep + (e ^ orders[c % 2][step]))
+            for c in range(n_ctx)
+            for e in range(n_ep)
+        ]
         mine = total.astype(jnp.bfloat16)
-        theirs = lax.ppermute(mine, "ep", [(i, i ^ bit) for i in range(n_ep)])
+        theirs = lax.ppermute(mine, ("ctx", "ep"), pairs)
         total = mine.astype(jnp.float32) + theirs.astype(jnp.float32)
-        bit *= 2
     return total
 
 
@@ -154,7 +159,7 @@
     latent_qgrad = lqg[None]
     rope_qgrad = jnp.transpose(rqg, (1, 2, 0))[None]
     total = causal_reduce_ctx(mine, theirs, n_ctx)
-    total = butterfly_sum_ep(total, n_ep).astype(jnp.bfloat16)
+    total = butterfly_sum_ep(total, n_ctx, n_ep).astype(jnp.bfloat16)
     latent_kgrad = total[None, :, :kvr]
     rope_kgrad = total[:, kvr:].T[None]
     return (attended, latent_qgrad, rope_qgrad, latent_kgrad, rope_kgrad)

time: 60.3 us -> 59.1 us (0.980)
  waiting for transfers between devices: 20.7 us -> 19.1 us
    ppermute x3, waiting for transfers between devices: 12.1 us -> 10.6 us  [butterfly_sum_ep(): theirs = lax.ppermute(mine, ('ctx', 'ep'), pairs)]
where the time goes in v13:
time: 59.1 us; the launch traced here: 58.5 us
  waiting for transfers between devices  19.1 us (32%)
  Pallas kernels  13.6 us (23%)
  blocking collectives  9.78 us (17%)
  starting transfers between devices  7.69 us (13%)
  local copies, waits for them, and re-layouts  5.48 us (9%)
  other arithmetic  2.19 us (4%)
  between operations  0.71 us (1%)
    pallas_call x1, Pallas kernels, body(): pl.pallas_call(attention_kernel, grid_spec=pltpu.PrefetchScalarGridSpec(n...  13.6 us
    ppermute x3, waiting for transfers between devices, butterfly_sum_ep(): theirs = lax.ppermute(mine, ('ctx', 'ep'), pairs)  10.6 us
    all_gather x1, blocking collectives, body(): whole_keys = lax.all_gather(local_keys, 'ctx', axis=0, tiled=True)  9.78 us
    ppermute x1, waiting for transfers between devices, causal_reduce_ctx(): lax.ppermute(sent, 'ctx', [(i, i - 2 * shift) for i in range(2 * shift, n...  7.04 us
    ppermute x3, starting transfers between devices, butterfly_sum_ep(): theirs = lax.ppermute(mine, ('ctx', 'ep'), pairs)  5.98 us
    unnamed x6, local copies, waits for them, and re-layouts  4.81 us
    ppermute x1, waiting for transfers between devices, causal_reduce_ctx(): got = lax.ppermute(theirs, 'ctx', [(i, i ^ 1) for i in range(n_ctx)])  1.49 us
    ppermute x1, starting transfers between devices, causal_reduce_ctx(): lax.ppermute(sent, 'ctx', [(i, i - 2 * shift) for i in range(2 * shift, n...  1.29 us
  transfers between devices with their start and end apart: 5, of which 5 were waited for; matrix products, arithmetic and copies ran while one was open for 2% of the time, Pallas kernels for 0%

profile of v13, /device:TPU:0, one launch (start us, length us, event | category | flops | bytes accessed | tf_op | source)
XLA Modules:
  0.0 58.5 jit_solution(17737924752871229975)
XLA Ops:
  0.6 2.1 %copy.10 = bf16[1,16,64,128]{2,1,3,0:T(8,128)(2,1)} copy(bf16[1,16,64,128]{3,2,1,0:T(8,128)(2,1)} %param.8) | data formatting | bytes 524288 | tf_op args[1]
  2.8 0.8 %copy.11 = bf16[1,64,128]{1,2,0:T(8,128)(2,1)S(1)} copy(bf16[1,64,128]{2,1,0:T(8,128)(2,1)} %param.10) | data formatting | bytes 32768 | tf_op args[3]
  3.6 0.9 %pad_maximum_fusion = bf16[128,576]{1,0:T(8,128)(2,1)S(1)} fusion(bf16[128,64]{1,0:T(8,128)(2,1)S(1)} %bitcast.29, bf16[128,512]{1,0:T(8,128)(2,1)} %bitcast.30), kind=kLoop, calls=%fused_computation.5 | loop fusion | flops 294912 | bytes 294912 | tf_op jit(solution)/shard_map/concatenate | solution.py:122
  4.5 9.8 %all_gather.3.keys_ref = bf16[512,576]{1,0:T(8,128)(2,1)} all-gather(bf16[128,576]{1,0:T(8,128)(2,1)S(1)} %pad_maximum_fusion), channel_id=1, replica_groups=mesh['ctx'=4,'ep'=8] {'ctx'}, dimensions={0}, use_global_device_ids=true | all-gather | bytes 737280 | tf_op jit(solution)/shard_map/all_gather | solution.py:123
  14.3 13.6 %shard_map.92 = (bf16[128,16,512]{2,1,0:T(8,128)(2,1)}, bf16[128,16,512]{2,1,0:T(8,128)(2,1)}, bf16[128,16,64]{2,1,0:T(8,128)(2,1)}, bf16[2,128,576]{2,1,0:T(8,128)(2,1)}, bf16[2,128,576]{2,1,0:T(8,128)(2,1)}) custom-call(s32[1]{0:T(128)} %bitcast.offset_ref, bf16[128,16,512]{2,1,0:T(8,128)(2,1)} %bitcast.25, bf16[128,16,64]{2,1,0:T(8,128)(2,1)} %bitcast.27, ...), custom_call_target="tpu_custom_call" | custom-call | tf_op jit(solution)/shard_map/pallas_call | solution.py:137
  27.9 0.0 copy-start
  27.9 0.4 collective-permute-start
  28.3 1.5 %collective-permute-done = bf16[2,128,576]{2,1,0:T(8,128)(2,1)S(1)} collective-permute-done((bf16[2,128,576]{2,1,0:T(8,128)(2,1)}, bf16[2,128,576]{2,1,0:T(8,128)(2,1)S(1)}, u32[]{:S(2)}, u32[]{:S(2)}) %collective-permute-start) | collective-permute-done | bytes 294944 | tf_op jit(solution)/shard_map/ppermute | solution.py:22
  29.8 1.1 %add_convert_fusion = bf16[2,128,576]{2,1,0:T(8,128)(2,1)S(1)} fusion(bf16[2,128,576]{2,1,0:T(8,128)(2,1)S(1)} %collective-permute-done, bf16[2,128,576]{2,1,0:T(8,128)(2,1)} %get-tuple-element.14), kind=kLoop, calls=%fused_computation | loop fusion | flops 589824 | bytes 884736 | tf_op jit(solution)/shard_map/convert_element_type | solution.py:23
  30.9 1.3 %collective-permute-start.1 = (bf16[128,576]{1,0:T(8,128)(2,1)S(1)}, bf16[128,576]{1,0:T(8,128)(2,1)S(1)}, u32[]{:S(2)}, u32[]{:S(2)}) collective-permute-start(bf16[128,576]{1,0:T(8,128)(2,1)S(1)} %select_bitcast_fusion), channel_id=1, source_target_pairs={{16,0},{24,8},{17,1},{25,9},{18,2},{26,10},{19,3},{27,11},{20,4},{... | collective-permute-start | bytes 442376 | tf_op jit(solution)/shard_map/ppermute | solution.py:27
  32.2 7.0 %collective-permute-done.1 = bf16[128,576]{1,0:T(8,128)(2,1)S(1)} collective-permute-done((bf16[128,576]{1,0:T(8,128)(2,1)S(1)}, bf16[128,576]{1,0:T(8,128)(2,1)S(1)}, u32[]{:S(2)}, u32[]{:S(2)}) %collective-permute-start.1) | collective-permute-done | bytes 147488 | tf_op jit(solution)/shard_map/ppermute | solution.py:27
  39.2 0.1 add_convert_fusion.4
  39.3 1.6 %collective-permute-start.2 = (bf16[128,576]{1,0:T(8,128)(2,1)S(1)}, bf16[128,576]{1,0:T(8,128)(2,1)S(1)}, u32[]{:S(2)}, u32[]{:S(2)}) collective-permute-start(bf16[128,576]{1,0:T(8,128)(2,1)S(1)} %add_convert_fusion.4), channel_id=1, source_target_pairs={{0,1},{1,0},{2,3},{3,2},{4,5},{5,4},{6,7},{7,6},{8,10},{9,11},{10,... | collective-permute-start | bytes 442376 | tf_op jit(solution)/shard_map/ppermute | solution.py:44
  40.9 3.8 %collective-permute-done.2 = bf16[128,576]{1,0:T(8,128)(2,1)S(1)} collective-permute-done((bf16[128,576]{1,0:T(8,128)(2,1)S(1)}, bf16[128,576]{1,0:T(8,128)(2,1)S(1)}, u32[]{:S(2)}, u32[]{:S(2)}) %collective-permute-start.2) | collective-permute-done | bytes 147488 | tf_op jit(solution)/shard_map/ppermute | solution.py:44
  44.7 1.6 %collective-permute-start.3 = (bf16[128,576]{1,0:T(8,128)(2,1)S(1)}, bf16[128,576]{1,0:T(8,128)(2,1)S(1)}, u32[]{:S(2)}, u32[]{:S(2)}) collective-permute-start(bf16[128,576]{1,0:T(8,128)(2,1)S(1)} %add_convert_fusion.3), channel_id=1, source_target_pairs={{0,2},{1,3},{2,0},{3,1},{4,6},{5,7},{6,4},{7,5},{8,12},{9,13},{10,... | collective-permute-start | bytes 442376 | tf_op jit(solution)/shard_map/ppermute | solution.py:44
  46.4 4.4 %collective-permute-done.3 = bf16[128,576]{1,0:T(8,128)(2,1)S(1)} collective-permute-done((bf16[128,576]{1,0:T(8,128)(2,1)S(1)}, bf16[128,576]{1,0:T(8,128)(2,1)S(1)}, u32[]{:S(2)}, u32[]{:S(2)}) %collective-permute-start.3) | collective-permute-done | bytes 147488 | tf_op jit(solution)/shard_map/ppermute | solution.py:44
  50.8 2.8 %collective-permute-start.4 = (bf16[128,576]{1,0:T(8,128)(2,1)S(1)}, bf16[128,576]{1,0:T(8,128)(2,1)S(1)}, u32[]{:S(2)}, u32[]{:S(2)}) collective-permute-start(bf16[128,576]{1,0:T(8,128)(2,1)S(1)} %add_convert_fusion.2), channel_id=1, source_target_pairs={{0,4},{1,5},{2,6},{3,7},{4,0},{5,1},{6,2},{7,3},{8,9},{9,8},{10,11... | collective-permute-start | bytes 442376 | tf_op jit(solution)/shard_map/ppermute | solution.py:44
  53.6 0.0 copy-done
  53.6 1.1 %copy.12 = bf16[1,16,64,128]{3,2,1,0:T(8,128)(2,1)} copy(bf16[1,16,64,128]{2,1,3,0:T(8,128)(2,1)S(1)} %bitcast.28) | data formatting | bytes 524288
  54.7 2.4 %collective-permute-done.4 = bf16[128,576]{1,0:T(8,128)(2,1)S(1)} collective-permute-done((bf16[128,576]{1,0:T(8,128)(2,1)S(1)}, bf16[128,576]{1,0:T(8,128)(2,1)S(1)}, u32[]{:S(2)}, u32[]{:S(2)}) %collective-permute-start.4) | collective-permute-done | bytes 147488 | tf_op jit(solution)/shard_map/ppermute | solution.py:44
  57.1 0.7 %slice_bitcast_fusion = bf16[1,128,512]{2,1,0:T(8,128)(2,1)} fusion(bf16[128,576]{1,0:T(8,128)(2,1)S(1)} %add_convert_fusion.1), kind=kLoop, calls=%fused_computation.7 | loop fusion | bytes 262144 | tf_op jit(solution)/shard_map/broadcast_in_dim | solution.py:163
  57.8 0.7 %copy.13 = bf16[1,64,128]{2,1,0:T(8,128)(2,1)} copy(bf16[1,64,128]{1,2,0:T(8,128)(2,1)S(1)} %slice_bitcast_fusion.1) | data formatting | bytes 32768
  (5 shorter events, 0.2 us)
Async XLA Ops:
  27.9 25.7 %copy-start = (bf16[128,16,64]{2,1,0:T(8,128)(2,1)S(1)}, bf16[128,16,64]{2,1,0:T(8,128)(2,1)}, u32[]{:S(2)}) copy-start(bf16[128,16,64]{2,1,0:T(8,128)(2,1)} %get-tuple-element.13) | copy-start | bytes 786436
  27.9 1.9 %collective-permute-start = (bf16[2,128,576]{2,1,0:T(8,128)(2,1)}, bf16[2,128,576]{2,1,0:T(8,128)(2,1)S(1)}, u32[]{:S(2)}, u32[]{:S(2)}) collective-permute-start(bf16[2,128,576]{2,1,0:T(8,128)(2,1)} %get-tuple-element.15), channel_id=1, source_target_pairs={{0,8},{8,0},{16,24},{24,16},{1,9},{9,1},{17,25},{25,17},{2,10},{10... | collective-permute-start | bytes 884744 | tf_op jit(solution)/shard_map/ppermute | solution.py:22
  30.9 8.3 %collective-permute-start.1 = (bf16[128,576]{1,0:T(8,128)(2,1)S(1)}, bf16[128,576]{1,0:T(8,128)(2,1)S(1)}, u32[]{:S(2)}, u32[]{:S(2)}) collective-permute-start(bf16[128,576]{1,0:T(8,128)(2,1)S(1)} %select_bitcast_fusion), channel_id=1, source_target_pairs={{16,0},{24,8},{17,1},{25,9},{18,2},{26,10},{19,3},{27,11},{20,4},{... | collective-permute-start | bytes 442376 | tf_op jit(solution)/shard_map/ppermute | solution.py:27
  39.3 5.4 %collective-permute-start.2 = (bf16[128,576]{1,0:T(8,128)(2,1)S(1)}, bf16[128,576]{1,0:T(8,128)(2,1)S(1)}, u32[]{:S(2)}, u32[]{:S(2)}) collective-permute-start(bf16[128,576]{1,0:T(8,128)(2,1)S(1)} %add_convert_fusion.4), channel_id=1, source_target_pairs={{0,1},{1,0},{2,3},{3,2},{4,5},{5,4},{6,7},{7,6},{8,10},{9,11},{10,... | collective-permute-start | bytes 442376 | tf_op jit(solution)/shard_map/ppermute | solution.py:44
  44.7 6.0 %collective-permute-start.3 = (bf16[128,576]{1,0:T(8,128)(2,1)S(1)}, bf16[128,576]{1,0:T(8,128)(2,1)S(1)}, u32[]{:S(2)}, u32[]{:S(2)}) collective-permute-start(bf16[128,576]{1,0:T(8,128)(2,1)S(1)} %add_convert_fusion.3), channel_id=1, source_target_pairs={{0,2},{1,3},{2,0},{3,1},{4,6},{5,7},{6,4},{7,5},{8,12},{9,13},{10,... | collective-permute-start | bytes 442376 | tf_op jit(solution)/shard_map/ppermute | solution.py:44
  50.8 6.3 %collective-permute-start.4 = (bf16[128,576]{1,0:T(8,128)(2,1)S(1)}, bf16[128,576]{1,0:T(8,128)(2,1)S(1)}, u32[]{:S(2)}, u32[]{:S(2)}) collective-permute-start(bf16[128,576]{1,0:T(8,128)(2,1)S(1)} %add_convert_fusion.2), channel_id=1, source_target_pairs={{0,4},{1,5},{2,6},{3,7},{4,0},{5,1},{6,2},{7,3},{8,9},{9,8},{10,11... | collective-permute-start | bytes 442376 | tf_op jit(solution)/shard_map/ppermute | solution.py:44

commit v14 on v13

--- a/solution.py
+++ b/solution.py
@@ -114,16 +114,29 @@
                 theirs_ref[slot] = jnp.zeros(theirs_ref.shape[1:], jnp.bfloat16)
 
 
+def prep_kernel(kl_ref, kr_ref, qr_ref, keys_ref, qrows_ref):
+    kvr = kl_ref.shape[1]
+    keys_ref[:, :kvr] = kl_ref[...]
+    keys_ref[:, kvr:] = kr_ref[...].astype(jnp.float32).T.astype(jnp.bfloat16)
+    for head in range(qr_ref.shape[0]):
+        qrows_ref[:, head, :] = qr_ref[head].astype(jnp.float32).T.astype(jnp.bfloat16)
+
+
 def body(query_latent, query_rope, key_latent, key_rope, output_grad):
     n_ctx = lax.axis_size("ctx")
     n_ep = lax.axis_size("ep")
     _, block_len, heads, kvr = query_latent.shape
     rope = query_rope.shape[2]
-    local_keys = jnp.concatenate([key_latent[0], key_rope[0].T], axis=1)
+    local_keys, qr = pl.pallas_call(
+        prep_kernel,
+        out_shape=[
+            jax.ShapeDtypeStruct((block_len, kvr + rope), jnp.bfloat16),
+            jax.ShapeDtypeStruct((block_len, heads, rope), jnp.bfloat16),
+        ],
+    )(key_latent[0], key_rope[0], query_rope[0])
     whole_keys = lax.all_gather(local_keys, "ctx", axis=0, tiled=True)
     length = whole_keys.shape[0]
     offset = (lax.axis_index("ctx") * block_len).astype(jnp.int32).reshape(1)
-    qr = jnp.transpose(query_rope[0], (2, 0, 1))
     t_blk = max(1, min(block_len, 1024 // heads))
     while block_len % t_blk:
         t_blk -= 1

time: 59.1 us -> 59.7 us (1.010)
  Pallas kernels: 13.6 us -> 17 us
  local copies, waits for them, and re-layouts: 5.48 us -> 2.51 us
  blocking collectives: 9.78 us -> 10.9 us
  other arithmetic: 2.19 us -> 1.26 us
    pallas_call x0 -> x1, Pallas kernels: none -> 3.48 us  [body(): pl.pallas_call(prep_kernel, out_shape=[jax.ShapeDtypeStruct((block_len, k...]
    unnamed x6 -> x4, local copies, waits for them, and re-layouts: 4.81 us -> 1.84 us
    all_gather x1, blocking collectives: 9.78 us -> 10.9 us  [body(): whole_keys = lax.all_gather(local_keys, 'ctx', axis=0, tiled=True)]
    concatenate x1 -> x0, other arithmetic: 0.93 us -> none  [body(): local_keys = jnp.concatenate([key_latent[0], key_rope[0].T], axis=1)]
where the time goes in v14:
time: 59.7 us; the launch traced here: 59.2 us
  waiting for transfers between devices  19.1 us (32%)
  Pallas kernels  17 us (28%)
  blocking collectives  10.9 us (18%)
  starting transfers between devices  7.7 us (13%)
  local copies, waits for them, and re-layouts  2.51 us (4%)
  other arithmetic  1.26 us (2%)
  between operations  0.7 us (1%)
    pallas_call x1, Pallas kernels, body(): pl.pallas_call(attention_kernel, grid_spec=pltpu.PrefetchScalarGridSpec(n...  13.5 us
    all_gather x1, blocking collectives, body(): whole_keys = lax.all_gather(local_keys, 'ctx', axis=0, tiled=True)  10.9 us
    ppermute x3, waiting for transfers between devices, butterfly_sum_ep(): theirs = lax.ppermute(mine, ('ctx', 'ep'), pairs)  10.6 us
    ppermute x1, waiting for transfers between devices, causal_reduce_ctx(): lax.ppermute(sent, 'ctx', [(i, i - 2 * shift) for i in range(2 * shift, n...  7.04 us
    ppermute x3, starting transfers between devices, butterfly_sum_ep(): theirs = lax.ppermute(mine, ('ctx', 'ep'), pairs)  5.99 us
    pallas_call x1, Pallas kernels, body(): pl.pallas_call(prep_kernel, out_shape=[jax.ShapeDtypeStruct((block_len, k...  3.48 us
    unnamed x4, local copies, waits for them, and re-layouts  1.84 us
    ppermute x1, waiting for transfers between devices, causal_reduce_ctx(): got = lax.ppermute(theirs, 'ctx', [(i, i ^ 1) for i in range(n_ctx)])  1.49 us
  transfers between devices with their start and end apart: 5, of which 5 were waited for; matrix products, arithmetic and copies ran while one was open for 2% of the time, Pallas kernels for 0%

profile of v14, /device:TPU:0, one launch (start us, length us, event | category | flops | bytes accessed | tf_op | source)
XLA Modules:
  0.0 59.2 jit_solution(16878161112388142036)
XLA Ops:
  0.6 3.5 %shard_map.92 = (bf16[128,576]{1,0:T(8,128)(2,1)}, bf16[128,16,64]{2,1,0:T(8,128)(2,1)}) custom-call(bf16[128,512]{1,0:T(8,128)(2,1)} %bitcast.25, bf16[64,128]{1,0:T(8,128)(2,1)} %bitcast.26, bf16[16,64,128]{2,1,0:T(8,128)(2,1)} %bitcast.24), custom_call_target="tpu_custom_call" | custom-call | tf_op jit(solution)/shard_map/pallas_call | solution.py:130
  4.1 10.9 %all_gather.3.keys_ref = bf16[512,576]{1,0:T(8,128)(2,1)} all-gather(bf16[128,576]{1,0:T(8,128)(2,1)} %get-tuple-element.14), channel_id=1, replica_groups=mesh['ctx'=4,'ep'=8] {'ctx'}, dimensions={0}, use_global_device_ids=true | all-gather | bytes 737280 | tf_op jit(solution)/shard_map/all_gather | solution.py:137
  15.0 13.5 %shard_map.93 = (bf16[128,16,512]{2,1,0:T(8,128)(2,1)}, bf16[128,16,512]{2,1,0:T(8,128)(2,1)}, bf16[128,16,64]{2,1,0:T(8,128)(2,1)}, bf16[2,128,576]{2,1,0:T(8,128)(2,1)}, bf16[2,128,576]{2,1,0:T(8,128)(2,1)}) custom-call(s32[1]{0:T(128)} %bitcast.offset_ref, bf16[128,16,512]{2,1,0:T(8,128)(2,1)} %bitcast.21, bf16[128,16,64]{2,1,0:T(8,128)(2,1)} %get-tuple-element.13.qr_ref, ...), custom_call_target="tpu_custom_call" | custom-call | tf_op jit(solution)/shard_map/pallas_call | solution.py:150
  28.5 0.0 copy-start
  28.6 0.4 collective-permute-start
  29.0 1.5 %collective-permute-done = bf16[2,128,576]{2,1,0:T(8,128)(2,1)S(1)} collective-permute-done((bf16[2,128,576]{2,1,0:T(8,128)(2,1)}, bf16[2,128,576]{2,1,0:T(8,128)(2,1)S(1)}, u32[]{:S(2)}, u32[]{:S(2)}) %collective-permute-start) | collective-permute-done | bytes 294944 | tf_op jit(solution)/shard_map/ppermute | solution.py:22
  30.5 1.1 %add_convert_fusion = bf16[2,128,576]{2,1,0:T(8,128)(2,1)S(1)} fusion(bf16[2,128,576]{2,1,0:T(8,128)(2,1)S(1)} %collective-permute-done, bf16[2,128,576]{2,1,0:T(8,128)(2,1)} %get-tuple-element.18), kind=kLoop, calls=%fused_computation | loop fusion | flops 589824 | bytes 884736 | tf_op jit(solution)/shard_map/convert_element_type | solution.py:23
  31.6 1.3 %collective-permute-start.1 = (bf16[128,576]{1,0:T(8,128)(2,1)S(1)}, bf16[128,576]{1,0:T(8,128)(2,1)S(1)}, u32[]{:S(2)}, u32[]{:S(2)}) collective-permute-start(bf16[128,576]{1,0:T(8,128)(2,1)S(1)} %select_bitcast_fusion), channel_id=1, source_target_pairs={{16,0},{24,8},{17,1},{25,9},{18,2},{26,10},{19,3},{27,11},{20,4},{... | collective-permute-start | bytes 442376 | tf_op jit(solution)/shard_map/ppermute | solution.py:27
  32.9 7.0 %collective-permute-done.1 = bf16[128,576]{1,0:T(8,128)(2,1)S(1)} collective-permute-done((bf16[128,576]{1,0:T(8,128)(2,1)S(1)}, bf16[128,576]{1,0:T(8,128)(2,1)S(1)}, u32[]{:S(2)}, u32[]{:S(2)}) %collective-permute-start.1) | collective-permute-done | bytes 147488 | tf_op jit(solution)/shard_map/ppermute | solution.py:27
  39.9 0.1 add_convert_fusion.4
  40.0 1.6 %collective-permute-start.2 = (bf16[128,576]{1,0:T(8,128)(2,1)S(1)}, bf16[128,576]{1,0:T(8,128)(2,1)S(1)}, u32[]{:S(2)}, u32[]{:S(2)}) collective-permute-start(bf16[128,576]{1,0:T(8,128)(2,1)S(1)} %add_convert_fusion.4), channel_id=1, source_target_pairs={{0,1},{1,0},{2,3},{3,2},{4,5},{5,4},{6,7},{7,6},{8,10},{9,11},{10,... | collective-permute-start | bytes 442376 | tf_op jit(solution)/shard_map/ppermute | solution.py:44
  41.5 3.8 %collective-permute-done.2 = bf16[128,576]{1,0:T(8,128)(2,1)S(1)} collective-permute-done((bf16[128,576]{1,0:T(8,128)(2,1)S(1)}, bf16[128,576]{1,0:T(8,128)(2,1)S(1)}, u32[]{:S(2)}, u32[]{:S(2)}) %collective-permute-start.2) | collective-permute-done | bytes 147488 | tf_op jit(solution)/shard_map/ppermute | solution.py:44
  45.4 1.6 %collective-permute-start.3 = (bf16[128,576]{1,0:T(8,128)(2,1)S(1)}, bf16[128,576]{1,0:T(8,128)(2,1)S(1)}, u32[]{:S(2)}, u32[]{:S(2)}) collective-permute-start(bf16[128,576]{1,0:T(8,128)(2,1)S(1)} %add_convert_fusion.3), channel_id=1, source_target_pairs={{0,2},{1,3},{2,0},{3,1},{4,6},{5,7},{6,4},{7,5},{8,12},{9,13},{10,... | collective-permute-start | bytes 442376 | tf_op jit(solution)/shard_map/ppermute | solution.py:44
  47.0 4.4 %collective-permute-done.3 = bf16[128,576]{1,0:T(8,128)(2,1)S(1)} collective-permute-done((bf16[128,576]{1,0:T(8,128)(2,1)S(1)}, bf16[128,576]{1,0:T(8,128)(2,1)S(1)}, u32[]{:S(2)}, u32[]{:S(2)}) %collective-permute-start.3) | collective-permute-done | bytes 147488 | tf_op jit(solution)/shard_map/ppermute | solution.py:44
  51.5 2.8 %collective-permute-start.4 = (bf16[128,576]{1,0:T(8,128)(2,1)S(1)}, bf16[128,576]{1,0:T(8,128)(2,1)S(1)}, u32[]{:S(2)}, u32[]{:S(2)}) collective-permute-start(bf16[128,576]{1,0:T(8,128)(2,1)S(1)} %add_convert_fusion.2), channel_id=1, source_target_pairs={{0,4},{1,5},{2,6},{3,7},{4,0},{5,1},{6,2},{7,3},{8,9},{9,8},{10,11... | collective-permute-start | bytes 442376 | tf_op jit(solution)/shard_map/ppermute | solution.py:44
  54.2 0.0 copy-done
  54.2 1.1 %copy.10 = bf16[1,16,64,128]{3,2,1,0:T(8,128)(2,1)} copy(bf16[1,16,64,128]{2,1,3,0:T(8,128)(2,1)S(1)} %bitcast.23) | data formatting | bytes 524288
  55.4 2.4 %collective-permute-done.4 = bf16[128,576]{1,0:T(8,128)(2,1)S(1)} collective-permute-done((bf16[128,576]{1,0:T(8,128)(2,1)S(1)}, bf16[128,576]{1,0:T(8,128)(2,1)S(1)}, u32[]{:S(2)}, u32[]{:S(2)}) %collective-permute-start.4) | collective-permute-done | bytes 147488 | tf_op jit(solution)/shard_map/ppermute | solution.py:44
  57.8 0.7 %slice_bitcast_fusion = bf16[1,128,512]{2,1,0:T(8,128)(2,1)} fusion(bf16[128,576]{1,0:T(8,128)(2,1)S(1)} %add_convert_fusion.1), kind=kLoop, calls=%fused_computation.6 | loop fusion | bytes 262144 | tf_op jit(solution)/shard_map/broadcast_in_dim | solution.py:176
  58.5 0.7 %copy.11 = bf16[1,64,128]{2,1,0:T(8,128)(2,1)} copy(bf16[1,64,128]{1,2,0:T(8,128)(2,1)S(1)} %slice_bitcast_fusion.1) | data formatting | bytes 32768
  (5 shorter events, 0.2 us)
Async XLA Ops:
  28.5 25.7 %copy-start = (bf16[128,16,64]{2,1,0:T(8,128)(2,1)S(1)}, bf16[128,16,64]{2,1,0:T(8,128)(2,1)}, u32[]{:S(2)}) copy-start(bf16[128,16,64]{2,1,0:T(8,128)(2,1)} %get-tuple-element.17) | copy-start | bytes 786436
  28.6 1.9 %collective-permute-start = (bf16[2,128,576]{2,1,0:T(8,128)(2,1)}, bf16[2,128,576]{2,1,0:T(8,128)(2,1)S(1)}, u32[]{:S(2)}, u32[]{:S(2)}) collective-permute-start(bf16[2,128,576]{2,1,0:T(8,128)(2,1)} %get-tuple-element.19), channel_id=1, source_target_pairs={{0,8},{8,0},{16,24},{24,16},{1,9},{9,1},{17,25},{25,17},{2,10},{10... | collective-permute-start | bytes 884744 | tf_op jit(solution)/shard_map/ppermute | solution.py:22
  31.6 8.4 %collective-permute-start.1 = (bf16[128,576]{1,0:T(8,128)(2,1)S(1)}, bf16[128,576]{1,0:T(8,128)(2,1)S(1)}, u32[]{:S(2)}, u32[]{:S(2)}) collective-permute-start(bf16[128,576]{1,0:T(8,128)(2,1)S(1)} %select_bitcast_fusion), channel_id=1, source_target_pairs={{16,0},{24,8},{17,1},{25,9},{18,2},{26,10},{19,3},{27,11},{20,4},{... | collective-permute-start | bytes 442376 | tf_op jit(solution)/shard_map/ppermute | solution.py:27
  40.0 5.4 %collective-permute-start.2 = (bf16[128,576]{1,0:T(8,128)(2,1)S(1)}, bf16[128,576]{1,0:T(8,128)(2,1)S(1)}, u32[]{:S(2)}, u32[]{:S(2)}) collective-permute-start(bf16[128,576]{1,0:T(8,128)(2,1)S(1)} %add_convert_fusion.4), channel_id=1, source_target_pairs={{0,1},{1,0},{2,3},{3,2},{4,5},{5,4},{6,7},{7,6},{8,10},{9,11},{10,... | collective-permute-start | bytes 442376 | tf_op jit(solution)/shard_map/ppermute | solution.py:44
  45.4 6.0 %collective-permute-start.3 = (bf16[128,576]{1,0:T(8,128)(2,1)S(1)}, bf16[128,576]{1,0:T(8,128)(2,1)S(1)}, u32[]{:S(2)}, u32[]{:S(2)}) collective-permute-start(bf16[128,576]{1,0:T(8,128)(2,1)S(1)} %add_convert_fusion.3), channel_id=1, source_target_pairs={{0,2},{1,3},{2,0},{3,1},{4,6},{5,7},{6,4},{7,5},{8,12},{9,13},{10,... | collective-permute-start | bytes 442376 | tf_op jit(solution)/shard_map/ppermute | solution.py:44
  51.5 6.3 %collective-permute-start.4 = (bf16[128,576]{1,0:T(8,128)(2,1)S(1)}, bf16[128,576]{1,0:T(8,128)(2,1)S(1)}, u32[]{:S(2)}, u32[]{:S(2)}) collective-permute-start(bf16[128,576]{1,0:T(8,128)(2,1)S(1)} %add_convert_fusion.2), channel_id=1, source_target_pairs={{0,4},{1,5},{2,6},{3,7},{4,0},{5,1},{6,2},{7,3},{8,9},{9,8},{10,11... | collective-permute-start | bytes 442376 | tf_op jit(solution)/shard_map/ppermute | solution.py:44

commit v15 on v13

--- a/solution.py
+++ b/solution.py
@@ -33,7 +33,7 @@
     if n_ep & (n_ep - 1):
         return lax.psum(total.astype(jnp.bfloat16), "ep").astype(jnp.float32)
     bits = [1 << k for k in range(n_ep.bit_length() - 1)]
-    orders = [bits, bits[1:] + bits[:1]]
+    orders = [bits, bits[-1:] + bits[:-1]]
     for step in range(len(bits)):
         pairs = [
             (c * n_ep + e, c * n_ep + (e ^ orders[c % 2][step]))

time: 59.1 us -> 58.9 us (level)
  no operation moved by 1% of the time
where the time goes in v15:
time: 58.9 us; the launch traced here: 58.6 us
  waiting for transfers between devices  19.3 us (33%)
  Pallas kernels  13.6 us (23%)
  blocking collectives  9.78 us (17%)
  starting transfers between devices  7.58 us (13%)
  local copies, waits for them, and re-layouts  5.48 us (9%)
  other arithmetic  2.19 us (4%)
  between operations  0.71 us (1%)
    pallas_call x1, Pallas kernels, body(): pl.pallas_call(attention_kernel, grid_spec=pltpu.PrefetchScalarGridSpec(n...  13.6 us
    ppermute x3, waiting for transfers between devices, butterfly_sum_ep(): theirs = lax.ppermute(mine, ('ctx', 'ep'), pairs)  10.8 us
    all_gather x1, blocking collectives, body(): whole_keys = lax.all_gather(local_keys, 'ctx', axis=0, tiled=True)  9.78 us
    ppermute x1, waiting for transfers between devices, causal_reduce_ctx(): lax.ppermute(sent, 'ctx', [(i, i - 2 * shift) for i in range(2 * shift, n...  7.04 us
    ppermute x3, starting transfers between devices, butterfly_sum_ep(): theirs = lax.ppermute(mine, ('ctx', 'ep'), pairs)  5.88 us
    unnamed x6, local copies, waits for them, and re-layouts  4.81 us
    ppermute x1, waiting for transfers between devices, causal_reduce_ctx(): got = lax.ppermute(theirs, 'ctx', [(i, i ^ 1) for i in range(n_ctx)])  1.49 us
    ppermute x1, starting transfers between devices, causal_reduce_ctx(): lax.ppermute(sent, 'ctx', [(i, i - 2 * shift) for i in range(2 * shift, n...  1.29 us
  transfers between devices with their start and end apart: 5, of which 5 were waited for; matrix products, arithmetic and copies ran while one was open for 2% of the time, Pallas kernels for 0%

profile of v15, /device:TPU:0, one launch (start us, length us, event | category | flops | bytes accessed | tf_op | source)
XLA Modules:
  0.0 58.6 jit_solution(17482179887531839617)
XLA Ops:
  0.6 2.1 %copy.10 = bf16[1,16,64,128]{2,1,3,0:T(8,128)(2,1)} copy(bf16[1,16,64,128]{3,2,1,0:T(8,128)(2,1)} %param.8) | data formatting | bytes 524288 | tf_op args[1]
  2.8 0.8 %copy.11 = bf16[1,64,128]{1,2,0:T(8,128)(2,1)S(1)} copy(bf16[1,64,128]{2,1,0:T(8,128)(2,1)} %param.10) | data formatting | bytes 32768 | tf_op args[3]
  3.6 0.9 %pad_maximum_fusion = bf16[128,576]{1,0:T(8,128)(2,1)S(1)} fusion(bf16[128,64]{1,0:T(8,128)(2,1)S(1)} %bitcast.29, bf16[128,512]{1,0:T(8,128)(2,1)} %bitcast.30), kind=kLoop, calls=%fused_computation.5 | loop fusion | flops 294912 | bytes 294912 | tf_op jit(solution)/shard_map/concatenate | solution.py:122
  4.5 9.8 %all_gather.3.keys_ref = bf16[512,576]{1,0:T(8,128)(2,1)} all-gather(bf16[128,576]{1,0:T(8,128)(2,1)S(1)} %pad_maximum_fusion), channel_id=1, replica_groups=mesh['ctx'=4,'ep'=8] {'ctx'}, dimensions={0}, use_global_device_ids=true | all-gather | bytes 737280 | tf_op jit(solution)/shard_map/all_gather | solution.py:123
  14.3 13.6 %shard_map.92 = (bf16[128,16,512]{2,1,0:T(8,128)(2,1)}, bf16[128,16,512]{2,1,0:T(8,128)(2,1)}, bf16[128,16,64]{2,1,0:T(8,128)(2,1)}, bf16[2,128,576]{2,1,0:T(8,128)(2,1)}, bf16[2,128,576]{2,1,0:T(8,128)(2,1)}) custom-call(s32[1]{0:T(128)} %bitcast.offset_ref, bf16[128,16,512]{2,1,0:T(8,128)(2,1)} %bitcast.25, bf16[128,16,64]{2,1,0:T(8,128)(2,1)} %bitcast.27, ...), custom_call_target="tpu_custom_call" | custom-call | tf_op jit(solution)/shard_map/pallas_call | solution.py:137
  27.9 0.0 copy-start
  27.9 0.4 collective-permute-start
  28.3 1.5 %collective-permute-done = bf16[2,128,576]{2,1,0:T(8,128)(2,1)S(1)} collective-permute-done((bf16[2,128,576]{2,1,0:T(8,128)(2,1)}, bf16[2,128,576]{2,1,0:T(8,128)(2,1)S(1)}, u32[]{:S(2)}, u32[]{:S(2)}) %collective-permute-start) | collective-permute-done | bytes 294944 | tf_op jit(solution)/shard_map/ppermute | solution.py:22
  29.8 1.1 %add_convert_fusion = bf16[2,128,576]{2,1,0:T(8,128)(2,1)S(1)} fusion(bf16[2,128,576]{2,1,0:T(8,128)(2,1)S(1)} %collective-permute-done, bf16[2,128,576]{2,1,0:T(8,128)(2,1)} %get-tuple-element.14), kind=kLoop, calls=%fused_computation | loop fusion | flops 589824 | bytes 884736 | tf_op jit(solution)/shard_map/convert_element_type | solution.py:23
  30.9 1.3 %collective-permute-start.1 = (bf16[128,576]{1,0:T(8,128)(2,1)S(1)}, bf16[128,576]{1,0:T(8,128)(2,1)S(1)}, u32[]{:S(2)}, u32[]{:S(2)}) collective-permute-start(bf16[128,576]{1,0:T(8,128)(2,1)S(1)} %select_bitcast_fusion), channel_id=1, source_target_pairs={{16,0},{24,8},{17,1},{25,9},{18,2},{26,10},{19,3},{27,11},{20,4},{... | collective-permute-start | bytes 442376 | tf_op jit(solution)/shard_map/ppermute | solution.py:27
  32.2 7.0 %collective-permute-done.1 = bf16[128,576]{1,0:T(8,128)(2,1)S(1)} collective-permute-done((bf16[128,576]{1,0:T(8,128)(2,1)S(1)}, bf16[128,576]{1,0:T(8,128)(2,1)S(1)}, u32[]{:S(2)}, u32[]{:S(2)}) %collective-permute-start.1) | collective-permute-done | bytes 147488 | tf_op jit(solution)/shard_map/ppermute | solution.py:27
  39.2 0.1 add_convert_fusion.4
  39.3 1.6 %collective-permute-start.2 = (bf16[128,576]{1,0:T(8,128)(2,1)S(1)}, bf16[128,576]{1,0:T(8,128)(2,1)S(1)}, u32[]{:S(2)}, u32[]{:S(2)}) collective-permute-start(bf16[128,576]{1,0:T(8,128)(2,1)S(1)} %add_convert_fusion.4), channel_id=1, source_target_pairs={{0,1},{1,0},{2,3},{3,2},{4,5},{5,4},{6,7},{7,6},{8,12},{9,13},{10,... | collective-permute-start | bytes 442376 | tf_op jit(solution)/shard_map/ppermute | solution.py:44
  40.9 3.8 %collective-permute-done.2 = bf16[128,576]{1,0:T(8,128)(2,1)S(1)} collective-permute-done((bf16[128,576]{1,0:T(8,128)(2,1)S(1)}, bf16[128,576]{1,0:T(8,128)(2,1)S(1)}, u32[]{:S(2)}, u32[]{:S(2)}) %collective-permute-start.2) | collective-permute-done | bytes 147488 | tf_op jit(solution)/shard_map/ppermute | solution.py:44
  44.7 1.6 %collective-permute-start.3 = (bf16[128,576]{1,0:T(8,128)(2,1)S(1)}, bf16[128,576]{1,0:T(8,128)(2,1)S(1)}, u32[]{:S(2)}, u32[]{:S(2)}) collective-permute-start(bf16[128,576]{1,0:T(8,128)(2,1)S(1)} %add_convert_fusion.3), channel_id=1, source_target_pairs={{0,2},{1,3},{2,0},{3,1},{4,6},{5,7},{6,4},{7,5},{8,9},{9,8},{10,11... | collective-permute-start | bytes 442376 | tf_op jit(solution)/shard_map/ppermute | solution.py:44
  46.4 3.7 %collective-permute-done.3 = bf16[128,576]{1,0:T(8,128)(2,1)S(1)} collective-permute-done((bf16[128,576]{1,0:T(8,128)(2,1)S(1)}, bf16[128,576]{1,0:T(8,128)(2,1)S(1)}, u32[]{:S(2)}, u32[]{:S(2)}) %collective-permute-start.3) | collective-permute-done | bytes 147488 | tf_op jit(solution)/shard_map/ppermute | solution.py:44
  50.2 2.6 %collective-permute-start.4 = (bf16[128,576]{1,0:T(8,128)(2,1)S(1)}, bf16[128,576]{1,0:T(8,128)(2,1)S(1)}, u32[]{:S(2)}, u32[]{:S(2)}) collective-permute-start(bf16[128,576]{1,0:T(8,128)(2,1)S(1)} %add_convert_fusion.2), channel_id=1, source_target_pairs={{0,4},{1,5},{2,6},{3,7},{4,0},{5,1},{6,2},{7,3},{8,10},{9,11},{10,... | collective-permute-start | bytes 442376 | tf_op jit(solution)/shard_map/ppermute | solution.py:44
  52.8 0.0 copy-done
  52.8 1.1 %copy.12 = bf16[1,16,64,128]{3,2,1,0:T(8,128)(2,1)} copy(bf16[1,16,64,128]{2,1,3,0:T(8,128)(2,1)S(1)} %bitcast.28) | data formatting | bytes 524288
  54.0 3.2 %collective-permute-done.4 = bf16[128,576]{1,0:T(8,128)(2,1)S(1)} collective-permute-done((bf16[128,576]{1,0:T(8,128)(2,1)S(1)}, bf16[128,576]{1,0:T(8,128)(2,1)S(1)}, u32[]{:S(2)}, u32[]{:S(2)}) %collective-permute-start.4) | collective-permute-done | bytes 147488 | tf_op jit(solution)/shard_map/ppermute | solution.py:44
  57.2 0.7 %slice_bitcast_fusion = bf16[1,128,512]{2,1,0:T(8,128)(2,1)} fusion(bf16[128,576]{1,0:T(8,128)(2,1)S(1)} %add_convert_fusion.1), kind=kLoop, calls=%fused_computation.7 | loop fusion | bytes 262144 | tf_op jit(solution)/shard_map/broadcast_in_dim | solution.py:163
  57.9 0.7 %copy.13 = bf16[1,64,128]{2,1,0:T(8,128)(2,1)} copy(bf16[1,64,128]{1,2,0:T(8,128)(2,1)S(1)} %slice_bitcast_fusion.1) | data formatting | bytes 32768
  (5 shorter events, 0.2 us)
Async XLA Ops:
  27.9 24.9 %copy-start = (bf16[128,16,64]{2,1,0:T(8,128)(2,1)S(1)}, bf16[128,16,64]{2,1,0:T(8,128)(2,1)}, u32[]{:S(2)}) copy-start(bf16[128,16,64]{2,1,0:T(8,128)(2,1)} %get-tuple-element.13) | copy-start | bytes 786436
  27.9 1.9 %collective-permute-start = (bf16[2,128,576]{2,1,0:T(8,128)(2,1)}, bf16[2,128,576]{2,1,0:T(8,128)(2,1)S(1)}, u32[]{:S(2)}, u32[]{:S(2)}) collective-permute-start(bf16[2,128,576]{2,1,0:T(8,128)(2,1)} %get-tuple-element.15), channel_id=1, source_target_pairs={{0,8},{8,0},{16,24},{24,16},{1,9},{9,1},{17,25},{25,17},{2,10},{10... | collective-permute-start | bytes 884744 | tf_op jit(solution)/shard_map/ppermute | solution.py:22
  30.9 8.3 %collective-permute-start.1 = (bf16[128,576]{1,0:T(8,128)(2,1)S(1)}, bf16[128,576]{1,0:T(8,128)(2,1)S(1)}, u32[]{:S(2)}, u32[]{:S(2)}) collective-permute-start(bf16[128,576]{1,0:T(8,128)(2,1)S(1)} %select_bitcast_fusion), channel_id=1, source_target_pairs={{16,0},{24,8},{17,1},{25,9},{18,2},{26,10},{19,3},{27,11},{20,4},{... | collective-permute-start | bytes 442376 | tf_op jit(solution)/shard_map/ppermute | solution.py:27
  39.3 5.4 %collective-permute-start.2 = (bf16[128,576]{1,0:T(8,128)(2,1)S(1)}, bf16[128,576]{1,0:T(8,128)(2,1)S(1)}, u32[]{:S(2)}, u32[]{:S(2)}) collective-permute-start(bf16[128,576]{1,0:T(8,128)(2,1)S(1)} %add_convert_fusion.4), channel_id=1, source_target_pairs={{0,1},{1,0},{2,3},{3,2},{4,5},{5,4},{6,7},{7,6},{8,12},{9,13},{10,... | collective-permute-start | bytes 442376 | tf_op jit(solution)/shard_map/ppermute | solution.py:44
  44.7 5.4 %collective-permute-start.3 = (bf16[128,576]{1,0:T(8,128)(2,1)S(1)}, bf16[128,576]{1,0:T(8,128)(2,1)S(1)}, u32[]{:S(2)}, u32[]{:S(2)}) collective-permute-start(bf16[128,576]{1,0:T(8,128)(2,1)S(1)} %add_convert_fusion.3), channel_id=1, source_target_pairs={{0,2},{1,3},{2,0},{3,1},{4,6},{5,7},{6,4},{7,5},{8,9},{9,8},{10,11... | collective-permute-start | bytes 442376 | tf_op jit(solution)/shard_map/ppermute | solution.py:44
  50.2 7.0 %collective-permute-start.4 = (bf16[128,576]{1,0:T(8,128)(2,1)S(1)}, bf16[128,576]{1,0:T(8,128)(2,1)S(1)}, u32[]{:S(2)}, u32[]{:S(2)}) collective-permute-start(bf16[128,576]{1,0:T(8,128)(2,1)S(1)} %add_convert_fusion.2), channel_id=1, source_target_pairs={{0,4},{1,5},{2,6},{3,7},{4,0},{5,1},{6,2},{7,3},{8,10},{9,11},{10,... | collective-permute-start | bytes 442376 | tf_op jit(solution)/shard_map/ppermute | solution.py:44

commit v16 on v15

--- a/solution.py
+++ b/solution.py
@@ -20,10 +20,14 @@
     pairs = n_ctx // 2
     mine = blocks
     got = lax.ppermute(theirs, "ctx", [(i, i ^ 1) for i in range(n_ctx)])
-    summed = (mine.astype(jnp.float32) + got.astype(jnp.float32)).astype(jnp.bfloat16)
-    total = jnp.take(summed, here // 2, axis=0).astype(jnp.float32)
+
+    def pair_sum(slot):
+        both = jnp.take(mine, slot, axis=0).astype(jnp.float32) + jnp.take(got, slot, axis=0).astype(jnp.float32)
+        return both.astype(jnp.bfloat16)
+
+    total = pair_sum(here // 2).astype(jnp.float32)
     for shift in range(1, pairs):
-        sent = jnp.take(summed, jnp.maximum(here // 2 - shift, 0), axis=0)
+        sent = pair_sum(jnp.maximum(here // 2 - shift, 0))
         got = lax.ppermute(sent, "ctx", [(i, i - 2 * shift) for i in range(2 * shift, n_ctx)])
         total = total + got.astype(jnp.float32)
     return total
@@ -159,9 +163,9 @@
     latent_qgrad = lqg[None]
     rope_qgrad = jnp.transpose(rqg, (1, 2, 0))[None]
     total = causal_reduce_ctx(mine, theirs, n_ctx)
-    total = butterfly_sum_ep(total, n_ctx, n_ep).astype(jnp.bfloat16)
-    latent_kgrad = total[None, :, :kvr]
-    rope_kgrad = total[:, kvr:].T[None]
+    total = butterfly_sum_ep(total, n_ctx, n_ep)
+    latent_kgrad = total[None, :, :kvr].astype(jnp.bfloat16)
+    rope_kgrad = total[:, kvr:].T[None].astype(jnp.bfloat16)
     return (attended, latent_qgrad, rope_qgrad, latent_kgrad, rope_kgrad)
 
 

time: 58.9 us -> 59.7 us (1.014)
  other arithmetic: 2.19 us -> 3.03 us
    convert_element_type x3, other arithmetic: 0.14 us -> 1.08 us  [butterfly_sum_ep(): mine = total.astype(jnp.bfloat16)]
    broadcast_in_dim x2 -> x0, local copies, waits for them, and re-layouts: 0.67 us -> none  [the longest x1 0.66 us: body(): latent_kgrad = total[None, :, :kvr]]
    convert_element_type x0 -> x2, local copies, waits for them, and re-layouts: none -> 0.67 us  [the longest x1 0.66 us: body(): latent_kgrad = total[None, :, :kvr].astype(jnp.bfloat16)]
where the time goes in v16:
time: 59.7 us; the launch traced here: 59.4 us
  waiting for transfers between devices  19.3 us (32%)
  Pallas kernels  13.6 us (23%)
  blocking collectives  9.78 us (16%)
  starting transfers between devices  7.58 us (13%)
  local copies, waits for them, and re-layouts  5.48 us (9%)
  other arithmetic  3.03 us (5%)
  between operations  0.7 us (1%)
    pallas_call x1, Pallas kernels, body(): pl.pallas_call(attention_kernel, grid_spec=pltpu.PrefetchScalarGridSpec(n...  13.6 us
    ppermute x3, waiting for transfers between devices, butterfly_sum_ep(): theirs = lax.ppermute(mine, ('ctx', 'ep'), pairs)  10.8 us
    all_gather x1, blocking collectives, body(): whole_keys = lax.all_gather(local_keys, 'ctx', axis=0, tiled=True)  9.78 us
    ppermute x1, waiting for transfers between devices, causal_reduce_ctx(): lax.ppermute(sent, 'ctx', [(i, i - 2 * shift) for i in range(2 * shift, n...  7.04 us
    ppermute x3, starting transfers between devices, butterfly_sum_ep(): theirs = lax.ppermute(mine, ('ctx', 'ep'), pairs)  5.88 us
    unnamed x6, local copies, waits for them, and re-layouts  4.81 us
    ppermute x1, waiting for transfers between devices, causal_reduce_ctx(): got = lax.ppermute(theirs, 'ctx', [(i, i ^ 1) for i in range(n_ctx)])  1.49 us
    ppermute x1, starting transfers between devices, causal_reduce_ctx(): lax.ppermute(sent, 'ctx', [(i, i - 2 * shift) for i in range(2 * shift, n...  1.29 us
  transfers between devices with their start and end apart: 5, of which 5 were waited for; matrix products, arithmetic and copies ran while one was open for 2% of the time, Pallas kernels for 0%

profile of v16, /device:TPU:0, one launch (start us, length us, event | category | flops | bytes accessed | tf_op | source)
XLA Modules:
  0.0 59.4 jit_solution(9328789486258456193)
XLA Ops:
  0.6 2.1 %copy.10 = bf16[1,16,64,128]{2,1,3,0:T(8,128)(2,1)} copy(bf16[1,16,64,128]{3,2,1,0:T(8,128)(2,1)} %param.8) | data formatting | bytes 524288 | tf_op args[1]
  2.8 0.8 %copy.11 = bf16[1,64,128]{1,2,0:T(8,128)(2,1)S(1)} copy(bf16[1,64,128]{2,1,0:T(8,128)(2,1)} %param.10) | data formatting | bytes 32768 | tf_op args[3]
  3.6 0.9 %pad_maximum_fusion = bf16[128,576]{1,0:T(8,128)(2,1)S(1)} fusion(bf16[128,64]{1,0:T(8,128)(2,1)S(1)} %bitcast.33, bf16[128,512]{1,0:T(8,128)(2,1)} %bitcast.34), kind=kLoop, calls=%fused_computation.6 | loop fusion | flops 294912 | bytes 294912 | tf_op jit(solution)/shard_map/concatenate | solution.py:126
  4.5 9.8 %all_gather.3.keys_ref = bf16[512,576]{1,0:T(8,128)(2,1)} all-gather(bf16[128,576]{1,0:T(8,128)(2,1)S(1)} %pad_maximum_fusion), channel_id=1, replica_groups=mesh['ctx'=4,'ep'=8] {'ctx'}, dimensions={0}, use_global_device_ids=true | all-gather | bytes 737280 | tf_op jit(solution)/shard_map/all_gather | solution.py:127
  14.3 13.6 %shard_map.92 = (bf16[128,16,512]{2,1,0:T(8,128)(2,1)}, bf16[128,16,512]{2,1,0:T(8,128)(2,1)}, bf16[128,16,64]{2,1,0:T(8,128)(2,1)}, bf16[2,128,576]{2,1,0:T(8,128)(2,1)}, bf16[2,128,576]{2,1,0:T(8,128)(2,1)}) custom-call(s32[1]{0:T(128)} %bitcast.offset_ref, bf16[128,16,512]{2,1,0:T(8,128)(2,1)} %bitcast.29, bf16[128,16,64]{2,1,0:T(8,128)(2,1)} %bitcast.31, ...), custom_call_target="tpu_custom_call" | custom-call | tf_op jit(solution)/shard_map/pallas_call | solution.py:141
  27.9 0.0 copy-start
  27.9 0.4 collective-permute-start
  28.3 1.5 %collective-permute-done = bf16[2,128,576]{2,1,0:T(8,128)(2,1)S(1)} collective-permute-done((bf16[2,128,576]{2,1,0:T(8,128)(2,1)}, bf16[2,128,576]{2,1,0:T(8,128)(2,1)S(1)}, u32[]{:S(2)}, u32[]{:S(2)}) %collective-permute-start) | collective-permute-done | bytes 294944 | tf_op jit(solution)/shard_map/ppermute | solution.py:22
  29.8 1.0 %add_convert_fusion.4 = bf16[128,576]{1,0:T(8,128)(2,1)S(1)} fusion(bf16[2,128,576]{2,1,0:T(8,128)(2,1)S(1)} %collective-permute-done, s32[]{:T(128)S(6)} %max.3, bf16[2,128,576]{2,1,0:T(8,128)(2,1)} %get-tuple-element.14, pred[]{:T(512)S(6)} %le.12), kind=kLoop, calls=%fused_computation.4 | loop fusion | flops 442368 | bytes 442373 | tf_op jit(solution)/shard_map/convert_element_type | solution.py:26
  30.8 1.3 %collective-permute-start.1 = (bf16[128,576]{1,0:T(8,128)(2,1)S(1)}, bf16[128,576]{1,0:T(8,128)(2,1)S(1)}, u32[]{:S(2)}, u32[]{:S(2)}) collective-permute-start(bf16[128,576]{1,0:T(8,128)(2,1)S(1)} %add_convert_fusion.4), channel_id=1, source_target_pairs={{16,0},{24,8},{17,1},{25,9},{18,2},{26,10},{19,3},{27,11},{20,4},{... | collective-permute-start | bytes 442376 | tf_op jit(solution)/shard_map/ppermute | solution.py:31
  32.1 7.0 %collective-permute-done.1 = bf16[128,576]{1,0:T(8,128)(2,1)S(1)} collective-permute-done((bf16[128,576]{1,0:T(8,128)(2,1)S(1)}, bf16[128,576]{1,0:T(8,128)(2,1)S(1)}, u32[]{:S(2)}, u32[]{:S(2)}) %collective-permute-start.1) | collective-permute-done | bytes 147488 | tf_op jit(solution)/shard_map/ppermute | solution.py:31
  39.1 1.0 %add_convert_fusion.3 = bf16[128,576]{1,0:T(8,128)(2,1)S(1)} fusion(bf16[128,576]{1,0:T(8,128)(2,1)S(1)} %collective-permute-done.1, bf16[2,128,576]{2,1,0:T(8,128)(2,1)S(1)} %collective-permute-done, s32[]{:T(128)S(6)} %select_n.23, bf16[2,128,576]{2,1,0:T(8,128)(2,1)} %get-tuple-element.14, pred[]{:T(512)S(6)} %and.18), kind=kLoop, calls=%fused_computation.3 | loop fusion | flops 737280 | bytes 589829 | tf_op jit(solution)/shard_map/convert_element_type | solution.py:47
  40.1 1.6 %collective-permute-start.2 = (bf16[128,576]{1,0:T(8,128)(2,1)S(1)}, bf16[128,576]{1,0:T(8,128)(2,1)S(1)}, u32[]{:S(2)}, u32[]{:S(2)}) collective-permute-start(bf16[128,576]{1,0:T(8,128)(2,1)S(1)} %add_convert_fusion.3), channel_id=1, source_target_pairs={{0,1},{1,0},{2,3},{3,2},{4,5},{5,4},{6,7},{7,6},{8,12},{9,13},{10,... | collective-permute-start | bytes 442376 | tf_op jit(solution)/shard_map/ppermute | solution.py:48
  41.7 3.8 %collective-permute-done.2 = bf16[128,576]{1,0:T(8,128)(2,1)S(1)} collective-permute-done((bf16[128,576]{1,0:T(8,128)(2,1)S(1)}, bf16[128,576]{1,0:T(8,128)(2,1)S(1)}, u32[]{:S(2)}, u32[]{:S(2)}) %collective-permute-start.2) | collective-permute-done | bytes 147488 | tf_op jit(solution)/shard_map/ppermute | solution.py:48
  45.6 1.6 %collective-permute-start.3 = (bf16[128,576]{1,0:T(8,128)(2,1)S(1)}, bf16[128,576]{1,0:T(8,128)(2,1)S(1)}, u32[]{:S(2)}, u32[]{:S(2)}) collective-permute-start(bf16[128,576]{1,0:T(8,128)(2,1)S(1)} %add_convert_fusion.2), channel_id=1, source_target_pairs={{0,2},{1,3},{2,0},{3,1},{4,6},{5,7},{6,4},{7,5},{8,9},{9,8},{10,11... | collective-permute-start | bytes 442376 | tf_op jit(solution)/shard_map/ppermute | solution.py:48
  47.2 3.7 %collective-permute-done.3 = bf16[128,576]{1,0:T(8,128)(2,1)S(1)} collective-permute-done((bf16[128,576]{1,0:T(8,128)(2,1)S(1)}, bf16[128,576]{1,0:T(8,128)(2,1)S(1)}, u32[]{:S(2)}, u32[]{:S(2)}) %collective-permute-start.3) | collective-permute-done | bytes 147488 | tf_op jit(solution)/shard_map/ppermute | solution.py:48
  51.0 2.6 %collective-permute-start.4 = (bf16[128,576]{1,0:T(8,128)(2,1)S(1)}, bf16[128,576]{1,0:T(8,128)(2,1)S(1)}, u32[]{:S(2)}, u32[]{:S(2)}) collective-permute-start(bf16[128,576]{1,0:T(8,128)(2,1)S(1)} %add_convert_fusion.1), channel_id=1, source_target_pairs={{0,4},{1,5},{2,6},{3,7},{4,0},{5,1},{6,2},{7,3},{8,10},{9,11},{10,... | collective-permute-start | bytes 442376 | tf_op jit(solution)/shard_map/ppermute | solution.py:48
  53.6 0.0 copy-done
  53.6 1.1 %copy.12 = bf16[1,16,64,128]{3,2,1,0:T(8,128)(2,1)} copy(bf16[1,16,64,128]{2,1,3,0:T(8,128)(2,1)S(1)} %bitcast.32) | data formatting | bytes 524288
  54.8 3.2 %collective-permute-done.4 = bf16[128,576]{1,0:T(8,128)(2,1)S(1)} collective-permute-done((bf16[128,576]{1,0:T(8,128)(2,1)S(1)}, bf16[128,576]{1,0:T(8,128)(2,1)S(1)}, u32[]{:S(2)}, u32[]{:S(2)}) %collective-permute-start.4) | collective-permute-done | bytes 147488 | tf_op jit(solution)/shard_map/ppermute | solution.py:48
  58.1 0.7 %slice_bitcast_fusion = bf16[1,128,512]{2,1,0:T(8,128)(2,1)} fusion(bf16[128,576]{1,0:T(8,128)(2,1)S(1)} %add_convert_fusion), kind=kLoop, calls=%fused_computation.7 | loop fusion | bytes 262144 | tf_op jit(solution)/shard_map/convert_element_type | solution.py:167
  58.7 0.7 %copy.13 = bf16[1,64,128]{2,1,0:T(8,128)(2,1)} copy(bf16[1,64,128]{1,2,0:T(8,128)(2,1)S(1)} %slice_bitcast_fusion.1) | data formatting | bytes 32768
  (4 shorter events, 0.1 us)
Async XLA Ops:
  27.9 25.8 %copy-start = (bf16[128,16,64]{2,1,0:T(8,128)(2,1)S(1)}, bf16[128,16,64]{2,1,0:T(8,128)(2,1)}, u32[]{:S(2)}) copy-start(bf16[128,16,64]{2,1,0:T(8,128)(2,1)} %get-tuple-element.13) | copy-start | bytes 786436
  27.9 1.9 %collective-permute-start = (bf16[2,128,576]{2,1,0:T(8,128)(2,1)}, bf16[2,128,576]{2,1,0:T(8,128)(2,1)S(1)}, u32[]{:S(2)}, u32[]{:S(2)}) collective-permute-start(bf16[2,128,576]{2,1,0:T(8,128)(2,1)} %get-tuple-element.15), channel_id=1, source_target_pairs={{0,8},{8,0},{16,24},{24,16},{1,9},{9,1},{17,25},{25,17},{2,10},{10... | collective-permute-start | bytes 884744 | tf_op jit(solution)/shard_map/ppermute | solution.py:22
  30.8 8.3 %collective-permute-start.1 = (bf16[128,576]{1,0:T(8,128)(2,1)S(1)}, bf16[128,576]{1,0:T(8,128)(2,1)S(1)}, u32[]{:S(2)}, u32[]{:S(2)}) collective-permute-start(bf16[128,576]{1,0:T(8,128)(2,1)S(1)} %add_convert_fusion.4), channel_id=1, source_target_pairs={{16,0},{24,8},{17,1},{25,9},{18,2},{26,10},{19,3},{27,11},{20,4},{... | collective-permute-start | bytes 442376 | tf_op jit(solution)/shard_map/ppermute | solution.py:31
  40.1 5.4 %collective-permute-start.2 = (bf16[128,576]{1,0:T(8,128)(2,1)S(1)}, bf16[128,576]{1,0:T(8,128)(2,1)S(1)}, u32[]{:S(2)}, u32[]{:S(2)}) collective-permute-start(bf16[128,576]{1,0:T(8,128)(2,1)S(1)} %add_convert_fusion.3), channel_id=1, source_target_pairs={{0,1},{1,0},{2,3},{3,2},{4,5},{5,4},{6,7},{7,6},{8,12},{9,13},{10,... | collective-permute-start | bytes 442376 | tf_op jit(solution)/shard_map/ppermute | solution.py:48
  45.6 5.4 %collective-permute-start.3 = (bf16[128,576]{1,0:T(8,128)(2,1)S(1)}, bf16[128,576]{1,0:T(8,128)(2,1)S(1)}, u32[]{:S(2)}, u32[]{:S(2)}) collective-permute-start(bf16[128,576]{1,0:T(8,128)(2,1)S(1)} %add_convert_fusion.2), channel_id=1, source_target_pairs={{0,2},{1,3},{2,0},{3,1},{4,6},{5,7},{6,4},{7,5},{8,9},{9,8},{10,11... | collective-permute-start | bytes 442376 | tf_op jit(solution)/shard_map/ppermute | solution.py:48
  51.0 7.0 %collective-permute-start.4 = (bf16[128,576]{1,0:T(8,128)(2,1)S(1)}, bf16[128,576]{1,0:T(8,128)(2,1)S(1)}, u32[]{:S(2)}, u32[]{:S(2)}) collective-permute-start(bf16[128,576]{1,0:T(8,128)(2,1)S(1)} %add_convert_fusion.1), channel_id=1, source_target_pairs={{0,4},{1,5},{2,6},{3,7},{4,0},{5,1},{6,2},{7,3},{8,10},{9,11},{10,... | collective-permute-start | bytes 442376 | tf_op jit(solution)/shard_map/ppermute | solution.py:48

commit v17 on v15

--- a/solution.py
+++ b/solution.py
@@ -51,38 +51,45 @@
     step = pl.program_id(0)
     t_blk, heads, kvr = ql_ref.shape
     rope = qr_ref.shape[2]
-    rows = t_blk * heads
     f32 = jnp.float32
     nt = (((1,), (1,)), ((), ()))
     tn = (((0,), (0,)), ((), ()))
-    q = ql_ref[...].reshape(rows, kvr)
-    qr = qr_ref[...].reshape(rows, rope)
     k = keys_ref[:, :kvr]
     kr = keys_ref[:, kvr:]
-    dout = do_ref[...].reshape(rows, kvr)
     length = k.shape[0]
-    scores = lax.dot_general(q, k, nt, preferred_element_type=f32)
-    scores = scores + lax.dot_general(qr, kr, nt, preferred_element_type=f32)
-    row = lax.broadcasted_iota(jnp.int32, (rows, 1), 0)
-    last_key = offset_ref[0] + step * t_blk + row // heads
-    col = lax.broadcasted_iota(jnp.int32, (1, length), 1)
-    scores = jnp.where(col <= last_key, scores * scale_factor, f32(-1e30))
-    row_max = jnp.max(scores, axis=-1, keepdims=True)
-    powers = jnp.exp(scores - row_max)
-    weights = powers * (1.0 / jnp.sum(powers, axis=-1, keepdims=True))
-    rounded = weights.astype(jnp.bfloat16)
-    att = jnp.dot(rounded, k, preferred_element_type=f32).astype(jnp.bfloat16)
-    att_ref[...] = att.reshape(t_blk, heads, kvr)
-    row_dots = jnp.sum(dout.astype(f32) * att.astype(f32), axis=-1, keepdims=True)
-    weight_grad = lax.dot_general(dout, k, nt, preferred_element_type=f32)
-    score_grad = (weights * (weight_grad - row_dots)).astype(jnp.bfloat16)
-    lqg = scale_factor * jnp.dot(score_grad, k, preferred_element_type=f32)
-    lqg_ref[...] = lqg.astype(jnp.bfloat16).reshape(t_blk, heads, kvr)
-    rqg = scale_factor * jnp.dot(score_grad, kr, preferred_element_type=f32)
-    rqg_ref[...] = rqg.astype(jnp.bfloat16).reshape(t_blk, heads, rope)
-    lt = scale_factor * lax.dot_general(score_grad, q, tn, preferred_element_type=f32)
-    lt = lt + lax.dot_general(rounded, dout, tn, preferred_element_type=f32)
-    rt = scale_factor * lax.dot_general(score_grad, qr, tn, preferred_element_type=f32)
+    n_sub = 2 if t_blk % 2 == 0 else 1
+    t_sub = t_blk // n_sub
+    rows = t_sub * heads
+    lt = None
+    for sub in range(n_sub):
+        part = pl.ds(sub * t_sub, t_sub)
+        q = ql_ref[part].reshape(rows, kvr)
+        qr = qr_ref[part].reshape(rows, rope)
+        dout = do_ref[part].reshape(rows, kvr)
+        scores = lax.dot_general(q, k, nt, preferred_element_type=f32)
+        scores = scores + lax.dot_general(qr, kr, nt, preferred_element_type=f32)
+        row = lax.broadcasted_iota(jnp.int32, (rows, 1), 0)
+        last_key = offset_ref[0] + step * t_blk + sub * t_sub + row // heads
+        col = lax.broadcasted_iota(jnp.int32, (1, length), 1)
+        scores = jnp.where(col <= last_key, scores * scale_factor, f32(-1e30))
+        row_max = jnp.max(scores, axis=-1, keepdims=True)
+        powers = jnp.exp(scores - row_max)
+        weights = powers * (1.0 / jnp.sum(powers, axis=-1, keepdims=True))
+        rounded = weights.astype(jnp.bfloat16)
+        att = jnp.dot(rounded, k, preferred_element_type=f32).astype(jnp.bfloat16)
+        att_ref[part] = att.reshape(t_sub, heads, kvr)
+        row_dots = jnp.sum(dout.astype(f32) * att.astype(f32), axis=-1, keepdims=True)
+        weight_grad = lax.dot_general(dout, k, nt, preferred_element_type=f32)
+        score_grad = (weights * (weight_grad - row_dots)).astype(jnp.bfloat16)
+        lqg = scale_factor * jnp.dot(score_grad, k, preferred_element_type=f32)
+        lqg_ref[part] = lqg.astype(jnp.bfloat16).reshape(t_sub, heads, kvr)
+        rqg = scale_factor * jnp.dot(score_grad, kr, preferred_element_type=f32)
+        rqg_ref[part] = rqg.astype(jnp.bfloat16).reshape(t_sub, heads, rope)
+        lt_part = scale_factor * lax.dot_general(score_grad, q, tn, preferred_element_type=f32)
+        lt_part = lt_part + lax.dot_general(rounded, dout, tn, preferred_element_type=f32)
+        rt_part = scale_factor * lax.dot_general(score_grad, qr, tn, preferred_element_type=f32)
+        lt = lt_part if lt is None else lt + lt_part
+        rt = rt_part if sub == 0 else rt + rt_part
 
     @pl.when(step == 0)
     def _():
@@ -93,6 +100,7 @@
     def _():
         lt_acc[...] += lt
         rt_acc[...] += rt
+
 
     @pl.when(step == pl.num_programs(0) - 1)
     def _():

time: 58.9 us -> 59.2 us (level)
  no operation moved by 1% of the time
where the time goes in v17:
time: 59.2 us; the launch traced here: 58.9 us
  waiting for transfers between devices  19.3 us (33%)
  Pallas kernels  13.9 us (23%)
  blocking collectives  9.78 us (17%)
  starting transfers between devices  7.58 us (13%)
  local copies, waits for them, and re-layouts  5.48 us (9%)
  other arithmetic  2.19 us (4%)
  between operations  0.71 us (1%)
    pallas_call x1, Pallas kernels, body(): pl.pallas_call(attention_kernel, grid_spec=pltpu.PrefetchScalarGridSpec(n...  13.9 us
    ppermute x3, waiting for transfers between devices, butterfly_sum_ep(): theirs = lax.ppermute(mine, ('ctx', 'ep'), pairs)  10.8 us
    all_gather x1, blocking collectives, body(): whole_keys = lax.all_gather(local_keys, 'ctx', axis=0, tiled=True)  9.78 us
    ppermute x1, waiting for transfers between devices, causal_reduce_ctx(): lax.ppermute(sent, 'ctx', [(i, i - 2 * shift) for i in range(2 * shift, n...  7.04 us
    ppermute x3, starting transfers between devices, butterfly_sum_ep(): theirs = lax.ppermute(mine, ('ctx', 'ep'), pairs)  5.87 us
    unnamed x6, local copies, waits for them, and re-layouts  4.81 us
    ppermute x1, waiting for transfers between devices, causal_reduce_ctx(): got = lax.ppermute(theirs, 'ctx', [(i, i ^ 1) for i in range(n_ctx)])  1.49 us
    ppermute x1, starting transfers between devices, causal_reduce_ctx(): lax.ppermute(sent, 'ctx', [(i, i - 2 * shift) for i in range(2 * shift, n...  1.29 us
  transfers between devices with their start and end apart: 5, of which 5 were waited for; matrix products, arithmetic and copies ran while one was open for 2% of the time, Pallas kernels for 0%

profile of v17, /device:TPU:0, one launch (start us, length us, event | category | flops | bytes accessed | tf_op | source)
XLA Modules:
  0.0 58.9 jit_solution(4094786070786137807)
XLA Ops:
  0.6 2.1 %copy.10 = bf16[1,16,64,128]{2,1,3,0:T(8,128)(2,1)} copy(bf16[1,16,64,128]{3,2,1,0:T(8,128)(2,1)} %param.8) | data formatting | bytes 524288 | tf_op args[1]
  2.8 0.8 %copy.11 = bf16[1,64,128]{1,2,0:T(8,128)(2,1)S(1)} copy(bf16[1,64,128]{2,1,0:T(8,128)(2,1)} %param.10) | data formatting | bytes 32768 | tf_op args[3]
  3.6 0.9 %pad_maximum_fusion = bf16[128,576]{1,0:T(8,128)(2,1)S(1)} fusion(bf16[128,64]{1,0:T(8,128)(2,1)S(1)} %bitcast.29, bf16[128,512]{1,0:T(8,128)(2,1)} %bitcast.30), kind=kLoop, calls=%fused_computation.5 | loop fusion | flops 294912 | bytes 294912 | tf_op jit(solution)/shard_map/concatenate | solution.py:130
  4.5 9.8 %all_gather.3.keys_ref = bf16[512,576]{1,0:T(8,128)(2,1)} all-gather(bf16[128,576]{1,0:T(8,128)(2,1)S(1)} %pad_maximum_fusion), channel_id=1, replica_groups=mesh['ctx'=4,'ep'=8] {'ctx'}, dimensions={0}, use_global_device_ids=true | all-gather | bytes 737280 | tf_op jit(solution)/shard_map/all_gather | solution.py:131
  14.3 13.9 %shard_map.92 = (bf16[128,16,512]{2,1,0:T(8,128)(2,1)}, bf16[128,16,512]{2,1,0:T(8,128)(2,1)}, bf16[128,16,64]{2,1,0:T(8,128)(2,1)}, bf16[2,128,576]{2,1,0:T(8,128)(2,1)}, bf16[2,128,576]{2,1,0:T(8,128)(2,1)}) custom-call(s32[1]{0:T(128)} %bitcast.offset_ref, bf16[128,16,512]{2,1,0:T(8,128)(2,1)} %bitcast.25, bf16[128,16,64]{2,1,0:T(8,128)(2,1)} %bitcast.27, ...), custom_call_target="tpu_custom_call" | custom-call | tf_op jit(solution)/shard_map/pallas_call | solution.py:145
  28.2 0.0 copy-start
  28.2 0.4 collective-permute-start
  28.7 1.5 %collective-permute-done = bf16[2,128,576]{2,1,0:T(8,128)(2,1)S(1)} collective-permute-done((bf16[2,128,576]{2,1,0:T(8,128)(2,1)}, bf16[2,128,576]{2,1,0:T(8,128)(2,1)S(1)}, u32[]{:S(2)}, u32[]{:S(2)}) %collective-permute-start) | collective-permute-done | bytes 294944 | tf_op jit(solution)/shard_map/ppermute | solution.py:22
  30.1 1.1 %add_convert_fusion = bf16[2,128,576]{2,1,0:T(8,128)(2,1)S(1)} fusion(bf16[2,128,576]{2,1,0:T(8,128)(2,1)S(1)} %collective-permute-done, bf16[2,128,576]{2,1,0:T(8,128)(2,1)} %get-tuple-element.14), kind=kLoop, calls=%fused_computation | loop fusion | flops 589824 | bytes 884736 | tf_op jit(solution)/shard_map/convert_element_type | solution.py:23
  31.2 1.3 %collective-permute-start.1 = (bf16[128,576]{1,0:T(8,128)(2,1)S(1)}, bf16[128,576]{1,0:T(8,128)(2,1)S(1)}, u32[]{:S(2)}, u32[]{:S(2)}) collective-permute-start(bf16[128,576]{1,0:T(8,128)(2,1)S(1)} %select_bitcast_fusion), channel_id=1, source_target_pairs={{16,0},{24,8},{17,1},{25,9},{18,2},{26,10},{19,3},{27,11},{20,4},{... | collective-permute-start | bytes 442376 | tf_op jit(solution)/shard_map/ppermute | solution.py:27
  32.5 7.0 %collective-permute-done.1 = bf16[128,576]{1,0:T(8,128)(2,1)S(1)} collective-permute-done((bf16[128,576]{1,0:T(8,128)(2,1)S(1)}, bf16[128,576]{1,0:T(8,128)(2,1)S(1)}, u32[]{:S(2)}, u32[]{:S(2)}) %collective-permute-start.1) | collective-permute-done | bytes 147488 | tf_op jit(solution)/shard_map/ppermute | solution.py:27
  39.6 0.1 add_convert_fusion.4
  39.6 1.6 %collective-permute-start.2 = (bf16[128,576]{1,0:T(8,128)(2,1)S(1)}, bf16[128,576]{1,0:T(8,128)(2,1)S(1)}, u32[]{:S(2)}, u32[]{:S(2)}) collective-permute-start(bf16[128,576]{1,0:T(8,128)(2,1)S(1)} %add_convert_fusion.4), channel_id=1, source_target_pairs={{0,1},{1,0},{2,3},{3,2},{4,5},{5,4},{6,7},{7,6},{8,12},{9,13},{10,... | collective-permute-start | bytes 442376 | tf_op jit(solution)/shard_map/ppermute | solution.py:44
  41.2 3.8 %collective-permute-done.2 = bf16[128,576]{1,0:T(8,128)(2,1)S(1)} collective-permute-done((bf16[128,576]{1,0:T(8,128)(2,1)S(1)}, bf16[128,576]{1,0:T(8,128)(2,1)S(1)}, u32[]{:S(2)}, u32[]{:S(2)}) %collective-permute-start.2) | collective-permute-done | bytes 147488 | tf_op jit(solution)/shard_map/ppermute | solution.py:44
  45.1 1.6 %collective-permute-start.3 = (bf16[128,576]{1,0:T(8,128)(2,1)S(1)}, bf16[128,576]{1,0:T(8,128)(2,1)S(1)}, u32[]{:S(2)}, u32[]{:S(2)}) collective-permute-start(bf16[128,576]{1,0:T(8,128)(2,1)S(1)} %add_convert_fusion.3), channel_id=1, source_target_pairs={{0,2},{1,3},{2,0},{3,1},{4,6},{5,7},{6,4},{7,5},{8,9},{9,8},{10,11... | collective-permute-start | bytes 442376 | tf_op jit(solution)/shard_map/ppermute | solution.py:44
  46.7 3.7 %collective-permute-done.3 = bf16[128,576]{1,0:T(8,128)(2,1)S(1)} collective-permute-done((bf16[128,576]{1,0:T(8,128)(2,1)S(1)}, bf16[128,576]{1,0:T(8,128)(2,1)S(1)}, u32[]{:S(2)}, u32[]{:S(2)}) %collective-permute-start.3) | collective-permute-done | bytes 147488 | tf_op jit(solution)/shard_map/ppermute | solution.py:44
  50.5 2.6 %collective-permute-start.4 = (bf16[128,576]{1,0:T(8,128)(2,1)S(1)}, bf16[128,576]{1,0:T(8,128)(2,1)S(1)}, u32[]{:S(2)}, u32[]{:S(2)}) collective-permute-start(bf16[128,576]{1,0:T(8,128)(2,1)S(1)} %add_convert_fusion.2), channel_id=1, source_target_pairs={{0,4},{1,5},{2,6},{3,7},{4,0},{5,1},{6,2},{7,3},{8,10},{9,11},{10,... | collective-permute-start | bytes 442376 | tf_op jit(solution)/shard_map/ppermute | solution.py:44
  53.1 0.0 copy-done
  53.2 1.1 %copy.12 = bf16[1,16,64,128]{3,2,1,0:T(8,128)(2,1)} copy(bf16[1,16,64,128]{2,1,3,0:T(8,128)(2,1)S(1)} %bitcast.28) | data formatting | bytes 524288
  54.3 3.2 %collective-permute-done.4 = bf16[128,576]{1,0:T(8,128)(2,1)S(1)} collective-permute-done((bf16[128,576]{1,0:T(8,128)(2,1)S(1)}, bf16[128,576]{1,0:T(8,128)(2,1)S(1)}, u32[]{:S(2)}, u32[]{:S(2)}) %collective-permute-start.4) | collective-permute-done | bytes 147488 | tf_op jit(solution)/shard_map/ppermute | solution.py:44
  57.6 0.7 %slice_bitcast_fusion = bf16[1,128,512]{2,1,0:T(8,128)(2,1)} fusion(bf16[128,576]{1,0:T(8,128)(2,1)S(1)} %add_convert_fusion.1), kind=kLoop, calls=%fused_computation.7 | loop fusion | bytes 262144 | tf_op jit(solution)/shard_map/broadcast_in_dim | solution.py:171
  58.2 0.7 %copy.13 = bf16[1,64,128]{2,1,0:T(8,128)(2,1)} copy(bf16[1,64,128]{1,2,0:T(8,128)(2,1)S(1)} %slice_bitcast_fusion.1) | data formatting | bytes 32768
  (5 shorter events, 0.2 us)
Async XLA Ops:
  28.2 24.9 %copy-start = (bf16[128,16,64]{2,1,0:T(8,128)(2,1)S(1)}, bf16[128,16,64]{2,1,0:T(8,128)(2,1)}, u32[]{:S(2)}) copy-start(bf16[128,16,64]{2,1,0:T(8,128)(2,1)} %get-tuple-element.13) | copy-start | bytes 786436
  28.2 1.9 %collective-permute-start = (bf16[2,128,576]{2,1,0:T(8,128)(2,1)}, bf16[2,128,576]{2,1,0:T(8,128)(2,1)S(1)}, u32[]{:S(2)}, u32[]{:S(2)}) collective-permute-start(bf16[2,128,576]{2,1,0:T(8,128)(2,1)} %get-tuple-element.15), channel_id=1, source_target_pairs={{0,8},{8,0},{16,24},{24,16},{1,9},{9,1},{17,25},{25,17},{2,10},{10... | collective-permute-start | bytes 884744 | tf_op jit(solution)/shard_map/ppermute | solution.py:22
  31.2 8.3 %collective-permute-start.1 = (bf16[128,576]{1,0:T(8,128)(2,1)S(1)}, bf16[128,576]{1,0:T(8,128)(2,1)S(1)}, u32[]{:S(2)}, u32[]{:S(2)}) collective-permute-start(bf16[128,576]{1,0:T(8,128)(2,1)S(1)} %select_bitcast_fusion), channel_id=1, source_target_pairs={{16,0},{24,8},{17,1},{25,9},{18,2},{26,10},{19,3},{27,11},{20,4},{... | collective-permute-start | bytes 442376 | tf_op jit(solution)/shard_map/ppermute | solution.py:27
  39.6 5.4 %collective-permute-start.2 = (bf16[128,576]{1,0:T(8,128)(2,1)S(1)}, bf16[128,576]{1,0:T(8,128)(2,1)S(1)}, u32[]{:S(2)}, u32[]{:S(2)}) collective-permute-start(bf16[128,576]{1,0:T(8,128)(2,1)S(1)} %add_convert_fusion.4), channel_id=1, source_target_pairs={{0,1},{1,0},{2,3},{3,2},{4,5},{5,4},{6,7},{7,6},{8,12},{9,13},{10,... | collective-permute-start | bytes 442376 | tf_op jit(solution)/shard_map/ppermute | solution.py:44
  45.1 5.4 %collective-permute-start.3 = (bf16[128,576]{1,0:T(8,128)(2,1)S(1)}, bf16[128,576]{1,0:T(8,128)(2,1)S(1)}, u32[]{:S(2)}, u32[]{:S(2)}) collective-permute-start(bf16[128,576]{1,0:T(8,128)(2,1)S(1)} %add_convert_fusion.3), channel_id=1, source_target_pairs={{0,2},{1,3},{2,0},{3,1},{4,6},{5,7},{6,4},{7,5},{8,9},{9,8},{10,11... | collective-permute-start | bytes 442376 | tf_op jit(solution)/shard_map/ppermute | solution.py:44
  50.5 7.0 %collective-permute-start.4 = (bf16[128,576]{1,0:T(8,128)(2,1)S(1)}, bf16[128,576]{1,0:T(8,128)(2,1)S(1)}, u32[]{:S(2)}, u32[]{:S(2)}) collective-permute-start(bf16[128,576]{1,0:T(8,128)(2,1)S(1)} %add_convert_fusion.2), channel_id=1, source_target_pairs={{0,4},{1,5},{2,6},{3,7},{4,0},{5,1},{6,2},{7,3},{8,10},{9,11},{10,... | collective-permute-start | bytes 442376 | tf_op jit(solution)/shard_map/ppermute | solution.py:44

commit v18 on v15

--- a/solution.py
+++ b/solution.py
@@ -27,6 +27,31 @@
         got = lax.ppermute(sent, "ctx", [(i, i - 2 * shift) for i in range(2 * shift, n_ctx)])
         total = total + got.astype(jnp.float32)
     return total
+
+
+def causal_gather_ctx(local, n_ctx):
+    if n_ctx % 2:
+        return lax.all_gather(local, "ctx", axis=0, tiled=True)
+    here = lax.axis_index("ctx")
+    partner = here + 1 - 2 * (here % 2)
+    pairs = n_ctx // 2
+    cross = [
+        lax.ppermute(local, "ctx", [(i, i + 2 * s) for i in range(n_ctx - 2 * s)])
+        for s in range(1, pairs)
+    ]
+    on_chip = lax.ppermute(local, "ctx", [(2 * p, 2 * p + 1) for p in range(pairs)])
+    if cross:
+        swapped = lax.ppermute(jnp.stack(cross), "ctx", [(i, i ^ 1) for i in range(n_ctx)])
+    zero = jnp.zeros_like(local)
+    slots = []
+    for m in range(n_ctx):
+        piece = jnp.where(m == here, local, zero)
+        piece = jnp.where((here % 2 == 1) & (m == here - 1), on_chip, piece)
+        for s in range(1, pairs):
+            piece = jnp.where(m == here - 2 * s, cross[s - 1], piece)
+            piece = jnp.where(m == partner - 2 * s, swapped[s - 1], piece)
+        slots.append(piece)
+    return jnp.concatenate(slots, axis=0)
 
 
 def butterfly_sum_ep(total, n_ctx, n_ep):
@@ -120,7 +145,7 @@
     _, block_len, heads, kvr = query_latent.shape
     rope = query_rope.shape[2]
     local_keys = jnp.concatenate([key_latent[0], key_rope[0].T], axis=1)
-    whole_keys = lax.all_gather(local_keys, "ctx", axis=0, tiled=True)
+    whole_keys = causal_gather_ctx(local_keys, n_ctx)
     length = whole_keys.shape[0]
     offset = (lax.axis_index("ctx") * block_len).astype(jnp.int32).reshape(1)
     qr = jnp.transpose(query_rope[0], (2, 0, 1))

time: 58.9 us -> 59 us (level)
  blocking collectives: 9.78 us -> 0 us
  starting transfers between devices: 7.58 us -> 14.1 us
  waiting for transfers between devices: 19.3 us -> 21.4 us
  other arithmetic: 2.19 us -> 3.46 us
    all_gather x1 -> x0, blocking collectives: 9.78 us -> none  [body(): whole_keys = lax.all_gather(local_keys, 'ctx', axis=0, tiled=True)]
    ppermute x0 -> x3, starting transfers between devices: none -> 6.32 us  [the longest x1 4.85 us: causal_gather_ctx(): lax.ppermute(local, 'ctx', [(i, i + 2 * s) for i in range(n_ctx - 2 * s)])]
    ppermute x0 -> x3, waiting for transfers between devices: none -> 1.96 us  [the longest x1 1.95 us: causal_gather_ctx(): lax.ppermute(local, 'ctx', [(i, i + 2 * s) for i in range(n_ctx - 2 * s)])]
    concatenate x0 -> x1, other arithmetic: none -> 0.9 us  [causal_gather_ctx(): return jnp.concatenate(slots, axis=0)]
    unnamed x6 -> x8, local copies, waits for them, and re-layouts: 4.81 us -> 4.84 us
  transfers between devices with their start and end apart: 5 -> 8, of which waited for: 5 -> 6; matrix products, arithmetic and copies ran while one was open for 2% -> 6% of each run, Pallas kernels for 0% -> 0%
where the time goes in v18:
time: 59 us; the launch traced here: 58.7 us
  waiting for transfers between devices  21.4 us (36%)
  starting transfers between devices  14.1 us (24%)
  Pallas kernels  13.5 us (23%)
  local copies, waits for them, and re-layouts  5.51 us (9%)
  other arithmetic  3.46 us (6%)
  between operations  0.75 us (1%)
    pallas_call x1, Pallas kernels, body(): pl.pallas_call(attention_kernel, grid_spec=pltpu.PrefetchScalarGridSpec(n...  13.5 us
    ppermute x3, waiting for transfers between devices, butterfly_sum_ep(): theirs = lax.ppermute(mine, ('ctx', 'ep'), pairs)  10.8 us
    ppermute x1, waiting for transfers between devices, causal_reduce_ctx(): lax.ppermute(sent, 'ctx', [(i, i - 2 * shift) for i in range(2 * shift, n...  7.18 us
    ppermute x3, starting transfers between devices, butterfly_sum_ep(): theirs = lax.ppermute(mine, ('ctx', 'ep'), pairs)  5.89 us
    ppermute x1, starting transfers between devices, causal_gather_ctx(): lax.ppermute(local, 'ctx', [(i, i + 2 * s) for i in range(n_ctx - 2 * s)])  4.85 us
    unnamed x8, local copies, waits for them, and re-layouts  4.84 us
    ppermute x1, waiting for transfers between devices, causal_gather_ctx(): lax.ppermute(local, 'ctx', [(i, i + 2 * s) for i in range(n_ctx - 2 * s)])  1.95 us
    ppermute x1, starting transfers between devices, causal_gather_ctx(): lax.ppermute(local, 'ctx', [(2 * p, 2 * p + 1) for p in range(pairs)])  1.47 us
  transfers between devices with their start and end apart: 8, of which 6 were waited for; matrix products, arithmetic and copies ran while one was open for 6% of the time, Pallas kernels for 0%

profile of v18, /device:TPU:0, one launch (start us, length us, event | category | flops | bytes accessed | tf_op | source)
XLA Modules:
  0.0 58.7 jit_solution(12832693944971398777)
XLA Ops:
  0.6 0.0 copy-start
  0.6 0.9 %copy.11 = bf16[1,64,128]{1,2,0:T(8,128)(2,1)S(1)} copy(bf16[1,64,128]{2,1,0:T(8,128)(2,1)} %param.10) | data formatting | bytes 32768 | tf_op args[3]
  1.5 0.9 %pad_maximum_fusion.1 = bf16[128,576]{1,0:T(8,128)(2,1)S(1)} fusion(bf16[128,64]{1,0:T(8,128)(2,1)S(1)} %bitcast.38, bf16[128,512]{1,0:T(8,128)(2,1)} %bitcast.34), kind=kLoop, calls=%fused_computation.6 | loop fusion | flops 294912 | bytes 294912 | tf_op jit(solution)/shard_map/concatenate | solution.py:147
  2.4 4.9 %collective-permute-start = (bf16[128,576]{1,0:T(8,128)(2,1)S(1)}, bf16[128,576]{1,0:T(8,128)(2,1)S(1)}, u32[]{:S(2)}, u32[]{:S(2)}) collective-permute-start(bf16[128,576]{1,0:T(8,128)(2,1)S(1)} %pad_maximum_fusion.1), channel_id=1, source_target_pairs={{0,16},{8,24},{1,17},{9,25},{2,18},{10,26},{3,19},{11,27},{4,20},{... | collective-permute-start | bytes 442376 | tf_op jit(solution)/shard_map/ppermute | solution.py:39
  7.3 1.5 %collective-permute-start.2 = (bf16[128,576]{1,0:T(8,128)(2,1)S(1)}, bf16[128,576]{1,0:T(8,128)(2,1)S(1)}, u32[]{:S(2)}, u32[]{:S(2)}) collective-permute-start(bf16[128,576]{1,0:T(8,128)(2,1)S(1)} %pad_maximum_fusion.1), channel_id=1, source_target_pairs={{0,8},{16,24},{1,9},{17,25},{2,10},{18,26},{3,11},{19,27},{4,12},{... | collective-permute-start | bytes 442376 | tf_op jit(solution)/shard_map/ppermute | solution.py:42
  8.8 2.0 %collective-permute-done = bf16[128,576]{1,0:T(8,128)(2,1)S(1)} collective-permute-done((bf16[128,576]{1,0:T(8,128)(2,1)S(1)}, bf16[128,576]{1,0:T(8,128)(2,1)S(1)}, u32[]{:S(2)}, u32[]{:S(2)}) %collective-permute-start) | collective-permute-done | bytes 147488 | tf_op jit(solution)/shard_map/ppermute | solution.py:39
  10.7 0.0 collective-permute-start.1
  10.7 2.1 %copy.10 = bf16[1,16,64,128]{2,1,3,0:T(8,128)(2,1)} copy(bf16[1,16,64,128]{3,2,1,0:T(8,128)(2,1)} %param.8) | data formatting | bytes 524288 | tf_op args[1]
  12.9 0.0 collective-permute-done.2
  12.9 0.0 collective-permute-done.1
  12.9 0.0 copy-done
  12.9 0.2 bitcast_select_fusion.1
  13.0 0.2 bitcast_select_fusion.3
  13.2 0.9 %pad_maximum_fusion.keys_ref = bf16[512,576]{1,0:T(8,128)(2,1)} fusion(bf16[128,576]{1,0:T(8,128)(2,1)S(1)} %get-tuple-element.35, bf16[128,576]{1,0:T(8,128)(2,1)S(1)} %get-tuple-element.34, bf16[128,576]{1,0:T(8,128)(2,1)S(1)} %get-tuple-element.33, bf16[128,576]{1,0:T(8,128)(2,1)S(1)} %get-tuple-element.32), kind=kLoop, calls=%fused_computation | loop fusion | flops 2359296 | bytes 1179648 | tf_op jit(solution)/shard_map/concatenate | solution.py:54
  14.1 13.5 %shard_map.92 = (bf16[128,16,512]{2,1,0:T(8,128)(2,1)}, bf16[128,16,512]{2,1,0:T(8,128)(2,1)}, bf16[128,16,64]{2,1,0:T(8,128)(2,1)}, bf16[2,128,576]{2,1,0:T(8,128)(2,1)}, bf16[2,128,576]{2,1,0:T(8,128)(2,1)}) custom-call(s32[1]{0:T(128)} %bitcast.offset_ref, bf16[128,16,512]{2,1,0:T(8,128)(2,1)} %bitcast.31, bf16[128,16,64]{2,1,0:T(8,128)(2,1)} %bitcast.33, ...), custom_call_target="tpu_custom_call" | custom-call | tf_op jit(solution)/shard_map/pallas_call | solution.py:162
  27.6 0.6 collective-permute-start.3
  28.2 1.5 %collective-permute-done.3 = bf16[2,128,576]{2,1,0:T(8,128)(2,1)S(1)} collective-permute-done((bf16[2,128,576]{2,1,0:T(8,128)(2,1)}, bf16[2,128,576]{2,1,0:T(8,128)(2,1)S(1)}, u32[]{:S(2)}, u32[]{:S(2)}) %collective-permute-start.3) | collective-permute-done | bytes 294944 | tf_op jit(solution)/shard_map/ppermute | solution.py:22
  29.7 0.0 copy-start.1
  29.7 1.1 %add_convert_fusion = bf16[2,128,576]{2,1,0:T(8,128)(2,1)S(1)} fusion(bf16[2,128,576]{2,1,0:T(8,128)(2,1)S(1)} %collective-permute-done.3, bf16[2,128,576]{2,1,0:T(8,128)(2,1)} %get-tuple-element.14), kind=kLoop, calls=%fused_computation.1 | loop fusion | flops 589824 | bytes 884736 | tf_op jit(solution)/shard_map/convert_element_type | solution.py:23
  30.8 1.3 %collective-permute-start.4 = (bf16[128,576]{1,0:T(8,128)(2,1)S(1)}, bf16[128,576]{1,0:T(8,128)(2,1)S(1)}, u32[]{:S(2)}, u32[]{:S(2)}) collective-permute-start(bf16[128,576]{1,0:T(8,128)(2,1)S(1)} %select_bitcast_fusion), channel_id=1, source_target_pairs={{16,0},{24,8},{17,1},{25,9},{18,2},{26,10},{19,3},{27,11},{20,4},{... | collective-permute-start | bytes 442376 | tf_op jit(solution)/shard_map/ppermute | solution.py:27
  32.1 7.2 %collective-permute-done.4 = bf16[128,576]{1,0:T(8,128)(2,1)S(1)} collective-permute-done((bf16[128,576]{1,0:T(8,128)(2,1)S(1)}, bf16[128,576]{1,0:T(8,128)(2,1)S(1)}, u32[]{:S(2)}, u32[]{:S(2)}) %collective-permute-start.4) | collective-permute-done | bytes 147488 | tf_op jit(solution)/shard_map/ppermute | solution.py:27
  39.3 0.1 add_convert_fusion.4
  39.4 1.6 %collective-permute-start.5 = (bf16[128,576]{1,0:T(8,128)(2,1)S(1)}, bf16[128,576]{1,0:T(8,128)(2,1)S(1)}, u32[]{:S(2)}, u32[]{:S(2)}) collective-permute-start(bf16[128,576]{1,0:T(8,128)(2,1)S(1)} %add_convert_fusion.4), channel_id=1, source_target_pairs={{0,1},{1,0},{2,3},{3,2},{4,5},{5,4},{6,7},{7,6},{8,12},{9,13},{10,... | collective-permute-start | bytes 442376 | tf_op jit(solution)/shard_map/ppermute | solution.py:69
  41.0 3.8 %collective-permute-done.5 = bf16[128,576]{1,0:T(8,128)(2,1)S(1)} collective-permute-done((bf16[128,576]{1,0:T(8,128)(2,1)S(1)}, bf16[128,576]{1,0:T(8,128)(2,1)S(1)}, u32[]{:S(2)}, u32[]{:S(2)}) %collective-permute-start.5) | collective-permute-done | bytes 147488 | tf_op jit(solution)/shard_map/ppermute | solution.py:69
  44.8 1.6 %collective-permute-start.6 = (bf16[128,576]{1,0:T(8,128)(2,1)S(1)}, bf16[128,576]{1,0:T(8,128)(2,1)S(1)}, u32[]{:S(2)}, u32[]{:S(2)}) collective-permute-start(bf16[128,576]{1,0:T(8,128)(2,1)S(1)} %add_convert_fusion.3), channel_id=1, source_target_pairs={{0,2},{1,3},{2,0},{3,1},{4,6},{5,7},{6,4},{7,5},{8,9},{9,8},{10,11... | collective-permute-start | bytes 442376 | tf_op jit(solution)/shard_map/ppermute | solution.py:69
  46.5 3.7 %collective-permute-done.6 = bf16[128,576]{1,0:T(8,128)(2,1)S(1)} collective-permute-done((bf16[128,576]{1,0:T(8,128)(2,1)S(1)}, bf16[128,576]{1,0:T(8,128)(2,1)S(1)}, u32[]{:S(2)}, u32[]{:S(2)}) %collective-permute-start.6) | collective-permute-done | bytes 147488 | tf_op jit(solution)/shard_map/ppermute | solution.py:69
  50.2 2.7 %collective-permute-start.7 = (bf16[128,576]{1,0:T(8,128)(2,1)S(1)}, bf16[128,576]{1,0:T(8,128)(2,1)S(1)}, u32[]{:S(2)}, u32[]{:S(2)}) collective-permute-start(bf16[128,576]{1,0:T(8,128)(2,1)S(1)} %add_convert_fusion.2), channel_id=1, source_target_pairs={{0,4},{1,5},{2,6},{3,7},{4,0},{5,1},{6,2},{7,3},{8,10},{9,11},{10,... | collective-permute-start | bytes 442376 | tf_op jit(solution)/shard_map/ppermute | solution.py:69
  52.9 0.0 copy-done.1
  52.9 1.1 %copy.12 = bf16[1,16,64,128]{3,2,1,0:T(8,128)(2,1)} copy(bf16[1,16,64,128]{2,1,3,0:T(8,128)(2,1)S(1)} %bitcast.41) | data formatting | bytes 524288
  54.0 3.2 %collective-permute-done.7 = bf16[128,576]{1,0:T(8,128)(2,1)S(1)} collective-permute-done((bf16[128,576]{1,0:T(8,128)(2,1)S(1)}, bf16[128,576]{1,0:T(8,128)(2,1)S(1)}, u32[]{:S(2)}, u32[]{:S(2)}) %collective-permute-start.7) | collective-permute-done | bytes 147488 | tf_op jit(solution)/shard_map/ppermute | solution.py:69
  57.3 0.7 %slice_bitcast_fusion = bf16[1,128,512]{2,1,0:T(8,128)(2,1)} fusion(bf16[128,576]{1,0:T(8,128)(2,1)S(1)} %add_convert_fusion.1), kind=kLoop, calls=%fused_computation.12 | loop fusion | bytes 262144 | tf_op jit(solution)/shard_map/broadcast_in_dim | solution.py:188
  58.0 0.7 %copy.13 = bf16[1,64,128]{2,1,0:T(8,128)(2,1)} copy(bf16[1,64,128]{1,2,0:T(8,128)(2,1)S(1)} %slice_bitcast_fusion.1) | data formatting | bytes 32768
  (5 shorter events, 0.2 us)
Async XLA Ops:
  0.6 12.2 %copy-start = (bf16[1,128,512]{2,1,0:T(8,128)(2,1)S(1)}, bf16[1,128,512]{2,1,0:T(8,128)(2,1)}, u32[]{:S(2)}) copy-start(bf16[1,128,512]{2,1,0:T(8,128)(2,1)} %param.9) | copy-start | bytes 393220
  2.4 8.3 %collective-permute-start = (bf16[128,576]{1,0:T(8,128)(2,1)S(1)}, bf16[128,576]{1,0:T(8,128)(2,1)S(1)}, u32[]{:S(2)}, u32[]{:S(2)}) collective-permute-start(bf16[128,576]{1,0:T(8,128)(2,1)S(1)} %pad_maximum_fusion.1), channel_id=1, source_target_pairs={{0,16},{8,24},{1,17},{9,25},{2,18},{10,26},{3,19},{11,27},{4,20},{... | collective-permute-start | bytes 442376 | tf_op jit(solution)/shard_map/ppermute | solution.py:39
  7.3 5.6 %collective-permute-start.2 = (bf16[128,576]{1,0:T(8,128)(2,1)S(1)}, bf16[128,576]{1,0:T(8,128)(2,1)S(1)}, u32[]{:S(2)}, u32[]{:S(2)}) collective-permute-start(bf16[128,576]{1,0:T(8,128)(2,1)S(1)} %pad_maximum_fusion.1), channel_id=1, source_target_pairs={{0,8},{16,24},{1,9},{17,25},{2,10},{18,26},{3,11},{19,27},{4,12},{... | collective-permute-start | bytes 442376 | tf_op jit(solution)/shard_map/ppermute | solution.py:42
  10.7 2.1 %collective-permute-start.1 = (bf16[1,128,576]{2,1,0:T(8,128)(2,1)S(1)}, bf16[1,128,576]{2,1,0:T(8,128)(2,1)S(1)}, u32[]{:S(2)}, u32[]{:S(2)}) collective-permute-start(bf16[1,128,576]{2,1,0:T(8,128)(2,1)S(1)} %bitcast.37), channel_id=1, source_target_pairs={{0,8},{8,0},{16,24},{24,16},{1,9},{9,1},{17,25},{25,17},{2,10},{10... | collective-permute-start | bytes 442376 | tf_op jit(solution)/shard_map/ppermute | solution.py:44
  27.6 2.0 %collective-permute-start.3 = (bf16[2,128,576]{2,1,0:T(8,128)(2,1)}, bf16[2,128,576]{2,1,0:T(8,128)(2,1)S(1)}, u32[]{:S(2)}, u32[]{:S(2)}) collective-permute-start(bf16[2,128,576]{2,1,0:T(8,128)(2,1)} %get-tuple-element.15), channel_id=1, source_target_pairs={{0,8},{8,0},{16,24},{24,16},{1,9},{9,1},{17,25},{25,17},{2,10},{10... | collective-permute-start | bytes 884744 | tf_op jit(solution)/shard_map/ppermute | solution.py:22
  29.7 23.2 %copy-start.1 = (bf16[128,16,64]{2,1,0:T(8,128)(2,1)S(1)}, bf16[128,16,64]{2,1,0:T(8,128)(2,1)}, u32[]{:S(2)}) copy-start(bf16[128,16,64]{2,1,0:T(8,128)(2,1)} %get-tuple-element.13) | copy-start | bytes 786436
  30.8 8.5 %collective-permute-start.4 = (bf16[128,576]{1,0:T(8,128)(2,1)S(1)}, bf16[128,576]{1,0:T(8,128)(2,1)S(1)}, u32[]{:S(2)}, u32[]{:S(2)}) collective-permute-start(bf16[128,576]{1,0:T(8,128)(2,1)S(1)} %select_bitcast_fusion), channel_id=1, source_target_pairs={{16,0},{24,8},{17,1},{25,9},{18,2},{26,10},{19,3},{27,11},{20,4},{... | collective-permute-start | bytes 442376 | tf_op jit(solution)/shard_map/ppermute | solution.py:27
  39.4 5.4 %collective-permute-start.5 = (bf16[128,576]{1,0:T(8,128)(2,1)S(1)}, bf16[128,576]{1,0:T(8,128)(2,1)S(1)}, u32[]{:S(2)}, u32[]{:S(2)}) collective-permute-start(bf16[128,576]{1,0:T(8,128)(2,1)S(1)} %add_convert_fusion.4), channel_id=1, source_target_pairs={{0,1},{1,0},{2,3},{3,2},{4,5},{5,4},{6,7},{7,6},{8,12},{9,13},{10,... | collective-permute-start | bytes 442376 | tf_op jit(solution)/shard_map/ppermute | solution.py:69
  44.8 5.4 %collective-permute-start.6 = (bf16[128,576]{1,0:T(8,128)(2,1)S(1)}, bf16[128,576]{1,0:T(8,128)(2,1)S(1)}, u32[]{:S(2)}, u32[]{:S(2)}) collective-permute-start(bf16[128,576]{1,0:T(8,128)(2,1)S(1)} %add_convert_fusion.3), channel_id=1, source_target_pairs={{0,2},{1,3},{2,0},{3,1},{4,6},{5,7},{6,4},{7,5},{8,9},{9,8},{10,11... | collective-permute-start | bytes 442376 | tf_op jit(solution)/shard_map/ppermute | solution.py:69
  50.2 7.0 %collective-permute-start.7 = (bf16[128,576]{1,0:T(8,128)(2,1)S(1)}, bf16[128,576]{1,0:T(8,128)(2,1)S(1)}, u32[]{:S(2)}, u32[]{:S(2)}) collective-permute-start(bf16[128,576]{1,0:T(8,128)(2,1)S(1)} %add_convert_fusion.2), channel_id=1, source_target_pairs={{0,4},{1,5},{2,6},{3,7},{4,0},{5,1},{6,2},{7,3},{8,10},{9,11},{10,... | collective-permute-start | bytes 442376 | tf_op jit(solution)/shard_map/ppermute | solution.py:69

commit v19 on v15

--- a/solution.py
+++ b/solution.py
@@ -124,7 +124,7 @@
     length = whole_keys.shape[0]
     offset = (lax.axis_index("ctx") * block_len).astype(jnp.int32).reshape(1)
     qr = jnp.transpose(query_rope[0], (2, 0, 1))
-    t_blk = max(1, min(block_len, 1024 // heads))
+    t_blk = max(1, min(block_len, 2048 // heads))
     while block_len % t_blk:
         t_blk -= 1
     by_rows = pl.BlockSpec((t_blk, heads, kvr), lambda i, off: (i, 0, 0))

time: 58.9 us -> 58.6 us (level)
  no operation moved by 1% of the time
where the time goes in v19:
time: 58.6 us; the launch traced here: 58.3 us
  waiting for transfers between devices  19.3 us (33%)
  Pallas kernels  13.3 us (23%)
  blocking collectives  9.78 us (17%)
  starting transfers between devices  7.53 us (13%)
  local copies, waits for them, and re-layouts  5.48 us (9%)
  other arithmetic  2.19 us (4%)
  between operations  0.7 us (1%)
    pallas_call x1, Pallas kernels, body(): pl.pallas_call(attention_kernel, grid_spec=pltpu.PrefetchScalarGridSpec(n...  13.3 us
    ppermute x3, waiting for transfers between devices, butterfly_sum_ep(): theirs = lax.ppermute(mine, ('ctx', 'ep'), pairs)  10.8 us
    all_gather x1, blocking collectives, body(): whole_keys = lax.all_gather(local_keys, 'ctx', axis=0, tiled=True)  9.78 us
    ppermute x1, waiting for transfers between devices, causal_reduce_ctx(): lax.ppermute(sent, 'ctx', [(i, i - 2 * shift) for i in range(2 * shift, n...  7.04 us
    ppermute x3, starting transfers between devices, butterfly_sum_ep(): theirs = lax.ppermute(mine, ('ctx', 'ep'), pairs)  5.88 us
    unnamed x6, local copies, waits for them, and re-layouts  4.81 us
    ppermute x1, waiting for transfers between devices, causal_reduce_ctx(): got = lax.ppermute(theirs, 'ctx', [(i, i ^ 1) for i in range(n_ctx)])  1.49 us
    ppermute x1, starting transfers between devices, causal_reduce_ctx(): lax.ppermute(sent, 'ctx', [(i, i - 2 * shift) for i in range(2 * shift, n...  1.29 us
  transfers between devices with their start and end apart: 5, of which 5 were waited for; matrix products, arithmetic and copies ran while one was open for 2% of the time, Pallas kernels for 0%

profile of v19, /device:TPU:0, one launch (start us, length us, event | category | flops | bytes accessed | tf_op | source)
XLA Modules:
  0.0 58.3 jit_solution(16385214528387560809)
XLA Ops:
  0.6 2.1 %copy.10 = bf16[1,16,64,128]{2,1,3,0:T(8,128)(2,1)} copy(bf16[1,16,64,128]{3,2,1,0:T(8,128)(2,1)} %param.8) | data formatting | bytes 524288 | tf_op args[1]
  2.8 0.8 %copy.11 = bf16[1,64,128]{1,2,0:T(8,128)(2,1)S(1)} copy(bf16[1,64,128]{2,1,0:T(8,128)(2,1)} %param.10) | data formatting | bytes 32768 | tf_op args[3]
  3.6 0.9 %pad_maximum_fusion = bf16[128,576]{1,0:T(8,128)(2,1)S(1)} fusion(bf16[128,64]{1,0:T(8,128)(2,1)S(1)} %bitcast.29, bf16[128,512]{1,0:T(8,128)(2,1)} %bitcast.30), kind=kLoop, calls=%fused_computation.5 | loop fusion | flops 294912 | bytes 294912 | tf_op jit(solution)/shard_map/concatenate | solution.py:122
  4.5 9.8 %all_gather.3.keys_ref = bf16[512,576]{1,0:T(8,128)(2,1)} all-gather(bf16[128,576]{1,0:T(8,128)(2,1)S(1)} %pad_maximum_fusion), channel_id=1, replica_groups=mesh['ctx'=4,'ep'=8] {'ctx'}, dimensions={0}, use_global_device_ids=true | all-gather | bytes 737280 | tf_op jit(solution)/shard_map/all_gather | solution.py:123
  14.3 13.3 %shard_map.92 = (bf16[128,16,512]{2,1,0:T(8,128)(2,1)}, bf16[128,16,512]{2,1,0:T(8,128)(2,1)}, bf16[128,16,64]{2,1,0:T(8,128)(2,1)}, bf16[2,128,576]{2,1,0:T(8,128)(2,1)}, bf16[2,128,576]{2,1,0:T(8,128)(2,1)}) custom-call(s32[1]{0:T(128)} %bitcast.offset_ref, bf16[128,16,512]{2,1,0:T(8,128)(2,1)} %bitcast.25, bf16[128,16,64]{2,1,0:T(8,128)(2,1)} %bitcast.27, ...), custom_call_target="tpu_custom_call" | custom-call | tf_op jit(solution)/shard_map/pallas_call | solution.py:137
  27.6 0.0 copy-start
  27.7 0.4 collective-permute-start
  28.0 1.5 %collective-permute-done = bf16[2,128,576]{2,1,0:T(8,128)(2,1)S(1)} collective-permute-done((bf16[2,128,576]{2,1,0:T(8,128)(2,1)}, bf16[2,128,576]{2,1,0:T(8,128)(2,1)S(1)}, u32[]{:S(2)}, u32[]{:S(2)}) %collective-permute-start) | collective-permute-done | bytes 294944 | tf_op jit(solution)/shard_map/ppermute | solution.py:22
  29.5 1.1 %add_convert_fusion = bf16[2,128,576]{2,1,0:T(8,128)(2,1)S(1)} fusion(bf16[2,128,576]{2,1,0:T(8,128)(2,1)S(1)} %collective-permute-done, bf16[2,128,576]{2,1,0:T(8,128)(2,1)} %get-tuple-element.14), kind=kLoop, calls=%fused_computation | loop fusion | flops 589824 | bytes 884736 | tf_op jit(solution)/shard_map/convert_element_type | solution.py:23
  30.6 1.3 %collective-permute-start.1 = (bf16[128,576]{1,0:T(8,128)(2,1)S(1)}, bf16[128,576]{1,0:T(8,128)(2,1)S(1)}, u32[]{:S(2)}, u32[]{:S(2)}) collective-permute-start(bf16[128,576]{1,0:T(8,128)(2,1)S(1)} %select_bitcast_fusion), channel_id=1, source_target_pairs={{16,0},{24,8},{17,1},{25,9},{18,2},{26,10},{19,3},{27,11},{20,4},{... | collective-permute-start | bytes 442376 | tf_op jit(solution)/shard_map/ppermute | solution.py:27
  31.9 7.0 %collective-permute-done.1 = bf16[128,576]{1,0:T(8,128)(2,1)S(1)} collective-permute-done((bf16[128,576]{1,0:T(8,128)(2,1)S(1)}, bf16[128,576]{1,0:T(8,128)(2,1)S(1)}, u32[]{:S(2)}, u32[]{:S(2)}) %collective-permute-start.1) | collective-permute-done | bytes 147488 | tf_op jit(solution)/shard_map/ppermute | solution.py:27
  38.9 0.1 add_convert_fusion.4
  39.0 1.6 %collective-permute-start.2 = (bf16[128,576]{1,0:T(8,128)(2,1)S(1)}, bf16[128,576]{1,0:T(8,128)(2,1)S(1)}, u32[]{:S(2)}, u32[]{:S(2)}) collective-permute-start(bf16[128,576]{1,0:T(8,128)(2,1)S(1)} %add_convert_fusion.4), channel_id=1, source_target_pairs={{0,1},{1,0},{2,3},{3,2},{4,5},{5,4},{6,7},{7,6},{8,12},{9,13},{10,... | collective-permute-start | bytes 442376 | tf_op jit(solution)/shard_map/ppermute | solution.py:44
  40.6 3.8 %collective-permute-done.2 = bf16[128,576]{1,0:T(8,128)(2,1)S(1)} collective-permute-done((bf16[128,576]{1,0:T(8,128)(2,1)S(1)}, bf16[128,576]{1,0:T(8,128)(2,1)S(1)}, u32[]{:S(2)}, u32[]{:S(2)}) %collective-permute-start.2) | collective-permute-done | bytes 147488 | tf_op jit(solution)/shard_map/ppermute | solution.py:44
  44.4 1.6 %collective-permute-start.3 = (bf16[128,576]{1,0:T(8,128)(2,1)S(1)}, bf16[128,576]{1,0:T(8,128)(2,1)S(1)}, u32[]{:S(2)}, u32[]{:S(2)}) collective-permute-start(bf16[128,576]{1,0:T(8,128)(2,1)S(1)} %add_convert_fusion.3), channel_id=1, source_target_pairs={{0,2},{1,3},{2,0},{3,1},{4,6},{5,7},{6,4},{7,5},{8,9},{9,8},{10,11... | collective-permute-start | bytes 442376 | tf_op jit(solution)/shard_map/ppermute | solution.py:44
  46.1 3.7 %collective-permute-done.3 = bf16[128,576]{1,0:T(8,128)(2,1)S(1)} collective-permute-done((bf16[128,576]{1,0:T(8,128)(2,1)S(1)}, bf16[128,576]{1,0:T(8,128)(2,1)S(1)}, u32[]{:S(2)}, u32[]{:S(2)}) %collective-permute-start.3) | collective-permute-done | bytes 147488 | tf_op jit(solution)/shard_map/ppermute | solution.py:44
  49.9 2.7 %collective-permute-start.4 = (bf16[128,576]{1,0:T(8,128)(2,1)S(1)}, bf16[128,576]{1,0:T(8,128)(2,1)S(1)}, u32[]{:S(2)}, u32[]{:S(2)}) collective-permute-start(bf16[128,576]{1,0:T(8,128)(2,1)S(1)} %add_convert_fusion.2), channel_id=1, source_target_pairs={{0,4},{1,5},{2,6},{3,7},{4,0},{5,1},{6,2},{7,3},{8,10},{9,11},{10,... | collective-permute-start | bytes 442376 | tf_op jit(solution)/shard_map/ppermute | solution.py:44
  52.5 0.0 copy-done
  52.5 1.1 %copy.12 = bf16[1,16,64,128]{3,2,1,0:T(8,128)(2,1)} copy(bf16[1,16,64,128]{2,1,3,0:T(8,128)(2,1)S(1)} %bitcast.28) | data formatting | bytes 524288
  53.7 3.2 %collective-permute-done.4 = bf16[128,576]{1,0:T(8,128)(2,1)S(1)} collective-permute-done((bf16[128,576]{1,0:T(8,128)(2,1)S(1)}, bf16[128,576]{1,0:T(8,128)(2,1)S(1)}, u32[]{:S(2)}, u32[]{:S(2)}) %collective-permute-start.4) | collective-permute-done | bytes 147488 | tf_op jit(solution)/shard_map/ppermute | solution.py:44
  56.9 0.7 %slice_bitcast_fusion = bf16[1,128,512]{2,1,0:T(8,128)(2,1)} fusion(bf16[128,576]{1,0:T(8,128)(2,1)S(1)} %add_convert_fusion.1), kind=kLoop, calls=%fused_computation.7 | loop fusion | bytes 262144 | tf_op jit(solution)/shard_map/broadcast_in_dim | solution.py:163
  57.6 0.7 %copy.13 = bf16[1,64,128]{2,1,0:T(8,128)(2,1)} copy(bf16[1,64,128]{1,2,0:T(8,128)(2,1)S(1)} %slice_bitcast_fusion.1) | data formatting | bytes 32768
  (5 shorter events, 0.2 us)
Async XLA Ops:
  27.6 24.9 %copy-start = (bf16[128,16,64]{2,1,0:T(8,128)(2,1)S(1)}, bf16[128,16,64]{2,1,0:T(8,128)(2,1)}, u32[]{:S(2)}) copy-start(bf16[128,16,64]{2,1,0:T(8,128)(2,1)} %get-tuple-element.13) | copy-start | bytes 786436
  27.7 1.8 %collective-permute-start = (bf16[2,128,576]{2,1,0:T(8,128)(2,1)}, bf16[2,128,576]{2,1,0:T(8,128)(2,1)S(1)}, u32[]{:S(2)}, u32[]{:S(2)}) collective-permute-start(bf16[2,128,576]{2,1,0:T(8,128)(2,1)} %get-tuple-element.15), channel_id=1, source_target_pairs={{0,8},{8,0},{16,24},{24,16},{1,9},{9,1},{17,25},{25,17},{2,10},{10... | collective-permute-start | bytes 884744 | tf_op jit(solution)/shard_map/ppermute | solution.py:22
  30.6 8.4 %collective-permute-start.1 = (bf16[128,576]{1,0:T(8,128)(2,1)S(1)}, bf16[128,576]{1,0:T(8,128)(2,1)S(1)}, u32[]{:S(2)}, u32[]{:S(2)}) collective-permute-start(bf16[128,576]{1,0:T(8,128)(2,1)S(1)} %select_bitcast_fusion), channel_id=1, source_target_pairs={{16,0},{24,8},{17,1},{25,9},{18,2},{26,10},{19,3},{27,11},{20,4},{... | collective-permute-start | bytes 442376 | tf_op jit(solution)/shard_map/ppermute | solution.py:27
  39.0 5.4 %collective-permute-start.2 = (bf16[128,576]{1,0:T(8,128)(2,1)S(1)}, bf16[128,576]{1,0:T(8,128)(2,1)S(1)}, u32[]{:S(2)}, u32[]{:S(2)}) collective-permute-start(bf16[128,576]{1,0:T(8,128)(2,1)S(1)} %add_convert_fusion.4), channel_id=1, source_target_pairs={{0,1},{1,0},{2,3},{3,2},{4,5},{5,4},{6,7},{7,6},{8,12},{9,13},{10,... | collective-permute-start | bytes 442376 | tf_op jit(solution)/shard_map/ppermute | solution.py:44
  44.4 5.4 %collective-permute-start.3 = (bf16[128,576]{1,0:T(8,128)(2,1)S(1)}, bf16[128,576]{1,0:T(8,128)(2,1)S(1)}, u32[]{:S(2)}, u32[]{:S(2)}) collective-permute-start(bf16[128,576]{1,0:T(8,128)(2,1)S(1)} %add_convert_fusion.3), channel_id=1, source_target_pairs={{0,2},{1,3},{2,0},{3,1},{4,6},{5,7},{6,4},{7,5},{8,9},{9,8},{10,11... | collective-permute-start | bytes 442376 | tf_op jit(solution)/shard_map/ppermute | solution.py:44
  49.9 7.0 %collective-permute-start.4 = (bf16[128,576]{1,0:T(8,128)(2,1)S(1)}, bf16[128,576]{1,0:T(8,128)(2,1)S(1)}, u32[]{:S(2)}, u32[]{:S(2)}) collective-permute-start(bf16[128,576]{1,0:T(8,128)(2,1)S(1)} %add_convert_fusion.2), channel_id=1, source_target_pairs={{0,4},{1,5},{2,6},{3,7},{4,0},{5,1},{6,2},{7,3},{8,10},{9,11},{10,... | collective-permute-start | bytes 442376 | tf_op jit(solution)/shard_map/ppermute | solution.py:44

commit v20 on v19

--- a/solution.py
+++ b/solution.py
@@ -84,6 +84,28 @@
     lt = lt + lax.dot_general(rounded, dout, tn, preferred_element_type=f32)
     rt = scale_factor * lax.dot_general(score_grad, qr, tn, preferred_element_type=f32)
 
+    block_len = mine_ref.shape[1]
+    n_blocks = length // block_len
+    even = n_blocks % 2 == 0
+    if pl.num_programs(0) == 1 and even:
+        side = (offset_ref[0] // block_len) % 2
+        for slot in range(n_blocks):
+            low, high = 2 * (slot // 2), 2 * (slot // 2) + 1
+            if slot % 2 == 0:
+                pick = side == 0
+                dest = mine_ref
+            else:
+                pick = side == 1
+                dest = theirs_ref
+            for acc, cols in ((lt, slice(None, kvr)), (rt, slice(kvr, None))):
+                block = jnp.where(
+                    pick,
+                    acc[low * block_len:(low + 1) * block_len],
+                    acc[high * block_len:(high + 1) * block_len],
+                )
+                dest[slot // 2, :, cols] = block.astype(jnp.bfloat16)
+        return
+
     @pl.when(step == 0)
     def _():
         lt_acc[...] = lt
@@ -96,9 +118,6 @@
 
     @pl.when(step == pl.num_programs(0) - 1)
     def _():
-        block_len = mine_ref.shape[1]
-        n_blocks = lt_acc.shape[0] // block_len
-        even = n_blocks % 2 == 0
         side = (offset_ref[0] // block_len) % 2 if even else 0
         for slot in range(mine_ref.shape[0]):
             start = (2 * slot + side) * block_len if even else slot * block_len

time: 58.6 us -> 58.4 us (level)
  no operation moved by 1% of the time
where the time goes in v20:
time: 58.4 us; the launch traced here: 58.1 us
  waiting for transfers between devices  19.3 us (33%)
  Pallas kernels  13.1 us (22%)
  blocking collectives  9.78 us (17%)
  starting transfers between devices  7.52 us (13%)
  local copies, waits for them, and re-layouts  5.48 us (9%)
  other arithmetic  2.19 us (4%)
  between operations  0.7 us (1%)
    pallas_call x1, Pallas kernels, body(): pl.pallas_call(attention_kernel, grid_spec=pltpu.PrefetchScalarGridSpec(n...  13.1 us
    ppermute x3, waiting for transfers between devices, butterfly_sum_ep(): theirs = lax.ppermute(mine, ('ctx', 'ep'), pairs)  10.8 us
    all_gather x1, blocking collectives, body(): whole_keys = lax.all_gather(local_keys, 'ctx', axis=0, tiled=True)  9.78 us
    ppermute x1, waiting for transfers between devices, causal_reduce_ctx(): lax.ppermute(sent, 'ctx', [(i, i - 2 * shift) for i in range(2 * shift, n...  7.03 us
    ppermute x3, starting transfers between devices, butterfly_sum_ep(): theirs = lax.ppermute(mine, ('ctx', 'ep'), pairs)  5.89 us
    unnamed x6, local copies, waits for them, and re-layouts  4.81 us
    ppermute x1, waiting for transfers between devices, causal_reduce_ctx(): got = lax.ppermute(theirs, 'ctx', [(i, i ^ 1) for i in range(n_ctx)])  1.49 us
    ppermute x1, starting transfers between devices, causal_reduce_ctx(): lax.ppermute(sent, 'ctx', [(i, i - 2 * shift) for i in range(2 * shift, n...  1.29 us
  transfers between devices with their start and end apart: 5, of which 5 were waited for; matrix products, arithmetic and copies ran while one was open for 2% of the time, Pallas kernels for 0%

profile of v20, /device:TPU:0, one launch (start us, length us, event | category | flops | bytes accessed | tf_op | source)
XLA Modules:
  0.0 58.1 jit_solution(13382317976310286386)
XLA Ops:
  0.6 2.1 %copy.10 = bf16[1,16,64,128]{2,1,3,0:T(8,128)(2,1)} copy(bf16[1,16,64,128]{3,2,1,0:T(8,128)(2,1)} %param.8) | data formatting | bytes 524288 | tf_op args[1]
  2.8 0.8 %copy.11 = bf16[1,64,128]{1,2,0:T(8,128)(2,1)S(1)} copy(bf16[1,64,128]{2,1,0:T(8,128)(2,1)} %param.10) | data formatting | bytes 32768 | tf_op args[3]
  3.6 0.9 %pad_maximum_fusion = bf16[128,576]{1,0:T(8,128)(2,1)S(1)} fusion(bf16[128,64]{1,0:T(8,128)(2,1)S(1)} %bitcast.29, bf16[128,512]{1,0:T(8,128)(2,1)} %bitcast.30), kind=kLoop, calls=%fused_computation.5 | loop fusion | flops 294912 | bytes 294912 | tf_op jit(solution)/shard_map/concatenate | solution.py:141
  4.5 9.8 %all_gather.3.keys_ref = bf16[512,576]{1,0:T(8,128)(2,1)} all-gather(bf16[128,576]{1,0:T(8,128)(2,1)S(1)} %pad_maximum_fusion), channel_id=1, replica_groups=mesh['ctx'=4,'ep'=8] {'ctx'}, dimensions={0}, use_global_device_ids=true | all-gather | bytes 737280 | tf_op jit(solution)/shard_map/all_gather | solution.py:142
  14.3 13.1 %shard_map.92 = (bf16[128,16,512]{2,1,0:T(8,128)(2,1)}, bf16[128,16,512]{2,1,0:T(8,128)(2,1)}, bf16[128,16,64]{2,1,0:T(8,128)(2,1)}, bf16[2,128,576]{2,1,0:T(8,128)(2,1)}, bf16[2,128,576]{2,1,0:T(8,128)(2,1)}) custom-call(s32[1]{0:T(128)} %bitcast.offset_ref, bf16[128,16,512]{2,1,0:T(8,128)(2,1)} %bitcast.25, bf16[128,16,64]{2,1,0:T(8,128)(2,1)} %bitcast.27, ...), custom_call_target="tpu_custom_call" | custom-call | tf_op jit(solution)/shard_map/pallas_call | solution.py:156
  27.4 0.0 copy-start
  27.4 0.3 collective-permute-start
  27.8 1.5 %collective-permute-done = bf16[2,128,576]{2,1,0:T(8,128)(2,1)S(1)} collective-permute-done((bf16[2,128,576]{2,1,0:T(8,128)(2,1)}, bf16[2,128,576]{2,1,0:T(8,128)(2,1)S(1)}, u32[]{:S(2)}, u32[]{:S(2)}) %collective-permute-start) | collective-permute-done | bytes 294944 | tf_op jit(solution)/shard_map/ppermute | solution.py:22
  29.3 1.1 %add_convert_fusion = bf16[2,128,576]{2,1,0:T(8,128)(2,1)S(1)} fusion(bf16[2,128,576]{2,1,0:T(8,128)(2,1)S(1)} %collective-permute-done, bf16[2,128,576]{2,1,0:T(8,128)(2,1)} %get-tuple-element.14), kind=kLoop, calls=%fused_computation | loop fusion | flops 589824 | bytes 884736 | tf_op jit(solution)/shard_map/convert_element_type | solution.py:23
  30.4 1.3 %collective-permute-start.1 = (bf16[128,576]{1,0:T(8,128)(2,1)S(1)}, bf16[128,576]{1,0:T(8,128)(2,1)S(1)}, u32[]{:S(2)}, u32[]{:S(2)}) collective-permute-start(bf16[128,576]{1,0:T(8,128)(2,1)S(1)} %select_bitcast_fusion), channel_id=1, source_target_pairs={{16,0},{24,8},{17,1},{25,9},{18,2},{26,10},{19,3},{27,11},{20,4},{... | collective-permute-start | bytes 442376 | tf_op jit(solution)/shard_map/ppermute | solution.py:27
  31.7 7.0 %collective-permute-done.1 = bf16[128,576]{1,0:T(8,128)(2,1)S(1)} collective-permute-done((bf16[128,576]{1,0:T(8,128)(2,1)S(1)}, bf16[128,576]{1,0:T(8,128)(2,1)S(1)}, u32[]{:S(2)}, u32[]{:S(2)}) %collective-permute-start.1) | collective-permute-done | bytes 147488 | tf_op jit(solution)/shard_map/ppermute | solution.py:27
  38.7 0.1 add_convert_fusion.4
  38.8 1.6 %collective-permute-start.2 = (bf16[128,576]{1,0:T(8,128)(2,1)S(1)}, bf16[128,576]{1,0:T(8,128)(2,1)S(1)}, u32[]{:S(2)}, u32[]{:S(2)}) collective-permute-start(bf16[128,576]{1,0:T(8,128)(2,1)S(1)} %add_convert_fusion.4), channel_id=1, source_target_pairs={{0,1},{1,0},{2,3},{3,2},{4,5},{5,4},{6,7},{7,6},{8,12},{9,13},{10,... | collective-permute-start | bytes 442376 | tf_op jit(solution)/shard_map/ppermute | solution.py:44
  40.4 3.8 %collective-permute-done.2 = bf16[128,576]{1,0:T(8,128)(2,1)S(1)} collective-permute-done((bf16[128,576]{1,0:T(8,128)(2,1)S(1)}, bf16[128,576]{1,0:T(8,128)(2,1)S(1)}, u32[]{:S(2)}, u32[]{:S(2)}) %collective-permute-start.2) | collective-permute-done | bytes 147488 | tf_op jit(solution)/shard_map/ppermute | solution.py:44
  44.2 1.6 %collective-permute-start.3 = (bf16[128,576]{1,0:T(8,128)(2,1)S(1)}, bf16[128,576]{1,0:T(8,128)(2,1)S(1)}, u32[]{:S(2)}, u32[]{:S(2)}) collective-permute-start(bf16[128,576]{1,0:T(8,128)(2,1)S(1)} %add_convert_fusion.3), channel_id=1, source_target_pairs={{0,2},{1,3},{2,0},{3,1},{4,6},{5,7},{6,4},{7,5},{8,9},{9,8},{10,11... | collective-permute-start | bytes 442376 | tf_op jit(solution)/shard_map/ppermute | solution.py:44
  45.9 3.7 %collective-permute-done.3 = bf16[128,576]{1,0:T(8,128)(2,1)S(1)} collective-permute-done((bf16[128,576]{1,0:T(8,128)(2,1)S(1)}, bf16[128,576]{1,0:T(8,128)(2,1)S(1)}, u32[]{:S(2)}, u32[]{:S(2)}) %collective-permute-start.3) | collective-permute-done | bytes 147488 | tf_op jit(solution)/shard_map/ppermute | solution.py:44
  49.6 2.7 %collective-permute-start.4 = (bf16[128,576]{1,0:T(8,128)(2,1)S(1)}, bf16[128,576]{1,0:T(8,128)(2,1)S(1)}, u32[]{:S(2)}, u32[]{:S(2)}) collective-permute-start(bf16[128,576]{1,0:T(8,128)(2,1)S(1)} %add_convert_fusion.2), channel_id=1, source_target_pairs={{0,4},{1,5},{2,6},{3,7},{4,0},{5,1},{6,2},{7,3},{8,10},{9,11},{10,... | collective-permute-start | bytes 442376 | tf_op jit(solution)/shard_map/ppermute | solution.py:44
  52.3 0.0 copy-done
  52.3 1.1 %copy.12 = bf16[1,16,64,128]{3,2,1,0:T(8,128)(2,1)} copy(bf16[1,16,64,128]{2,1,3,0:T(8,128)(2,1)S(1)} %bitcast.28) | data formatting | bytes 524288
  53.4 3.2 %collective-permute-done.4 = bf16[128,576]{1,0:T(8,128)(2,1)S(1)} collective-permute-done((bf16[128,576]{1,0:T(8,128)(2,1)S(1)}, bf16[128,576]{1,0:T(8,128)(2,1)S(1)}, u32[]{:S(2)}, u32[]{:S(2)}) %collective-permute-start.4) | collective-permute-done | bytes 147488 | tf_op jit(solution)/shard_map/ppermute | solution.py:44
  56.7 0.7 %slice_bitcast_fusion = bf16[1,128,512]{2,1,0:T(8,128)(2,1)} fusion(bf16[128,576]{1,0:T(8,128)(2,1)S(1)} %add_convert_fusion.1), kind=kLoop, calls=%fused_computation.7 | loop fusion | bytes 262144 | tf_op jit(solution)/shard_map/broadcast_in_dim | solution.py:182
  57.4 0.7 %copy.13 = bf16[1,64,128]{2,1,0:T(8,128)(2,1)} copy(bf16[1,64,128]{1,2,0:T(8,128)(2,1)S(1)} %slice_bitcast_fusion.1) | data formatting | bytes 32768
  (5 shorter events, 0.2 us)
Async XLA Ops:
  27.4 24.9 %copy-start = (bf16[128,16,64]{2,1,0:T(8,128)(2,1)S(1)}, bf16[128,16,64]{2,1,0:T(8,128)(2,1)}, u32[]{:S(2)}) copy-start(bf16[128,16,64]{2,1,0:T(8,128)(2,1)} %get-tuple-element.13) | copy-start | bytes 786436
  27.4 1.8 %collective-permute-start = (bf16[2,128,576]{2,1,0:T(8,128)(2,1)}, bf16[2,128,576]{2,1,0:T(8,128)(2,1)S(1)}, u32[]{:S(2)}, u32[]{:S(2)}) collective-permute-start(bf16[2,128,576]{2,1,0:T(8,128)(2,1)} %get-tuple-element.15), channel_id=1, source_target_pairs={{0,8},{8,0},{16,24},{24,16},{1,9},{9,1},{17,25},{25,17},{2,10},{10... | collective-permute-start | bytes 884744 | tf_op jit(solution)/shard_map/ppermute | solution.py:22
  30.4 8.3 %collective-permute-start.1 = (bf16[128,576]{1,0:T(8,128)(2,1)S(1)}, bf16[128,576]{1,0:T(8,128)(2,1)S(1)}, u32[]{:S(2)}, u32[]{:S(2)}) collective-permute-start(bf16[128,576]{1,0:T(8,128)(2,1)S(1)} %select_bitcast_fusion), channel_id=1, source_target_pairs={{16,0},{24,8},{17,1},{25,9},{18,2},{26,10},{19,3},{27,11},{20,4},{... | collective-permute-start | bytes 442376 | tf_op jit(solution)/shard_map/ppermute | solution.py:27
  38.8 5.4 %collective-permute-start.2 = (bf16[128,576]{1,0:T(8,128)(2,1)S(1)}, bf16[128,576]{1,0:T(8,128)(2,1)S(1)}, u32[]{:S(2)}, u32[]{:S(2)}) collective-permute-start(bf16[128,576]{1,0:T(8,128)(2,1)S(1)} %add_convert_fusion.4), channel_id=1, source_target_pairs={{0,1},{1,0},{2,3},{3,2},{4,5},{5,4},{6,7},{7,6},{8,12},{9,13},{10,... | collective-permute-start | bytes 442376 | tf_op jit(solution)/shard_map/ppermute | solution.py:44
  44.2 5.4 %collective-permute-start.3 = (bf16[128,576]{1,0:T(8,128)(2,1)S(1)}, bf16[128,576]{1,0:T(8,128)(2,1)S(1)}, u32[]{:S(2)}, u32[]{:S(2)}) collective-permute-start(bf16[128,576]{1,0:T(8,128)(2,1)S(1)} %add_convert_fusion.3), channel_id=1, source_target_pairs={{0,2},{1,3},{2,0},{3,1},{4,6},{5,7},{6,4},{7,5},{8,9},{9,8},{10,11... | collective-permute-start | bytes 442376 | tf_op jit(solution)/shard_map/ppermute | solution.py:44
  49.6 7.0 %collective-permute-start.4 = (bf16[128,576]{1,0:T(8,128)(2,1)S(1)}, bf16[128,576]{1,0:T(8,128)(2,1)S(1)}, u32[]{:S(2)}, u32[]{:S(2)}) collective-permute-start(bf16[128,576]{1,0:T(8,128)(2,1)S(1)} %add_convert_fusion.2), channel_id=1, source_target_pairs={{0,4},{1,5},{2,6},{3,7},{4,0},{5,1},{6,2},{7,3},{8,10},{9,11},{10,... | collective-permute-start | bytes 442376 | tf_op jit(solution)/shard_map/ppermute | solution.py:44

commit v21 on v20

--- a/solution.py
+++ b/solution.py
@@ -47,7 +47,8 @@
 
 
 def attention_kernel(offset_ref, ql_ref, qr_ref, keys_ref, do_ref,
-                     att_ref, lqg_ref, rqg_ref, mine_ref, theirs_ref, lt_acc, rt_acc):
+                     att_hbm, lqg_ref, rqg_ref, mine_ref, theirs_ref, lt_acc, rt_acc,
+                     att_ref, att_sem):
     step = pl.program_id(0)
     t_blk, heads, kvr = ql_ref.shape
     rope = qr_ref.shape[2]
@@ -73,6 +74,8 @@
     rounded = weights.astype(jnp.bfloat16)
     att = jnp.dot(rounded, k, preferred_element_type=f32).astype(jnp.bfloat16)
     att_ref[...] = att.reshape(t_blk, heads, kvr)
+    att_copy = pltpu.make_async_copy(att_ref, att_hbm.at[pl.ds(step * t_blk, t_blk)], att_sem)
+    att_copy.start()
     row_dots = jnp.sum(dout.astype(f32) * att.astype(f32), axis=-1, keepdims=True)
     weight_grad = lax.dot_general(dout, k, nt, preferred_element_type=f32)
     score_grad = (weights * (weight_grad - row_dots)).astype(jnp.bfloat16)
@@ -104,7 +107,9 @@
                     acc[high * block_len:(high + 1) * block_len],
                 )
                 dest[slot // 2, :, cols] = block.astype(jnp.bfloat16)
+        att_copy.wait()
         return
+    att_copy.wait()
 
     @pl.when(step == 0)
     def _():
@@ -159,10 +164,18 @@
             num_scalar_prefetch=1,
             grid=(block_len // t_blk,),
             in_specs=[by_rows, rope_rows, fixed, by_rows],
-            out_specs=[by_rows, by_rows, rope_rows, mine_blocks, their_blocks],
+            out_specs=[
+                pl.BlockSpec(memory_space=pl.ANY),
+                by_rows,
+                rope_rows,
+                mine_blocks,
+                their_blocks,
+            ],
             scratch_shapes=[
                 pltpu.VMEM((length, kvr), jnp.float32),
                 pltpu.VMEM((length, rope), jnp.float32),
+                pltpu.VMEM((t_blk, heads, kvr), jnp.bfloat16),
+                pltpu.SemaphoreType.DMA,
             ],
         ),
         out_shape=[

time: 58.4 us -> 59.3 us (1.015)
  Pallas kernels: 13.1 us -> 14 us
    pallas_call x1, Pallas kernels: 13.1 us -> 14 us  [body(): pl.pallas_call(attention_kernel, grid_spec=pltpu.PrefetchScalarGridSpec(n...]
where the time goes in v21:
time: 59.3 us; the launch traced here: 59 us
  waiting for transfers between devices  19.3 us (33%)
  Pallas kernels  14 us (24%)
  blocking collectives  9.78 us (16%)
  starting transfers between devices  7.59 us (13%)
  local copies, waits for them, and re-layouts  5.48 us (9%)
  other arithmetic  2.19 us (4%)
  between operations  0.71 us (1%)
    pallas_call x1, Pallas kernels, body(): pl.pallas_call(attention_kernel, grid_spec=pltpu.PrefetchScalarGridSpec(n...  14 us
    ppermute x3, waiting for transfers between devices, butterfly_sum_ep(): theirs = lax.ppermute(mine, ('ctx', 'ep'), pairs)  10.8 us
    all_gather x1, blocking collectives, body(): whole_keys = lax.all_gather(local_keys, 'ctx', axis=0, tiled=True)  9.78 us
    ppermute x1, waiting for transfers between devices, causal_reduce_ctx(): lax.ppermute(sent, 'ctx', [(i, i - 2 * shift) for i in range(2 * shift, n...  7.03 us
    ppermute x3, starting transfers between devices, butterfly_sum_ep(): theirs = lax.ppermute(mine, ('ctx', 'ep'), pairs)  5.89 us
    unnamed x6, local copies, waits for them, and re-layouts  4.81 us
    ppermute x1, waiting for transfers between devices, causal_reduce_ctx(): got = lax.ppermute(theirs, 'ctx', [(i, i ^ 1) for i in range(n_ctx)])  1.49 us
    ppermute x1, starting transfers between devices, causal_reduce_ctx(): lax.ppermute(sent, 'ctx', [(i, i - 2 * shift) for i in range(2 * shift, n...  1.29 us
  transfers between devices with their start and end apart: 5, of which 5 were waited for; matrix products, arithmetic and copies ran while one was open for 2% of the time, Pallas kernels for 0%

profile of v21, /device:TPU:0, one launch (start us, length us, event | category | flops | bytes accessed | tf_op | source)
XLA Modules:
  0.0 59.0 jit_solution(3631882960671107580)
XLA Ops:
  0.6 2.1 %copy.10 = bf16[1,16,64,128]{2,1,3,0:T(8,128)(2,1)} copy(bf16[1,16,64,128]{3,2,1,0:T(8,128)(2,1)} %param.8) | data formatting | bytes 524288 | tf_op args[1]
  2.8 0.8 %copy.11 = bf16[1,64,128]{1,2,0:T(8,128)(2,1)S(1)} copy(bf16[1,64,128]{2,1,0:T(8,128)(2,1)} %param.10) | data formatting | bytes 32768 | tf_op args[3]
  3.6 0.9 %pad_maximum_fusion = bf16[128,576]{1,0:T(8,128)(2,1)S(1)} fusion(bf16[128,64]{1,0:T(8,128)(2,1)S(1)} %bitcast.29, bf16[128,512]{1,0:T(8,128)(2,1)} %bitcast.30), kind=kLoop, calls=%fused_computation.5 | loop fusion | flops 294912 | bytes 294912 | tf_op jit(solution)/shard_map/concatenate | solution.py:146
  4.5 9.8 %all_gather.3.keys_ref = bf16[512,576]{1,0:T(8,128)(2,1)} all-gather(bf16[128,576]{1,0:T(8,128)(2,1)S(1)} %pad_maximum_fusion), channel_id=1, replica_groups=mesh['ctx'=4,'ep'=8] {'ctx'}, dimensions={0}, use_global_device_ids=true | all-gather | bytes 737280 | tf_op jit(solution)/shard_map/all_gather | solution.py:147
  14.3 14.0 %shard_map.92 = (bf16[128,16,512]{2,1,0:T(8,128)(2,1)}, bf16[128,16,512]{2,1,0:T(8,128)(2,1)}, bf16[128,16,64]{2,1,0:T(8,128)(2,1)}, bf16[2,128,576]{2,1,0:T(8,128)(2,1)}, bf16[2,128,576]{2,1,0:T(8,128)(2,1)}) custom-call(s32[1]{0:T(128)} %bitcast.offset_ref, bf16[128,16,512]{2,1,0:T(8,128)(2,1)} %bitcast.25, bf16[128,16,64]{2,1,0:T(8,128)(2,1)} %bitcast.27, ...), custom_call_target="tpu_custom_call" | custom-call | tf_op jit(solution)/shard_map/pallas_call | solution.py:161
  28.3 0.0 copy-start
  28.3 0.4 collective-permute-start
  28.7 1.5 %collective-permute-done = bf16[2,128,576]{2,1,0:T(8,128)(2,1)S(1)} collective-permute-done((bf16[2,128,576]{2,1,0:T(8,128)(2,1)}, bf16[2,128,576]{2,1,0:T(8,128)(2,1)S(1)}, u32[]{:S(2)}, u32[]{:S(2)}) %collective-permute-start) | collective-permute-done | bytes 294944 | tf_op jit(solution)/shard_map/ppermute | solution.py:22
  30.2 1.1 %add_convert_fusion = bf16[2,128,576]{2,1,0:T(8,128)(2,1)S(1)} fusion(bf16[2,128,576]{2,1,0:T(8,128)(2,1)S(1)} %collective-permute-done, bf16[2,128,576]{2,1,0:T(8,128)(2,1)} %get-tuple-element.14), kind=kLoop, calls=%fused_computation | loop fusion | flops 589824 | bytes 884736 | tf_op jit(solution)/shard_map/convert_element_type | solution.py:23
  31.3 1.3 %collective-permute-start.1 = (bf16[128,576]{1,0:T(8,128)(2,1)S(1)}, bf16[128,576]{1,0:T(8,128)(2,1)S(1)}, u32[]{:S(2)}, u32[]{:S(2)}) collective-permute-start(bf16[128,576]{1,0:T(8,128)(2,1)S(1)} %select_bitcast_fusion), channel_id=1, source_target_pairs={{16,0},{24,8},{17,1},{25,9},{18,2},{26,10},{19,3},{27,11},{20,4},{... | collective-permute-start | bytes 442376 | tf_op jit(solution)/shard_map/ppermute | solution.py:27
  32.6 7.0 %collective-permute-done.1 = bf16[128,576]{1,0:T(8,128)(2,1)S(1)} collective-permute-done((bf16[128,576]{1,0:T(8,128)(2,1)S(1)}, bf16[128,576]{1,0:T(8,128)(2,1)S(1)}, u32[]{:S(2)}, u32[]{:S(2)}) %collective-permute-start.1) | collective-permute-done | bytes 147488 | tf_op jit(solution)/shard_map/ppermute | solution.py:27
  39.7 0.1 add_convert_fusion.4
  39.7 1.6 %collective-permute-start.2 = (bf16[128,576]{1,0:T(8,128)(2,1)S(1)}, bf16[128,576]{1,0:T(8,128)(2,1)S(1)}, u32[]{:S(2)}, u32[]{:S(2)}) collective-permute-start(bf16[128,576]{1,0:T(8,128)(2,1)S(1)} %add_convert_fusion.4), channel_id=1, source_target_pairs={{0,1},{1,0},{2,3},{3,2},{4,5},{5,4},{6,7},{7,6},{8,12},{9,13},{10,... | collective-permute-start | bytes 442376 | tf_op jit(solution)/shard_map/ppermute | solution.py:44
  41.3 3.8 %collective-permute-done.2 = bf16[128,576]{1,0:T(8,128)(2,1)S(1)} collective-permute-done((bf16[128,576]{1,0:T(8,128)(2,1)S(1)}, bf16[128,576]{1,0:T(8,128)(2,1)S(1)}, u32[]{:S(2)}, u32[]{:S(2)}) %collective-permute-start.2) | collective-permute-done | bytes 147488 | tf_op jit(solution)/shard_map/ppermute | solution.py:44
  45.2 1.6 %collective-permute-start.3 = (bf16[128,576]{1,0:T(8,128)(2,1)S(1)}, bf16[128,576]{1,0:T(8,128)(2,1)S(1)}, u32[]{:S(2)}, u32[]{:S(2)}) collective-permute-start(bf16[128,576]{1,0:T(8,128)(2,1)S(1)} %add_convert_fusion.3), channel_id=1, source_target_pairs={{0,2},{1,3},{2,0},{3,1},{4,6},{5,7},{6,4},{7,5},{8,9},{9,8},{10,11... | collective-permute-start | bytes 442376 | tf_op jit(solution)/shard_map/ppermute | solution.py:44
  46.8 3.7 %collective-permute-done.3 = bf16[128,576]{1,0:T(8,128)(2,1)S(1)} collective-permute-done((bf16[128,576]{1,0:T(8,128)(2,1)S(1)}, bf16[128,576]{1,0:T(8,128)(2,1)S(1)}, u32[]{:S(2)}, u32[]{:S(2)}) %collective-permute-start.3) | collective-permute-done | bytes 147488 | tf_op jit(solution)/shard_map/ppermute | solution.py:44
  50.6 2.7 %collective-permute-start.4 = (bf16[128,576]{1,0:T(8,128)(2,1)S(1)}, bf16[128,576]{1,0:T(8,128)(2,1)S(1)}, u32[]{:S(2)}, u32[]{:S(2)}) collective-permute-start(bf16[128,576]{1,0:T(8,128)(2,1)S(1)} %add_convert_fusion.2), channel_id=1, source_target_pairs={{0,4},{1,5},{2,6},{3,7},{4,0},{5,1},{6,2},{7,3},{8,10},{9,11},{10,... | collective-permute-start | bytes 442376 | tf_op jit(solution)/shard_map/ppermute | solution.py:44
  53.2 0.0 copy-done
  53.3 1.1 %copy.12 = bf16[1,16,64,128]{3,2,1,0:T(8,128)(2,1)} copy(bf16[1,16,64,128]{2,1,3,0:T(8,128)(2,1)S(1)} %bitcast.28) | data formatting | bytes 524288
  54.4 3.2 %collective-permute-done.4 = bf16[128,576]{1,0:T(8,128)(2,1)S(1)} collective-permute-done((bf16[128,576]{1,0:T(8,128)(2,1)S(1)}, bf16[128,576]{1,0:T(8,128)(2,1)S(1)}, u32[]{:S(2)}, u32[]{:S(2)}) %collective-permute-start.4) | collective-permute-done | bytes 147488 | tf_op jit(solution)/shard_map/ppermute | solution.py:44
  57.7 0.7 %slice_bitcast_fusion = bf16[1,128,512]{2,1,0:T(8,128)(2,1)} fusion(bf16[128,576]{1,0:T(8,128)(2,1)S(1)} %add_convert_fusion.1), kind=kLoop, calls=%fused_computation.7 | loop fusion | bytes 262144 | tf_op jit(solution)/shard_map/broadcast_in_dim | solution.py:195
  58.3 0.7 %copy.13 = bf16[1,64,128]{2,1,0:T(8,128)(2,1)} copy(bf16[1,64,128]{1,2,0:T(8,128)(2,1)S(1)} %slice_bitcast_fusion.1) | data formatting | bytes 32768
  (5 shorter events, 0.2 us)
Async XLA Ops:
  28.3 24.9 %copy-start = (bf16[128,16,64]{2,1,0:T(8,128)(2,1)S(1)}, bf16[128,16,64]{2,1,0:T(8,128)(2,1)}, u32[]{:S(2)}) copy-start(bf16[128,16,64]{2,1,0:T(8,128)(2,1)} %get-tuple-element.13) | copy-start | bytes 786436
  28.3 1.9 %collective-permute-start = (bf16[2,128,576]{2,1,0:T(8,128)(2,1)}, bf16[2,128,576]{2,1,0:T(8,128)(2,1)S(1)}, u32[]{:S(2)}, u32[]{:S(2)}) collective-permute-start(bf16[2,128,576]{2,1,0:T(8,128)(2,1)} %get-tuple-element.15), channel_id=1, source_target_pairs={{0,8},{8,0},{16,24},{24,16},{1,9},{9,1},{17,25},{25,17},{2,10},{10... | collective-permute-start | bytes 884744 | tf_op jit(solution)/shard_map/ppermute | solution.py:22
  31.3 8.3 %collective-permute-start.1 = (bf16[128,576]{1,0:T(8,128)(2,1)S(1)}, bf16[128,576]{1,0:T(8,128)(2,1)S(1)}, u32[]{:S(2)}, u32[]{:S(2)}) collective-permute-start(bf16[128,576]{1,0:T(8,128)(2,1)S(1)} %select_bitcast_fusion), channel_id=1, source_target_pairs={{16,0},{24,8},{17,1},{25,9},{18,2},{26,10},{19,3},{27,11},{20,4},{... | collective-permute-start | bytes 442376 | tf_op jit(solution)/shard_map/ppermute | solution.py:27
  39.7 5.4 %collective-permute-start.2 = (bf16[128,576]{1,0:T(8,128)(2,1)S(1)}, bf16[128,576]{1,0:T(8,128)(2,1)S(1)}, u32[]{:S(2)}, u32[]{:S(2)}) collective-permute-start(bf16[128,576]{1,0:T(8,128)(2,1)S(1)} %add_convert_fusion.4), channel_id=1, source_target_pairs={{0,1},{1,0},{2,3},{3,2},{4,5},{5,4},{6,7},{7,6},{8,12},{9,13},{10,... | collective-permute-start | bytes 442376 | tf_op jit(solution)/shard_map/ppermute | solution.py:44
  45.2 5.4 %collective-permute-start.3 = (bf16[128,576]{1,0:T(8,128)(2,1)S(1)}, bf16[128,576]{1,0:T(8,128)(2,1)S(1)}, u32[]{:S(2)}, u32[]{:S(2)}) collective-permute-start(bf16[128,576]{1,0:T(8,128)(2,1)S(1)} %add_convert_fusion.3), channel_id=1, source_target_pairs={{0,2},{1,3},{2,0},{3,1},{4,6},{5,7},{6,4},{7,5},{8,9},{9,8},{10,11... | collective-permute-start | bytes 442376 | tf_op jit(solution)/shard_map/ppermute | solution.py:44
  50.6 7.0 %collective-permute-start.4 = (bf16[128,576]{1,0:T(8,128)(2,1)S(1)}, bf16[128,576]{1,0:T(8,128)(2,1)S(1)}, u32[]{:S(2)}, u32[]{:S(2)}) collective-permute-start(bf16[128,576]{1,0:T(8,128)(2,1)S(1)} %add_convert_fusion.2), channel_id=1, source_target_pairs={{0,4},{1,5},{2,6},{3,7},{4,0},{5,1},{6,2},{7,3},{8,10},{9,11},{10,... | collective-permute-start | bytes 442376 | tf_op jit(solution)/shard_map/ppermute | solution.py:44

commit v22 on v20

--- a/solution.py
+++ b/solution.py
@@ -33,7 +33,7 @@
     if n_ep & (n_ep - 1):
         return lax.psum(total.astype(jnp.bfloat16), "ep").astype(jnp.float32)
     bits = [1 << k for k in range(n_ep.bit_length() - 1)]
-    orders = [bits, bits[-1:] + bits[:-1]]
+    orders = [bits[1:2] + bits[:1] + bits[2:], bits[:1] + bits[2:] + bits[1:2]]
     for step in range(len(bits)):
         pairs = [
             (c * n_ep + e, c * n_ep + (e ^ orders[c % 2][step]))

time: 58.4 us -> 58.4 us (level)
  no operation moved by 1% of the time
where the time goes in v22:
time: 58.4 us; the launch traced here: 58.1 us
  waiting for transfers between devices  19.3 us (33%)
  Pallas kernels  13.1 us (22%)
  blocking collectives  9.78 us (17%)
  starting transfers between devices  7.52 us (13%)
  local copies, waits for them, and re-layouts  5.48 us (9%)
  other arithmetic  2.19 us (4%)
  between operations  0.7 us (1%)
    pallas_call x1, Pallas kernels, body(): pl.pallas_call(attention_kernel, grid_spec=pltpu.PrefetchScalarGridSpec(n...  13.1 us
    ppermute x3, waiting for transfers between devices, butterfly_sum_ep(): theirs = lax.ppermute(mine, ('ctx', 'ep'), pairs)  10.8 us
    all_gather x1, blocking collectives, body(): whole_keys = lax.all_gather(local_keys, 'ctx', axis=0, tiled=True)  9.78 us
    ppermute x1, waiting for transfers between devices, causal_reduce_ctx(): lax.ppermute(sent, 'ctx', [(i, i - 2 * shift) for i in range(2 * shift, n...  7.03 us
    ppermute x3, starting transfers between devices, butterfly_sum_ep(): theirs = lax.ppermute(mine, ('ctx', 'ep'), pairs)  5.89 us
    unnamed x6, local copies, waits for them, and re-layouts  4.81 us
    ppermute x1, waiting for transfers between devices, causal_reduce_ctx(): got = lax.ppermute(theirs, 'ctx', [(i, i ^ 1) for i in range(n_ctx)])  1.49 us
    ppermute x1, starting transfers between devices, causal_reduce_ctx(): lax.ppermute(sent, 'ctx', [(i, i - 2 * shift) for i in range(2 * shift, n...  1.29 us
  transfers between devices with their start and end apart: 5, of which 5 were waited for; matrix products, arithmetic and copies ran while one was open for 2% of the time, Pallas kernels for 0%

profile of v22, /device:TPU:0, one launch (start us, length us, event | category | flops | bytes accessed | tf_op | source)
XLA Modules:
  0.0 58.1 jit_solution(3476697427366411268)
XLA Ops:
  0.6 2.1 %copy.10 = bf16[1,16,64,128]{2,1,3,0:T(8,128)(2,1)} copy(bf16[1,16,64,128]{3,2,1,0:T(8,128)(2,1)} %param.8) | data formatting | bytes 524288 | tf_op args[1]
  2.8 0.8 %copy.11 = bf16[1,64,128]{1,2,0:T(8,128)(2,1)S(1)} copy(bf16[1,64,128]{2,1,0:T(8,128)(2,1)} %param.10) | data formatting | bytes 32768 | tf_op args[3]
  3.6 0.9 %pad_maximum_fusion = bf16[128,576]{1,0:T(8,128)(2,1)S(1)} fusion(bf16[128,64]{1,0:T(8,128)(2,1)S(1)} %bitcast.29, bf16[128,512]{1,0:T(8,128)(2,1)} %bitcast.30), kind=kLoop, calls=%fused_computation.5 | loop fusion | flops 294912 | bytes 294912 | tf_op jit(solution)/shard_map/concatenate | solution.py:141
  4.5 9.8 %all_gather.3.keys_ref = bf16[512,576]{1,0:T(8,128)(2,1)} all-gather(bf16[128,576]{1,0:T(8,128)(2,1)S(1)} %pad_maximum_fusion), channel_id=1, replica_groups=mesh['ctx'=4,'ep'=8] {'ctx'}, dimensions={0}, use_global_device_ids=true | all-gather | bytes 737280 | tf_op jit(solution)/shard_map/all_gather | solution.py:142
  14.3 13.1 %shard_map.92 = (bf16[128,16,512]{2,1,0:T(8,128)(2,1)}, bf16[128,16,512]{2,1,0:T(8,128)(2,1)}, bf16[128,16,64]{2,1,0:T(8,128)(2,1)}, bf16[2,128,576]{2,1,0:T(8,128)(2,1)}, bf16[2,128,576]{2,1,0:T(8,128)(2,1)}) custom-call(s32[1]{0:T(128)} %bitcast.offset_ref, bf16[128,16,512]{2,1,0:T(8,128)(2,1)} %bitcast.25, bf16[128,16,64]{2,1,0:T(8,128)(2,1)} %bitcast.27, ...), custom_call_target="tpu_custom_call" | custom-call | tf_op jit(solution)/shard_map/pallas_call | solution.py:156
  27.4 0.0 copy-start
  27.4 0.3 collective-permute-start
  27.8 1.5 %collective-permute-done = bf16[2,128,576]{2,1,0:T(8,128)(2,1)S(1)} collective-permute-done((bf16[2,128,576]{2,1,0:T(8,128)(2,1)}, bf16[2,128,576]{2,1,0:T(8,128)(2,1)S(1)}, u32[]{:S(2)}, u32[]{:S(2)}) %collective-permute-start) | collective-permute-done | bytes 294944 | tf_op jit(solution)/shard_map/ppermute | solution.py:22
  29.3 1.1 %add_convert_fusion = bf16[2,128,576]{2,1,0:T(8,128)(2,1)S(1)} fusion(bf16[2,128,576]{2,1,0:T(8,128)(2,1)S(1)} %collective-permute-done, bf16[2,128,576]{2,1,0:T(8,128)(2,1)} %get-tuple-element.14), kind=kLoop, calls=%fused_computation | loop fusion | flops 589824 | bytes 884736 | tf_op jit(solution)/shard_map/convert_element_type | solution.py:23
  30.4 1.3 %collective-permute-start.1 = (bf16[128,576]{1,0:T(8,128)(2,1)S(1)}, bf16[128,576]{1,0:T(8,128)(2,1)S(1)}, u32[]{:S(2)}, u32[]{:S(2)}) collective-permute-start(bf16[128,576]{1,0:T(8,128)(2,1)S(1)} %select_bitcast_fusion), channel_id=1, source_target_pairs={{16,0},{24,8},{17,1},{25,9},{18,2},{26,10},{19,3},{27,11},{20,4},{... | collective-permute-start | bytes 442376 | tf_op jit(solution)/shard_map/ppermute | solution.py:27
  31.7 7.0 %collective-permute-done.1 = bf16[128,576]{1,0:T(8,128)(2,1)S(1)} collective-permute-done((bf16[128,576]{1,0:T(8,128)(2,1)S(1)}, bf16[128,576]{1,0:T(8,128)(2,1)S(1)}, u32[]{:S(2)}, u32[]{:S(2)}) %collective-permute-start.1) | collective-permute-done | bytes 147488 | tf_op jit(solution)/shard_map/ppermute | solution.py:27
  38.7 0.1 add_convert_fusion.4
  38.8 1.6 %collective-permute-start.2 = (bf16[128,576]{1,0:T(8,128)(2,1)S(1)}, bf16[128,576]{1,0:T(8,128)(2,1)S(1)}, u32[]{:S(2)}, u32[]{:S(2)}) collective-permute-start(bf16[128,576]{1,0:T(8,128)(2,1)S(1)} %add_convert_fusion.4), channel_id=1, source_target_pairs={{0,2},{1,3},{2,0},{3,1},{4,6},{5,7},{6,4},{7,5},{8,9},{9,8},{10,11... | collective-permute-start | bytes 442376 | tf_op jit(solution)/shard_map/ppermute | solution.py:44
  40.4 3.7 %collective-permute-done.2 = bf16[128,576]{1,0:T(8,128)(2,1)S(1)} collective-permute-done((bf16[128,576]{1,0:T(8,128)(2,1)S(1)}, bf16[128,576]{1,0:T(8,128)(2,1)S(1)}, u32[]{:S(2)}, u32[]{:S(2)}) %collective-permute-start.2) | collective-permute-done | bytes 147488 | tf_op jit(solution)/shard_map/ppermute | solution.py:44
  44.2 1.6 %collective-permute-start.3 = (bf16[128,576]{1,0:T(8,128)(2,1)S(1)}, bf16[128,576]{1,0:T(8,128)(2,1)S(1)}, u32[]{:S(2)}, u32[]{:S(2)}) collective-permute-start(bf16[128,576]{1,0:T(8,128)(2,1)S(1)} %add_convert_fusion.3), channel_id=1, source_target_pairs={{0,1},{1,0},{2,3},{3,2},{4,5},{5,4},{6,7},{7,6},{8,12},{9,13},{10,... | collective-permute-start | bytes 442376 | tf_op jit(solution)/shard_map/ppermute | solution.py:44
  45.8 3.8 %collective-permute-done.3 = bf16[128,576]{1,0:T(8,128)(2,1)S(1)} collective-permute-done((bf16[128,576]{1,0:T(8,128)(2,1)S(1)}, bf16[128,576]{1,0:T(8,128)(2,1)S(1)}, u32[]{:S(2)}, u32[]{:S(2)}) %collective-permute-start.3) | collective-permute-done | bytes 147488 | tf_op jit(solution)/shard_map/ppermute | solution.py:44
  49.6 2.7 %collective-permute-start.4 = (bf16[128,576]{1,0:T(8,128)(2,1)S(1)}, bf16[128,576]{1,0:T(8,128)(2,1)S(1)}, u32[]{:S(2)}, u32[]{:S(2)}) collective-permute-start(bf16[128,576]{1,0:T(8,128)(2,1)S(1)} %add_convert_fusion.2), channel_id=1, source_target_pairs={{0,4},{1,5},{2,6},{3,7},{4,0},{5,1},{6,2},{7,3},{8,10},{9,11},{10,... | collective-permute-start | bytes 442376 | tf_op jit(solution)/shard_map/ppermute | solution.py:44
  52.3 0.0 copy-done
  52.3 1.1 %copy.12 = bf16[1,16,64,128]{3,2,1,0:T(8,128)(2,1)} copy(bf16[1,16,64,128]{2,1,3,0:T(8,128)(2,1)S(1)} %bitcast.28) | data formatting | bytes 524288
  53.4 3.3 %collective-permute-done.4 = bf16[128,576]{1,0:T(8,128)(2,1)S(1)} collective-permute-done((bf16[128,576]{1,0:T(8,128)(2,1)S(1)}, bf16[128,576]{1,0:T(8,128)(2,1)S(1)}, u32[]{:S(2)}, u32[]{:S(2)}) %collective-permute-start.4) | collective-permute-done | bytes 147488 | tf_op jit(solution)/shard_map/ppermute | solution.py:44
  56.8 0.7 %slice_bitcast_fusion = bf16[1,128,512]{2,1,0:T(8,128)(2,1)} fusion(bf16[128,576]{1,0:T(8,128)(2,1)S(1)} %add_convert_fusion.1), kind=kLoop, calls=%fused_computation.7 | loop fusion | bytes 262144 | tf_op jit(solution)/shard_map/broadcast_in_dim | solution.py:182
  57.4 0.7 %copy.13 = bf16[1,64,128]{2,1,0:T(8,128)(2,1)} copy(bf16[1,64,128]{1,2,0:T(8,128)(2,1)S(1)} %slice_bitcast_fusion.1) | data formatting | bytes 32768
  (5 shorter events, 0.2 us)
Async XLA Ops:
  27.4 24.9 %copy-start = (bf16[128,16,64]{2,1,0:T(8,128)(2,1)S(1)}, bf16[128,16,64]{2,1,0:T(8,128)(2,1)}, u32[]{:S(2)}) copy-start(bf16[128,16,64]{2,1,0:T(8,128)(2,1)} %get-tuple-element.13) | copy-start | bytes 786436
  27.4 1.8 %collective-permute-start = (bf16[2,128,576]{2,1,0:T(8,128)(2,1)}, bf16[2,128,576]{2,1,0:T(8,128)(2,1)S(1)}, u32[]{:S(2)}, u32[]{:S(2)}) collective-permute-start(bf16[2,128,576]{2,1,0:T(8,128)(2,1)} %get-tuple-element.15), channel_id=1, source_target_pairs={{0,8},{8,0},{16,24},{24,16},{1,9},{9,1},{17,25},{25,17},{2,10},{10... | collective-permute-start | bytes 884744 | tf_op jit(solution)/shard_map/ppermute | solution.py:22
  30.4 8.3 %collective-permute-start.1 = (bf16[128,576]{1,0:T(8,128)(2,1)S(1)}, bf16[128,576]{1,0:T(8,128)(2,1)S(1)}, u32[]{:S(2)}, u32[]{:S(2)}) collective-permute-start(bf16[128,576]{1,0:T(8,128)(2,1)S(1)} %select_bitcast_fusion), channel_id=1, source_target_pairs={{16,0},{24,8},{17,1},{25,9},{18,2},{26,10},{19,3},{27,11},{20,4},{... | collective-permute-start | bytes 442376 | tf_op jit(solution)/shard_map/ppermute | solution.py:27
  38.8 5.4 %collective-permute-start.2 = (bf16[128,576]{1,0:T(8,128)(2,1)S(1)}, bf16[128,576]{1,0:T(8,128)(2,1)S(1)}, u32[]{:S(2)}, u32[]{:S(2)}) collective-permute-start(bf16[128,576]{1,0:T(8,128)(2,1)S(1)} %add_convert_fusion.4), channel_id=1, source_target_pairs={{0,2},{1,3},{2,0},{3,1},{4,6},{5,7},{6,4},{7,5},{8,9},{9,8},{10,11... | collective-permute-start | bytes 442376 | tf_op jit(solution)/shard_map/ppermute | solution.py:44
  44.2 5.4 %collective-permute-start.3 = (bf16[128,576]{1,0:T(8,128)(2,1)S(1)}, bf16[128,576]{1,0:T(8,128)(2,1)S(1)}, u32[]{:S(2)}, u32[]{:S(2)}) collective-permute-start(bf16[128,576]{1,0:T(8,128)(2,1)S(1)} %add_convert_fusion.3), channel_id=1, source_target_pairs={{0,1},{1,0},{2,3},{3,2},{4,5},{5,4},{6,7},{7,6},{8,12},{9,13},{10,... | collective-permute-start | bytes 442376 | tf_op jit(solution)/shard_map/ppermute | solution.py:44
  49.6 7.1 %collective-permute-start.4 = (bf16[128,576]{1,0:T(8,128)(2,1)S(1)}, bf16[128,576]{1,0:T(8,128)(2,1)S(1)}, u32[]{:S(2)}, u32[]{:S(2)}) collective-permute-start(bf16[128,576]{1,0:T(8,128)(2,1)S(1)} %add_convert_fusion.2), channel_id=1, source_target_pairs={{0,4},{1,5},{2,6},{3,7},{4,0},{5,1},{6,2},{7,3},{8,10},{9,11},{10,... | collective-permute-start | bytes 442376 | tf_op jit(solution)/shard_map/ppermute | solution.py:44
